TPU v7x, 128 devices: a whole 4x4x4 slice. The times are simulated.
128 devices in a mesh: lon: 16 (over y_hi, z, core), lat: 8 (over y_lo, x).
Axes of the slice: x: 4, y: 4 (y_hi: 2, y_lo: 2; y = y_hi * 2 + y_lo), z: 4, core: 2. Of those that a mesh axis runs over, the one named last changes fastest.
Arguments:
- temp_before: float32 [25, 512, 2048], P(None, 'lat', 'lon'), may hold values from -8 to 8
- temp_now: float32 [25, 512, 2048], P(None, 'lat', 'lon'), may hold values from -8 to 8
- salt_before: float32 [25, 512, 2048], P(None, 'lat', 'lon'), may hold values from -4 to 4
- salt_now: float32 [25, 512, 2048], P(None, 'lat', 'lon'), may hold values from -4 to 4
- east_velocity: float32 [25, 512, 2048], P(None, 'lat', 'lon'), may hold values from -0.3 to 0.3, as said below
- north_velocity: float32 [25, 512, 2048], P(None, 'lat', 'lon'), may hold values from -0.3 to 0.3, as said below
- bottom_level: int32 [512, 2048], P('lat', 'lon'), may hold values from 0 to 25, as said below
Outputs:
- temp_out: float32 [25, 512, 2048], P(None, 'lat', 'lon')
- salt_out: float32 [25, 512, 2048], P(None, 'lat', 'lon')
- density_out: float32 [25, 512, 2048], P(None, 'lat', 'lon')
Inputs may be any that keep to these rules, and one draw needn't show every extreme that they name: `bottom_level`: cells at levels below a column's value are ocean, the others land; every column of row 0 is land. `east_velocity`: zero on every face that touches a land cell; the face east of column 2047 touches column 0. `north_velocity`: zero on every face that touches a land cell; on row 511 the north face of column i touches cell (511, 2047 - i) and carries the negative of that column's value.
All inputs are finite; a program needn't handle non-finite values.
Results may differ from a plain program's by a relative error of at most 0.00002.
Values sent between devices are 32-bit elements; how exact they have to be, the bound alone decides.
No kernel may reach another device: no remote copies, remote signals or barrier semaphores. Data moves between devices by JAX's collectives and lax.ppermute only.
A program may use at most 256 MiB of HBM per device.

v0:
```python
import jax
import jax.numpy as jnp
from jax import lax
from jax.sharding import PartitionSpec as P

asselin_gamma = 0.1
nu_base = 0.05
nu_conv = 0.2
level_depth = 160.0
alpha_zero = 0.1655
beta_zero = 0.76554
lambda_one = 0.05952
lambda_two = 0.00054914
mu_one = 0.0001497
mu_two = 1.109e-05
nu_cross = 0.0024341


def extended_2(value, sides, width, wrap):
    for axis, dim in sides:
        count, length = (lax.axis_size(axis), value.shape[dim])
        up = [(i, (i + 1) % count) for i in range(count if wrap else count - 1)]
        down = [(j, i) for i, j in up]
        last = lax.slice_in_dim(value, length - width, length, axis=dim)
        leading = lax.slice_in_dim(value, 0, width, axis=dim)
        before = lax.ppermute(last, axis, up)
        after = lax.ppermute(leading, axis, down)
        value = jnp.concatenate([before, value, after], axis=dim)
    return value


def passed_along(block, axis, distance):
    devices = range(lax.axis_size(axis))
    route = [((i - distance) % len(devices), i) for i in devices]
    return lax.ppermute(block, axis, route)


def from_behind(value, axis, by):
    count = lax.axis_size(axis)
    pairs = [(i, i + by) for i in range(count) if 0 <= i + by < count]
    return lax.ppermute(value, axis, pairs)


def density(temp, salt):
    depth = level_depth * (jnp.arange(temp.shape[0], dtype=jnp.float32) + 0.5)[:, None, None]
    warm = -alpha_zero * (1.0 + 0.5 * lambda_one * temp + mu_one * depth) * temp
    salty = beta_zero * (1.0 - 0.5 * lambda_two * salt - mu_two * depth) * salt
    return warm + salty - nu_cross * temp * salt


def divergence(extended, velocity, along):
    face_count = velocity.shape[along - 1]
    behind_far = lax.slice_in_dim(extended, 0, face_count, axis=along)
    behind = lax.slice_in_dim(extended, 1, face_count + 1, axis=along)
    ahead = lax.slice_in_dim(extended, 2, face_count + 2, axis=along)
    ahead_far = lax.slice_in_dim(extended, 3, face_count + 3, axis=along)
    flux = velocity * (7.0 * (behind + ahead) - (behind_far + ahead_far)) / 12.0
    flux = flux + jnp.abs(velocity) * (ahead_far - behind_far - 3.0 * (ahead - behind)) / 12.0
    return lax.slice_in_dim(flux, 1, face_count, axis=along) - lax.slice_in_dim(
        flux, 0, face_count - 1, axis=along
    )


def vertical_mixing(before, now, ocean_mask):
    density_now = density(now[0], now[1])
    density_jump = density_now[1:] - density_now[:-1]
    mixing_rates = (nu_base + nu_conv * jax.nn.sigmoid(-4.0 * density_jump)) * ocean_mask[1:]
    flux = mixing_rates * (before[:, 1:] - before[:, :-1])
    padding = jnp.zeros_like(flux[:, :1])
    return jnp.concatenate([flux, padding], 1) - jnp.concatenate([padding, flux], 1)


def advance(before, now, x_ext, y_ext, east_faces, north_faces, ocean_mask):
    change = -(divergence(x_ext, east_faces, 3) + divergence(y_ext, north_faces, 2))
    change = change + vertical_mixing(before, now, ocean_mask)
    after = (before + 2.0 * change) * ocean_mask
    filtered = now + asselin_gamma * (before - 2.0 * now + after)
    return (filtered, after)


def extend_tracers(now, at_fold, columns):
    x_ext = extended_2(now, (("lon", 3),), 2, True)
    y_part = extended_2(now, (("lat", 2),), 2, False)
    edge_rows = now[:, :, -2:, :]
    cycle_size = lax.axis_size("lon")
    pieces = edge_rows.reshape(
        edge_rows.shape[0], edge_rows.shape[1], 2, cycle_size, columns // cycle_size
    )
    spread = lax.all_to_all(pieces, "lon", split_axis=3, concat_axis=3, tiled=True)
    returned = lax.all_to_all(
        spread[:, :, :, ::-1, :], "lon", split_axis=3, concat_axis=3, tiled=True
    )
    partner_rows = returned.reshape(edge_rows.shape)
    mirror = partner_rows[:, :, ::-1, ::-1]
    north_rows = jnp.where(at_fold, mirror, y_part[:, :, -2:, :])
    y_ext = jnp.concatenate([y_part[:, :, :-2, :], north_rows], 2)
    return (x_ext, y_ext)


def on_device(
    temp_before, temp_now, salt_before, salt_now, east_velocity, north_velocity, bottom_level
):
    levels = temp_now.shape[0]
    columns = temp_now.shape[2]
    ocean_mask = (jnp.arange(levels, dtype=jnp.int32)[:, None, None] < bottom_level[None]).astype(
        jnp.float32
    )
    before = jnp.stack([temp_before, salt_before]) * ocean_mask
    now = jnp.stack([temp_now, salt_now]) * ocean_mask
    west_column = passed_along(east_velocity[:, :, -1:], "lon", 1)
    east_faces = jnp.concatenate([west_column, east_velocity], 2)
    south_row = from_behind(north_velocity[:, -1:, :], "lat", 1)
    north_faces = jnp.concatenate([south_row, north_velocity], 1)
    at_fold = lax.axis_index("lat") == lax.axis_size("lat") - 1
    for step_index in range(2):
        x_ext, y_ext = extend_tracers(now, at_fold, columns)
        before, now = advance(before, now, x_ext, y_ext, east_faces, north_faces, ocean_mask)
    final_density = density(now[0], now[1]) * ocean_mask
    return (now[0], now[1], final_density)


def solution(mesh):
    return jax.shard_map(
        on_device,
        mesh=mesh,
        in_specs=(
            P(None, "lat", "lon"),
            P(None, "lat", "lon"),
            P(None, "lat", "lon"),
            P(None, "lat", "lon"),
            P(None, "lat", "lon"),
            P(None, "lat", "lon"),
            P("lat", "lon"),
        ),
        out_specs=(P(None, "lat", "lon"), P(None, "lat", "lon"), P(None, "lat", "lon")),
        check_vma=False,
    )
```

profile of v0, /device:TPU:8, one launch (start us, length us, event | category | flops | bytes accessed | tf_op | source)
XLA Modules:
  0.0 145.8 jit_solution(7164898051214208194)
XLA Ops:
  0.7 1.6 %slice.173 = f32[25,1,128]{2,1,0:T(1,128)} slice(f32[25,64,128]{2,1,0:T(8,128)} %param.12), slice={[0:25], [63:64], [0:128]} | slice | bytes 25600 | tf_op jit(solution)/shard_map/slice | solution.py:112
  2.2 3.4 %collective-permute-start.3 = (f32[25,1,128]{2,1,0:T(1,128)}, f32[25,1,128]{2,1,0:T(1,128)}, u32[]{:S(2)}, u32[]{:S(2)}) collective-permute-start(f32[25,1,128]{2,1,0:T(1,128)} %slice.173), channel_id=1, source_target_pairs={{0,1},{1,2},{2,3},{3,4},{4,5},{5,6},{6,7},{8,9},{9,10},{10,11},{11... | collective-permute-start | bytes 38408 | tf_op jit(solution)/shard_map/ppermute | solution.py:41
  5.6 1.4 slice.164
  7.6 3.6 %maximum_multiply_fusion.1 = (f32[2,25,64,128]{3,2,1,0:T(8,128)}, f32[2,25,64,128]{3,2,1,0:T(8,128)S(1)}) fusion(f32[1,25,64,128]{3,2,1,0:T(8,128)S(1)} %bitcast.54, f32[1,25,64,128]{3,2,1,0:T(8,128)} %bitcast.55, f32[25,64,128]{2,1,0:T(8,128)S(1)} %fusion.14, f32[1,25,64,128]{3,2,1,0:T(8,128)} %bitcast.56, f32[1,25,64,128]{3,2,1,0:T(8,128)} %bitcast.57), kind=kLoop, calls=%fused_computation.37 | loop fusion | flops 1638400 | bytes 7372800 | tf_op jit(solution)/shard_map/mul | solution.py:108
  11.9 4.5 %collective-permute-start.5 = (f32[2,25,2,128]{3,2,1,0:T(2,128)}, f32[2,25,2,128]{3,2,1,0:T(2,128)}, u32[]{:S(2)}, u32[]{:S(2)}) collective-permute-start(f32[2,25,2,128]{3,2,1,0:T(2,128)} %get-tuple-element.25), channel_id=1, source_target_pairs={{1,0},{2,1},{3,2},{4,3},{5,4},{6,5},{7,6},{9,8},{10,9},{11,10},{12... | collective-permute-start | bytes 153608 | tf_op jit(solution)/shard_map/ppermute | solution.py:27
  16.5 1.9 %collective-permute-start.4 = (f32[2,25,2,128]{3,2,1,0:T(2,128)}, f32[2,25,2,128]{3,2,1,0:T(2,128)}, u32[]{:S(2)}, u32[]{:S(2)}) collective-permute-start(f32[2,25,2,128]{3,2,1,0:T(2,128)} %get-tuple-element.26), channel_id=1, source_target_pairs={{0,1},{1,2},{2,3},{3,4},{4,5},{5,6},{6,7},{8,9},{9,10},{10,11},{11... | collective-permute-start | bytes 153608 | tf_op jit(solution)/shard_map/ppermute | solution.py:26
  18.4 0.9 copy.99
  19.4 0.9 reshape.71
  20.3 8.0 %all-to-all-start = ((f32[16,1,800]{2,1,0:T(1,128)}), f32[16,1,800]{2,1,0:T(1,128)S(1)}, u32[]{:S(2)}, u32[]{:S(2)}) async-start(f32[16,1,800]{2,1,0:T(1,128)} %reshape.71), calls=%async_computation | async-start | bytes 114688 | tf_op jit(solution)/shard_map/all_to_all | solution.py:89
  28.3 2.3 %fusion.34 = (f32[2,25,64,2]{3,2,1,0:T(8,128)}, f32[2,25,64,2]{3,2,1,0:T(8,128)}) fusion(f32[2,25,64,128]{3,2,1,0:T(8,128)S(1)} %get-tuple-element.30), kind=kLoop, calls=%fused_computation.83 | loop fusion | bytes 102400 | tf_op jit(solution)/shard_map/slice | solution.py:25
  30.6 2.0 %copy.95 = f32[2,25,64,2]{2,3,1,0:T(2,128)S(1)} copy(f32[2,25,64,2]{3,2,1,0:T(8,128)} %get-tuple-element.24) | data formatting | bytes 51200 | tf_op jit(solution)/shard_map/slice | solution.py:24
  33.7 1.2 copy-done.3
  34.9 1.5 %fusion.13 = f32[2,24,64,128]{3,2,1,0:T(8,128)} fusion(f32[2,25,64,128]{3,2,1,0:T(8,128)S(1)} %copy-done.3, f32[24,64,128]{2,1,0:T(8,128)S(1)} %add_multiply_fusion.5), kind=kLoop, calls=%fused_computation.43 | loop fusion | flops 786432 | bytes 5505024 | tf_op jit(solution)/shard_map/mul | solution.py:68
  37.4 5.0 %collective-permute-start.2 = (f32[2,25,64,2]{2,3,1,0:T(2,128)S(1)}, f32[2,25,64,2]{2,3,1,0:T(2,128)S(1)}, u32[]{:S(2)}, u32[]{:S(2)}) collective-permute-start(f32[2,25,64,2]{2,3,1,0:T(2,128)S(1)} %copy.97), channel_id=1, source_target_pairs={{8,0},{16,8},{24,16},{32,24},{40,32},{48,40},{56,48},{64,56},{72,6... | collective-permute-start | bytes 76808 | tf_op jit(solution)/shard_map/ppermute | solution.py:27
  42.4 1.9 %copy.94 = f32[25,64,1]{2,1,0:T(8,128)} copy(f32[25,64,1]{1,0,2:T(8,128)} %collective-permute-done) | data formatting | bytes 12800 | tf_op jit(solution)/shard_map/ppermute | solution.py:35
  44.4 3.1 %pad_maximum_fusion.8 = (f32[25,64,129]{2,1,0:T(8,128)S(1)}, f32[25,64,129]{2,1,0:T(8,128)}) fusion(f32[25,64,128]{2,1,0:T(8,128)} %param.11, f32[25,64,1]{2,1,0:T(8,128)} %copy.94), kind=kLoop, calls=%fused_computation.38 | loop fusion | flops 412800 | bytes 2476800 | tf_op jit(solution)/shard_map/concatenate | solution.py:111
  47.5 2.1 %pad_maximum_fusion.9 = (f32[25,65,128]{2,1,0:T(8,128)}, f32[25,65,128]{2,1,0:T(8,128)}) fusion(f32[25,64,128]{2,1,0:T(8,128)S(1)} %copy-done.12, f32[25,1,128]{2,1,0:T(1,128)} %collective-permute-done.3), kind=kLoop, calls=%fused_computation.44 | loop fusion | flops 416000 | bytes 2496000 | tf_op jit(solution)/shard_map/concatenate | solution.py:113
  49.6 1.7 %copy.98 = f32[2,25,64,2]{3,2,1,0:T(8,128)} copy(f32[2,25,64,2]{2,3,1,0:T(2,128)S(1)} %collective-permute-done.2) | data formatting | bytes 51200 | tf_op jit(solution)/shard_map/ppermute | solution.py:27
  51.4 1.8 %copy.96 = f32[2,25,64,2]{3,2,1,0:T(8,128)} copy(f32[2,25,64,2]{2,3,1,0:T(2,128)S(1)} %collective-permute-done.1) | data formatting | bytes 51200 | tf_op jit(solution)/shard_map/ppermute | solution.py:26
  53.7 1.4 reduce
  55.1 1.1 reshape.72
  56.9 1.8 %reshape.73 = f32[16,1,800]{2,1,0:T(1,128)} reshape(f32[16,2,2,8,25]{4,3,2,1,0:T(8,128)} %reverse_bitcast_fusion.1) | data formatting | bytes 102400
  58.7 4.8 %all-to-all-start.1 = ((f32[16,1,800]{2,1,0:T(1,128)}), f32[16,1,800]{2,1,0:T(1,128)S(1)}, u32[]{:S(2)}, u32[]{:S(2)}) async-start(f32[16,1,800]{2,1,0:T(1,128)} %reshape.73), calls=%async_computation.1 | async-start | bytes 114688 | tf_op jit(solution)/shard_map/all_to_all | solution.py:90
  63.5 7.0 %add_multiply_fusion.1 = f32[2,25,64,129]{3,2,1,0:T(8,128)} fusion(f32[2,25,64,128]{3,2,1,0:T(8,128)S(1)} %get-tuple-element.30, f32[2,25,64,2]{3,2,1,0:T(8,128)} %copy.96, f32[2,25,64,2]{3,2,1,0:T(8,128)} %copy.98, f32[25,64,129]{2,1,0:T(8,128)} %get-tuple-element.22, f32[25,64,129]{2,1,0:T(8,128)S(1)} %get-tuple-element.21), kind=kLoop, calls=%fused_computation.9 | loop fusion | flops 6604800 | bytes 4992000 | tf_op jit(solution)/shard_map/add | solution.py:58
  71.2 0.7 reduce.1
  72.6 0.8 broadcast_select_fusion.1
  73.5 2.6 %add_multiply_fusion.3 = f32[2,25,65,128]{3,2,1,0:T(8,128)S(1)} fusion(f32[2,25,64,128]{3,2,1,0:T(8,128)S(1)} %get-tuple-element.30, f32[2,25,2,128]{3,2,1,0:T(2,128)} %collective-permute-done.4, f32[2,25,2,128]{3,2,1,0:T(2,128)S(1)} %broadcast_select_fusion.1, f32[25,65,128]{2,1,0:T(8,128)} %get-tuple-element.28, f32[25,65,128]{2,1,0:T(8,128)S(1)} %copy-done.8), kind=kLoop, calls=%fused_computation.19 | loop fusion | flops 6656000 | bytes 5068800 | tf_op jit(solution)/shard_map/add | solution.py:58
  76.2 5.1 %multiply_add_fusion = (f32[2,25,64,128]{3,2,1,0:T(8,128)}, f32[2,25,64,128]{3,2,1,0:T(8,128)S(1)}) fusion(f32[2,25,64,128]{3,2,1,0:T(8,128)S(1)} %get-tuple-element.30, f32[2,25,64,128]{3,2,1,0:T(8,128)S(1)} %copy-done.4, f32[25,64,128]{2,1,0:T(8,128)S(1)} %copy-done.1, f32[2,24,64,128]{3,2,1,0:T(8,128)S(1)} %copy-done.10, ...), kind=kLoop, calls=%fused_computation.39 | loop fusion | flops 5734400 | bytes 15499264 | tf_op jit(solution)/shard_map/add | solution.py:77
  81.9 2.5 %collective-permute-start.8 = (f32[2,25,2,128]{3,2,1,0:T(2,128)}, f32[2,25,2,128]{3,2,1,0:T(2,128)}, u32[]{:S(2)}, u32[]{:S(2)}) collective-permute-start(f32[2,25,2,128]{3,2,1,0:T(2,128)} %get-tuple-element.20), channel_id=1, source_target_pairs={{0,1},{1,2},{2,3},{3,4},{4,5},{5,6},{6,7},{8,9},{9,10},{10,11},{11... | collective-permute-start | bytes 153608 | tf_op jit(solution)/shard_map/ppermute | solution.py:26
  84.4 0.9 copy.107
  85.8 2.3 %fusion.32 = (f32[2,25,64,2]{3,2,1,0:T(8,128)}, f32[2,25,64,2]{3,2,1,0:T(8,128)}) fusion(f32[2,25,64,128]{3,2,1,0:T(8,128)S(1)} %get-tuple-element.16), kind=kLoop, calls=%fused_computation.81 | loop fusion | bytes 102400 | tf_op jit(solution)/shard_map/slice | solution.py:25
  88.1 5.8 %collective-permute-start.9 = (f32[2,25,2,128]{3,2,1,0:T(2,128)}, f32[2,25,2,128]{3,2,1,0:T(2,128)}, u32[]{:S(2)}, u32[]{:S(2)}) collective-permute-start(f32[2,25,2,128]{3,2,1,0:T(2,128)} %get-tuple-element.19), channel_id=1, source_target_pairs={{1,0},{2,1},{3,2},{4,3},{5,4},{6,5},{7,6},{9,8},{10,9},{11,10},{12... | collective-permute-start | bytes 153608 | tf_op jit(solution)/shard_map/ppermute | solution.py:27
  94.6 1.8 %reshape.75 = f32[16,1,800]{2,1,0:T(1,128)} reshape(f32[16,2,2,8,25]{4,3,2,1,0:T(8,128)} %copy_bitcast_fusion.2) | data formatting | bytes 102400
  96.4 6.4 %all-to-all-start.2 = ((f32[16,1,800]{2,1,0:T(1,128)}), f32[16,1,800]{2,1,0:T(1,128)S(1)}, u32[]{:S(2)}, u32[]{:S(2)}) async-start(f32[16,1,800]{2,1,0:T(1,128)} %reshape.75), calls=%async_computation.2 | async-start | bytes 114688 | tf_op jit(solution)/shard_map/all_to_all | solution.py:89
  102.8 1.1 add_multiply_fusion.4
  103.9 2.1 %copy.105 = f32[2,25,64,2]{2,3,1,0:T(2,128)S(1)} copy(f32[2,25,64,2]{3,2,1,0:T(8,128)} %get-tuple-element.17) | data formatting | bytes 51200 | tf_op jit(solution)/shard_map/slice | solution.py:25
  105.9 2.0 %copy.103 = f32[2,25,64,2]{2,3,1,0:T(2,128)S(1)} copy(f32[2,25,64,2]{3,2,1,0:T(8,128)} %get-tuple-element.18) | data formatting | bytes 51200 | tf_op jit(solution)/shard_map/slice | solution.py:24
  108.4 5.0 %collective-permute-start.7 = (f32[2,25,64,2]{2,3,1,0:T(2,128)S(1)}, f32[2,25,64,2]{2,3,1,0:T(2,128)S(1)}, u32[]{:S(2)}, u32[]{:S(2)}) collective-permute-start(f32[2,25,64,2]{2,3,1,0:T(2,128)S(1)} %copy.105), channel_id=1, source_target_pairs={{8,0},{16,8},{24,16},{32,24},{40,32},{48,40},{56,48},{64,56},{72,6... | collective-permute-start | bytes 76808 | tf_op jit(solution)/shard_map/ppermute | solution.py:27
  113.4 3.6 %fusion.12 = f32[2,24,64,128]{3,2,1,0:T(8,128)} fusion(f32[2,25,64,128]{3,2,1,0:T(8,128)} %get-tuple-element.15, f32[24,64,128]{2,1,0:T(8,128)S(1)} %copy-done.11), kind=kLoop, calls=%fused_computation.41 | loop fusion | flops 786432 | bytes 5505024 | tf_op jit(solution)/shard_map/mul | solution.py:68
  116.9 1.7 %copy.106 = f32[2,25,64,2]{3,2,1,0:T(8,128)} copy(f32[2,25,64,2]{2,3,1,0:T(2,128)S(1)} %collective-permute-done.7) | data formatting | bytes 51200 | tf_op jit(solution)/shard_map/ppermute | solution.py:27
  118.7 1.8 %copy.104 = f32[2,25,64,2]{3,2,1,0:T(8,128)} copy(f32[2,25,64,2]{2,3,1,0:T(2,128)S(1)} %collective-permute-done.6) | data formatting | bytes 51200 | tf_op jit(solution)/shard_map/ppermute | solution.py:26
  121.5 0.9 reshape.77
  122.4 5.4 %all-to-all-start.3 = ((f32[16,1,800]{2,1,0:T(1,128)}), f32[16,1,800]{2,1,0:T(1,128)S(1)}, u32[]{:S(2)}, u32[]{:S(2)}) async-start(f32[16,1,800]{2,1,0:T(1,128)} %reshape.77), calls=%async_computation.3 | async-start | bytes 114688 | tf_op jit(solution)/shard_map/all_to_all | solution.py:90
  127.8 7.2 %add_multiply_fusion = f32[2,25,64,129]{3,2,1,0:T(8,128)} fusion(f32[2,25,64,128]{3,2,1,0:T(8,128)S(1)} %get-tuple-element.16, f32[2,25,64,2]{3,2,1,0:T(8,128)} %copy.104, f32[2,25,64,2]{3,2,1,0:T(8,128)} %copy.106, f32[25,64,129]{2,1,0:T(8,128)} %get-tuple-element.22, f32[25,64,129]{2,1,0:T(8,128)} %copy-done.6), kind=kLoop, calls=%fused_computation.8 | loop fusion | flops 6604800 | bytes 4992000 | tf_op jit(solution)/shard_map/add | solution.py:58
  136.9 0.8 broadcast_select_fusion
  137.8 2.7 %add_multiply_fusion.2 = f32[2,25,65,128]{3,2,1,0:T(8,128)S(1)} fusion(f32[2,25,64,128]{3,2,1,0:T(8,128)S(1)} %get-tuple-element.16, f32[2,25,2,128]{3,2,1,0:T(2,128)} %collective-permute-done.8, f32[2,25,2,128]{3,2,1,0:T(2,128)S(1)} %broadcast_select_fusion, f32[25,65,128]{2,1,0:T(8,128)} %get-tuple-element.28, f32[25,65,128]{2,1,0:T(8,128)} %get-tuple-element.27), kind=kLoop, calls=%fused_computation.18 | loop fusion | flops 6656000 | bytes 5068800 | tf_op jit(solution)/shard_map/add | solution.py:58
  140.8 3.2 %fusion.5 = f32[2,25,64,128]{3,2,1,0:T(8,128)S(1)} fusion(f32[2,25,64,128]{3,2,1,0:T(8,128)S(1)} %copy-done.5, f32[2,25,65,128]{3,2,1,0:T(8,128)S(1)} %add_multiply_fusion.2, f32[2,25,64,129]{3,2,1,0:T(8,128)S(1)} %copy-done.7, f32[2,24,64,128]{3,2,1,0:T(8,128)} %fusion.12, f32[25,64,128]{2,1,0:T(8,128)S(1)} %copy-done.2), kind=kLoop, calls=%fused_computation.26 | loop fusion | flops 3686400 | bytes 12222464 | tf_op jit(solution)/shard_map/mul | solution.py:76
  144.0 1.9 %subtract_select_fusion = (f32[25,64,128]{2,1,0:T(8,128)}, f32[25,64,128]{2,1,0:T(8,128)}, f32[25,64,128]{2,1,0:T(8,128)}) fusion(f32[25]{0:T(128)S(1)} %get-tuple-element.31, f32[25]{0:T(128)S(1)} %get-tuple-element.32, s32[64,128]{1,0:T(8,128)S(1)} %copy-done.15, f32[2,25,64,128]{3,2,1,0:T(8,128)S(1)} %fusion.5), kind=kLoop, calls=%fused_computation.51 | loop fusion | flops 3276800 | bytes 4128968 | tf_op jit(solution)/shard_map/mul | solution.py:118
  (73 shorter events, 11.4 us)
Async XLA Ops:
  0.6 6.9 %copy-start.14 = (s32[64,128]{1,0:T(8,128)S(1)}, s32[64,128]{1,0:T(8,128)}, u32[]{:S(2)}) copy-start(s32[64,128]{1,0:T(8,128)} %param.13) | copy-start | bytes 98308
  0.6 7.0 %copy-start.13 = (f32[25,64,128]{2,1,0:T(8,128)S(1)}, f32[25,64,128]{2,1,0:T(8,128)}, u32[]{:S(2)}) copy-start(f32[25,64,128]{2,1,0:T(8,128)} %param.9) | copy-start | bytes 2457604
  2.2 45.3 %collective-permute-start.3 = (f32[25,1,128]{2,1,0:T(1,128)}, f32[25,1,128]{2,1,0:T(1,128)}, u32[]{:S(2)}, u32[]{:S(2)}) collective-permute-start(f32[25,1,128]{2,1,0:T(1,128)} %slice.173), channel_id=1, source_target_pairs={{0,1},{1,2},{2,3},{3,4},{4,5},{5,6},{6,7},{8,9},{9,10},{10,11},{11... | collective-permute-start | bytes 38408 | tf_op jit(solution)/shard_map/ppermute | solution.py:41
  7.4 30.0 %collective-permute-start = (f32[25,64,1]{1,0,2:T(8,128)S(1)}, f32[25,64,1]{1,0,2:T(8,128)}, u32[]{:S(2)}, u32[]{:S(2)}) collective-permute-start(f32[25,64,1]{1,0,2:T(8,128)S(1)} %copy.111), channel_id=1, source_target_pairs={{120,0},{0,8},{8,16},{16,24},{24,32},{32,40},{40,48},{48,56},{56,6... | collective-permute-start | bytes 19208 | tf_op jit(solution)/shard_map/ppermute | solution.py:35
  7.6 25.8 %copy-start = (f32[25,64,128]{2,1,0:T(8,128)}, f32[25,64,128]{2,1,0:T(8,128)S(1)}, u32[]{:S(2)}) copy-start(f32[25,64,128]{2,1,0:T(8,128)S(1)} %fusion.14) | copy-start | bytes 2457604
  11.9 60.7 %collective-permute-start.5 = (f32[2,25,2,128]{3,2,1,0:T(2,128)}, f32[2,25,2,128]{3,2,1,0:T(2,128)}, u32[]{:S(2)}, u32[]{:S(2)}) collective-permute-start(f32[2,25,2,128]{3,2,1,0:T(2,128)} %get-tuple-element.25), channel_id=1, source_target_pairs={{1,0},{2,1},{3,2},{4,3},{5,4},{6,5},{7,6},{9,8},{10,9},{11,10},{12... | collective-permute-start | bytes 153608 | tf_op jit(solution)/shard_map/ppermute | solution.py:27
  16.5 57.0 %collective-permute-start.4 = (f32[2,25,2,128]{3,2,1,0:T(2,128)}, f32[2,25,2,128]{3,2,1,0:T(2,128)}, u32[]{:S(2)}, u32[]{:S(2)}) collective-permute-start(f32[2,25,2,128]{3,2,1,0:T(2,128)} %get-tuple-element.26), channel_id=1, source_target_pairs={{0,1},{1,2},{2,3},{3,4},{4,5},{5,6},{6,7},{8,9},{9,10},{10,11},{11... | collective-permute-start | bytes 153608 | tf_op jit(solution)/shard_map/ppermute | solution.py:26
  20.3 32.9 %all-to-all-start = ((f32[16,1,800]{2,1,0:T(1,128)}), f32[16,1,800]{2,1,0:T(1,128)S(1)}, u32[]{:S(2)}, u32[]{:S(2)}) async-start(f32[16,1,800]{2,1,0:T(1,128)} %reshape.71), calls=%async_computation | async-start | bytes 114688 | tf_op jit(solution)/shard_map/all_to_all | solution.py:89
  32.5 18.8 %collective-permute-start.1 = (f32[2,25,64,2]{2,3,1,0:T(2,128)S(1)}, f32[2,25,64,2]{2,3,1,0:T(2,128)S(1)}, u32[]{:S(2)}, u32[]{:S(2)}) collective-permute-start(f32[2,25,64,2]{2,3,1,0:T(2,128)S(1)} %copy.95), channel_id=1, source_target_pairs={{0,8},{8,16},{16,24},{24,32},{32,40},{40,48},{48,56},{56,64},{64,7... | collective-permute-start | bytes 76808 | tf_op jit(solution)/shard_map/ppermute | solution.py:26
  33.4 1.4 copy-start.3
  34.9 2.0 %copy-start.9 = (f32[2,25,64,2]{3,2,1,0:T(8,128)S(1)}, f32[2,25,64,2]{3,2,1,0:T(8,128)}, u32[]{:S(2)}) copy-start(f32[2,25,64,2]{3,2,1,0:T(8,128)} %get-tuple-element.23) | copy-start | bytes 76804
  37.4 12.2 %collective-permute-start.2 = (f32[2,25,64,2]{2,3,1,0:T(2,128)S(1)}, f32[2,25,64,2]{2,3,1,0:T(2,128)S(1)}, u32[]{:S(2)}, u32[]{:S(2)}) collective-permute-start(f32[2,25,64,2]{2,3,1,0:T(2,128)S(1)} %copy.97), channel_id=1, source_target_pairs={{8,0},{16,8},{24,16},{32,24},{40,32},{48,40},{56,48},{64,56},{72,6... | collective-permute-start | bytes 76808 | tf_op jit(solution)/shard_map/ppermute | solution.py:27
  44.4 3.1 %copy-start.12 = (f32[25,64,128]{2,1,0:T(8,128)S(1)}, f32[25,64,128]{2,1,0:T(8,128)}, u32[]{:S(2)}) copy-start(f32[25,64,128]{2,1,0:T(8,128)} %param.12) | copy-start | bytes 2457604
  47.5 16.0 %copy-start.6 = (f32[25,64,129]{2,1,0:T(8,128)}, f32[25,64,129]{2,1,0:T(8,128)S(1)}, u32[]{:S(2)}) copy-start(f32[25,64,129]{2,1,0:T(8,128)S(1)} %get-tuple-element.21) | copy-start | bytes 2476804
  58.7 12.5 %all-to-all-start.1 = ((f32[16,1,800]{2,1,0:T(1,128)}), f32[16,1,800]{2,1,0:T(1,128)S(1)}, u32[]{:S(2)}, u32[]{:S(2)}) async-start(f32[16,1,800]{2,1,0:T(1,128)} %reshape.73), calls=%async_computation.1 | async-start | bytes 114688 | tf_op jit(solution)/shard_map/all_to_all | solution.py:90
  70.6 2.9 %copy-start.8 = (f32[25,65,128]{2,1,0:T(8,128)S(1)}, f32[25,65,128]{2,1,0:T(8,128)}, u32[]{:S(2)}) copy-start(f32[25,65,128]{2,1,0:T(8,128)} %get-tuple-element.27) | copy-start | bytes 2496004
  73.5 2.6 %copy-start.1 = (f32[25,64,128]{2,1,0:T(8,128)S(1)}, f32[25,64,128]{2,1,0:T(8,128)}, u32[]{:S(2)}) copy-start(f32[25,64,128]{2,1,0:T(8,128)} %copy-done) | copy-start | bytes 2457604
  73.5 2.6 %copy-start.4 = (f32[2,25,64,128]{3,2,1,0:T(8,128)S(1)}, f32[2,25,64,128]{3,2,1,0:T(8,128)}, u32[]{:S(2)}) copy-start(f32[2,25,64,128]{3,2,1,0:T(8,128)} %get-tuple-element.29) | copy-start | bytes 4915204
  73.5 2.6 %copy-start.10 = (f32[2,24,64,128]{3,2,1,0:T(8,128)S(1)}, f32[2,24,64,128]{3,2,1,0:T(8,128)}, u32[]{:S(2)}) copy-start(f32[2,24,64,128]{3,2,1,0:T(8,128)} %fusion.13) | copy-start | bytes 4718596
  81.9 55.9 %collective-permute-start.8 = (f32[2,25,2,128]{3,2,1,0:T(2,128)}, f32[2,25,2,128]{3,2,1,0:T(2,128)}, u32[]{:S(2)}, u32[]{:S(2)}) collective-permute-start(f32[2,25,2,128]{3,2,1,0:T(2,128)} %get-tuple-element.20), channel_id=1, source_target_pairs={{0,1},{1,2},{2,3},{3,4},{4,5},{5,6},{6,7},{8,9},{9,10},{10,11},{11... | collective-permute-start | bytes 153608 | tf_op jit(solution)/shard_map/ppermute | solution.py:26
  85.8 17.0 %copy-start.2 = (f32[25,64,128]{2,1,0:T(8,128)S(1)}, f32[25,64,128]{2,1,0:T(8,128)}, u32[]{:S(2)}) copy-start(f32[25,64,128]{2,1,0:T(8,128)} %copy-done) | copy-start | bytes 2457604
  88.1 48.8 %collective-permute-start.9 = (f32[2,25,2,128]{3,2,1,0:T(2,128)}, f32[2,25,2,128]{3,2,1,0:T(2,128)}, u32[]{:S(2)}, u32[]{:S(2)}) collective-permute-start(f32[2,25,2,128]{3,2,1,0:T(2,128)} %get-tuple-element.19), channel_id=1, source_target_pairs={{1,0},{2,1},{3,2},{4,3},{5,4},{6,5},{7,6},{9,8},{10,9},{11,10},{12... | collective-permute-start | bytes 153608 | tf_op jit(solution)/shard_map/ppermute | solution.py:27
  96.4 24.1 %all-to-all-start.2 = ((f32[16,1,800]{2,1,0:T(1,128)}), f32[16,1,800]{2,1,0:T(1,128)S(1)}, u32[]{:S(2)}, u32[]{:S(2)}) async-start(f32[16,1,800]{2,1,0:T(1,128)} %reshape.75), calls=%async_computation.2 | async-start | bytes 114688 | tf_op jit(solution)/shard_map/all_to_all | solution.py:89
  103.9 9.5 %copy-start.11 = (f32[24,64,128]{2,1,0:T(8,128)S(1)}, f32[24,64,128]{2,1,0:T(8,128)}, u32[]{:S(2)}) copy-start(f32[24,64,128]{2,1,0:T(8,128)} %add_multiply_fusion.4) | copy-start | bytes 2359300
  107.9 10.7 %collective-permute-start.6 = (f32[2,25,64,2]{2,3,1,0:T(2,128)S(1)}, f32[2,25,64,2]{2,3,1,0:T(2,128)S(1)}, u32[]{:S(2)}, u32[]{:S(2)}) collective-permute-start(f32[2,25,64,2]{2,3,1,0:T(2,128)S(1)} %copy.103), channel_id=1, source_target_pairs={{0,8},{8,16},{16,24},{24,32},{32,40},{40,48},{48,56},{56,64},{64,7... | collective-permute-start | bytes 76808 | tf_op jit(solution)/shard_map/ppermute | solution.py:26
  108.4 8.5 %collective-permute-start.7 = (f32[2,25,64,2]{2,3,1,0:T(2,128)S(1)}, f32[2,25,64,2]{2,3,1,0:T(2,128)S(1)}, u32[]{:S(2)}, u32[]{:S(2)}) collective-permute-start(f32[2,25,64,2]{2,3,1,0:T(2,128)S(1)} %copy.105), channel_id=1, source_target_pairs={{8,0},{16,8},{24,16},{32,24},{40,32},{48,40},{56,48},{64,56},{72,6... | collective-permute-start | bytes 76808 | tf_op jit(solution)/shard_map/ppermute | solution.py:27
  122.4 13.1 %all-to-all-start.3 = ((f32[16,1,800]{2,1,0:T(1,128)}), f32[16,1,800]{2,1,0:T(1,128)S(1)}, u32[]{:S(2)}, u32[]{:S(2)}) async-start(f32[16,1,800]{2,1,0:T(1,128)} %reshape.77), calls=%async_computation.3 | async-start | bytes 114688 | tf_op jit(solution)/shard_map/all_to_all | solution.py:90
  137.8 2.8 %copy-start.5 = (f32[2,25,64,128]{3,2,1,0:T(8,128)S(1)}, f32[2,25,64,128]{3,2,1,0:T(8,128)}, u32[]{:S(2)}) copy-start(f32[2,25,64,128]{3,2,1,0:T(8,128)} %get-tuple-element.15) | copy-start | bytes 4915204
  137.8 3.0 %copy-start.7 = (f32[2,25,64,129]{3,2,1,0:T(8,128)S(1)}, f32[2,25,64,129]{3,2,1,0:T(8,128)}, u32[]{:S(2)}) copy-start(f32[2,25,64,129]{3,2,1,0:T(8,128)} %add_multiply_fusion) | copy-start | bytes 4953604
  140.8 3.2 %copy-start.15 = (s32[64,128]{1,0:T(8,128)S(1)}, s32[64,128]{1,0:T(8,128)}, u32[]{:S(2)}) copy-start(s32[64,128]{1,0:T(8,128)} %param.13) | copy-start | bytes 98308
where the time goes:
time: 148 us; the launch traced here: 146 us
  starting transfers between devices  53.7 us (36%)
  other arithmetic  51.1 us (35%)
  local copies, waits for them, and re-layouts  38.8 us (26%)
    ppermute x4, starting transfers between devices, extended_2(): after = lax.ppermute(leading, axis, down)  20.3 us
    add x4, other arithmetic, divergence(): flux + jnp.abs(velocity) * (ahead_far - behind_far - 3.0 * (ahead - behin...  19.6 us
    all_to_all x2, starting transfers between devices, extend_tracers(): lax.all_to_all(pieces, 'lon', split_axis=3, concat_axis=3, tiled=True)  14.4 us
    unnamed x45, local copies, waits for them, and re-layouts  11.2 us
    all_to_all x2, starting transfers between devices, extend_tracers(): lax.all_to_all(spread[:, :, :, ::-1, :], 'lon', split_axis=3, concat_axis...  10.3 us
    slice x6, local copies, waits for them, and re-layouts, extended_2(): leading = lax.slice_in_dim(value, 0, width, axis=dim)  8.48 us
    slice x4, local copies, waits for them, and re-layouts, extended_2(): last = lax.slice_in_dim(value, length - width, length, axis=dim)  5.87 us
    ppermute x4, starting transfers between devices, extended_2(): before = lax.ppermute(last, axis, up)  5.34 us
  transfers between devices with their start and end apart: 14, of which 2 were waited for; matrix products, arithmetic and copies ran while one was open for 48% of the time, Pallas kernels for 0%

commit v1 on v0

--- a/solution.py
+++ b/solution.py
@@ -82,15 +82,10 @@
     x_ext = extended_2(now, (("lon", 3),), 2, True)
     y_part = extended_2(now, (("lat", 2),), 2, False)
     edge_rows = now[:, :, -2:, :]
-    cycle_size = lax.axis_size("lon")
-    pieces = edge_rows.reshape(
-        edge_rows.shape[0], edge_rows.shape[1], 2, cycle_size, columns // cycle_size
-    )
-    spread = lax.all_to_all(pieces, "lon", split_axis=3, concat_axis=3, tiled=True)
-    returned = lax.all_to_all(
-        spread[:, :, :, ::-1, :], "lon", split_axis=3, concat_axis=3, tiled=True
-    )
-    partner_rows = returned.reshape(edge_rows.shape)
+    lon_count, lat_count = (lax.axis_size("lon"), lax.axis_size("lat"))
+    top = lat_count - 1
+    pairs = [(d * lat_count + top, (lon_count - 1 - d) * lat_count + top) for d in range(lon_count)]
+    partner_rows = lax.ppermute(edge_rows, ("lon", "lat"), pairs)
     mirror = partner_rows[:, :, ::-1, ::-1]
     north_rows = jnp.where(at_fold, mirror, y_part[:, :, -2:, :])
     y_ext = jnp.concatenate([y_part[:, :, :-2, :], north_rows], 2)

time: 148 us -> 246 us (1.66)
  the two profiles are of different devices: /device:TPU:8 before, /device:TPU:12 now
where the time goes in v1:
time: 246 us; the launch traced here: 241 us
  local copies, waits for them, and re-layouts  130 us (53%)
  other arithmetic  73.9 us (30%)
  starting transfers between devices  34.7 us (14%)
    rev x2, local copies, waits for them, and re-layouts, extend_tracers(): mirror = partner_rows[:, :, ::-1, ::-1]  53.6 us
    add x4, other arithmetic, divergence(): flux + jnp.abs(velocity) * (ahead_far - behind_far - 3.0 * (ahead - behin...  27.9 us
    unnamed x61, local copies, waits for them, and re-layouts  19 us
    ppermute x4, starting transfers between devices, extended_2(): after = lax.ppermute(leading, axis, down)  16.7 us
    slice x6, local copies, waits for them, and re-layouts, extended_2(): leading = lax.slice_in_dim(value, 0, width, axis=dim)  14.2 us
    ppermute x4, starting transfers between devices, extended_2(): before = lax.ppermute(last, axis, up)  10.9 us
    select_n x2, other arithmetic, extend_tracers(): north_rows = jnp.where(at_fold, mirror, y_part[:, :, -2:, :])  8.91 us
    mul x2, other arithmetic, vertical_mixing(): flux = mixing_rates * (before[:, 1:] - before[:, :-1])  8.11 us
  transfers between devices with their start and end apart: 12, of which 1 were waited for; matrix products, arithmetic and copies ran while one was open for 52% of the time, Pallas kernels for 0%

profile of v1, /device:TPU:12, one launch (start us, length us, event | category | flops | bytes accessed | tf_op | source)
XLA Modules:
  0.0 241.0 jit_solution(14937174585200495749)
XLA Ops:
  3.0 2.9 %copy.24 = f32[25,64,128]{1,2,0:T(8,128)} copy(f32[25,64,128]{2,1,0:T(8,128)} %param.8) | data formatting | bytes 1638400 | tf_op args[1]
  5.9 1.8 copy.25
  7.6 1.7 copy.27
  9.3 1.7 copy.28
  11.0 6.7 %maximum_multiply_fusion.1 = (f32[2,25,64,128]{2,3,1,0:T(8,128)}, f32[2,25,64,128]{2,3,1,0:T(8,128)S(1)}) fusion(f32[1,25,64,128]{2,3,1,0:T(8,128)} %bitcast.31, f32[1,25,64,128]{2,3,1,0:T(8,128)} %bitcast.30, f32[25,64,128]{1,2,0:T(8,128)} %fusion.14, f32[1,25,64,128]{2,3,1,0:T(8,128)} %bitcast.29, f32[1,25,64,128]{2,3,1,0:T(8,128)} %bitcast.28), kind=kLoop, calls=%fused_computation.35 | loop fusion | flops 1638400 | bytes 7372800 | tf_op jit(solution)/shard_map/mul | solution.py:103
  17.7 4.0 %fusion.35 = (f32[2,25,2,128]{2,3,1,0:T(8,128)}, f32[2,25,2,128]{2,3,1,0:T(8,128)}) fusion(f32[2,25,64,128]{2,3,1,0:T(8,128)S(1)} %get-tuple-element.24), kind=kLoop, calls=%fused_computation.82 | loop fusion | bytes 204800 | tf_op jit(solution)/shard_map/slice | solution.py:25
  21.7 3.0 %copy.34 = f32[2,25,2,128]{3,2,1,0:T(2,128)} copy(f32[2,25,2,128]{2,3,1,0:T(8,128)} %get-tuple-element.20) | data formatting | bytes 102400 | tf_op jit(solution)/shard_map/slice | solution.py:24
  26.0 9.0 %collective-permute-start.4 = (f32[2,25,2,128]{3,2,1,0:T(2,128)}, f32[2,25,2,128]{3,2,1,0:T(2,128)}, u32[]{:S(2)}, u32[]{:S(2)}) collective-permute-start(f32[2,25,2,128]{3,2,1,0:T(2,128)} %copy.34), channel_id=1, source_target_pairs={{0,1},{1,2},{2,3},{3,4},{4,5},{5,6},{6,7},{8,9},{9,10},{10,11},{11... | collective-permute-start | bytes 153608 | tf_op jit(solution)/shard_map/ppermute | solution.py:26
  34.9 3.1 %copy.38 = f32[2,25,2,128]{3,2,1,0:T(2,128)} copy(f32[2,25,2,128]{2,3,1,0:T(8,128)} %get-tuple-element.19) | data formatting | bytes 102400 | tf_op jit(solution)/shard_map/slice | solution.py:25
  38.0 1.9 collective-permute-start.6
  41.4 4.5 %collective-permute-start.3 = (f32[25,1,128]{2,1,0:T(1,128)}, f32[25,1,128]{2,1,0:T(1,128)S(1)}, u32[]{:S(2)}, u32[]{:S(2)}) collective-permute-start(f32[25,1,128]{2,1,0:T(1,128)} %slice.173), channel_id=1, source_target_pairs={{0,1},{1,2},{2,3},{3,4},{4,5},{5,6},{6,7},{8,9},{9,10},{10,11},{11... | collective-permute-start | bytes 38408 | tf_op jit(solution)/shard_map/ppermute | solution.py:41
  45.9 2.3 slice.164
  48.3 1.5 copy.50
  53.1 2.1 fusion.13
  57.8 3.6 %pad_maximum_fusion.8 = (f32[25,64,129]{2,1,0:T(8,128)}, f32[25,64,129]{2,1,0:T(8,128)}) fusion(f32[25,64,128]{2,1,0:T(8,128)} %param.11, f32[25,64,1]{2,1,0:T(8,128)} %copy.30), kind=kLoop, calls=%fused_computation.49 | loop fusion | flops 412800 | bytes 2476800 | tf_op jit(solution)/shard_map/concatenate | solution.py:106
  61.4 2.9 %copy.31 = f32[25,64,129]{1,2,0:T(8,128)} copy(f32[25,64,129]{2,1,0:T(8,128)} %get-tuple-element.21) | data formatting | bytes 1651200 | tf_op jit(solution)/shard_map/concatenate | solution.py:106
  64.3 2.9 %copy.32 = f32[25,64,129]{1,2,0:T(8,128)} copy(f32[25,64,129]{2,1,0:T(8,128)} %get-tuple-element.22) | data formatting | bytes 1651200 | tf_op jit(solution)/shard_map/abs | solution.py:58
  67.8 5.4 %collective-permute-start.2 = (f32[2,25,64,2]{2,3,1,0:T(2,128)S(1)}, f32[2,25,64,2]{2,3,1,0:T(2,128)S(1)}, u32[]{:S(2)}, u32[]{:S(2)}) collective-permute-start(f32[2,25,64,2]{2,3,1,0:T(2,128)S(1)} %get-tuple-element.17), channel_id=1, source_target_pairs={{8,0},{16,8},{24,16},{32,24},{40,32},{48,40},{56,48},{64,56},{72,6... | collective-permute-start | bytes 76808 | tf_op jit(solution)/shard_map/ppermute | solution.py:27
  73.1 2.5 %pad_maximum_fusion.9 = (f32[25,65,128]{2,1,0:T(8,128)}, f32[25,65,128]{2,1,0:T(8,128)}) fusion(f32[25,64,128]{2,1,0:T(8,128)} %param.12, f32[25,1,128]{2,1,0:T(1,128)} %copy-done.19), kind=kLoop, calls=%fused_computation.73 | loop fusion | flops 416000 | bytes 2496000 | tf_op jit(solution)/shard_map/concatenate | solution.py:108
  75.7 2.9 %copy.33 = f32[25,65,128]{1,2,0:T(8,128)} copy(f32[25,65,128]{2,1,0:T(8,128)} %get-tuple-element.25) | data formatting | bytes 1664000 | tf_op jit(solution)/shard_map/concatenate | solution.py:108
  78.6 3.0 %copy.40 = f32[25,65,128]{1,2,0:T(8,128)} copy(f32[25,65,128]{2,1,0:T(8,128)} %get-tuple-element.26) | data formatting | bytes 1664000 | tf_op jit(solution)/shard_map/abs | solution.py:58
  81.6 5.9 %add_multiply_fusion.1 = f32[2,25,64,129]{2,3,1,0:T(8,128)} fusion(f32[2,25,64,128]{2,3,1,0:T(8,128)S(1)} %get-tuple-element.24, f32[2,25,64,2]{2,3,1,0:T(2,128)S(1)} %collective-permute-done.1, f32[2,25,64,2]{2,3,1,0:T(2,128)S(1)} %collective-permute-done.2, f32[25,64,129]{1,2,0:T(8,128)} %copy.32, f32[25,64,129]{1,2,0:T(8,128)} %copy.31), kind=kLoop, calls=%fused_computation.9 | loop fusion | flops 6604800 | bytes 4992000 | tf_op jit(solution)/shard_map/add | solution.py:58
  87.5 3.1 %copy.37 = f32[2,25,2,128]{2,3,1,0:T(8,128)} copy(f32[2,25,2,128]{3,2,1,0:T(2,128)} %collective-permute-done.5) | data formatting | bytes 102400 | tf_op jit(solution)/shard_map/ppermute | solution.py:88
  90.5 26.8 %rev.6 = f32[2,25,2,128]{2,3,1,0:T(8,128)} reverse(f32[2,25,2,128]{2,3,1,0:T(8,128)} %copy.37), dimensions={2,3} | reverse | bytes 102400 | tf_op jit(solution)/shard_map/rev | solution.py:89
  117.3 3.1 %copy.39 = f32[2,25,2,128]{2,3,1,0:T(8,128)} copy(f32[2,25,2,128]{3,2,1,0:T(2,128)} %collective-permute-done.6) | data formatting | bytes 102400 | tf_op jit(solution)/shard_map/ppermute | solution.py:27
  120.4 4.4 %broadcast_select_fusion.1 = f32[2,25,2,128]{2,3,1,0:T(8,128)} fusion(f32[2,25,2,128]{2,3,1,0:T(8,128)} %rev.6, f32[2,25,2,128]{2,3,1,0:T(8,128)} %copy.39, pred[]{:T(512)S(6)} %eq.3), kind=kLoop, calls=%fused_computation.56 | loop fusion | flops 12800 | bytes 153601 | tf_op jit(solution)/shard_map/jit(_where)/select_n | solution.py:90
  124.8 3.1 %copy.35 = f32[2,25,2,128]{2,3,1,0:T(8,128)} copy(f32[2,25,2,128]{3,2,1,0:T(2,128)} %collective-permute-done.4) | data formatting | bytes 102400 | tf_op jit(solution)/shard_map/ppermute | solution.py:26
  127.9 8.9 %add_multiply_fusion.3 = f32[2,25,65,128]{2,3,1,0:T(8,128)S(1)} fusion(f32[2,25,64,128]{2,3,1,0:T(8,128)S(1)} %get-tuple-element.24, f32[2,25,2,128]{2,3,1,0:T(8,128)} %copy.35, f32[2,25,2,128]{2,3,1,0:T(8,128)} %broadcast_select_fusion.1, f32[25,65,128]{1,2,0:T(8,128)} %copy.40, f32[25,65,128]{1,2,0:T(8,128)} %copy.33), kind=kLoop, calls=%fused_computation.37 | loop fusion | flops 6656000 | bytes 5068800 | tf_op jit(solution)/shard_map/add | solution.py:58
  136.9 6.4 %multiply_add_fusion = (f32[2,25,64,128]{2,3,1,0:T(8,128)}, f32[2,25,64,128]{2,3,1,0:T(8,128)S(1)}) fusion(f32[2,25,64,128]{2,3,1,0:T(8,128)S(1)} %get-tuple-element.24, f32[2,25,64,128]{2,3,1,0:T(8,128)S(1)} %copy-done.7, f32[25,64,128]{1,2,0:T(8,128)S(1)} %copy-done.3, f32[2,24,64,128]{2,3,1,0:T(8,128)} %fusion.13, ...), kind=kLoop, calls=%fused_computation.38 | loop fusion | flops 5734400 | bytes 15499264 | tf_op jit(solution)/shard_map/add | solution.py:77
  144.2 4.0 %fusion.33 = (f32[2,25,2,128]{2,3,1,0:T(8,128)}, f32[2,25,2,128]{2,3,1,0:T(8,128)}) fusion(f32[2,25,64,128]{2,3,1,0:T(8,128)S(1)} %get-tuple-element.10), kind=kLoop, calls=%fused_computation.80 | loop fusion | bytes 204800 | tf_op jit(solution)/shard_map/slice | solution.py:25
  148.1 3.2 %copy.41 = f32[2,25,2,128]{3,2,1,0:T(2,128)} copy(f32[2,25,2,128]{2,3,1,0:T(8,128)} %get-tuple-element.16) | data formatting | bytes 102400 | tf_op jit(solution)/shard_map/slice | solution.py:24
  152.6 1.9 collective-permute-start.9
  154.6 1.6 add_multiply_fusion.4
  156.2 5.4 %collective-permute-start.8 = (f32[2,25,64,2]{2,3,1,0:T(2,128)S(1)}, f32[2,25,64,2]{2,3,1,0:T(2,128)S(1)}, u32[]{:S(2)}, u32[]{:S(2)}) collective-permute-start(f32[2,25,64,2]{2,3,1,0:T(2,128)S(1)} %get-tuple-element.13), channel_id=1, source_target_pairs={{8,0},{16,8},{24,16},{32,24},{40,32},{48,40},{56,48},{64,56},{72,6... | collective-permute-start | bytes 76808 | tf_op jit(solution)/shard_map/ppermute | solution.py:27
  161.5 3.0 %copy.45 = f32[2,25,2,128]{3,2,1,0:T(2,128)} copy(f32[2,25,2,128]{2,3,1,0:T(8,128)} %get-tuple-element.15) | data formatting | bytes 102400 | tf_op jit(solution)/shard_map/slice | solution.py:25
  164.6 4.1 %collective-permute-start.11 = (f32[2,25,2,128]{3,2,1,0:T(2,128)}, f32[2,25,2,128]{3,2,1,0:T(2,128)}, u32[]{:S(2)}, u32[]{:S(2)}) collective-permute-start(f32[2,25,2,128]{3,2,1,0:T(2,128)} %copy.45), channel_id=1, source_target_pairs={{1,0},{2,1},{3,2},{4,3},{5,4},{6,5},{7,6},{9,8},{10,9},{11,10},{12... | collective-permute-start | bytes 153608 | tf_op jit(solution)/shard_map/ppermute | solution.py:27
  168.7 6.0 %fusion.12 = f32[2,24,64,128]{2,3,1,0:T(8,128)} fusion(f32[2,25,64,128]{2,3,1,0:T(8,128)} %get-tuple-element.9, f32[24,64,128]{1,2,0:T(8,128)} %add_multiply_fusion.4), kind=kLoop, calls=%fused_computation.40 | loop fusion | flops 786432 | bytes 5505024 | tf_op jit(solution)/shard_map/mul | solution.py:68
  174.8 4.2 %add_multiply_fusion = f32[2,25,64,129]{2,3,1,0:T(8,128)} fusion(f32[2,25,64,128]{2,3,1,0:T(8,128)S(1)} %copy-done.1, f32[2,25,64,2]{2,3,1,0:T(2,128)S(1)} %collective-permute-done.7, f32[2,25,64,2]{2,3,1,0:T(2,128)S(1)} %collective-permute-done.8, f32[25,64,129]{1,2,0:T(8,128)S(1)} %copy-done.12, f32[25,64,129]{1,2,0:T(8,128)S(1)} %copy-done.11), kind=kLoop, calls=%fused_computation.8 | loop fusion | flops 6604800 | bytes 4992000 | tf_op jit(solution)/shard_map/add | solution.py:58
  178.9 3.0 %copy.44 = f32[2,25,2,128]{2,3,1,0:T(8,128)} copy(f32[2,25,2,128]{3,2,1,0:T(2,128)} %collective-permute-done.10) | data formatting | bytes 102400 | tf_op jit(solution)/shard_map/ppermute | solution.py:88
  182.0 26.8 %rev.7 = f32[2,25,2,128]{2,3,1,0:T(8,128)} reverse(f32[2,25,2,128]{2,3,1,0:T(8,128)} %copy.44), dimensions={2,3} | reverse | bytes 102400 | tf_op jit(solution)/shard_map/rev | solution.py:89
  208.8 3.0 %copy.46 = f32[2,25,2,128]{2,3,1,0:T(8,128)} copy(f32[2,25,2,128]{3,2,1,0:T(2,128)} %collective-permute-done.11) | data formatting | bytes 102400 | tf_op jit(solution)/shard_map/ppermute | solution.py:27
  211.8 4.5 %broadcast_select_fusion = f32[2,25,2,128]{2,3,1,0:T(8,128)} fusion(f32[2,25,2,128]{2,3,1,0:T(8,128)} %rev.7, f32[2,25,2,128]{2,3,1,0:T(8,128)} %copy.46, pred[]{:T(512)S(6)} %eq.3), kind=kLoop, calls=%fused_computation.55 | loop fusion | flops 12800 | bytes 153601 | tf_op jit(solution)/shard_map/jit(_where)/select_n | solution.py:90
  216.3 3.0 %copy.42 = f32[2,25,2,128]{2,3,1,0:T(8,128)} copy(f32[2,25,2,128]{3,2,1,0:T(2,128)} %collective-permute-done.9) | data formatting | bytes 102400 | tf_op jit(solution)/shard_map/ppermute | solution.py:26
  219.4 8.9 %add_multiply_fusion.2 = f32[2,25,65,128]{2,3,1,0:T(8,128)S(1)} fusion(f32[2,25,64,128]{2,3,1,0:T(8,128)S(1)} %copy-done.1, f32[2,25,2,128]{2,3,1,0:T(8,128)} %copy.42, f32[2,25,2,128]{2,3,1,0:T(8,128)} %broadcast_select_fusion, f32[25,65,128]{1,2,0:T(8,128)} %copy.40, f32[25,65,128]{1,2,0:T(8,128)} %copy.33), kind=kLoop, calls=%fused_computation.36 | loop fusion | flops 6656000 | bytes 5068800 | tf_op jit(solution)/shard_map/add | solution.py:58
  228.5 2.6 %fusion.5 = f32[2,25,64,128]{2,3,1,0:T(8,128)S(1)} fusion(f32[2,25,64,128]{2,3,1,0:T(8,128)S(1)} %copy-done.8, f32[2,25,65,128]{2,3,1,0:T(8,128)S(1)} %add_multiply_fusion.2, f32[2,25,64,129]{2,3,1,0:T(8,128)S(1)} %copy-done.9, f32[2,24,64,128]{2,3,1,0:T(8,128)S(1)} %copy-done.13, f32[25,64,128]{1,2,0:T(8,128)S(1)} %copy-done.5), kind=kLoop, calls=%fused_computation.16 | loop fusion | flops 3686400 | bytes 12222464 | tf_op jit(solution)/shard_map/mul | solution.py:76
  231.1 2.1 slice_bitcast_fusion
  233.1 2.1 subtract_select_fusion
  235.2 3.0 %copy.47 = f32[25,64,128]{2,1,0:T(8,128)} copy(f32[25,64,128]{1,2,0:T(8,128)} %get-tuple-element.12) | data formatting | bytes 1638400
  (81 shorter events, 16.8 us)
Async XLA Ops:
  0.6 5.2 %copy-start.16 = (f32[25,64,128]{2,1,0:T(8,128)S(1)}, f32[25,64,128]{2,1,0:T(8,128)}, u32[]{:S(2)}) copy-start(f32[25,64,128]{2,1,0:T(8,128)} %param.10) | copy-start | bytes 2457604
  1.6 6.1 %copy-start.17 = (f32[25,64,128]{2,1,0:T(8,128)S(1)}, f32[25,64,128]{2,1,0:T(8,128)}, u32[]{:S(2)}) copy-start(f32[25,64,128]{2,1,0:T(8,128)} %param.7) | copy-start | bytes 2457604
  3.0 6.4 %copy-start.18 = (f32[25,64,128]{2,1,0:T(8,128)S(1)}, f32[25,64,128]{2,1,0:T(8,128)}, u32[]{:S(2)}) copy-start(f32[25,64,128]{2,1,0:T(8,128)} %param.9) | copy-start | bytes 2457604
  24.7 62.7 %collective-permute-start.5 = (f32[2,25,2,128]{3,2,1,0:T(2,128)}, f32[2,25,2,128]{3,2,1,0:T(2,128)}, u32[]{:S(2)}, u32[]{:S(2)}) collective-permute-start(f32[2,25,2,128]{3,2,1,0:T(2,128)} %copy.34), channel_id=1, source_target_pairs={{7,127},{15,119},{23,111},{31,103},{39,95},{47,87},{55,79},{63,71}... | collective-permute-start | bytes 153608 | tf_op jit(solution)/shard_map/ppermute | solution.py:88
  26.0 98.9 %collective-permute-start.4 = (f32[2,25,2,128]{3,2,1,0:T(2,128)}, f32[2,25,2,128]{3,2,1,0:T(2,128)}, u32[]{:S(2)}, u32[]{:S(2)}) collective-permute-start(f32[2,25,2,128]{3,2,1,0:T(2,128)} %copy.34), channel_id=1, source_target_pairs={{0,1},{1,2},{2,3},{3,4},{4,5},{5,6},{6,7},{8,9},{9,10},{10,11},{11... | collective-permute-start | bytes 153608 | tf_op jit(solution)/shard_map/ppermute | solution.py:26
  38.0 79.3 %collective-permute-start.6 = (f32[2,25,2,128]{3,2,1,0:T(2,128)}, f32[2,25,2,128]{3,2,1,0:T(2,128)}, u32[]{:S(2)}, u32[]{:S(2)}) collective-permute-start(f32[2,25,2,128]{3,2,1,0:T(2,128)} %copy.38), channel_id=1, source_target_pairs={{1,0},{2,1},{3,2},{4,3},{5,4},{6,5},{7,6},{9,8},{10,9},{11,10},{12... | collective-permute-start | bytes 153608 | tf_op jit(solution)/shard_map/ppermute | solution.py:27
  41.4 25.8 %collective-permute-start.3 = (f32[25,1,128]{2,1,0:T(1,128)}, f32[25,1,128]{2,1,0:T(1,128)S(1)}, u32[]{:S(2)}, u32[]{:S(2)}) collective-permute-start(f32[25,1,128]{2,1,0:T(1,128)} %slice.173), channel_id=1, source_target_pairs={{0,1},{1,2},{2,3},{3,4},{4,5},{5,6},{6,7},{8,9},{9,10},{10,11},{11... | collective-permute-start | bytes 38408 | tf_op jit(solution)/shard_map/ppermute | solution.py:41
  49.8 1.5 copy-start.2
  49.8 6.8 %collective-permute-start = (f32[25,64,1]{1,0,2:T(8,128)S(1)}, f32[25,64,1]{1,0,2:T(8,128)S(1)}, u32[]{:S(2)}, u32[]{:S(2)}) collective-permute-start(f32[25,64,1]{1,0,2:T(8,128)S(1)} %copy.50), channel_id=1, source_target_pairs={{120,0},{0,8},{8,16},{16,24},{24,32},{32,40},{40,48},{48,56},{56,6... | collective-permute-start | bytes 19208 | tf_op jit(solution)/shard_map/ppermute | solution.py:35
  49.8 1.8 copy-start.20
  49.9 1.8 copy-start.23
  51.2 1.9 copy-start.6
  56.6 25.0 %collective-permute-start.1 = (f32[2,25,64,2]{2,3,1,0:T(2,128)S(1)}, f32[2,25,64,2]{2,3,1,0:T(2,128)S(1)}, u32[]{:S(2)}, u32[]{:S(2)}) collective-permute-start(f32[2,25,64,2]{2,3,1,0:T(2,128)S(1)} %get-tuple-element.18), channel_id=1, source_target_pairs={{0,8},{8,16},{16,24},{24,32},{32,40},{40,48},{48,56},{56,64},{64,7... | collective-permute-start | bytes 76808 | tf_op jit(solution)/shard_map/ppermute | solution.py:26
  67.2 0.6 copy-start.19
  67.8 13.8 %collective-permute-start.2 = (f32[2,25,64,2]{2,3,1,0:T(2,128)S(1)}, f32[2,25,64,2]{2,3,1,0:T(2,128)S(1)}, u32[]{:S(2)}, u32[]{:S(2)}) collective-permute-start(f32[2,25,64,2]{2,3,1,0:T(2,128)S(1)} %get-tuple-element.17), channel_id=1, source_target_pairs={{8,0},{16,8},{24,16},{32,24},{40,32},{48,40},{56,48},{64,56},{72,6... | collective-permute-start | bytes 76808 | tf_op jit(solution)/shard_map/ppermute | solution.py:27
  127.9 8.9 %copy-start.3 = (f32[25,64,128]{1,2,0:T(8,128)S(1)}, f32[25,64,128]{1,2,0:T(8,128)}, u32[]{:S(2)}) copy-start(f32[25,64,128]{1,2,0:T(8,128)} %fusion.14) | copy-start | bytes 2457604
  127.9 8.9 %copy-start.7 = (f32[2,25,64,128]{2,3,1,0:T(8,128)S(1)}, f32[2,25,64,128]{2,3,1,0:T(8,128)}, u32[]{:S(2)}) copy-start(f32[2,25,64,128]{2,3,1,0:T(8,128)} %get-tuple-element.23) | copy-start | bytes 4915204
  127.9 8.9 %copy-start.10 = (f32[2,25,64,129]{2,3,1,0:T(8,128)S(1)}, f32[2,25,64,129]{2,3,1,0:T(8,128)}, u32[]{:S(2)}) copy-start(f32[2,25,64,129]{2,3,1,0:T(8,128)} %add_multiply_fusion.1) | copy-start | bytes 4953604
  136.9 6.4 %copy-start.21 = (f32[25]{0:T(128)S(1)}, f32[25]{0:T(128)}, u32[]{:S(2)}) copy-start(f32[25]{0:T(128)} %copy-done.20) | copy-start | bytes 304
  136.9 6.4 %copy-start.24 = (f32[25]{0:T(128)S(1)}, f32[25]{0:T(128)}, u32[]{:S(2)}) copy-start(f32[25]{0:T(128)} %copy-done.23) | copy-start | bytes 304
  143.2 4.9 %copy-start = (f32[2,25,64,128]{2,3,1,0:T(8,128)}, f32[2,25,64,128]{2,3,1,0:T(8,128)S(1)}, u32[]{:S(2)}) copy-start(f32[2,25,64,128]{2,3,1,0:T(8,128)S(1)} %get-tuple-element.10) | copy-start | bytes 4915204
  148.1 6.4 %copy-start.4 = (f32[25,64,128]{1,2,0:T(8,128)S(1)}, f32[25,64,128]{1,2,0:T(8,128)}, u32[]{:S(2)}) copy-start(f32[25,64,128]{1,2,0:T(8,128)} %fusion.14) | copy-start | bytes 2457604
  151.3 27.6 %collective-permute-start.10 = (f32[2,25,2,128]{3,2,1,0:T(2,128)}, f32[2,25,2,128]{3,2,1,0:T(2,128)}, u32[]{:S(2)}, u32[]{:S(2)}) collective-permute-start(f32[2,25,2,128]{3,2,1,0:T(2,128)} %copy.41), channel_id=1, source_target_pairs={{7,127},{15,119},{23,111},{31,103},{39,95},{47,87},{55,79},{63,71}... | collective-permute-start | bytes 153608 | tf_op jit(solution)/shard_map/ppermute | solution.py:88
  152.6 63.7 %collective-permute-start.9 = (f32[2,25,2,128]{3,2,1,0:T(2,128)}, f32[2,25,2,128]{3,2,1,0:T(2,128)}, u32[]{:S(2)}, u32[]{:S(2)}) collective-permute-start(f32[2,25,2,128]{3,2,1,0:T(2,128)} %copy.41), channel_id=1, source_target_pairs={{0,1},{1,2},{2,3},{3,4},{4,5},{5,6},{6,7},{8,9},{9,10},{10,11},{11... | collective-permute-start | bytes 153608 | tf_op jit(solution)/shard_map/ppermute | solution.py:26
  156.2 18.6 %collective-permute-start.7 = (f32[2,25,64,2]{2,3,1,0:T(2,128)S(1)}, f32[2,25,64,2]{2,3,1,0:T(2,128)S(1)}, u32[]{:S(2)}, u32[]{:S(2)}) collective-permute-start(f32[2,25,64,2]{2,3,1,0:T(2,128)S(1)} %get-tuple-element.14), channel_id=1, source_target_pairs={{0,8},{8,16},{16,24},{24,32},{32,40},{40,48},{48,56},{56,64},{64,7... | collective-permute-start | bytes 76808 | tf_op jit(solution)/shard_map/ppermute | solution.py:26
  156.2 18.6 %collective-permute-start.8 = (f32[2,25,64,2]{2,3,1,0:T(2,128)S(1)}, f32[2,25,64,2]{2,3,1,0:T(2,128)S(1)}, u32[]{:S(2)}, u32[]{:S(2)}) collective-permute-start(f32[2,25,64,2]{2,3,1,0:T(2,128)S(1)} %get-tuple-element.13), channel_id=1, source_target_pairs={{8,0},{16,8},{24,16},{32,24},{40,32},{48,40},{56,48},{64,56},{72,6... | collective-permute-start | bytes 76808 | tf_op jit(solution)/shard_map/ppermute | solution.py:27
  164.6 44.2 %collective-permute-start.11 = (f32[2,25,2,128]{3,2,1,0:T(2,128)}, f32[2,25,2,128]{3,2,1,0:T(2,128)}, u32[]{:S(2)}, u32[]{:S(2)}) collective-permute-start(f32[2,25,2,128]{3,2,1,0:T(2,128)} %copy.45), channel_id=1, source_target_pairs={{1,0},{2,1},{3,2},{4,3},{5,4},{6,5},{7,6},{9,8},{10,9},{11,10},{12... | collective-permute-start | bytes 153608 | tf_op jit(solution)/shard_map/ppermute | solution.py:27
  168.7 6.1 %copy-start.1 = (f32[2,25,64,128]{2,3,1,0:T(8,128)S(1)}, f32[2,25,64,128]{2,3,1,0:T(8,128)}, u32[]{:S(2)}) copy-start(f32[2,25,64,128]{2,3,1,0:T(8,128)} %copy-done) | copy-start | bytes 4915204
  168.7 6.1 %copy-start.11 = (f32[25,64,129]{1,2,0:T(8,128)S(1)}, f32[25,64,129]{1,2,0:T(8,128)}, u32[]{:S(2)}) copy-start(f32[25,64,129]{1,2,0:T(8,128)} %copy.31) | copy-start | bytes 2476804
  168.7 6.1 %copy-start.12 = (f32[25,64,129]{1,2,0:T(8,128)S(1)}, f32[25,64,129]{1,2,0:T(8,128)}, u32[]{:S(2)}) copy-start(f32[25,64,129]{1,2,0:T(8,128)} %copy.32) | copy-start | bytes 2476804
  219.3 8.9 %copy-start.5 = (f32[25,64,128]{1,2,0:T(8,128)S(1)}, f32[25,64,128]{1,2,0:T(8,128)}, u32[]{:S(2)}) copy-start(f32[25,64,128]{1,2,0:T(8,128)} %fusion.14) | copy-start | bytes 2457604
  219.3 9.0 %copy-start.8 = (f32[2,25,64,128]{2,3,1,0:T(8,128)S(1)}, f32[2,25,64,128]{2,3,1,0:T(8,128)}, u32[]{:S(2)}) copy-start(f32[2,25,64,128]{2,3,1,0:T(8,128)} %get-tuple-element.9) | copy-start | bytes 4915204
  219.4 9.0 %copy-start.9 = (f32[2,25,64,129]{2,3,1,0:T(8,128)S(1)}, f32[2,25,64,129]{2,3,1,0:T(8,128)}, u32[]{:S(2)}) copy-start(f32[2,25,64,129]{2,3,1,0:T(8,128)} %add_multiply_fusion) | copy-start | bytes 4953604
  219.4 9.1 %copy-start.13 = (f32[2,24,64,128]{2,3,1,0:T(8,128)S(1)}, f32[2,24,64,128]{2,3,1,0:T(8,128)}, u32[]{:S(2)}) copy-start(f32[2,24,64,128]{2,3,1,0:T(8,128)} %fusion.12) | copy-start | bytes 4718596
  231.1 2.1 copy-start.22
  231.1 2.1 copy-start.25
  235.2 3.0 %copy-start.14 = (f32[25,64,128]{1,2,0:T(8,128)S(1)}, f32[25,64,128]{1,2,0:T(8,128)}, u32[]{:S(2)}) copy-start(f32[25,64,128]{1,2,0:T(8,128)} %get-tuple-element.11) | copy-start | bytes 2457604
  235.2 4.3 %copy-start.15 = (f32[25,64,128]{1,2,0:T(8,128)S(1)}, f32[25,64,128]{1,2,0:T(8,128)}, u32[]{:S(2)}) copy-start(f32[25,64,128]{1,2,0:T(8,128)} %subtract_select_fusion) | copy-start | bytes 2457604

commit v2 on v1

v2 whole, which is shorter than its diff:
```python
import functools
import jax
import jax.numpy as jnp
from jax import lax
from jax.experimental import pallas as pl
from jax.experimental.pallas import tpu as pltpu
from jax.sharding import PartitionSpec as P

asselin_gamma = 0.1
nu_base = 0.05
nu_conv = 0.2
level_depth = 160.0
alpha_zero = 0.1655
beta_zero = 0.76554
lambda_one = 0.05952
lambda_two = 0.00054914
mu_one = 0.0001497
mu_two = 1.109e-05
nu_cross = 0.0024341


def density_at(temp, salt, depth):
    warm = -alpha_zero * (1.0 + 0.5 * lambda_one * temp + mu_one * depth) * temp
    salty = beta_zero * (1.0 - 0.5 * lambda_two * salt - mu_two * depth) * salt
    return warm + salty - nu_cross * temp * salt


def face_flux(u, q1, q2, q3, q4):
    flux = u * (7.0 * (q2 + q3) - (q1 + q4)) / 12.0
    return flux + jnp.abs(u) * ((q4 - q1) - 3.0 * (q3 - q2)) / 12.0


def step_kernel(mask_inputs, final, bl_ref, nt_ref, ns_ref, bt_ref, bs_ref, h_ref, yh_ref,
                ue_ref, vn_ref, *rest):
    outs, fv = rest[:-1], rest[-1]
    levels, rows, cols = nt_ref.shape
    lane = lax.broadcasted_iota(jnp.int32, (rows, cols), 1)
    row = lax.broadcasted_iota(jnp.int32, (rows, cols), 0)
    now_refs, bef_refs = (nt_ref, ns_ref), (bt_ref, bs_ref)

    def mask(k):
        return (k < bl_ref[...]).astype(jnp.float32)

    def depth(k):
        return level_depth * (k.astype(jnp.float32) + 0.5)

    def load(ref, k, m):
        v = ref[k]
        return v * m if mask_inputs else v

    zero = jnp.zeros((rows, cols), jnp.float32)
    for f in range(2):
        fv[f, 0] = zero
        fv[f, levels] = zero

    def mixing(k, carry):
        m0, m1 = mask(k), mask(k + 1)
        e0 = density_at(load(nt_ref, k, m0), load(ns_ref, k, m0), depth(k))
        e1 = density_at(load(nt_ref, k + 1, m1), load(ns_ref, k + 1, m1), depth(k + 1))
        rates = (nu_base + nu_conv * jax.nn.sigmoid(-4.0 * (e1 - e0))) * m1
        for f in range(2):
            fv[f, k + 1] = rates * (load(bef_refs[f], k + 1, m1) - load(bef_refs[f], k, m0))
        return carry

    lax.fori_loop(0, levels - 1, mixing, 0)

    def level(k, carry):
        m = mask(k)
        ue, vn = ue_ref[k], vn_ref[k]
        uw = jnp.where(lane < 1, pltpu.roll(h_ref[0, k], cols - 4, 1), pltpu.roll(ue, 1, 1))
        vs = jnp.where(row < 1, jnp.broadcast_to(yh_ref[0, k][4:5], (rows, cols)), pltpu.roll(vn, 1, 0))
        afters = []
        for f in range(2):
            q = load(now_refs[f], k, m)
            b = load(bef_refs[f], k, m)
            h = h_ref[f, k]
            yh = yh_ref[f, k]
            qm1 = jnp.where(lane < 1, pltpu.roll(h, cols - 3, 1), pltpu.roll(q, 1, 1))
            qm2 = jnp.where(lane < 2, pltpu.roll(h, cols - 2, 1), pltpu.roll(q, 2, 1))
            qp1 = jnp.where(lane >= cols - 1, pltpu.roll(h, cols - 1, 1), pltpu.roll(q, cols - 1, 1))
            qp2 = jnp.where(lane >= cols - 2, pltpu.roll(h, cols - 2, 1), pltpu.roll(q, cols - 2, 1))
            div_x = face_flux(ue, qm1, q, qp1, qp2) - face_flux(uw, qm2, qm1, q, qp1)
            s2 = jnp.broadcast_to(yh[0:1], (rows, cols))
            s1 = jnp.broadcast_to(yh[1:2], (rows, cols))
            n1 = jnp.broadcast_to(yh[2:3], (rows, cols))
            n2 = jnp.broadcast_to(yh[3:4], (rows, cols))
            qs1 = jnp.where(row < 1, s1, pltpu.roll(q, 1, 0))
            qs2 = jnp.where(row < 1, s2, jnp.where(row < 2, s1, pltpu.roll(q, 2, 0)))
            qn1 = jnp.where(row >= rows - 1, n1, pltpu.roll(q, rows - 1, 0))
            qn2 = jnp.where(row >= rows - 1, n2, jnp.where(row >= rows - 2, n1, pltpu.roll(q, rows - 2, 0)))
            div_y = face_flux(vn, qs1, q, qn1, qn2) - face_flux(vs, qs2, qs1, q, qn1)
            change = -(div_x + div_y)
            change = change + (fv[f, k + 1] - fv[f, k])
            after = (b + 2.0 * change) * m
            afters.append(after)
            if not final:
                outs[f][k] = q + asselin_gamma * (b - 2.0 * q + after)
                outs[2 + f][k] = after
        if final:
            outs[0][k] = afters[0]
            outs[1][k] = afters[1]
            outs[2][k] = density_at(afters[0], afters[1], depth(k)) * m
        return carry

    lax.fori_loop(0, levels, level, 0)


def step_call(mask_inputs, final, bl, nt, ns, bt, bs, h, yh, ue, vn):
    levels, rows, cols = nt.shape
    field = jax.ShapeDtypeStruct(nt.shape, jnp.float32)
    n_out = 3 if final else 4
    vspec = pl.BlockSpec(memory_space=pltpu.VMEM)
    return pl.pallas_call(
        functools.partial(step_kernel, mask_inputs, final),
        out_shape=tuple([field] * n_out),
        in_specs=[vspec] * 9,
        out_specs=tuple([vspec] * n_out),
        scratch_shapes=[pltpu.VMEM((2, levels + 1, rows, cols), jnp.float32)],
        compiler_params=pltpu.CompilerParams(vmem_limit_bytes=48 * 1024 * 1024),
        cost_estimate=pl.CostEstimate(
            flops=400 * 2 * levels * rows * cols, transcendentals=levels * rows * cols,
            bytes_accessed=4 * levels * rows * cols * (9 + n_out)),
    )(bl, nt, ns, bt, bs, h, yh, ue, vn)


def exchange(t, s, west_column, south_row, at_fold):
    lon_count, lat_count = (lax.axis_size("lon"), lax.axis_size("lat"))
    cols_first = jnp.stack([t[..., :2], s[..., :2]])
    cols_last = jnp.stack([t[..., -2:], s[..., -2:]])
    rows_first = jnp.stack([t[:, :2], s[:, :2]])
    rows_last = jnp.stack([t[:, -2:], s[:, -2:]])
    east = lax.ppermute(cols_first, "lon", [(i, (i - 1) % lon_count) for i in range(lon_count)])
    west = lax.ppermute(cols_last, "lon", [(i, (i + 1) % lon_count) for i in range(lon_count)])
    north = lax.ppermute(rows_first, "lat", [(i, i - 1) for i in range(1, lat_count)])
    south = lax.ppermute(rows_last, "lat", [(i, i + 1) for i in range(lat_count - 1)])
    top = lat_count - 1
    fold_pairs = [(d * lat_count + top, (lon_count - 1 - d) * lat_count + top) for d in range(lon_count)]
    partner = lax.ppermute(rows_last, ("lon", "lat"), fold_pairs)[:, :, ::-1, :]
    cols = t.shape[-1]
    flip = (jnp.arange(cols)[:, None] + jnp.arange(cols)[None, :] == cols - 1).astype(jnp.float32)
    mirror = jnp.einsum("fkrc,cd->fkrd", partner, flip, precision=lax.Precision.HIGHEST)
    north = jnp.where(at_fold, mirror, north)
    shape = cols_first.shape
    halo_x = jnp.concatenate(
        [east, west, jnp.broadcast_to(west_column[None], shape[:3] + (1,)),
         jnp.zeros(shape[:3] + (cols - 5,), jnp.float32)], 3)
    halo_y = jnp.concatenate(
        [south, north, jnp.broadcast_to(south_row[None], (2,) + south_row.shape),
         jnp.zeros((2, t.shape[0], 3, cols), jnp.float32)], 2)
    return halo_x, halo_y


def on_device(
    temp_before, temp_now, salt_before, salt_now, east_velocity, north_velocity, bottom_level
):
    levels = temp_now.shape[0]
    ocean_mask = (jnp.arange(levels, dtype=jnp.int32)[:, None, None] < bottom_level[None]).astype(
        jnp.float32
    )
    lon_count, lat_count = (lax.axis_size("lon"), lax.axis_size("lat"))
    west_column = lax.ppermute(
        east_velocity[:, :, -1:], "lon", [(i, (i + 1) % lon_count) for i in range(lon_count)])
    south_row = lax.ppermute(
        north_velocity[:, -1:, :], "lat", [(i, i + 1) for i in range(lat_count - 1)])
    at_fold = lax.axis_index("lat") == lat_count - 1
    halo_x, halo_y = exchange(temp_now * ocean_mask, salt_now * ocean_mask, west_column, south_row, at_fold)
    ft, fs, at, as_ = step_call(True, False, bottom_level, temp_now, salt_now, temp_before, salt_before,
                                halo_x, halo_y, east_velocity, north_velocity)
    halo_x, halo_y = exchange(at, as_, west_column, south_row, at_fold)
    return step_call(False, True, bottom_level, at, as_, ft, fs, halo_x, halo_y,
                     east_velocity, north_velocity)


def solution(mesh):
    return jax.shard_map(
        on_device,
        mesh=mesh,
        in_specs=(
            P(None, "lat", "lon"),
            P(None, "lat", "lon"),
            P(None, "lat", "lon"),
            P(None, "lat", "lon"),
            P(None, "lat", "lon"),
            P(None, "lat", "lon"),
            P("lat", "lon"),
        ),
        out_specs=(P(None, "lat", "lon"), P(None, "lat", "lon"), P(None, "lat", "lon")),
        check_vma=False,
    )
```

time: 246 us -> 102 us (0.41)
  the two profiles are of different devices: /device:TPU:12 before, /device:TPU:14 now
where the time goes in v2:
time: 102 us; the launch traced here: 101 us
  starting transfers between devices  37.2 us (36%)
  local copies, waits for them, and re-layouts  28.4 us (28%)
  Pallas kernels  22 us (22%)
  other arithmetic  12.4 us (12%)
    pallas_call x2, Pallas kernels, step_call(): pl.pallas_call(functools.partial(step_kernel, mask_inputs, final), out_sh...  22 us
    ppermute x2, starting transfers between devices, exchange(): partner = lax.ppermute(rows_last, ('lon', 'lat'), fold_pairs)[:, :, ::-1, :]  11.1 us
    ppermute x2, starting transfers between devices, exchange(): lax.ppermute(cols_first, 'lon', [(i, (i - 1) % lon_count) for i in range(...  10.8 us
    ppermute x2, starting transfers between devices, exchange(): lax.ppermute(rows_first, 'lat', [(i, i - 1) for i in range(1, lat_count)])  10.7 us
    concatenate x2, other arithmetic, exchange(): jnp.concatenate([east, west, jnp.broadcast_to(west_column[None], shape[:3...  8.77 us
    another operation x4, local copies, waits for them, and re-layouts, exchange(): cols_last = jnp.stack([t[..., -2:], s[..., -2:]])  5.85 us
    another operation x7, local copies, waits for them, and re-layouts, exchange(): cols_first = jnp.stack([t[..., :2], s[..., :2]])  5.68 us
    unnamed x28, local copies, waits for them, and re-layouts  4.77 us
  transfers between devices with their start and end apart: 12, of which 0 were waited for; matrix products, arithmetic and copies ran while one was open for 31% of the time, Pallas kernels for 0%

profile of v2, /device:TPU:14, one launch (start us, length us, event | category | flops | bytes accessed | tf_op | source)
XLA Modules:
  0.0 101.4 jit_solution(7181732991929211309)
XLA Ops:
  0.6 1.6 %fusion.3 = (f32[25,64,128]{2,1,0:T(8,128)S(1)}, f32[25,64,128]{2,1,0:T(8,128)S(1)}) fusion(f32[25,64,128]{2,1,0:T(8,128)} %nt_ref.1, s32[64,128]{1,0:T(8,128)} %bl_ref.3, f32[25,64,128]{2,1,0:T(8,128)} %ns_ref.1), kind=kLoop, calls=%fused_computation.14 | loop fusion | flops 614400 | bytes 3309568 | tf_op jit(solution)/shard_map/mul | solution.py:166
  2.4 7.1 %collective-permute-start.4 = (f32[2,25,2,128]{3,2,1,0:T(2,128)S(1)}, f32[2,25,2,128]{3,2,1,0:T(2,128)S(1)}, u32[]{:S(2)}, u32[]{:S(2)}) collective-permute-start(f32[2,25,2,128]{3,2,1,0:T(2,128)S(1)} %pad_maximum_fusion.6), channel_id=1, source_target_pairs={{7,127},{15,119},{23,111},{31,103},{39,95},{47,87},{55,79},{63,71}... | collective-permute-start | bytes 153608 | tf_op jit(solution)/shard_map/ppermute | solution.py:138
  9.5 1.3 %collective-permute-start.3 = (f32[2,25,2,128]{3,2,1,0:T(2,128)S(1)}, f32[2,25,2,128]{3,2,1,0:T(2,128)S(1)}, u32[]{:S(2)}, u32[]{:S(2)}) collective-permute-start(f32[2,25,2,128]{3,2,1,0:T(2,128)S(1)} %pad_maximum_fusion.6), channel_id=1, source_target_pairs={{0,1},{1,2},{2,3},{3,4},{4,5},{5,6},{6,7},{8,9},{9,10},{10,11},{11... | collective-permute-start | bytes 153608 | tf_op jit(solution)/shard_map/ppermute | solution.py:135
  10.8 0.3 slice.58
  11.1 1.0 copy.39
  12.0 0.7 collective-permute-start.2
  12.7 1.8 %slice_bitcast_fusion.2 = (f32[1,25,64,2]{3,2,1,0:T(8,128)S(1)}, f32[1,25,64,2]{3,2,1,0:T(8,128)}, f32[1,25,64,2]{3,2,1,0:T(8,128)}, f32[1,25,64,2]{3,2,1,0:T(8,128)S(1)}) fusion(f32[25,64,128]{2,1,0:T(8,128)S(1)} %get-tuple-element.28, f32[25,64,128]{2,1,0:T(8,128)S(1)} %get-tuple-element.27), kind=kLoop, calls=%fused_computation.6 | loop fusion | bytes 102400 | tf_op jit(solution)/shard_map/stack | solution.py:128
  14.5 1.5 %copy.23 = f32[1,25,64,2]{2,3,1,0:T(2,128)S(1)} copy(f32[1,25,64,2]{3,2,1,0:T(8,128)} %get-tuple-element.26) | data formatting | bytes 25600 | tf_op jit(solution)/shard_map/stack | solution.py:129
  16.0 1.5 %copy.22 = f32[1,25,64,2]{2,3,1,0:T(2,128)S(1)} copy(f32[1,25,64,2]{3,2,1,0:T(8,128)} %get-tuple-element.29) | data formatting | bytes 25600 | tf_op jit(solution)/shard_map/stack | solution.py:129
  17.5 0.1 collective-permute-start.1
  17.6 0.3 copy.21
  17.9 0.3 copy.20
  18.3 5.4 %collective-permute-start = (f32[2,25,64,2]{2,3,1,0:T(2,128)S(1)}, f32[2,25,64,2]{2,3,1,0:T(2,128)S(1)}, u32[]{:S(2)}, u32[]{:S(2)}) collective-permute-start(f32[2,25,64,2]{2,3,1,0:T(2,128)S(1)} %pad_maximum_fusion.4), channel_id=1, source_target_pairs={{0,120},{8,0},{16,8},{24,16},{32,24},{40,32},{48,40},{56,48},{64,5... | collective-permute-start | bytes 76808 | tf_op jit(solution)/shard_map/ppermute | solution.py:132
  23.7 0.9 slice.63
  24.7 0.1 pad.19.clone
  24.8 1.3 %collective-permute-start.6 = (f32[25,1,128]{2,0,1:T(8,128)S(1)}, f32[25,1,128]{2,0,1:T(8,128)}, u32[]{:S(2)}, u32[]{:S(2)}) collective-permute-start(f32[25,1,128]{2,0,1:T(8,128)S(1)} %copy.40), channel_id=1, source_target_pairs={{0,1},{1,2},{2,3},{3,4},{4,5},{5,6},{6,7},{8,9},{9,10},{10,11},{11... | collective-permute-start | bytes 38408 | tf_op jit(solution)/shard_map/ppermute | solution.py:163
  26.1 1.8 %copy.26 = f32[2,25,64,2]{3,2,1,0:T(8,128)} copy(f32[2,25,64,2]{2,3,1,0:T(2,128)S(1)} %collective-permute-done.1) | data formatting | bytes 51200 | tf_op jit(solution)/shard_map/ppermute | solution.py:133
  27.9 5.5 %collective-permute-start.5 = (f32[2,25,2,128]{3,2,1,0:T(2,128)S(1)}, f32[2,25,2,128]{3,2,1,0:T(2,128)}, u32[]{:S(2)}, u32[]{:S(2)}) collective-permute-start(f32[2,25,2,128]{3,2,1,0:T(2,128)S(1)} %pad_maximum_fusion.7), channel_id=1, source_target_pairs={{1,0},{2,1},{3,2},{4,3},{5,4},{6,5},{7,6},{9,8},{10,9},{11,10},{12... | collective-permute-start | bytes 153608 | tf_op jit(solution)/shard_map/ppermute | solution.py:134
  33.4 1.7 %copy.25 = f32[2,25,64,2]{3,2,1,0:T(8,128)} copy(f32[2,25,64,2]{2,3,1,0:T(2,128)S(1)} %collective-permute-done) | data formatting | bytes 51200 | tf_op jit(solution)/shard_map/ppermute | solution.py:132
  35.1 1.1 %broadcast_in_dim.9 = f32[2,25,64,1]{3,2,1,0:T(8,128)S(1)} broadcast(f32[25,64]{1,0:T(8,128)} %bitcast.4), dimensions={1,2} | broadcast | bytes 19200 | tf_op jit(solution)/shard_map/broadcast_in_dim | solution.py:145
  36.2 0.3 copy-done.12
  36.6 4.2 %fusion.h_ref = f32[2,25,64,128]{3,2,1,0:T(8,128)} fusion(f32[2,25,64,1]{3,2,1,0:T(8,128)S(1)} %broadcast_in_dim.9, f32[2,25,64,2]{3,2,1,0:T(8,128)S(1)} %copy-done.12, f32[2,25,64,2]{3,2,1,0:T(8,128)} %copy.25, f32[128]{0:T(128)S(1)} %pad.27.clone), kind=kLoop, calls=%fused_computation.2 | loop fusion | flops 1228800 | bytes 1702912 | tf_op jit(solution)/shard_map/concatenate | solution.py:144
  40.7 0.1 rev.6
  40.8 0.2 fusion.8
  41.1 0.7 broadcast_in_dim.11
  41.9 0.1 fusion.4.yh_ref
  42.0 1.1 %copy-done.5 = f32[25,64,128]{2,1,0:T(8,128)S(1)} copy-done((f32[25,64,128]{2,1,0:T(8,128)S(1)}, f32[25,64,128]{2,1,0:T(8,128)}, u32[]{:S(2)}) %copy-start.5) | copy-done | bytes 819224
  43.1 10.6 %shard_map.94 = (f32[25,64,128]{2,1,0:T(8,128)S(1)}, f32[25,64,128]{2,1,0:T(8,128)S(1)}, f32[25,64,128]{2,1,0:T(8,128)S(1)}, f32[25,64,128]{2,1,0:T(8,128)S(1)}) custom-call(s32[64,128]{1,0:T(8,128)S(1)} %copy-done.10, f32[25,64,128]{2,1,0:T(8,128)S(1)} %copy-done.3, f32[25,64,128]{2,1,0:T(8,128)S(1)} %copy-done.4, f32[25,64,128]{2,1,0:T(8,128)S(1)} %copy-done.5, ...), custom_call_target="tpu_custom_call" | custom-call | flops 163840000 | bytes 10649600 | tf_op jit(solution)/shard_map/pallas_call | solution.py:113
  53.8 1.4 %slice_bitcast_fusion.6 = (f32[1,25,64,2]{3,2,1,0:T(8,128)S(1)}, f32[1,25,64,2]{3,2,1,0:T(8,128)}) fusion(f32[25,64,128]{2,1,0:T(8,128)S(1)} %get-tuple-element.8.ns_ref), kind=kLoop, calls=%fused_computation.10 | loop fusion | bytes 51200 | tf_op jit(solution)/shard_map/stack | solution.py:128
  55.2 1.2 %slice_bitcast_fusion.7 = (f32[1,25,64,2]{3,2,1,0:T(8,128)S(1)}, f32[1,25,64,2]{3,2,1,0:T(8,128)}) fusion(f32[25,64,128]{2,1,0:T(8,128)S(1)} %get-tuple-element.7.nt_ref), kind=kLoop, calls=%fused_computation.11 | loop fusion | bytes 51200 | tf_op jit(solution)/shard_map/stack | solution.py:128
  56.5 4.0 %collective-permute-start.10 = (f32[2,25,2,128]{3,2,1,0:T(2,128)S(1)}, f32[2,25,2,128]{3,2,1,0:T(2,128)}, u32[]{:S(2)}, u32[]{:S(2)}) collective-permute-start(f32[2,25,2,128]{3,2,1,0:T(2,128)S(1)} %pad_maximum_fusion.10), channel_id=1, source_target_pairs={{7,127},{15,119},{23,111},{31,103},{39,95},{47,87},{55,79},{63,71}... | collective-permute-start | bytes 153608 | tf_op jit(solution)/shard_map/ppermute | solution.py:138
  60.5 1.3 %collective-permute-start.9 = (f32[2,25,2,128]{3,2,1,0:T(2,128)S(1)}, f32[2,25,2,128]{3,2,1,0:T(2,128)}, u32[]{:S(2)}, u32[]{:S(2)}) collective-permute-start(f32[2,25,2,128]{3,2,1,0:T(2,128)S(1)} %pad_maximum_fusion.10), channel_id=1, source_target_pairs={{0,1},{1,2},{2,3},{3,4},{4,5},{5,6},{6,7},{8,9},{9,10},{10,11},{11... | collective-permute-start | bytes 153608 | tf_op jit(solution)/shard_map/ppermute | solution.py:135
  61.8 1.5 %copy.33 = f32[1,25,64,2]{2,3,1,0:T(2,128)S(1)} copy(f32[1,25,64,2]{3,2,1,0:T(8,128)} %get-tuple-element.18) | data formatting | bytes 25600 | tf_op jit(solution)/shard_map/stack | solution.py:129
  63.2 1.5 %copy.32 = f32[1,25,64,2]{2,3,1,0:T(2,128)S(1)} copy(f32[1,25,64,2]{3,2,1,0:T(8,128)} %get-tuple-element.16) | data formatting | bytes 25600 | tf_op jit(solution)/shard_map/stack | solution.py:129
  64.7 0.7 pad_maximum_fusion.9
  65.4 0.3 copy.31
  65.7 0.3 copy.30
  66.1 5.4 %collective-permute-start.7 = (f32[2,25,64,2]{2,3,1,0:T(2,128)S(1)}, f32[2,25,64,2]{2,3,1,0:T(2,128)S(1)}, u32[]{:S(2)}, u32[]{:S(2)}) collective-permute-start(f32[2,25,64,2]{2,3,1,0:T(2,128)S(1)} %pad_maximum_fusion.8), channel_id=1, source_target_pairs={{0,120},{8,0},{16,8},{24,16},{32,24},{40,32},{48,40},{56,48},{64,5... | collective-permute-start | bytes 76808 | tf_op jit(solution)/shard_map/ppermute | solution.py:132
  71.5 5.2 %collective-permute-start.11 = (f32[2,25,2,128]{3,2,1,0:T(2,128)S(1)}, f32[2,25,2,128]{3,2,1,0:T(2,128)}, u32[]{:S(2)}, u32[]{:S(2)}) collective-permute-start(f32[2,25,2,128]{3,2,1,0:T(2,128)S(1)} %pad_maximum_fusion.11), channel_id=1, source_target_pairs={{1,0},{2,1},{3,2},{4,3},{5,4},{6,5},{7,6},{9,8},{10,9},{11,10},{12... | collective-permute-start | bytes 153608 | tf_op jit(solution)/shard_map/ppermute | solution.py:134
  76.7 2.5 %copy.35 = f32[2,25,64,2]{3,2,1,0:T(8,128)} copy(f32[2,25,64,2]{2,3,1,0:T(2,128)} %collective-permute-done.8) | data formatting | bytes 51200 | tf_op jit(solution)/shard_map/ppermute | solution.py:133
  79.3 1.8 %copy.34 = f32[2,25,64,2]{3,2,1,0:T(8,128)} copy(f32[2,25,64,2]{2,3,1,0:T(2,128)S(1)} %collective-permute-done.7) | data formatting | bytes 51200 | tf_op jit(solution)/shard_map/ppermute | solution.py:132
  81.0 4.6 %fusion.1.h_ref = f32[2,25,64,128]{3,2,1,0:T(8,128)} fusion(f32[2,25,64,1]{3,2,1,0:T(8,128)} %copy-done.11, f32[2,25,64,2]{3,2,1,0:T(8,128)} %copy.35, f32[2,25,64,2]{3,2,1,0:T(8,128)} %copy.34, f32[128]{0:T(128)S(1)} %pad.27.clone), kind=kLoop, calls=%fused_computation.3 | loop fusion | flops 1228800 | bytes 1702912 | tf_op jit(solution)/shard_map/concatenate | solution.py:144
  85.7 0.9 rev.7
  86.6 0.2 fusion.6
  86.8 0.9 fusion.5.yh_ref
  87.8 1.1 %copy-done.7 = f32[25,64,128]{2,1,0:T(8,128)S(1)} copy-done((f32[25,64,128]{2,1,0:T(8,128)S(1)}, f32[25,64,128]{2,1,0:T(8,128)}, u32[]{:S(2)}) %copy-start.7) | copy-done | bytes 819224
  88.9 1.1 %copy-done.9 = f32[25,64,128]{2,1,0:T(8,128)S(1)} copy-done((f32[25,64,128]{2,1,0:T(8,128)S(1)}, f32[25,64,128]{2,1,0:T(8,128)}, u32[]{:S(2)}) %copy-start.9) | copy-done | bytes 819224
  90.0 11.4 %shard_map.95 = (f32[25,64,128]{2,1,0:T(8,128)}, f32[25,64,128]{2,1,0:T(8,128)}, f32[25,64,128]{2,1,0:T(8,128)}) custom-call(s32[64,128]{1,0:T(8,128)S(1)} %copy-done.10, f32[25,64,128]{2,1,0:T(8,128)S(1)} %get-tuple-element.7.nt_ref, f32[25,64,128]{2,1,0:T(8,128)S(1)} %get-tuple-element.8.ns_ref, f32[25,64,128]{2,1,0:T(8,128)S(1)} %copy-done.7, ...), custom_call_target="tpu_custom_call" | custom-call | flops 163840000 | bytes 9830400 | tf_op jit(solution)/shard_map/pallas_call | solution.py:113
  (51 shorter events, 0.6 us)
Async XLA Ops:
  0.6 10.2 %copy-start = (f32[25,64,128]{2,1,0:T(8,128)S(1)}, f32[25,64,128]{2,1,0:T(8,128)}, u32[]{:S(2)}) copy-start(f32[25,64,128]{2,1,0:T(8,128)} %ue_ref.3) | copy-start | bytes 2457604
  2.4 38.4 %collective-permute-start.4 = (f32[2,25,2,128]{3,2,1,0:T(2,128)S(1)}, f32[2,25,2,128]{3,2,1,0:T(2,128)S(1)}, u32[]{:S(2)}, u32[]{:S(2)}) collective-permute-start(f32[2,25,2,128]{3,2,1,0:T(2,128)S(1)} %pad_maximum_fusion.6), channel_id=1, source_target_pairs={{7,127},{15,119},{23,111},{31,103},{39,95},{47,87},{55,79},{63,71}... | collective-permute-start | bytes 153608 | tf_op jit(solution)/shard_map/ppermute | solution.py:138
  9.5 31.6 %collective-permute-start.3 = (f32[2,25,2,128]{3,2,1,0:T(2,128)S(1)}, f32[2,25,2,128]{3,2,1,0:T(2,128)S(1)}, u32[]{:S(2)}, u32[]{:S(2)}) collective-permute-start(f32[2,25,2,128]{3,2,1,0:T(2,128)S(1)} %pad_maximum_fusion.6), channel_id=1, source_target_pairs={{0,1},{1,2},{2,3},{3,4},{4,5},{5,6},{6,7},{8,9},{9,10},{10,11},{11... | collective-permute-start | bytes 153608 | tf_op jit(solution)/shard_map/ppermute | solution.py:135
  12.0 23.1 %collective-permute-start.2 = (f32[25,64,1]{1,0,2:T(8,128)}, f32[25,64,1]{1,0,2:T(8,128)}, u32[]{:S(2)}, u32[]{:S(2)}) collective-permute-start(f32[25,64,1]{1,0,2:T(8,128)} %copy.39), channel_id=1, source_target_pairs={{0,8},{8,16},{16,24},{24,32},{32,40},{40,48},{48,56},{56,64},{64,7... | collective-permute-start | bytes 19208 | tf_op jit(solution)/shard_map/ppermute | solution.py:161
  17.5 7.3 %collective-permute-start.1 = (f32[2,25,64,2]{2,3,1,0:T(2,128)S(1)}, f32[2,25,64,2]{2,3,1,0:T(2,128)S(1)}, u32[]{:S(2)}, u32[]{:S(2)}) collective-permute-start(f32[2,25,64,2]{2,3,1,0:T(2,128)S(1)} %pad_maximum_fusion.5), channel_id=1, source_target_pairs={{0,8},{8,16},{16,24},{24,32},{32,40},{40,48},{48,56},{56,64},{64,7... | collective-permute-start | bytes 76808 | tf_op jit(solution)/shard_map/ppermute | solution.py:133
  18.3 9.6 %collective-permute-start = (f32[2,25,64,2]{2,3,1,0:T(2,128)S(1)}, f32[2,25,64,2]{2,3,1,0:T(2,128)S(1)}, u32[]{:S(2)}, u32[]{:S(2)}) collective-permute-start(f32[2,25,64,2]{2,3,1,0:T(2,128)S(1)} %pad_maximum_fusion.4), channel_id=1, source_target_pairs={{0,120},{8,0},{16,8},{24,16},{32,24},{40,32},{48,40},{56,48},{64,5... | collective-permute-start | bytes 76808 | tf_op jit(solution)/shard_map/ppermute | solution.py:132
  24.8 16.3 %collective-permute-start.6 = (f32[25,1,128]{2,0,1:T(8,128)S(1)}, f32[25,1,128]{2,0,1:T(8,128)}, u32[]{:S(2)}, u32[]{:S(2)}) collective-permute-start(f32[25,1,128]{2,0,1:T(8,128)S(1)} %copy.40), channel_id=1, source_target_pairs={{0,1},{1,2},{2,3},{3,4},{4,5},{5,6},{6,7},{8,9},{9,10},{10,11},{11... | collective-permute-start | bytes 38408 | tf_op jit(solution)/shard_map/ppermute | solution.py:163
  27.9 13.2 %collective-permute-start.5 = (f32[2,25,2,128]{3,2,1,0:T(2,128)S(1)}, f32[2,25,2,128]{3,2,1,0:T(2,128)}, u32[]{:S(2)}, u32[]{:S(2)}) collective-permute-start(f32[2,25,2,128]{3,2,1,0:T(2,128)S(1)} %pad_maximum_fusion.7), channel_id=1, source_target_pairs={{1,0},{2,1},{3,2},{4,3},{5,4},{6,5},{7,6},{9,8},{10,9},{11,10},{12... | collective-permute-start | bytes 153608 | tf_op jit(solution)/shard_map/ppermute | solution.py:134
  35.1 1.4 %copy-start.12 = (f32[2,25,64,2]{3,2,1,0:T(8,128)S(1)}, f32[2,25,64,2]{3,2,1,0:T(8,128)}, u32[]{:S(2)}) copy-start(f32[2,25,64,2]{3,2,1,0:T(8,128)} %copy.26) | copy-start | bytes 76804
  36.6 4.2 %copy-start.11 = (f32[2,25,64,1]{3,2,1,0:T(8,128)}, f32[2,25,64,1]{3,2,1,0:T(8,128)S(1)}, u32[]{:S(2)}) copy-start(f32[2,25,64,1]{3,2,1,0:T(8,128)S(1)} %broadcast_in_dim.9) | copy-start | bytes 38404
  36.6 5.4 %copy-start.3 = (f32[25,64,128]{2,1,0:T(8,128)S(1)}, f32[25,64,128]{2,1,0:T(8,128)}, u32[]{:S(2)}) copy-start(f32[25,64,128]{2,1,0:T(8,128)} %nt_ref.1) | copy-start | bytes 2457604
  36.6 5.4 %copy-start.4 = (f32[25,64,128]{2,1,0:T(8,128)S(1)}, f32[25,64,128]{2,1,0:T(8,128)}, u32[]{:S(2)}) copy-start(f32[25,64,128]{2,1,0:T(8,128)} %ns_ref.1) | copy-start | bytes 2457604
  36.6 5.4 %copy-start.10 = (s32[64,128]{1,0:T(8,128)S(1)}, s32[64,128]{1,0:T(8,128)}, u32[]{:S(2)}) copy-start(s32[64,128]{1,0:T(8,128)} %bl_ref.3) | copy-start | bytes 98308
  42.0 1.1 %copy-start.5 = (f32[25,64,128]{2,1,0:T(8,128)S(1)}, f32[25,64,128]{2,1,0:T(8,128)}, u32[]{:S(2)}) copy-start(f32[25,64,128]{2,1,0:T(8,128)} %bt_ref.1) | copy-start | bytes 2457604
  53.8 1.4 %copy-start.6 = (f32[25,64,128]{2,1,0:T(8,128)}, f32[25,64,128]{2,1,0:T(8,128)S(1)}, u32[]{:S(2)}) copy-start(f32[25,64,128]{2,1,0:T(8,128)S(1)} %get-tuple-element.9.bt_ref) | copy-start | bytes 2457604
  53.8 1.4 %copy-start.8 = (f32[25,64,128]{2,1,0:T(8,128)}, f32[25,64,128]{2,1,0:T(8,128)S(1)}, u32[]{:S(2)}) copy-start(f32[25,64,128]{2,1,0:T(8,128)S(1)} %get-tuple-element.10.bs_ref) | copy-start | bytes 2457604
  56.5 29.1 %collective-permute-start.10 = (f32[2,25,2,128]{3,2,1,0:T(2,128)S(1)}, f32[2,25,2,128]{3,2,1,0:T(2,128)}, u32[]{:S(2)}, u32[]{:S(2)}) collective-permute-start(f32[2,25,2,128]{3,2,1,0:T(2,128)S(1)} %pad_maximum_fusion.10), channel_id=1, source_target_pairs={{7,127},{15,119},{23,111},{31,103},{39,95},{47,87},{55,79},{63,71}... | collective-permute-start | bytes 153608 | tf_op jit(solution)/shard_map/ppermute | solution.py:138
  60.5 26.3 %collective-permute-start.9 = (f32[2,25,2,128]{3,2,1,0:T(2,128)S(1)}, f32[2,25,2,128]{3,2,1,0:T(2,128)}, u32[]{:S(2)}, u32[]{:S(2)}) collective-permute-start(f32[2,25,2,128]{3,2,1,0:T(2,128)S(1)} %pad_maximum_fusion.10), channel_id=1, source_target_pairs={{0,1},{1,2},{2,3},{3,4},{4,5},{5,6},{6,7},{8,9},{9,10},{10,11},{11... | collective-permute-start | bytes 153608 | tf_op jit(solution)/shard_map/ppermute | solution.py:135
  65.4 11.3 %collective-permute-start.8 = (f32[2,25,64,2]{2,3,1,0:T(2,128)}, f32[2,25,64,2]{2,3,1,0:T(2,128)}, u32[]{:S(2)}, u32[]{:S(2)}) collective-permute-start(f32[2,25,64,2]{2,3,1,0:T(2,128)} %pad_maximum_fusion.9), channel_id=1, source_target_pairs={{0,8},{8,16},{16,24},{24,32},{32,40},{40,48},{48,56},{56,64},{64,7... | collective-permute-start | bytes 76808 | tf_op jit(solution)/shard_map/ppermute | solution.py:133
  66.1 13.2 %collective-permute-start.7 = (f32[2,25,64,2]{2,3,1,0:T(2,128)S(1)}, f32[2,25,64,2]{2,3,1,0:T(2,128)S(1)}, u32[]{:S(2)}, u32[]{:S(2)}) collective-permute-start(f32[2,25,64,2]{2,3,1,0:T(2,128)S(1)} %pad_maximum_fusion.8), channel_id=1, source_target_pairs={{0,120},{8,0},{16,8},{24,16},{32,24},{40,32},{48,40},{56,48},{64,5... | collective-permute-start | bytes 76808 | tf_op jit(solution)/shard_map/ppermute | solution.py:132
  71.5 15.2 %collective-permute-start.11 = (f32[2,25,2,128]{3,2,1,0:T(2,128)S(1)}, f32[2,25,2,128]{3,2,1,0:T(2,128)}, u32[]{:S(2)}, u32[]{:S(2)}) collective-permute-start(f32[2,25,2,128]{3,2,1,0:T(2,128)S(1)} %pad_maximum_fusion.11), channel_id=1, source_target_pairs={{1,0},{2,1},{3,2},{4,3},{5,4},{6,5},{7,6},{9,8},{10,9},{11,10},{12... | collective-permute-start | bytes 153608 | tf_op jit(solution)/shard_map/ppermute | solution.py:134
  81.0 6.7 %copy-start.1 = (f32[25,64,128]{2,1,0:T(8,128)S(1)}, f32[25,64,128]{2,1,0:T(8,128)}, u32[]{:S(2)}) copy-start(f32[25,64,128]{2,1,0:T(8,128)} %ue_ref.3) | copy-start | bytes 2457604
  81.0 6.7 %copy-start.2 = (f32[25,64,128]{2,1,0:T(8,128)S(1)}, f32[25,64,128]{2,1,0:T(8,128)}, u32[]{:S(2)}) copy-start(f32[25,64,128]{2,1,0:T(8,128)} %vn_ref.3) | copy-start | bytes 2457604
  87.8 1.1 %copy-start.7 = (f32[25,64,128]{2,1,0:T(8,128)S(1)}, f32[25,64,128]{2,1,0:T(8,128)}, u32[]{:S(2)}) copy-start(f32[25,64,128]{2,1,0:T(8,128)} %copy-done.6) | copy-start | bytes 2457604
  88.9 1.1 %copy-start.9 = (f32[25,64,128]{2,1,0:T(8,128)S(1)}, f32[25,64,128]{2,1,0:T(8,128)}, u32[]{:S(2)}) copy-start(f32[25,64,128]{2,1,0:T(8,128)} %copy-done.8) | copy-start | bytes 2457604

commit v3 on v2

--- a/solution.py
+++ b/solution.py
@@ -30,12 +30,55 @@
     return flux + jnp.abs(u) * ((q4 - q1) - 3.0 * (q3 - q2)) / 12.0
 
 
-def step_kernel(mask_inputs, final, bl_ref, nt_ref, ns_ref, bt_ref, bs_ref, h_ref, yh_ref,
+def edge_tiles(rows, cols):
+    r = lax.broadcasted_iota(jnp.int32, (8, cols), 0)
+    c = lax.broadcasted_iota(jnp.int32, (8, cols), 1)
+    picked = ((r == 0) & (c == 0)) | ((r == 1) & (c == 1))
+    picked = picked | ((r == 2) & (c == cols - 2)) | ((r == 3) & (c == cols - 1))
+    return picked.astype(jnp.float32), (r == c).astype(jnp.float32)
+
+
+def write_packs(value, xpack_ref, ypack_ref, f, k, select):
+    rows, cols = value.shape
+    if select is not None:
+        write_columns(value, xpack_ref, f, k, select)
+    ypack_ref[f, k, 0:2, :] = value[0:2]
+    ypack_ref[f, k, 2:4, :] = value[rows - 2:rows]
+    ypack_ref[f, k, 4:8, :] = jnp.zeros((4, cols), jnp.float32)
+
+
+def write_columns(value, xpack_ref, f, k, select):
+    xpack_ref[f, k] = lax.dot_general(
+        select, value, (((1,), (1,)), ((), ())), precision=lax.Precision.HIGHEST,
+        preferred_element_type=jnp.float32)
+
+
+def expand_columns(tile, spread):
+    return lax.dot_general(
+        tile, spread, (((0,), (0,)), ((), ())), precision=lax.Precision.HIGHEST,
+        preferred_element_type=jnp.float32)
+
+
+def edge_kernel(bl_ref, nt_ref, ns_ref, xpack_ref, ypack_ref):
+    levels, rows, cols = nt_ref.shape
+    select, _ = edge_tiles(rows, cols)
+
+    def level(k, carry):
+        m = (k < bl_ref[...]).astype(jnp.float32)
+        for f, ref in enumerate((nt_ref, ns_ref)):
+            write_packs(ref[k] * m, xpack_ref, ypack_ref, f, k, select)
+        return carry
+
+    lax.fori_loop(0, levels, level, 0)
+
+
+def step_kernel(mask_inputs, final, bl_ref, nt_ref, ns_ref, bt_ref, bs_ref, xh_ref, yh_ref,
                 ue_ref, vn_ref, *rest):
-    outs, fv = rest[:-1], rest[-1]
+    outs, fv, hs = rest[:-2], rest[-2], rest[-1]
     levels, rows, cols = nt_ref.shape
     lane = lax.broadcasted_iota(jnp.int32, (rows, cols), 1)
     row = lax.broadcasted_iota(jnp.int32, (rows, cols), 0)
+    select, spread = edge_tiles(rows, cols)
     now_refs, bef_refs = (nt_ref, ns_ref), (bt_ref, bs_ref)
 
     def mask(k):
@@ -64,17 +107,25 @@
 
     lax.fori_loop(0, levels - 1, mixing, 0)
 
+    def expand(k, carry):
+        for f in range(2):
+            hs[f, k] = expand_columns(xh_ref[f, k], spread)
+        return carry
+
+    lax.fori_loop(0, levels, expand, 0, unroll=True)
+
     def level(k, carry):
         m = mask(k)
         ue, vn = ue_ref[k], vn_ref[k]
-        uw = jnp.where(lane < 1, pltpu.roll(h_ref[0, k], cols - 4, 1), pltpu.roll(ue, 1, 1))
-        vs = jnp.where(row < 1, jnp.broadcast_to(yh_ref[0, k][4:5], (rows, cols)), pltpu.roll(vn, 1, 0))
         afters = []
         for f in range(2):
             q = load(now_refs[f], k, m)
             b = load(bef_refs[f], k, m)
-            h = h_ref[f, k]
+            h = hs[f, k]
             yh = yh_ref[f, k]
+            if f == 0:
+                uw = jnp.where(lane < 1, pltpu.roll(h, cols - 4, 1), pltpu.roll(ue, 1, 1))
+                vs = jnp.where(row < 1, jnp.broadcast_to(yh[4:5], (rows, cols)), pltpu.roll(vn, 1, 0))
             qm1 = jnp.where(lane < 1, pltpu.roll(h, cols - 3, 1), pltpu.roll(q, 1, 1))
             qm2 = jnp.where(lane < 2, pltpu.roll(h, cols - 2, 1), pltpu.roll(q, 2, 1))
             qp1 = jnp.where(lane >= cols - 1, pltpu.roll(h, cols - 1, 1), pltpu.roll(q, cols - 1, 1))
@@ -96,6 +147,7 @@
             if not final:
                 outs[f][k] = q + asselin_gamma * (b - 2.0 * q + after)
                 outs[2 + f][k] = after
+                write_packs(after, outs[4], outs[5], f, k, None)
         if final:
             outs[0][k] = afters[0]
             outs[1][k] = afters[1]
@@ -104,69 +156,95 @@
 
     lax.fori_loop(0, levels, level, 0)
 
-
-def step_call(mask_inputs, final, bl, nt, ns, bt, bs, h, yh, ue, vn):
+    if not final:
+        def columns(k, carry):
+            for f in range(2):
+                write_columns(outs[2 + f][k], outs[4], f, k, select)
+            return carry
+
+        lax.fori_loop(0, levels, columns, 0, unroll=True)
+
+
+VMEM_SPEC = pl.BlockSpec(memory_space=pltpu.VMEM)
+
+
+def pack_shapes(levels, rows, cols):
+    return (jax.ShapeDtypeStruct((2, levels, 8, rows), jnp.float32),
+            jax.ShapeDtypeStruct((2, levels, 8, cols), jnp.float32))
+
+
+def edge_call(bl, nt, ns):
+    levels, rows, cols = nt.shape
+    return pl.pallas_call(
+        edge_kernel,
+        out_shape=pack_shapes(levels, rows, cols),
+        in_specs=[VMEM_SPEC] * 3,
+        out_specs=(VMEM_SPEC, VMEM_SPEC),
+        cost_estimate=pl.CostEstimate(
+            flops=2 * 2 * levels * 8 * rows * cols, transcendentals=0,
+            bytes_accessed=4 * levels * rows * cols * 3),
+    )(bl, nt, ns)
+
+
+def step_call(mask_inputs, final, bl, nt, ns, bt, bs, xh, yh, ue, vn):
     levels, rows, cols = nt.shape
     field = jax.ShapeDtypeStruct(nt.shape, jnp.float32)
-    n_out = 3 if final else 4
-    vspec = pl.BlockSpec(memory_space=pltpu.VMEM)
+    out_shape = (field,) * 3 if final else (field,) * 4 + pack_shapes(levels, rows, cols)
     return pl.pallas_call(
         functools.partial(step_kernel, mask_inputs, final),
-        out_shape=tuple([field] * n_out),
-        in_specs=[vspec] * 9,
-        out_specs=tuple([vspec] * n_out),
-        scratch_shapes=[pltpu.VMEM((2, levels + 1, rows, cols), jnp.float32)],
+        out_shape=out_shape,
+        in_specs=[VMEM_SPEC] * 9,
+        out_specs=tuple([VMEM_SPEC] * len(out_shape)),
+        scratch_shapes=[pltpu.VMEM((2, levels + 1, rows, cols), jnp.float32),
+                        pltpu.VMEM((2, levels, rows, cols), jnp.float32)],
         compiler_params=pltpu.CompilerParams(vmem_limit_bytes=48 * 1024 * 1024),
         cost_estimate=pl.CostEstimate(
             flops=400 * 2 * levels * rows * cols, transcendentals=levels * rows * cols,
-            bytes_accessed=4 * levels * rows * cols * (9 + n_out)),
-    )(bl, nt, ns, bt, bs, h, yh, ue, vn)
-
-
-def exchange(t, s, west_column, south_row, at_fold):
+            bytes_accessed=4 * levels * rows * cols * (9 + len(out_shape))),
+    )(bl, nt, ns, bt, bs, xh, yh, ue, vn)
+
+
+def exchange(xpack, ypack, west_column, south_row, at_fold):
     lon_count, lat_count = (lax.axis_size("lon"), lax.axis_size("lat"))
-    cols_first = jnp.stack([t[..., :2], s[..., :2]])
-    cols_last = jnp.stack([t[..., -2:], s[..., -2:]])
-    rows_first = jnp.stack([t[:, :2], s[:, :2]])
-    rows_last = jnp.stack([t[:, -2:], s[:, -2:]])
-    east = lax.ppermute(cols_first, "lon", [(i, (i - 1) % lon_count) for i in range(lon_count)])
-    west = lax.ppermute(cols_last, "lon", [(i, (i + 1) % lon_count) for i in range(lon_count)])
-    north = lax.ppermute(rows_first, "lat", [(i, i - 1) for i in range(1, lat_count)])
-    south = lax.ppermute(rows_last, "lat", [(i, i + 1) for i in range(lat_count - 1)])
+    from_east = lax.ppermute(xpack, "lon", [(i, (i - 1) % lon_count) for i in range(lon_count)])
+    from_west = lax.ppermute(xpack, "lon", [(i, (i + 1) % lon_count) for i in range(lon_count)])
+    from_north = lax.ppermute(ypack, "lat", [(i, i - 1) for i in range(1, lat_count)])
+    from_south = lax.ppermute(ypack, "lat", [(i, i + 1) for i in range(lat_count - 1)])
     top = lat_count - 1
     fold_pairs = [(d * lat_count + top, (lon_count - 1 - d) * lat_count + top) for d in range(lon_count)]
-    partner = lax.ppermute(rows_last, ("lon", "lat"), fold_pairs)[:, :, ::-1, :]
-    cols = t.shape[-1]
+    partner = lax.ppermute(ypack[:, :, 2:4], ("lon", "lat"), fold_pairs)
+    cols = ypack.shape[-1]
     flip = (jnp.arange(cols)[:, None] + jnp.arange(cols)[None, :] == cols - 1).astype(jnp.float32)
-    mirror = jnp.einsum("fkrc,cd->fkrd", partner, flip, precision=lax.Precision.HIGHEST)
-    north = jnp.where(at_fold, mirror, north)
-    shape = cols_first.shape
+    flipped = jnp.einsum("fkrc,cd->fkrd", partner, flip, precision=lax.Precision.HIGHEST)
+    mirror = jnp.concatenate([flipped[:, :, 1:2], flipped[:, :, 0:1]], 2)
+    north = jnp.where(at_fold, mirror, from_north[:, :, 0:2])
+    two, levels, _, rows = xpack.shape
     halo_x = jnp.concatenate(
-        [east, west, jnp.broadcast_to(west_column[None], shape[:3] + (1,)),
-         jnp.zeros(shape[:3] + (cols - 5,), jnp.float32)], 3)
+        [from_east[:, :, 0:2], from_west[:, :, 2:4],
+         jnp.broadcast_to(west_column[None, :, None, :], (two, levels, 1, rows)),
+         jnp.zeros((two, levels, 3, rows), jnp.float32)], 2)
     halo_y = jnp.concatenate(
-        [south, north, jnp.broadcast_to(south_row[None], (2,) + south_row.shape),
-         jnp.zeros((2, t.shape[0], 3, cols), jnp.float32)], 2)
+        [from_south[:, :, 2:4], north,
+         jnp.broadcast_to(south_row[None, :, None, :], (two, levels, 1, cols)),
+         jnp.zeros((two, levels, 3, cols), jnp.float32)], 2)
     return halo_x, halo_y
 
 
 def on_device(
     temp_before, temp_now, salt_before, salt_now, east_velocity, north_velocity, bottom_level
 ):
-    levels = temp_now.shape[0]
-    ocean_mask = (jnp.arange(levels, dtype=jnp.int32)[:, None, None] < bottom_level[None]).astype(
-        jnp.float32
-    )
     lon_count, lat_count = (lax.axis_size("lon"), lax.axis_size("lat"))
     west_column = lax.ppermute(
-        east_velocity[:, :, -1:], "lon", [(i, (i + 1) % lon_count) for i in range(lon_count)])
+        east_velocity[:, :, -1], "lon", [(i, (i + 1) % lon_count) for i in range(lon_count)])
     south_row = lax.ppermute(
-        north_velocity[:, -1:, :], "lat", [(i, i + 1) for i in range(lat_count - 1)])
+        north_velocity[:, -1, :], "lat", [(i, i + 1) for i in range(lat_count - 1)])
     at_fold = lax.axis_index("lat") == lat_count - 1
-    halo_x, halo_y = exchange(temp_now * ocean_mask, salt_now * ocean_mask, west_column, south_row, at_fold)
-    ft, fs, at, as_ = step_call(True, False, bottom_level, temp_now, salt_now, temp_before, salt_before,
-                                halo_x, halo_y, east_velocity, north_velocity)
-    halo_x, halo_y = exchange(at, as_, west_column, south_row, at_fold)
+    xpack, ypack = edge_call(bottom_level, temp_now, salt_now)
+    halo_x, halo_y = exchange(xpack, ypack, west_column, south_row, at_fold)
+    ft, fs, at, as_, xpack, ypack = step_call(
+        True, False, bottom_level, temp_now, salt_now, temp_before, salt_before,
+        halo_x, halo_y, east_velocity, north_velocity)
+    halo_x, halo_y = exchange(xpack, ypack, west_column, south_row, at_fold)
     return step_call(False, True, bottom_level, at, as_, ft, fs, halo_x, halo_y,
                      east_velocity, north_velocity)
 

time: 102 us -> 81 us (0.79)
  the two profiles are of different devices: /device:TPU:14 before, /device:TPU:8 now
where the time goes in v3:
time: 81 us; the launch traced here: 80.5 us
  Pallas kernels  33.7 us (42%)
  starting transfers between devices  28.5 us (35%)
  waiting for transfers between devices  12.9 us (16%)
  local copies, waits for them, and re-layouts  3.58 us (4%)
  between operations  1.01 us (1%)
    pallas_call x2, Pallas kernels, step_call(): pl.pallas_call(functools.partial(step_kernel, mask_inputs, final), out_sh...  26 us
    ppermute x2, starting transfers between devices, exchange(): lax.ppermute(xpack, 'lon', [(i, (i - 1) % lon_count) for i in range(lon_c...  10.7 us
    ppermute x2, starting transfers between devices, exchange(): lax.ppermute(ypack, 'lat', [(i, i - 1) for i in range(1, lat_count)])  10.4 us
    pallas_call x1, Pallas kernels, edge_call(): pl.pallas_call(edge_kernel, out_shape=pack_shapes(levels, rows, cols), in...  7.63 us
    ppermute x2, waiting for transfers between devices, exchange(): lax.ppermute(ypack, 'lat', [(i, i + 1) for i in range(lat_count - 1)])  7.37 us
    ppermute x1, waiting for transfers between devices, on_device(): lax.ppermute(east_velocity[:, :, -1], 'lon', [(i, (i + 1) % lon_count) fo...  4.47 us
    ppermute x2, starting transfers between devices, exchange(): lax.ppermute(ypack, 'lat', [(i, i + 1) for i in range(lat_count - 1)])  3.84 us
    ppermute x1, starting transfers between devices, on_device(): lax.ppermute(north_velocity[:, -1, :], 'lat', [(i, i + 1) for i in range(...  1.94 us
  transfers between devices with their start and end apart: 12, of which 3 were waited for; matrix products, arithmetic and copies ran while one was open for 3% of the time, Pallas kernels for 0%

profile of v3, /device:TPU:8, one launch (start us, length us, event | category | flops | bytes accessed | tf_op | source)
XLA Modules:
  0.0 80.5 jit_solution(141584858563274969)
XLA Ops:
  0.6 0.0 copy-start
  0.6 7.6 %shard_map.94 = (f32[2,25,8,64]{3,2,1,0:T(8,128)}, f32[2,25,8,128]{3,2,1,0:T(8,128)}) custom-call(s32[64,128]{1,0:T(8,128)} %bl_ref.5, f32[25,64,128]{2,1,0:T(8,128)} %nt_ref.3, f32[25,64,128]{2,1,0:T(8,128)} %ns_ref.3), custom_call_target="tpu_custom_call" | custom-call | flops 6553600 | bytes 2457600 | tf_op jit(solution)/shard_map/pallas_call | solution.py:178
  8.3 1.0 %slice.52 = f32[2,25,2,128]{3,2,1,0:T(2,128)S(1)} slice(f32[2,25,8,128]{3,2,1,0:T(8,128)} %get-tuple-element.12), slice={[0:2], [0:25], [2:4], [0:128]} | slice | bytes 102400 | tf_op jit(solution)/shard_map/slice | solution.py:215
  9.2 0.7 collective-permute-start.4
  9.9 0.1 collective-permute-start.1
  10.0 5.3 %collective-permute-start = (f32[2,25,8,64]{3,2,1,0:T(8,128)}, f32[2,25,8,64]{3,2,1,0:T(8,128)S(1)}, u32[]{:S(2)}, u32[]{:S(2)}) collective-permute-start(f32[2,25,8,64]{3,2,1,0:T(8,128)} %get-tuple-element.11), channel_id=1, source_target_pairs={{0,120},{8,0},{16,8},{24,16},{32,24},{40,32},{48,40},{56,48},{64,5... | collective-permute-start | bytes 307208 | tf_op jit(solution)/shard_map/ppermute | solution.py:209
  15.3 5.4 %collective-permute-start.5 = (f32[2,25,8,128]{3,2,1,0:T(8,128)}, f32[2,25,8,128]{3,2,1,0:T(8,128)S(1)}, u32[]{:S(2)}, u32[]{:S(2)}) collective-permute-start(f32[2,25,8,128]{3,2,1,0:T(8,128)} %get-tuple-element.12), channel_id=1, source_target_pairs={{1,0},{2,1},{3,2},{4,3},{5,4},{6,5},{7,6},{9,8},{10,9},{11,10},{12... | collective-permute-start | bytes 614408 | tf_op jit(solution)/shard_map/ppermute | solution.py:211
  20.7 1.9 %collective-permute-start.3 = (f32[2,25,8,128]{3,2,1,0:T(8,128)}, f32[2,25,8,128]{3,2,1,0:T(8,128)S(1)}, u32[]{:S(2)}, u32[]{:S(2)}) collective-permute-start(f32[2,25,8,128]{3,2,1,0:T(8,128)} %get-tuple-element.12), channel_id=1, source_target_pairs={{0,1},{1,2},{2,3},{3,4},{4,5},{5,6},{6,7},{8,9},{9,10},{10,11},{11... | collective-permute-start | bytes 614408 | tf_op jit(solution)/shard_map/ppermute | solution.py:212
  22.6 0.9 %slice.56 = f32[25,1,128]{2,1,0:T(1,128)S(1)} slice(f32[25,64,128]{2,1,0:T(8,128)} %vn_ref.3), slice={[0:25], [63:64], [0:128]} | slice | bytes 25600 | tf_op jit(solution)/shard_map/slice | solution.py:240
  23.6 0.0 copy-done
  23.6 0.3 slice.50
  23.9 0.0 copy-start.4
  23.9 0.4 copy.25
  24.2 0.1 pad.19.clone
  24.3 0.0 collective-permute-done.4
  24.3 0.0 collective-permute-start.2
  24.4 0.2 fusion.6
  24.6 0.0 collective-permute-done.1
  24.6 1.9 %collective-permute-start.6 = (f32[25,128]{1,0:T(8,128)S(1)}, f32[25,128]{1,0:T(8,128)S(1)}, u32[]{:S(2)}, u32[]{:S(2)}) collective-permute-start(f32[25,128]{1,0:T(8,128)S(1)} %bitcast.11), channel_id=1, source_target_pairs={{0,1},{1,2},{2,3},{3,4},{4,5},{5,6},{6,7},{8,9},{9,10},{10,11},{11... | collective-permute-start | bytes 38408 | tf_op jit(solution)/shard_map/ppermute | solution.py:239
  26.6 0.0 collective-permute-done
  26.7 4.5 %collective-permute-done.2 = f32[25,64]{1,0:T(8,128)S(1)} collective-permute-done((f32[25,64]{1,0:T(8,128)S(1)}, f32[25,64]{1,0:T(8,128)S(1)}, u32[]{:S(2)}, u32[]{:S(2)}) %collective-permute-start.2) | collective-permute-done | bytes 6432 | tf_op jit(solution)/shard_map/ppermute | solution.py:237
  31.1 0.1 fusion.2.xh_ref
  31.2 0.0 collective-permute-done.5
  31.2 0.1 slice_select_fusion.1
  31.3 0.0 collective-permute-done.3
  31.4 1.0 %collective-permute-done.6 = f32[25,128]{1,0:T(8,128)S(1)} collective-permute-done((f32[25,128]{1,0:T(8,128)S(1)}, f32[25,128]{1,0:T(8,128)S(1)}, u32[]{:S(2)}, u32[]{:S(2)}) %collective-permute-start.6) | collective-permute-done | bytes 12832 | tf_op jit(solution)/shard_map/ppermute | solution.py:239
  32.4 0.0 copy-start.5
  32.4 0.1 fusion.yh_ref
  32.5 0.0 copy-done.4
  32.5 0.6 copy-done.5
  33.2 14.6 %shard_map.95 = (f32[25,64,128]{2,1,0:T(8,128)S(1)}, f32[25,64,128]{2,1,0:T(8,128)S(1)}, f32[25,64,128]{2,1,0:T(8,128)S(1)}, f32[25,64,128]{2,1,0:T(8,128)S(1)},...) custom-call(s32[64,128]{1,0:T(8,128)S(1)} %copy-done.5, f32[25,64,128]{2,1,0:T(8,128)S(1)} %copy-done.3, ...), custom_call_target="tpu_custom_call" | custom-call | flops 163840000 | bytes 12288000 | tf_op jit(solution)/shard_map/pallas_call | solution.py:193
  47.8 0.8 collective-permute-start.10
  48.6 0.1 collective-permute-start.8
  48.7 5.3 %collective-permute-start.7 = (f32[2,25,8,64]{3,2,1,0:T(8,128)S(1)}, f32[2,25,8,64]{3,2,1,0:T(8,128)S(1)}, u32[]{:S(2)}, u32[]{:S(2)}) collective-permute-start(f32[2,25,8,64]{3,2,1,0:T(8,128)S(1)} %get-tuple-element.17), channel_id=1, source_target_pairs={{0,120},{8,0},{16,8},{24,16},{32,24},{40,32},{48,40},{56,48},{64,5... | collective-permute-start | bytes 307208 | tf_op jit(solution)/shard_map/ppermute | solution.py:209
  54.0 5.0 %collective-permute-start.11 = (f32[2,25,8,128]{3,2,1,0:T(8,128)S(1)}, f32[2,25,8,128]{3,2,1,0:T(8,128)S(1)}, u32[]{:S(2)}, u32[]{:S(2)}) collective-permute-start(f32[2,25,8,128]{3,2,1,0:T(8,128)S(1)} %get-tuple-element.18), channel_id=1, source_target_pairs={{1,0},{2,1},{3,2},{4,3},{5,4},{6,5},{7,6},{9,8},{10,9},{11,10},{12... | collective-permute-start | bytes 614408 | tf_op jit(solution)/shard_map/ppermute | solution.py:211
  59.0 1.9 %collective-permute-start.9 = (f32[2,25,8,128]{3,2,1,0:T(8,128)S(1)}, f32[2,25,8,128]{3,2,1,0:T(8,128)S(1)}, u32[]{:S(2)}, u32[]{:S(2)}) collective-permute-start(f32[2,25,8,128]{3,2,1,0:T(8,128)S(1)} %get-tuple-element.18), channel_id=1, source_target_pairs={{0,1},{1,2},{2,3},{3,4},{4,5},{5,6},{6,7},{8,9},{9,10},{10,11},{11... | collective-permute-start | bytes 614408 | tf_op jit(solution)/shard_map/ppermute | solution.py:212
  61.0 0.0 collective-permute-done.10
  61.0 0.2 fusion.4
  61.2 0.0 collective-permute-done.8
  61.3 0.0 collective-permute-done.7
  61.3 0.1 fusion.3.xh_ref
  61.4 7.4 %collective-permute-done.9 = f32[2,25,8,128]{3,2,1,0:T(8,128)S(1)} collective-permute-done((f32[2,25,8,128]{3,2,1,0:T(8,128)S(1)}, f32[2,25,8,128]{3,2,1,0:T(8,128)S(1)}, u32[]{:S(2)}, u32[]{:S(2)}) %collective-permute-start.9) | collective-permute-done | bytes 204832 | tf_op jit(solution)/shard_map/ppermute | solution.py:212
  68.8 0.0 collective-permute-done.11
  68.8 0.1 slice_select_fusion
  68.9 0.1 fusion.1.yh_ref
  69.0 0.0 copy-done.2
  69.0 0.0 copy-done.1
  69.0 11.4 %shard_map.96 = (f32[25,64,128]{2,1,0:T(8,128)}, f32[25,64,128]{2,1,0:T(8,128)}, f32[25,64,128]{2,1,0:T(8,128)}) custom-call(s32[64,128]{1,0:T(8,128)S(1)} %copy-done.5, f32[25,64,128]{2,1,0:T(8,128)S(1)} %get-tuple-element.13.nt_ref, f32[25,64,128]{2,1,0:T(8,128)S(1)} %get-tuple-element.14.ns_ref, f32[25,64,128]{2,1,0:T(8,128)S(1)} %get-tuple-element.15.bt_ref, ...), custom_call_target="tpu_custom_call" | custom-call | flops 163840000 | bytes 9830400 | tf_op jit(solution)/shard_map/pallas_call | solution.py:193
  (21 shorter events, 0.3 us)
Async XLA Ops:
  0.6 22.9 %copy-start = (f32[25,64,128]{2,1,0:T(8,128)S(1)}, f32[25,64,128]{2,1,0:T(8,128)}, u32[]{:S(2)}) copy-start(f32[25,64,128]{2,1,0:T(8,128)} %ue_ref.3) | copy-start | bytes 2457604
  9.2 15.1 %collective-permute-start.4 = (f32[2,25,2,128]{3,2,1,0:T(2,128)S(1)}, f32[2,25,2,128]{3,2,1,0:T(2,128)S(1)}, u32[]{:S(2)}, u32[]{:S(2)}) collective-permute-start(f32[2,25,2,128]{3,2,1,0:T(2,128)S(1)} %slice.52), channel_id=1, source_target_pairs={{7,127},{15,119},{23,111},{31,103},{39,95},{47,87},{55,79},{63,71}... | collective-permute-start | bytes 153608 | tf_op jit(solution)/shard_map/ppermute | solution.py:215
  9.9 14.7 %collective-permute-start.1 = (f32[2,25,8,64]{3,2,1,0:T(8,128)}, f32[2,25,8,64]{3,2,1,0:T(8,128)S(1)}, u32[]{:S(2)}, u32[]{:S(2)}) collective-permute-start(f32[2,25,8,64]{3,2,1,0:T(8,128)} %get-tuple-element.11), channel_id=1, source_target_pairs={{0,8},{8,16},{16,24},{24,32},{32,40},{40,48},{48,56},{56,64},{64,7... | collective-permute-start | bytes 307208 | tf_op jit(solution)/shard_map/ppermute | solution.py:210
  10.0 16.6 %collective-permute-start = (f32[2,25,8,64]{3,2,1,0:T(8,128)}, f32[2,25,8,64]{3,2,1,0:T(8,128)S(1)}, u32[]{:S(2)}, u32[]{:S(2)}) collective-permute-start(f32[2,25,8,64]{3,2,1,0:T(8,128)} %get-tuple-element.11), channel_id=1, source_target_pairs={{0,120},{8,0},{16,8},{24,16},{32,24},{40,32},{48,40},{56,48},{64,5... | collective-permute-start | bytes 307208 | tf_op jit(solution)/shard_map/ppermute | solution.py:209
  15.3 15.9 %collective-permute-start.5 = (f32[2,25,8,128]{3,2,1,0:T(8,128)}, f32[2,25,8,128]{3,2,1,0:T(8,128)S(1)}, u32[]{:S(2)}, u32[]{:S(2)}) collective-permute-start(f32[2,25,8,128]{3,2,1,0:T(8,128)} %get-tuple-element.12), channel_id=1, source_target_pairs={{1,0},{2,1},{3,2},{4,3},{5,4},{6,5},{7,6},{9,8},{10,9},{11,10},{12... | collective-permute-start | bytes 614408 | tf_op jit(solution)/shard_map/ppermute | solution.py:211
  20.7 10.6 %collective-permute-start.3 = (f32[2,25,8,128]{3,2,1,0:T(8,128)}, f32[2,25,8,128]{3,2,1,0:T(8,128)S(1)}, u32[]{:S(2)}, u32[]{:S(2)}) collective-permute-start(f32[2,25,8,128]{3,2,1,0:T(8,128)} %get-tuple-element.12), channel_id=1, source_target_pairs={{0,1},{1,2},{2,3},{3,4},{4,5},{5,6},{6,7},{8,9},{9,10},{10,11},{11... | collective-permute-start | bytes 614408 | tf_op jit(solution)/shard_map/ppermute | solution.py:212
  23.9 8.7 %copy-start.4 = (f32[25,64,128]{2,1,0:T(8,128)S(1)}, f32[25,64,128]{2,1,0:T(8,128)}, u32[]{:S(2)}) copy-start(f32[25,64,128]{2,1,0:T(8,128)} %ns_ref.3) | copy-start | bytes 2457604
  24.2 8.3 %copy-start.3 = (f32[25,64,128]{2,1,0:T(8,128)S(1)}, f32[25,64,128]{2,1,0:T(8,128)}, u32[]{:S(2)}) copy-start(f32[25,64,128]{2,1,0:T(8,128)} %nt_ref.3) | copy-start | bytes 2457604
  24.3 6.8 %collective-permute-start.2 = (f32[25,64]{1,0:T(8,128)S(1)}, f32[25,64]{1,0:T(8,128)S(1)}, u32[]{:S(2)}, u32[]{:S(2)}) collective-permute-start(f32[25,64]{1,0:T(8,128)S(1)} %bitcast.10), channel_id=1, source_target_pairs={{0,8},{8,16},{16,24},{24,32},{32,40},{40,48},{48,56},{56,64},{64,7... | collective-permute-start | bytes 19208 | tf_op jit(solution)/shard_map/ppermute | solution.py:237
  24.6 7.7 %collective-permute-start.6 = (f32[25,128]{1,0:T(8,128)S(1)}, f32[25,128]{1,0:T(8,128)S(1)}, u32[]{:S(2)}, u32[]{:S(2)}) collective-permute-start(f32[25,128]{1,0:T(8,128)S(1)} %bitcast.11), channel_id=1, source_target_pairs={{0,1},{1,2},{2,3},{3,4},{4,5},{5,6},{6,7},{8,9},{9,10},{10,11},{11... | collective-permute-start | bytes 38408 | tf_op jit(solution)/shard_map/ppermute | solution.py:239
  32.4 0.8 copy-start.5
  33.2 35.8 %copy-start.2 = (f32[25,64,128]{2,1,0:T(8,128)S(1)}, f32[25,64,128]{2,1,0:T(8,128)}, u32[]{:S(2)}) copy-start(f32[25,64,128]{2,1,0:T(8,128)} %vn_ref.3) | copy-start | bytes 2457604
  47.7 21.3 %copy-start.1 = (f32[25,64,128]{2,1,0:T(8,128)S(1)}, f32[25,64,128]{2,1,0:T(8,128)}, u32[]{:S(2)}) copy-start(f32[25,64,128]{2,1,0:T(8,128)} %ue_ref.3) | copy-start | bytes 2457604
  47.8 13.2 %collective-permute-start.10 = (f32[2,25,2,128]{3,2,1,0:T(2,128)S(1)}, f32[2,25,2,128]{3,2,1,0:T(2,128)S(1)}, u32[]{:S(2)}, u32[]{:S(2)}) collective-permute-start(f32[2,25,2,128]{3,2,1,0:T(2,128)S(1)} %slice.60), channel_id=1, source_target_pairs={{7,127},{15,119},{23,111},{31,103},{39,95},{47,87},{55,79},{63,71}... | collective-permute-start | bytes 153608 | tf_op jit(solution)/shard_map/ppermute | solution.py:215
  48.6 12.7 %collective-permute-start.8 = (f32[2,25,8,64]{3,2,1,0:T(8,128)S(1)}, f32[2,25,8,64]{3,2,1,0:T(8,128)S(1)}, u32[]{:S(2)}, u32[]{:S(2)}) collective-permute-start(f32[2,25,8,64]{3,2,1,0:T(8,128)S(1)} %get-tuple-element.17), channel_id=1, source_target_pairs={{0,8},{8,16},{16,24},{24,32},{32,40},{40,48},{48,56},{56,64},{64,7... | collective-permute-start | bytes 307208 | tf_op jit(solution)/shard_map/ppermute | solution.py:210
  48.7 12.6 %collective-permute-start.7 = (f32[2,25,8,64]{3,2,1,0:T(8,128)S(1)}, f32[2,25,8,64]{3,2,1,0:T(8,128)S(1)}, u32[]{:S(2)}, u32[]{:S(2)}) collective-permute-start(f32[2,25,8,64]{3,2,1,0:T(8,128)S(1)} %get-tuple-element.17), channel_id=1, source_target_pairs={{0,120},{8,0},{16,8},{24,16},{32,24},{40,32},{48,40},{56,48},{64,5... | collective-permute-start | bytes 307208 | tf_op jit(solution)/shard_map/ppermute | solution.py:209
  54.0 14.8 %collective-permute-start.11 = (f32[2,25,8,128]{3,2,1,0:T(8,128)S(1)}, f32[2,25,8,128]{3,2,1,0:T(8,128)S(1)}, u32[]{:S(2)}, u32[]{:S(2)}) collective-permute-start(f32[2,25,8,128]{3,2,1,0:T(8,128)S(1)} %get-tuple-element.18), channel_id=1, source_target_pairs={{1,0},{2,1},{3,2},{4,3},{5,4},{6,5},{7,6},{9,8},{10,9},{11,10},{12... | collective-permute-start | bytes 614408 | tf_op jit(solution)/shard_map/ppermute | solution.py:211
  59.0 9.8 %collective-permute-start.9 = (f32[2,25,8,128]{3,2,1,0:T(8,128)S(1)}, f32[2,25,8,128]{3,2,1,0:T(8,128)S(1)}, u32[]{:S(2)}, u32[]{:S(2)}) collective-permute-start(f32[2,25,8,128]{3,2,1,0:T(8,128)S(1)} %get-tuple-element.18), channel_id=1, source_target_pairs={{0,1},{1,2},{2,3},{3,4},{4,5},{5,6},{6,7},{8,9},{9,10},{10,11},{11... | collective-permute-start | bytes 614408 | tf_op jit(solution)/shard_map/ppermute | solution.py:212

commit v4 on v3

--- a/solution.py
+++ b/solution.py
@@ -35,22 +35,25 @@
     c = lax.broadcasted_iota(jnp.int32, (8, cols), 1)
     picked = ((r == 0) & (c == 0)) | ((r == 1) & (c == 1))
     picked = picked | ((r == 2) & (c == cols - 2)) | ((r == 3) & (c == cols - 1))
-    return picked.astype(jnp.float32), (r == c).astype(jnp.float32)
-
-
-def write_packs(value, xpack_ref, ypack_ref, f, k, select):
+    velocity = (r == 4) & (c == cols - 1)
+    return picked.astype(jnp.float32), velocity.astype(jnp.float32), (r == c).astype(jnp.float32)
+
+
+def write_columns(value, east_v, xpack_ref, f, k, select, select_v):
+    dims = (((1,), (1,)), ((), ()))
+    xpack_ref[f, k] = lax.dot_general(
+        select, value, dims, precision=lax.Precision.HIGHEST,
+        preferred_element_type=jnp.float32) + lax.dot_general(
+        select_v, east_v, dims, precision=lax.Precision.HIGHEST,
+        preferred_element_type=jnp.float32)
+
+
+def write_rows(value, north_v, ypack_ref, f, k):
     rows, cols = value.shape
-    if select is not None:
-        write_columns(value, xpack_ref, f, k, select)
     ypack_ref[f, k, 0:2, :] = value[0:2]
     ypack_ref[f, k, 2:4, :] = value[rows - 2:rows]
-    ypack_ref[f, k, 4:8, :] = jnp.zeros((4, cols), jnp.float32)
-
-
-def write_columns(value, xpack_ref, f, k, select):
-    xpack_ref[f, k] = lax.dot_general(
-        select, value, (((1,), (1,)), ((), ())), precision=lax.Precision.HIGHEST,
-        preferred_element_type=jnp.float32)
+    ypack_ref[f, k, 4:5, :] = north_v[rows - 1:rows]
+    ypack_ref[f, k, 5:8, :] = jnp.zeros((3, cols), jnp.float32)
 
 
 def expand_columns(tile, spread):
@@ -59,17 +62,19 @@
         preferred_element_type=jnp.float32)
 
 
-def edge_kernel(bl_ref, nt_ref, ns_ref, xpack_ref, ypack_ref):
+def edge_kernel(bl_ref, nt_ref, ns_ref, ue_ref, vn_ref, xpack_ref, ypack_ref):
     levels, rows, cols = nt_ref.shape
-    select, _ = edge_tiles(rows, cols)
+    select, select_v, _ = edge_tiles(rows, cols)
 
     def level(k, carry):
         m = (k < bl_ref[...]).astype(jnp.float32)
         for f, ref in enumerate((nt_ref, ns_ref)):
-            write_packs(ref[k] * m, xpack_ref, ypack_ref, f, k, select)
-        return carry
-
-    lax.fori_loop(0, levels, level, 0)
+            value = ref[k] * m
+            write_columns(value, ue_ref[k], xpack_ref, f, k, select, select_v)
+            write_rows(value, vn_ref[k], ypack_ref, f, k)
+        return carry
+
+    lax.fori_loop(0, levels, level, 0, unroll=True)
 
 
 def step_kernel(mask_inputs, final, bl_ref, nt_ref, ns_ref, bt_ref, bs_ref, xh_ref, yh_ref,
@@ -78,7 +83,7 @@
     levels, rows, cols = nt_ref.shape
     lane = lax.broadcasted_iota(jnp.int32, (rows, cols), 1)
     row = lax.broadcasted_iota(jnp.int32, (rows, cols), 0)
-    select, spread = edge_tiles(rows, cols)
+    select, select_v, spread = edge_tiles(rows, cols)
     now_refs, bef_refs = (nt_ref, ns_ref), (bt_ref, bs_ref)
 
     def mask(k):
@@ -147,7 +152,7 @@
             if not final:
                 outs[f][k] = q + asselin_gamma * (b - 2.0 * q + after)
                 outs[2 + f][k] = after
-                write_packs(after, outs[4], outs[5], f, k, None)
+                write_rows(after, vn, outs[5], f, k)
         if final:
             outs[0][k] = afters[0]
             outs[1][k] = afters[1]
@@ -159,7 +164,7 @@
     if not final:
         def columns(k, carry):
             for f in range(2):
-                write_columns(outs[2 + f][k], outs[4], f, k, select)
+                write_columns(outs[2 + f][k], ue_ref[k], outs[4], f, k, select, select_v)
             return carry
 
         lax.fori_loop(0, levels, columns, 0, unroll=True)
@@ -173,17 +178,17 @@
             jax.ShapeDtypeStruct((2, levels, 8, cols), jnp.float32))
 
 
-def edge_call(bl, nt, ns):
+def edge_call(bl, nt, ns, ue, vn):
     levels, rows, cols = nt.shape
     return pl.pallas_call(
         edge_kernel,
         out_shape=pack_shapes(levels, rows, cols),
-        in_specs=[VMEM_SPEC] * 3,
+        in_specs=[VMEM_SPEC] * 5,
         out_specs=(VMEM_SPEC, VMEM_SPEC),
         cost_estimate=pl.CostEstimate(
             flops=2 * 2 * levels * 8 * rows * cols, transcendentals=0,
-            bytes_accessed=4 * levels * rows * cols * 3),
-    )(bl, nt, ns)
+            bytes_accessed=4 * levels * rows * cols * 5),
+    )(bl, nt, ns, ue, vn)
 
 
 def step_call(mask_inputs, final, bl, nt, ns, bt, bs, xh, yh, ue, vn):
@@ -204,7 +209,7 @@
     )(bl, nt, ns, bt, bs, xh, yh, ue, vn)
 
 
-def exchange(xpack, ypack, west_column, south_row, at_fold):
+def exchange(xpack, ypack, at_fold):
     lon_count, lat_count = (lax.axis_size("lon"), lax.axis_size("lat"))
     from_east = lax.ppermute(xpack, "lon", [(i, (i - 1) % lon_count) for i in range(lon_count)])
     from_west = lax.ppermute(xpack, "lon", [(i, (i + 1) % lon_count) for i in range(lon_count)])
@@ -221,30 +226,23 @@
     two, levels, _, rows = xpack.shape
     halo_x = jnp.concatenate(
         [from_east[:, :, 0:2], from_west[:, :, 2:4],
-         jnp.broadcast_to(west_column[None, :, None, :], (two, levels, 1, rows)),
-         jnp.zeros((two, levels, 3, rows), jnp.float32)], 2)
+         from_west[:, :, 4:5], jnp.zeros((two, levels, 3, rows), jnp.float32)], 2)
     halo_y = jnp.concatenate(
         [from_south[:, :, 2:4], north,
-         jnp.broadcast_to(south_row[None, :, None, :], (two, levels, 1, cols)),
-         jnp.zeros((two, levels, 3, cols), jnp.float32)], 2)
+         from_south[:, :, 4:5], jnp.zeros((two, levels, 3, cols), jnp.float32)], 2)
     return halo_x, halo_y
 
 
 def on_device(
     temp_before, temp_now, salt_before, salt_now, east_velocity, north_velocity, bottom_level
 ):
-    lon_count, lat_count = (lax.axis_size("lon"), lax.axis_size("lat"))
-    west_column = lax.ppermute(
-        east_velocity[:, :, -1], "lon", [(i, (i + 1) % lon_count) for i in range(lon_count)])
-    south_row = lax.ppermute(
-        north_velocity[:, -1, :], "lat", [(i, i + 1) for i in range(lat_count - 1)])
-    at_fold = lax.axis_index("lat") == lat_count - 1
-    xpack, ypack = edge_call(bottom_level, temp_now, salt_now)
-    halo_x, halo_y = exchange(xpack, ypack, west_column, south_row, at_fold)
+    at_fold = lax.axis_index("lat") == lax.axis_size("lat") - 1
+    xpack, ypack = edge_call(bottom_level, temp_now, salt_now, east_velocity, north_velocity)
+    halo_x, halo_y = exchange(xpack, ypack, at_fold)
     ft, fs, at, as_, xpack, ypack = step_call(
         True, False, bottom_level, temp_now, salt_now, temp_before, salt_before,
         halo_x, halo_y, east_velocity, north_velocity)
-    halo_x, halo_y = exchange(xpack, ypack, west_column, south_row, at_fold)
+    halo_x, halo_y = exchange(xpack, ypack, at_fold)
     return step_call(False, True, bottom_level, at, as_, ft, fs, halo_x, halo_y,
                      east_velocity, north_velocity)
 

time: 81 us -> 78.6 us (0.970)
  starting transfers between devices: 28.5 us -> 25.3 us
  Pallas kernels: 33.7 us -> 36.2 us
  local copies, waits for them, and re-layouts: 3.58 us -> 2.04 us
    ppermute x2, waiting for transfers between devices: 7.37 us -> 12.9 us  [exchange(): lax.ppermute(ypack, 'lat', [(i, i + 1) for i in range(lat_count - 1)])]
    ppermute x2 -> x0, waiting for transfers between devices: 5.49 us -> none  [the longest x1 4.47 us: on_device(): lax.ppermute(east_velocity[:, :, -1], 'lon', [(i, (i + 1) % lon_count) fo...]
    ppermute x2, starting transfers between devices: 10.4 us -> 7.28 us  [exchange(): lax.ppermute(ypack, 'lat', [(i, i - 1) for i in range(1, lat_count)])]
    pallas_call x2, Pallas kernels: 26 us -> 28.4 us  [step_call(): pl.pallas_call(functools.partial(step_kernel, mask_inputs, final), out_sh...]
    ppermute x2, starting transfers between devices: 3.84 us -> 5.84 us  [exchange(): lax.ppermute(ypack, 'lat', [(i, i + 1) for i in range(lat_count - 1)])]
    ppermute x2 -> x0, starting transfers between devices: 1.96 us -> none  [the longest x1 1.94 us: on_device(): lax.ppermute(north_velocity[:, -1, :], 'lat', [(i, i + 1) for i in range(...]
    slice x2, local copies, waits for them, and re-layouts: 1.19 us -> 0.05 us  [exchange(): from_south[:, :, 4:5]]
  transfers between devices with their start and end apart: 12 -> 10, of which waited for: 3 -> 2; matrix products, arithmetic and copies ran while one was open for 3% -> 1% of each run, Pallas kernels for 0% -> 0%
where the time goes in v4:
time: 78.6 us; the launch traced here: 78.2 us
  Pallas kernels  36.2 us (46%)
  starting transfers between devices  25.3 us (32%)
  waiting for transfers between devices  12.9 us (16%)
  local copies, waits for them, and re-layouts  2.04 us (3%)
  between operations  0.98 us (1%)
    pallas_call x2, Pallas kernels, step_call(): pl.pallas_call(functools.partial(step_kernel, mask_inputs, final), out_sh...  28.4 us
    ppermute x2, waiting for transfers between devices, exchange(): lax.ppermute(ypack, 'lat', [(i, i + 1) for i in range(lat_count - 1)])  12.9 us
    ppermute x2, starting transfers between devices, exchange(): lax.ppermute(xpack, 'lon', [(i, (i - 1) % lon_count) for i in range(lon_c...  10.7 us
    pallas_call x1, Pallas kernels, edge_call(): pl.pallas_call(edge_kernel, out_shape=pack_shapes(levels, rows, cols), in...  7.77 us
    ppermute x2, starting transfers between devices, exchange(): lax.ppermute(ypack, 'lat', [(i, i - 1) for i in range(1, lat_count)])  7.28 us
    ppermute x2, starting transfers between devices, exchange(): lax.ppermute(ypack, 'lat', [(i, i + 1) for i in range(lat_count - 1)])  5.84 us
  transfers between devices with their start and end apart: 10, of which 2 were waited for; matrix products, arithmetic and copies ran while one was open for 1% of the time, Pallas kernels for 0%

profile of v4, /device:TPU:8, one launch (start us, length us, event | category | flops | bytes accessed | tf_op | source)
XLA Modules:
  0.0 78.2 jit_solution(9412403333393177448)
XLA Ops:
  0.6 7.8 %shard_map.94 = (f32[2,25,8,64]{3,2,1,0:T(8,128)}, f32[2,25,8,128]{3,2,1,0:T(8,128)}) custom-call(s32[64,128]{1,0:T(8,128)} %bl_ref.5, f32[25,64,128]{2,1,0:T(8,128)} %nt_ref.3, f32[25,64,128]{2,1,0:T(8,128)} %ns_ref.3, f32[25,64,128]{2,1,0:T(8,128)} %ue_ref.5, f32[25,64,128]{2,1,0:T(8,128)} %vn_ref.5), custom_call_target="tpu_custom_call" | custom-call | flops 6553600 | bytes 4096000 | tf_op jit(solution)/shard_map/pallas_call | solution.py:183
  8.4 1.0 %slice.55 = f32[2,25,2,128]{3,2,1,0:T(2,128)S(1)} slice(f32[2,25,8,128]{3,2,1,0:T(8,128)} %get-tuple-element.12), slice={[0:2], [0:25], [2:4], [0:128]} | slice | bytes 102400 | tf_op jit(solution)/shard_map/slice | solution.py:220
  9.4 0.7 collective-permute-start.3
  10.0 0.1 collective-permute-start.1
  10.1 5.3 %collective-permute-start = (f32[2,25,8,64]{3,2,1,0:T(8,128)}, f32[2,25,8,64]{3,2,1,0:T(8,128)S(1)}, u32[]{:S(2)}, u32[]{:S(2)}) collective-permute-start(f32[2,25,8,64]{3,2,1,0:T(8,128)} %get-tuple-element.11), channel_id=1, source_target_pairs={{0,120},{8,0},{16,8},{24,16},{32,24},{40,32},{48,40},{56,48},{64,5... | collective-permute-start | bytes 307208 | tf_op jit(solution)/shard_map/ppermute | solution.py:214
  15.5 5.4 %collective-permute-start.4 = (f32[2,25,8,128]{3,2,1,0:T(8,128)}, f32[2,25,8,128]{3,2,1,0:T(8,128)S(1)}, u32[]{:S(2)}, u32[]{:S(2)}) collective-permute-start(f32[2,25,8,128]{3,2,1,0:T(8,128)} %get-tuple-element.12), channel_id=1, source_target_pairs={{1,0},{2,1},{3,2},{4,3},{5,4},{6,5},{7,6},{9,8},{10,9},{11,10},{12... | collective-permute-start | bytes 614408 | tf_op jit(solution)/shard_map/ppermute | solution.py:216
  20.8 1.9 %collective-permute-start.2 = (f32[2,25,8,128]{3,2,1,0:T(8,128)}, f32[2,25,8,128]{3,2,1,0:T(8,128)S(1)}, u32[]{:S(2)}, u32[]{:S(2)}) collective-permute-start(f32[2,25,8,128]{3,2,1,0:T(8,128)} %get-tuple-element.12), channel_id=1, source_target_pairs={{0,1},{1,2},{2,3},{3,4},{4,5},{5,6},{6,7},{8,9},{9,10},{10,11},{11... | collective-permute-start | bytes 614408 | tf_op jit(solution)/shard_map/ppermute | solution.py:217
  22.8 0.1 pad.17.clone
  22.9 0.0 copy-start.2
  22.9 0.0 copy-start.3
  22.9 0.0 collective-permute-done.3
  22.9 0.2 fusion.2
  23.1 0.0 collective-permute-done.1
  23.2 0.0 collective-permute-done
  23.2 0.1 maximum_maximum_fusion.xh_ref
  23.3 7.5 %collective-permute-done.2 = f32[2,25,8,128]{3,2,1,0:T(8,128)S(1)} collective-permute-done((f32[2,25,8,128]{3,2,1,0:T(8,128)}, f32[2,25,8,128]{3,2,1,0:T(8,128)S(1)}, u32[]{:S(2)}, u32[]{:S(2)}) %collective-permute-start.2) | collective-permute-done | bytes 204832 | tf_op jit(solution)/shard_map/ppermute | solution.py:217
  30.9 0.0 collective-permute-done.4
  30.9 0.1 slice_select_fusion.1
  30.9 0.0 copy-start.4
  30.9 0.1 maximum_maximum_fusion.1.yh_ref
  31.0 0.0 copy-done.2
  31.0 0.0 copy-done.3
  31.1 0.6 copy-done.4
  31.7 17.0 %shard_map.95 = (f32[25,64,128]{2,1,0:T(8,128)S(1)}, f32[25,64,128]{2,1,0:T(8,128)S(1)}, f32[25,64,128]{2,1,0:T(8,128)S(1)}, f32[25,64,128]{2,1,0:T(8,128)S(1)},...) custom-call(s32[64,128]{1,0:T(8,128)S(1)} %copy-done.4, f32[25,64,128]{2,1,0:T(8,128)S(1)} %copy-done.2, ...), custom_call_target="tpu_custom_call" | custom-call | flops 163840000 | bytes 12288000 | tf_op jit(solution)/shard_map/pallas_call | solution.py:198
  48.7 0.7 collective-permute-start.8
  49.4 0.0 copy-start
  49.4 0.0 copy-start.1
  49.4 0.1 collective-permute-start.6
  49.5 5.3 %collective-permute-start.5 = (f32[2,25,8,64]{3,2,1,0:T(8,128)S(1)}, f32[2,25,8,64]{3,2,1,0:T(8,128)S(1)}, u32[]{:S(2)}, u32[]{:S(2)}) collective-permute-start(f32[2,25,8,64]{3,2,1,0:T(8,128)S(1)} %get-tuple-element.17), channel_id=1, source_target_pairs={{0,120},{8,0},{16,8},{24,16},{32,24},{40,32},{48,40},{56,48},{64,5... | collective-permute-start | bytes 307208 | tf_op jit(solution)/shard_map/ppermute | solution.py:214
  54.9 1.9 %collective-permute-start.9 = (f32[2,25,8,128]{3,2,1,0:T(8,128)S(1)}, f32[2,25,8,128]{3,2,1,0:T(8,128)S(1)}, u32[]{:S(2)}, u32[]{:S(2)}) collective-permute-start(f32[2,25,8,128]{3,2,1,0:T(8,128)S(1)} %get-tuple-element.18), channel_id=1, source_target_pairs={{1,0},{2,1},{3,2},{4,3},{5,4},{6,5},{7,6},{9,8},{10,9},{11,10},{12... | collective-permute-start | bytes 614408 | tf_op jit(solution)/shard_map/ppermute | solution.py:216
  56.8 3.9 %collective-permute-start.7 = (f32[2,25,8,128]{3,2,1,0:T(8,128)S(1)}, f32[2,25,8,128]{3,2,1,0:T(8,128)S(1)}, u32[]{:S(2)}, u32[]{:S(2)}) collective-permute-start(f32[2,25,8,128]{3,2,1,0:T(8,128)S(1)} %get-tuple-element.18), channel_id=1, source_target_pairs={{0,1},{1,2},{2,3},{3,4},{4,5},{5,6},{6,7},{8,9},{9,10},{10,11},{11... | collective-permute-start | bytes 614408 | tf_op jit(solution)/shard_map/ppermute | solution.py:217
  60.7 0.0 collective-permute-done.8
  60.7 0.2 fusion
  61.0 0.0 collective-permute-done.6
  61.0 0.0 collective-permute-done.5
  61.1 0.1 maximum_maximum_fusion.2.xh_ref
  61.2 5.4 %collective-permute-done.7 = f32[2,25,8,128]{3,2,1,0:T(8,128)S(1)} collective-permute-done((f32[2,25,8,128]{3,2,1,0:T(8,128)S(1)}, f32[2,25,8,128]{3,2,1,0:T(8,128)S(1)}, u32[]{:S(2)}, u32[]{:S(2)}) %collective-permute-start.7) | collective-permute-done | bytes 204832 | tf_op jit(solution)/shard_map/ppermute | solution.py:217
  66.6 0.0 collective-permute-done.9
  66.6 0.1 slice_select_fusion
  66.7 0.1 maximum_maximum_fusion.3.yh_ref
  66.8 0.0 copy-done
  66.8 0.0 copy-done.1
  66.8 11.4 %shard_map.96 = (f32[25,64,128]{2,1,0:T(8,128)}, f32[25,64,128]{2,1,0:T(8,128)}, f32[25,64,128]{2,1,0:T(8,128)}) custom-call(s32[64,128]{1,0:T(8,128)S(1)} %copy-done.4, f32[25,64,128]{2,1,0:T(8,128)S(1)} %get-tuple-element.13.nt_ref, f32[25,64,128]{2,1,0:T(8,128)S(1)} %get-tuple-element.14.ns_ref, f32[25,64,128]{2,1,0:T(8,128)S(1)} %get-tuple-element.15.bt_ref, ...), custom_call_target="tpu_custom_call" | custom-call | flops 163840000 | bytes 9830400 | tf_op jit(solution)/shard_map/pallas_call | solution.py:198
  (16 shorter events, 0.4 us)
Async XLA Ops:
  9.4 13.5 %collective-permute-start.3 = (f32[2,25,2,128]{3,2,1,0:T(2,128)S(1)}, f32[2,25,2,128]{3,2,1,0:T(2,128)S(1)}, u32[]{:S(2)}, u32[]{:S(2)}) collective-permute-start(f32[2,25,2,128]{3,2,1,0:T(2,128)S(1)} %slice.55), channel_id=1, source_target_pairs={{7,127},{15,119},{23,111},{31,103},{39,95},{47,87},{55,79},{63,71}... | collective-permute-start | bytes 153608 | tf_op jit(solution)/shard_map/ppermute | solution.py:220
  10.0 13.1 %collective-permute-start.1 = (f32[2,25,8,64]{3,2,1,0:T(8,128)}, f32[2,25,8,64]{3,2,1,0:T(8,128)S(1)}, u32[]{:S(2)}, u32[]{:S(2)}) collective-permute-start(f32[2,25,8,64]{3,2,1,0:T(8,128)} %get-tuple-element.11), channel_id=1, source_target_pairs={{0,8},{8,16},{16,24},{24,32},{32,40},{40,48},{48,56},{56,64},{64,7... | collective-permute-start | bytes 307208 | tf_op jit(solution)/shard_map/ppermute | solution.py:215
  10.1 13.1 %collective-permute-start = (f32[2,25,8,64]{3,2,1,0:T(8,128)}, f32[2,25,8,64]{3,2,1,0:T(8,128)S(1)}, u32[]{:S(2)}, u32[]{:S(2)}) collective-permute-start(f32[2,25,8,64]{3,2,1,0:T(8,128)} %get-tuple-element.11), channel_id=1, source_target_pairs={{0,120},{8,0},{16,8},{24,16},{32,24},{40,32},{48,40},{56,48},{64,5... | collective-permute-start | bytes 307208 | tf_op jit(solution)/shard_map/ppermute | solution.py:214
  15.5 15.4 %collective-permute-start.4 = (f32[2,25,8,128]{3,2,1,0:T(8,128)}, f32[2,25,8,128]{3,2,1,0:T(8,128)S(1)}, u32[]{:S(2)}, u32[]{:S(2)}) collective-permute-start(f32[2,25,8,128]{3,2,1,0:T(8,128)} %get-tuple-element.12), channel_id=1, source_target_pairs={{1,0},{2,1},{3,2},{4,3},{5,4},{6,5},{7,6},{9,8},{10,9},{11,10},{12... | collective-permute-start | bytes 614408 | tf_op jit(solution)/shard_map/ppermute | solution.py:216
  20.8 10.0 %collective-permute-start.2 = (f32[2,25,8,128]{3,2,1,0:T(8,128)}, f32[2,25,8,128]{3,2,1,0:T(8,128)S(1)}, u32[]{:S(2)}, u32[]{:S(2)}) collective-permute-start(f32[2,25,8,128]{3,2,1,0:T(8,128)} %get-tuple-element.12), channel_id=1, source_target_pairs={{0,1},{1,2},{2,3},{3,4},{4,5},{5,6},{6,7},{8,9},{9,10},{10,11},{11... | collective-permute-start | bytes 614408 | tf_op jit(solution)/shard_map/ppermute | solution.py:217
  22.9 8.2 %copy-start.2 = (f32[25,64,128]{2,1,0:T(8,128)S(1)}, f32[25,64,128]{2,1,0:T(8,128)}, u32[]{:S(2)}) copy-start(f32[25,64,128]{2,1,0:T(8,128)} %nt_ref.3) | copy-start | bytes 2457604
  22.9 8.2 %copy-start.3 = (f32[25,64,128]{2,1,0:T(8,128)S(1)}, f32[25,64,128]{2,1,0:T(8,128)}, u32[]{:S(2)}) copy-start(f32[25,64,128]{2,1,0:T(8,128)} %ns_ref.3) | copy-start | bytes 2457604
  30.9 0.8 copy-start.4
  48.7 12.0 %collective-permute-start.8 = (f32[2,25,2,128]{3,2,1,0:T(2,128)S(1)}, f32[2,25,2,128]{3,2,1,0:T(2,128)S(1)}, u32[]{:S(2)}, u32[]{:S(2)}) collective-permute-start(f32[2,25,2,128]{3,2,1,0:T(2,128)S(1)} %slice.63), channel_id=1, source_target_pairs={{7,127},{15,119},{23,111},{31,103},{39,95},{47,87},{55,79},{63,71}... | collective-permute-start | bytes 153608 | tf_op jit(solution)/shard_map/ppermute | solution.py:220
  49.4 17.4 %copy-start = (f32[25,64,128]{2,1,0:T(8,128)S(1)}, f32[25,64,128]{2,1,0:T(8,128)}, u32[]{:S(2)}) copy-start(f32[25,64,128]{2,1,0:T(8,128)} %ue_ref.5) | copy-start | bytes 2457604
  49.4 17.4 %copy-start.1 = (f32[25,64,128]{2,1,0:T(8,128)S(1)}, f32[25,64,128]{2,1,0:T(8,128)}, u32[]{:S(2)}) copy-start(f32[25,64,128]{2,1,0:T(8,128)} %vn_ref.5) | copy-start | bytes 2457604
  49.4 11.6 %collective-permute-start.6 = (f32[2,25,8,64]{3,2,1,0:T(8,128)S(1)}, f32[2,25,8,64]{3,2,1,0:T(8,128)S(1)}, u32[]{:S(2)}, u32[]{:S(2)}) collective-permute-start(f32[2,25,8,64]{3,2,1,0:T(8,128)S(1)} %get-tuple-element.17), channel_id=1, source_target_pairs={{0,8},{8,16},{16,24},{24,32},{32,40},{40,48},{48,56},{56,64},{64,7... | collective-permute-start | bytes 307208 | tf_op jit(solution)/shard_map/ppermute | solution.py:215
  49.5 11.5 %collective-permute-start.5 = (f32[2,25,8,64]{3,2,1,0:T(8,128)S(1)}, f32[2,25,8,64]{3,2,1,0:T(8,128)S(1)}, u32[]{:S(2)}, u32[]{:S(2)}) collective-permute-start(f32[2,25,8,64]{3,2,1,0:T(8,128)S(1)} %get-tuple-element.17), channel_id=1, source_target_pairs={{0,120},{8,0},{16,8},{24,16},{32,24},{40,32},{48,40},{56,48},{64,5... | collective-permute-start | bytes 307208 | tf_op jit(solution)/shard_map/ppermute | solution.py:214
  54.9 11.7 %collective-permute-start.9 = (f32[2,25,8,128]{3,2,1,0:T(8,128)S(1)}, f32[2,25,8,128]{3,2,1,0:T(8,128)S(1)}, u32[]{:S(2)}, u32[]{:S(2)}) collective-permute-start(f32[2,25,8,128]{3,2,1,0:T(8,128)S(1)} %get-tuple-element.18), channel_id=1, source_target_pairs={{1,0},{2,1},{3,2},{4,3},{5,4},{6,5},{7,6},{9,8},{10,9},{11,10},{12... | collective-permute-start | bytes 614408 | tf_op jit(solution)/shard_map/ppermute | solution.py:216
  56.8 9.8 %collective-permute-start.7 = (f32[2,25,8,128]{3,2,1,0:T(8,128)S(1)}, f32[2,25,8,128]{3,2,1,0:T(8,128)S(1)}, u32[]{:S(2)}, u32[]{:S(2)}) collective-permute-start(f32[2,25,8,128]{3,2,1,0:T(8,128)S(1)} %get-tuple-element.18), channel_id=1, source_target_pairs={{0,1},{1,2},{2,3},{3,4},{4,5},{5,6},{6,7},{8,9},{9,10},{10,11},{11... | collective-permute-start | bytes 614408 | tf_op jit(solution)/shard_map/ppermute | solution.py:217

commit v5 on v4

--- a/solution.py
+++ b/solution.py
@@ -30,22 +30,34 @@
     return flux + jnp.abs(u) * ((q4 - q1) - 3.0 * (q3 - q2)) / 12.0
 
 
-def edge_tiles(rows, cols):
-    r = lax.broadcasted_iota(jnp.int32, (8, cols), 0)
-    c = lax.broadcasted_iota(jnp.int32, (8, cols), 1)
-    picked = ((r == 0) & (c == 0)) | ((r == 1) & (c == 1))
-    picked = picked | ((r == 2) & (c == cols - 2)) | ((r == 3) & (c == cols - 1))
-    velocity = (r == 4) & (c == cols - 1)
-    return picked.astype(jnp.float32), velocity.astype(jnp.float32), (r == c).astype(jnp.float32)
-
-
-def write_columns(value, east_v, xpack_ref, f, k, select, select_v):
-    dims = (((1,), (1,)), ((), ()))
-    xpack_ref[f, k] = lax.dot_general(
-        select, value, dims, precision=lax.Precision.HIGHEST,
-        preferred_element_type=jnp.float32) + lax.dot_general(
-        select_v, east_v, dims, precision=lax.Precision.HIGHEST,
-        preferred_element_type=jnp.float32)
+def lane_roll(value, shift):
+    shift = shift % value.shape[-1]
+    return value if shift == 0 else pltpu.roll(value, shift, 1)
+
+
+def column_pack(value, east_v):
+    rows, cols = value.shape
+    lane = lax.broadcasted_iota(jnp.int32, (8, cols), 1)
+    pack = jnp.zeros((8, cols), jnp.float32)
+    for a in range(rows // 8):
+        part = value[8 * a:8 * a + 8]
+        pack = jnp.where((lane >= 4 * a) & (lane < 4 * a + 2), lane_roll(part, 4 * a), pack)
+        pack = jnp.where((lane >= 4 * a + 2) & (lane < 4 * a + 4), lane_roll(part, 4 * a + 4), pack)
+        pack = jnp.where(lane == 64 + 4 * a, lane_roll(east_v[8 * a:8 * a + 8], 4 * a + 65), pack)
+    return pack
+
+
+def column_unpack(from_east, from_west, with_velocity):
+    cols = from_east.shape[-1]
+    lane = lax.broadcasted_iota(jnp.int32, (8, cols), 1)
+    both = jnp.where(lane % 4 < 2, from_east, from_west)
+    parts = []
+    for a in range(8):
+        part = lane_roll(both, -4 * a)
+        if with_velocity:
+            part = jnp.where(lane == 4, lane_roll(from_west, 68 - 4 * a), part)
+        parts.append(part)
+    return jnp.concatenate(parts, 0)
 
 
 def write_rows(value, north_v, ypack_ref, f, k):
@@ -56,34 +68,26 @@
     ypack_ref[f, k, 5:8, :] = jnp.zeros((3, cols), jnp.float32)
 
 
-def expand_columns(tile, spread):
-    return lax.dot_general(
-        tile, spread, (((0,), (0,)), ((), ())), precision=lax.Precision.HIGHEST,
-        preferred_element_type=jnp.float32)
-
-
 def edge_kernel(bl_ref, nt_ref, ns_ref, ue_ref, vn_ref, xpack_ref, ypack_ref):
     levels, rows, cols = nt_ref.shape
-    select, select_v, _ = edge_tiles(rows, cols)
 
     def level(k, carry):
         m = (k < bl_ref[...]).astype(jnp.float32)
         for f, ref in enumerate((nt_ref, ns_ref)):
             value = ref[k] * m
-            write_columns(value, ue_ref[k], xpack_ref, f, k, select, select_v)
+            xpack_ref[f, k] = column_pack(value, ue_ref[k])
             write_rows(value, vn_ref[k], ypack_ref, f, k)
         return carry
 
     lax.fori_loop(0, levels, level, 0, unroll=True)
 
 
-def step_kernel(mask_inputs, final, bl_ref, nt_ref, ns_ref, bt_ref, bs_ref, xh_ref, yh_ref,
+def step_kernel(mask_inputs, final, bl_ref, nt_ref, ns_ref, bt_ref, bs_ref, xe_ref, xw_ref, yh_ref,
                 ue_ref, vn_ref, *rest):
-    outs, fv, hs = rest[:-2], rest[-2], rest[-1]
+    outs, fv = rest[:-1], rest[-1]
     levels, rows, cols = nt_ref.shape
     lane = lax.broadcasted_iota(jnp.int32, (rows, cols), 1)
     row = lax.broadcasted_iota(jnp.int32, (rows, cols), 0)
-    select, select_v, spread = edge_tiles(rows, cols)
     now_refs, bef_refs = (nt_ref, ns_ref), (bt_ref, bs_ref)
 
     def mask(k):
@@ -112,13 +116,6 @@
 
     lax.fori_loop(0, levels - 1, mixing, 0)
 
-    def expand(k, carry):
-        for f in range(2):
-            hs[f, k] = expand_columns(xh_ref[f, k], spread)
-        return carry
-
-    lax.fori_loop(0, levels, expand, 0, unroll=True)
-
     def level(k, carry):
         m = mask(k)
         ue, vn = ue_ref[k], vn_ref[k]
@@ -126,7 +123,7 @@
         for f in range(2):
             q = load(now_refs[f], k, m)
             b = load(bef_refs[f], k, m)
-            h = hs[f, k]
+            h = column_unpack(xe_ref[f, k], xw_ref[f, k], f == 0)
             yh = yh_ref[f, k]
             if f == 0:
                 uw = jnp.where(lane < 1, pltpu.roll(h, cols - 4, 1), pltpu.roll(ue, 1, 1))
@@ -152,6 +149,7 @@
             if not final:
                 outs[f][k] = q + asselin_gamma * (b - 2.0 * q + after)
                 outs[2 + f][k] = after
+                outs[4][f, k] = column_pack(after, ue)
                 write_rows(after, vn, outs[5], f, k)
         if final:
             outs[0][k] = afters[0]
@@ -161,20 +159,12 @@
 
     lax.fori_loop(0, levels, level, 0)
 
-    if not final:
-        def columns(k, carry):
-            for f in range(2):
-                write_columns(outs[2 + f][k], ue_ref[k], outs[4], f, k, select, select_v)
-            return carry
-
-        lax.fori_loop(0, levels, columns, 0, unroll=True)
-
 
 VMEM_SPEC = pl.BlockSpec(memory_space=pltpu.VMEM)
 
 
 def pack_shapes(levels, rows, cols):
-    return (jax.ShapeDtypeStruct((2, levels, 8, rows), jnp.float32),
+    return (jax.ShapeDtypeStruct((2, levels, 8, cols), jnp.float32),
             jax.ShapeDtypeStruct((2, levels, 8, cols), jnp.float32))
 
 
@@ -191,22 +181,21 @@
     )(bl, nt, ns, ue, vn)
 
 
-def step_call(mask_inputs, final, bl, nt, ns, bt, bs, xh, yh, ue, vn):
+def step_call(mask_inputs, final, bl, nt, ns, bt, bs, xe, xw, yh, ue, vn):
     levels, rows, cols = nt.shape
     field = jax.ShapeDtypeStruct(nt.shape, jnp.float32)
     out_shape = (field,) * 3 if final else (field,) * 4 + pack_shapes(levels, rows, cols)
     return pl.pallas_call(
         functools.partial(step_kernel, mask_inputs, final),
         out_shape=out_shape,
-        in_specs=[VMEM_SPEC] * 9,
+        in_specs=[VMEM_SPEC] * 10,
         out_specs=tuple([VMEM_SPEC] * len(out_shape)),
-        scratch_shapes=[pltpu.VMEM((2, levels + 1, rows, cols), jnp.float32),
-                        pltpu.VMEM((2, levels, rows, cols), jnp.float32)],
+        scratch_shapes=[pltpu.VMEM((2, levels + 1, rows, cols), jnp.float32)],
         compiler_params=pltpu.CompilerParams(vmem_limit_bytes=48 * 1024 * 1024),
         cost_estimate=pl.CostEstimate(
             flops=400 * 2 * levels * rows * cols, transcendentals=levels * rows * cols,
             bytes_accessed=4 * levels * rows * cols * (9 + len(out_shape))),
-    )(bl, nt, ns, bt, bs, xh, yh, ue, vn)
+    )(bl, nt, ns, bt, bs, xe, xw, yh, ue, vn)
 
 
 def exchange(xpack, ypack, at_fold):
@@ -223,14 +212,11 @@
     flipped = jnp.einsum("fkrc,cd->fkrd", partner, flip, precision=lax.Precision.HIGHEST)
     mirror = jnp.concatenate([flipped[:, :, 1:2], flipped[:, :, 0:1]], 2)
     north = jnp.where(at_fold, mirror, from_north[:, :, 0:2])
-    two, levels, _, rows = xpack.shape
-    halo_x = jnp.concatenate(
-        [from_east[:, :, 0:2], from_west[:, :, 2:4],
-         from_west[:, :, 4:5], jnp.zeros((two, levels, 3, rows), jnp.float32)], 2)
+    two, levels = xpack.shape[:2]
     halo_y = jnp.concatenate(
         [from_south[:, :, 2:4], north,
          from_south[:, :, 4:5], jnp.zeros((two, levels, 3, cols), jnp.float32)], 2)
-    return halo_x, halo_y
+    return from_east, from_west, halo_y
 
 
 def on_device(
@@ -238,12 +224,12 @@
 ):
     at_fold = lax.axis_index("lat") == lax.axis_size("lat") - 1
     xpack, ypack = edge_call(bottom_level, temp_now, salt_now, east_velocity, north_velocity)
-    halo_x, halo_y = exchange(xpack, ypack, at_fold)
+    from_east, from_west, halo_y = exchange(xpack, ypack, at_fold)
     ft, fs, at, as_, xpack, ypack = step_call(
         True, False, bottom_level, temp_now, salt_now, temp_before, salt_before,
-        halo_x, halo_y, east_velocity, north_velocity)
-    halo_x, halo_y = exchange(xpack, ypack, at_fold)
-    return step_call(False, True, bottom_level, at, as_, ft, fs, halo_x, halo_y,
+        from_east, from_west, halo_y, east_velocity, north_velocity)
+    from_east, from_west, halo_y = exchange(xpack, ypack, at_fold)
+    return step_call(False, True, bottom_level, at, as_, ft, fs, from_east, from_west, halo_y,
                      east_velocity, north_velocity)
 
 

time: 78.6 us -> 70.9 us (0.902)
  Pallas kernels: 36.2 us -> 28.4 us
    pallas_call x2, Pallas kernels: 28.4 us -> 24.4 us  [step_call(): pl.pallas_call(functools.partial(step_kernel, mask_inputs, final), out_sh...]
    pallas_call x1, Pallas kernels: 7.77 us -> 3.94 us  [edge_call(): pl.pallas_call(edge_kernel, out_shape=pack_shapes(levels, rows, cols), in...]
where the time goes in v5:
time: 70.9 us; the launch traced here: 70.6 us
  Pallas kernels  28.4 us (40%)
  starting transfers between devices  25.4 us (36%)
  waiting for transfers between devices  13.2 us (19%)
  local copies, waits for them, and re-layouts  1.99 us (3%)
  between operations  0.94 us (1%)
    pallas_call x2, Pallas kernels, step_call(): pl.pallas_call(functools.partial(step_kernel, mask_inputs, final), out_sh...  24.4 us
    ppermute x2, waiting for transfers between devices, exchange(): lax.ppermute(ypack, 'lat', [(i, i + 1) for i in range(lat_count - 1)])  13.2 us
    ppermute x2, starting transfers between devices, exchange(): lax.ppermute(xpack, 'lon', [(i, (i - 1) % lon_count) for i in range(lon_c...  10.7 us
    ppermute x2, starting transfers between devices, exchange(): lax.ppermute(ypack, 'lat', [(i, i - 1) for i in range(1, lat_count)])  7.28 us
    ppermute x2, starting transfers between devices, exchange(): lax.ppermute(ypack, 'lat', [(i, i + 1) for i in range(lat_count - 1)])  5.84 us
    pallas_call x1, Pallas kernels, edge_call(): pl.pallas_call(edge_kernel, out_shape=pack_shapes(levels, rows, cols), in...  3.94 us
    ppermute x2, starting transfers between devices, exchange(): partner = lax.ppermute(ypack[:, :, 2:4], ('lon', 'lat'), fold_pairs)  1.46 us
  transfers between devices with their start and end apart: 10, of which 2 were waited for; matrix products, arithmetic and copies ran while one was open for 1% of the time, Pallas kernels for 0%

profile of v5, /device:TPU:8, one launch (start us, length us, event | category | flops | bytes accessed | tf_op | source)
XLA Modules:
  0.0 70.6 jit_solution(1937960339535756488)
XLA Ops:
  0.6 0.0 copy-start.3
  0.6 3.9 %shard_map.94 = (f32[2,25,8,128]{3,2,1,0:T(8,128)}, f32[2,25,8,128]{3,2,1,0:T(8,128)}) custom-call(s32[64,128]{1,0:T(8,128)} %bl_ref.5, f32[25,64,128]{2,1,0:T(8,128)} %nt_ref.3, f32[25,64,128]{2,1,0:T(8,128)} %ns_ref.3, f32[25,64,128]{2,1,0:T(8,128)} %ue_ref.5, f32[25,64,128]{2,1,0:T(8,128)} %vn_ref.5), custom_call_target="tpu_custom_call" | custom-call | flops 6553600 | bytes 4096000 | tf_op jit(solution)/shard_map/pallas_call | solution.py:173
  4.6 0.0 copy-start.2
  4.6 1.0 %slice.37 = f32[2,25,2,128]{3,2,1,0:T(2,128)S(1)} slice(f32[2,25,8,128]{3,2,1,0:T(8,128)} %get-tuple-element.12), slice={[0:2], [0:25], [2:4], [0:128]} | slice | bytes 102400 | tf_op jit(solution)/shard_map/slice | solution.py:209
  5.6 0.7 collective-permute-start.3
  6.3 0.1 collective-permute-start.1
  6.4 5.3 %collective-permute-start = (f32[2,25,8,128]{3,2,1,0:T(8,128)}, f32[2,25,8,128]{3,2,1,0:T(8,128)S(1)}, u32[]{:S(2)}, u32[]{:S(2)}) collective-permute-start(f32[2,25,8,128]{3,2,1,0:T(8,128)} %get-tuple-element.11), channel_id=1, source_target_pairs={{0,120},{8,0},{16,8},{24,16},{32,24},{40,32},{48,40},{56,48},{64,5... | collective-permute-start | bytes 614408 | tf_op jit(solution)/shard_map/ppermute | solution.py:203
  11.7 5.4 %collective-permute-start.4 = (f32[2,25,8,128]{3,2,1,0:T(8,128)}, f32[2,25,8,128]{3,2,1,0:T(8,128)S(1)}, u32[]{:S(2)}, u32[]{:S(2)}) collective-permute-start(f32[2,25,8,128]{3,2,1,0:T(8,128)} %get-tuple-element.12), channel_id=1, source_target_pairs={{1,0},{2,1},{3,2},{4,3},{5,4},{6,5},{7,6},{9,8},{10,9},{11,10},{12... | collective-permute-start | bytes 614408 | tf_op jit(solution)/shard_map/ppermute | solution.py:205
  17.1 1.9 %collective-permute-start.2 = (f32[2,25,8,128]{3,2,1,0:T(8,128)}, f32[2,25,8,128]{3,2,1,0:T(8,128)S(1)}, u32[]{:S(2)}, u32[]{:S(2)}) collective-permute-start(f32[2,25,8,128]{3,2,1,0:T(8,128)} %get-tuple-element.12), channel_id=1, source_target_pairs={{0,1},{1,2},{2,3},{3,4},{4,5},{5,6},{6,7},{8,9},{9,10},{10,11},{11... | collective-permute-start | bytes 614408 | tf_op jit(solution)/shard_map/ppermute | solution.py:206
  19.0 0.1 pad.9.clone
  19.1 0.0 collective-permute-done.3
  19.1 0.2 fusion.2
  19.4 7.7 %collective-permute-done.2 = f32[2,25,8,128]{3,2,1,0:T(8,128)S(1)} collective-permute-done((f32[2,25,8,128]{3,2,1,0:T(8,128)}, f32[2,25,8,128]{3,2,1,0:T(8,128)S(1)}, u32[]{:S(2)}, u32[]{:S(2)}) %collective-permute-start.2) | collective-permute-done | bytes 204832 | tf_op jit(solution)/shard_map/ppermute | solution.py:206
  27.1 0.0 collective-permute-done.4
  27.1 0.1 slice_select_fusion.1
  27.2 0.0 copy-start.4
  27.2 0.1 maximum_maximum_fusion.yh_ref
  27.3 0.0 collective-permute-done.1.xw_ref
  27.3 0.0 collective-permute-done.xe_ref
  27.3 0.0 copy-done.3
  27.3 0.0 copy-done.2
  27.3 0.6 copy-done.4
  28.0 0.0 copy-start.1
  28.0 13.2 %shard_map.95 = (f32[25,64,128]{2,1,0:T(8,128)S(1)}, f32[25,64,128]{2,1,0:T(8,128)S(1)}, f32[25,64,128]{2,1,0:T(8,128)S(1)}, f32[25,64,128]{2,1,0:T(8,128)S(1)},...) custom-call(s32[64,128]{1,0:T(8,128)S(1)} %copy-done.4, f32[25,64,128]{2,1,0:T(8,128)S(1)} %copy-done.2, ...), custom_call_target="tpu_custom_call" | custom-call | flops 163840000 | bytes 12288000 | tf_op jit(solution)/shard_map/pallas_call | solution.py:188
  41.2 0.0 copy-start
  41.2 0.8 %collective-permute-start.8 = (f32[2,25,2,128]{3,2,1,0:T(2,128)S(1)}, f32[2,25,2,128]{3,2,1,0:T(2,128)S(1)}, u32[]{:S(2)}, u32[]{:S(2)}) collective-permute-start(f32[2,25,2,128]{3,2,1,0:T(2,128)S(1)} %slice.43), channel_id=1, source_target_pairs={{7,127},{15,119},{23,111},{31,103},{39,95},{47,87},{55,79},{63,71}... | collective-permute-start | bytes 153608 | tf_op jit(solution)/shard_map/ppermute | solution.py:209
  42.0 0.1 collective-permute-start.6
  42.1 5.3 %collective-permute-start.5 = (f32[2,25,8,128]{3,2,1,0:T(8,128)S(1)}, f32[2,25,8,128]{3,2,1,0:T(8,128)S(1)}, u32[]{:S(2)}, u32[]{:S(2)}) collective-permute-start(f32[2,25,8,128]{3,2,1,0:T(8,128)S(1)} %get-tuple-element.17), channel_id=1, source_target_pairs={{0,120},{8,0},{16,8},{24,16},{32,24},{40,32},{48,40},{56,48},{64,5... | collective-permute-start | bytes 614408 | tf_op jit(solution)/shard_map/ppermute | solution.py:203
  47.4 1.9 %collective-permute-start.9 = (f32[2,25,8,128]{3,2,1,0:T(8,128)S(1)}, f32[2,25,8,128]{3,2,1,0:T(8,128)S(1)}, u32[]{:S(2)}, u32[]{:S(2)}) collective-permute-start(f32[2,25,8,128]{3,2,1,0:T(8,128)S(1)} %get-tuple-element.18), channel_id=1, source_target_pairs={{1,0},{2,1},{3,2},{4,3},{5,4},{6,5},{7,6},{9,8},{10,9},{11,10},{12... | collective-permute-start | bytes 614408 | tf_op jit(solution)/shard_map/ppermute | solution.py:205
  49.4 3.9 %collective-permute-start.7 = (f32[2,25,8,128]{3,2,1,0:T(8,128)S(1)}, f32[2,25,8,128]{3,2,1,0:T(8,128)S(1)}, u32[]{:S(2)}, u32[]{:S(2)}) collective-permute-start(f32[2,25,8,128]{3,2,1,0:T(8,128)S(1)} %get-tuple-element.18), channel_id=1, source_target_pairs={{0,1},{1,2},{2,3},{3,4},{4,5},{5,6},{6,7},{8,9},{9,10},{10,11},{11... | collective-permute-start | bytes 614408 | tf_op jit(solution)/shard_map/ppermute | solution.py:206
  53.3 0.0 collective-permute-done.8
  53.3 0.2 fusion
  53.6 5.5 %collective-permute-done.7 = f32[2,25,8,128]{3,2,1,0:T(8,128)S(1)} collective-permute-done((f32[2,25,8,128]{3,2,1,0:T(8,128)S(1)}, f32[2,25,8,128]{3,2,1,0:T(8,128)S(1)}, u32[]{:S(2)}, u32[]{:S(2)}) %collective-permute-start.7) | collective-permute-done | bytes 204832 | tf_op jit(solution)/shard_map/ppermute | solution.py:206
  59.2 0.0 collective-permute-done.9
  59.2 0.1 slice_select_fusion
  59.3 0.1 maximum_maximum_fusion.1.yh_ref
  59.3 0.0 collective-permute-done.6.xw_ref
  59.4 0.0 collective-permute-done.5.xe_ref
  59.4 0.0 copy-done.1
  59.4 0.0 copy-done
  59.4 11.2 %shard_map.96 = (f32[25,64,128]{2,1,0:T(8,128)}, f32[25,64,128]{2,1,0:T(8,128)}, f32[25,64,128]{2,1,0:T(8,128)}) custom-call(s32[64,128]{1,0:T(8,128)S(1)} %copy-done.4, f32[25,64,128]{2,1,0:T(8,128)S(1)} %get-tuple-element.13.nt_ref, f32[25,64,128]{2,1,0:T(8,128)S(1)} %get-tuple-element.14.ns_ref, f32[25,64,128]{2,1,0:T(8,128)S(1)} %get-tuple-element.15.bt_ref, ...), custom_call_target="tpu_custom_call" | custom-call | flops 163840000 | bytes 9830400 | tf_op jit(solution)/shard_map/pallas_call | solution.py:188
  (12 shorter events, 0.2 us)
Async XLA Ops:
  0.6 26.7 %copy-start.3 = (f32[25,64,128]{2,1,0:T(8,128)S(1)}, f32[25,64,128]{2,1,0:T(8,128)}, u32[]{:S(2)}) copy-start(f32[25,64,128]{2,1,0:T(8,128)} %ns_ref.3) | copy-start | bytes 2457604
  4.6 22.8 %copy-start.2 = (f32[25,64,128]{2,1,0:T(8,128)S(1)}, f32[25,64,128]{2,1,0:T(8,128)}, u32[]{:S(2)}) copy-start(f32[25,64,128]{2,1,0:T(8,128)} %nt_ref.3) | copy-start | bytes 2457604
  5.6 13.5 %collective-permute-start.3 = (f32[2,25,2,128]{3,2,1,0:T(2,128)S(1)}, f32[2,25,2,128]{3,2,1,0:T(2,128)S(1)}, u32[]{:S(2)}, u32[]{:S(2)}) collective-permute-start(f32[2,25,2,128]{3,2,1,0:T(2,128)S(1)} %slice.37), channel_id=1, source_target_pairs={{7,127},{15,119},{23,111},{31,103},{39,95},{47,87},{55,79},{63,71}... | collective-permute-start | bytes 153608 | tf_op jit(solution)/shard_map/ppermute | solution.py:209
  6.3 21.0 %collective-permute-start.1 = (f32[2,25,8,128]{3,2,1,0:T(8,128)}, f32[2,25,8,128]{3,2,1,0:T(8,128)S(1)}, u32[]{:S(2)}, u32[]{:S(2)}) collective-permute-start(f32[2,25,8,128]{3,2,1,0:T(8,128)} %get-tuple-element.11), channel_id=1, source_target_pairs={{0,8},{8,16},{16,24},{24,32},{32,40},{40,48},{48,56},{56,64},{64,7... | collective-permute-start | bytes 614408 | tf_op jit(solution)/shard_map/ppermute | solution.py:204
  6.4 20.9 %collective-permute-start = (f32[2,25,8,128]{3,2,1,0:T(8,128)}, f32[2,25,8,128]{3,2,1,0:T(8,128)S(1)}, u32[]{:S(2)}, u32[]{:S(2)}) collective-permute-start(f32[2,25,8,128]{3,2,1,0:T(8,128)} %get-tuple-element.11), channel_id=1, source_target_pairs={{0,120},{8,0},{16,8},{24,16},{32,24},{40,32},{48,40},{56,48},{64,5... | collective-permute-start | bytes 614408 | tf_op jit(solution)/shard_map/ppermute | solution.py:203
  11.7 15.4 %collective-permute-start.4 = (f32[2,25,8,128]{3,2,1,0:T(8,128)}, f32[2,25,8,128]{3,2,1,0:T(8,128)S(1)}, u32[]{:S(2)}, u32[]{:S(2)}) collective-permute-start(f32[2,25,8,128]{3,2,1,0:T(8,128)} %get-tuple-element.12), channel_id=1, source_target_pairs={{1,0},{2,1},{3,2},{4,3},{5,4},{6,5},{7,6},{9,8},{10,9},{11,10},{12... | collective-permute-start | bytes 614408 | tf_op jit(solution)/shard_map/ppermute | solution.py:205
  17.1 10.0 %collective-permute-start.2 = (f32[2,25,8,128]{3,2,1,0:T(8,128)}, f32[2,25,8,128]{3,2,1,0:T(8,128)S(1)}, u32[]{:S(2)}, u32[]{:S(2)}) collective-permute-start(f32[2,25,8,128]{3,2,1,0:T(8,128)} %get-tuple-element.12), channel_id=1, source_target_pairs={{0,1},{1,2},{2,3},{3,4},{4,5},{5,6},{6,7},{8,9},{9,10},{10,11},{11... | collective-permute-start | bytes 614408 | tf_op jit(solution)/shard_map/ppermute | solution.py:206
  27.2 0.8 %copy-start.4 = (s32[64,128]{1,0:T(8,128)S(1)}, s32[64,128]{1,0:T(8,128)}, u32[]{:S(2)}) copy-start(s32[64,128]{1,0:T(8,128)} %bl_ref.5) | copy-start | bytes 98308
  28.0 31.4 %copy-start.1 = (f32[25,64,128]{2,1,0:T(8,128)S(1)}, f32[25,64,128]{2,1,0:T(8,128)}, u32[]{:S(2)}) copy-start(f32[25,64,128]{2,1,0:T(8,128)} %vn_ref.5) | copy-start | bytes 2457604
  41.2 18.2 %copy-start = (f32[25,64,128]{2,1,0:T(8,128)S(1)}, f32[25,64,128]{2,1,0:T(8,128)}, u32[]{:S(2)}) copy-start(f32[25,64,128]{2,1,0:T(8,128)} %ue_ref.5) | copy-start | bytes 2457604
  41.2 12.1 %collective-permute-start.8 = (f32[2,25,2,128]{3,2,1,0:T(2,128)S(1)}, f32[2,25,2,128]{3,2,1,0:T(2,128)S(1)}, u32[]{:S(2)}, u32[]{:S(2)}) collective-permute-start(f32[2,25,2,128]{3,2,1,0:T(2,128)S(1)} %slice.43), channel_id=1, source_target_pairs={{7,127},{15,119},{23,111},{31,103},{39,95},{47,87},{55,79},{63,71}... | collective-permute-start | bytes 153608 | tf_op jit(solution)/shard_map/ppermute | solution.py:209
  42.0 17.3 %collective-permute-start.6 = (f32[2,25,8,128]{3,2,1,0:T(8,128)S(1)}, f32[2,25,8,128]{3,2,1,0:T(8,128)S(1)}, u32[]{:S(2)}, u32[]{:S(2)}) collective-permute-start(f32[2,25,8,128]{3,2,1,0:T(8,128)S(1)} %get-tuple-element.17), channel_id=1, source_target_pairs={{0,8},{8,16},{16,24},{24,32},{32,40},{40,48},{48,56},{56,64},{64,7... | collective-permute-start | bytes 614408 | tf_op jit(solution)/shard_map/ppermute | solution.py:204
  42.1 17.3 %collective-permute-start.5 = (f32[2,25,8,128]{3,2,1,0:T(8,128)S(1)}, f32[2,25,8,128]{3,2,1,0:T(8,128)S(1)}, u32[]{:S(2)}, u32[]{:S(2)}) collective-permute-start(f32[2,25,8,128]{3,2,1,0:T(8,128)S(1)} %get-tuple-element.17), channel_id=1, source_target_pairs={{0,120},{8,0},{16,8},{24,16},{32,24},{40,32},{48,40},{56,48},{64,5... | collective-permute-start | bytes 614408 | tf_op jit(solution)/shard_map/ppermute | solution.py:203
  47.4 11.7 %collective-permute-start.9 = (f32[2,25,8,128]{3,2,1,0:T(8,128)S(1)}, f32[2,25,8,128]{3,2,1,0:T(8,128)S(1)}, u32[]{:S(2)}, u32[]{:S(2)}) collective-permute-start(f32[2,25,8,128]{3,2,1,0:T(8,128)S(1)} %get-tuple-element.18), channel_id=1, source_target_pairs={{1,0},{2,1},{3,2},{4,3},{5,4},{6,5},{7,6},{9,8},{10,9},{11,10},{12... | collective-permute-start | bytes 614408 | tf_op jit(solution)/shard_map/ppermute | solution.py:205
  49.4 9.8 %collective-permute-start.7 = (f32[2,25,8,128]{3,2,1,0:T(8,128)S(1)}, f32[2,25,8,128]{3,2,1,0:T(8,128)S(1)}, u32[]{:S(2)}, u32[]{:S(2)}) collective-permute-start(f32[2,25,8,128]{3,2,1,0:T(8,128)S(1)} %get-tuple-element.18), channel_id=1, source_target_pairs={{0,1},{1,2},{2,3},{3,4},{4,5},{5,6},{6,7},{8,9},{9,10},{10,11},{11... | collective-permute-start | bytes 614408 | tf_op jit(solution)/shard_map/ppermute | solution.py:206

commit v6 on v5

--- a/solution.py
+++ b/solution.py
@@ -57,7 +57,12 @@
         if with_velocity:
             part = jnp.where(lane == 4, lane_roll(from_west, 68 - 4 * a), part)
         parts.append(part)
-    return jnp.concatenate(parts, 0)
+    return parts
+
+
+def sub_roll(value, shift):
+    shift = shift % value.shape[0]
+    return value if shift == 0 else pltpu.roll(value, shift, 0)
 
 
 def write_rows(value, north_v, ypack_ref, f, k):
@@ -116,45 +121,69 @@
 
     lax.fori_loop(0, levels - 1, mixing, 0)
 
+    strips = rows // 8
+    lane8 = lax.broadcasted_iota(jnp.int32, (8, cols), 1)
+    sub8 = lax.broadcasted_iota(jnp.int32, (8, cols), 0)
+
+    def split(value):
+        return [value[8 * a:8 * a + 8] for a in range(strips)]
+
     def level(k, carry):
-        m = mask(k)
-        ue, vn = ue_ref[k], vn_ref[k]
-        afters = []
+        m = split(mask(k))
+        ue, vn = split(ue_ref[k]), split(vn_ref[k])
+        yh0 = yh_ref[0, k]
+        south_v = jnp.where(sub8 == 7, jnp.broadcast_to(yh0[4:5], (8, cols)), 0.0)
+        depth_k = depth(k)
+        afters = [[None] * strips for _ in range(2)]
         for f in range(2):
-            q = load(now_refs[f], k, m)
-            b = load(bef_refs[f], k, m)
-            h = column_unpack(xe_ref[f, k], xw_ref[f, k], f == 0)
+            q = split(load(now_refs[f], k, mask(k)))
+            b = split(load(bef_refs[f], k, mask(k)))
+            hs = column_unpack(xe_ref[f, k], xw_ref[f, k], f == 0)
             yh = yh_ref[f, k]
-            if f == 0:
-                uw = jnp.where(lane < 1, pltpu.roll(h, cols - 4, 1), pltpu.roll(ue, 1, 1))
-                vs = jnp.where(row < 1, jnp.broadcast_to(yh[4:5], (rows, cols)), pltpu.roll(vn, 1, 0))
-            qm1 = jnp.where(lane < 1, pltpu.roll(h, cols - 3, 1), pltpu.roll(q, 1, 1))
-            qm2 = jnp.where(lane < 2, pltpu.roll(h, cols - 2, 1), pltpu.roll(q, 2, 1))
-            qp1 = jnp.where(lane >= cols - 1, pltpu.roll(h, cols - 1, 1), pltpu.roll(q, cols - 1, 1))
-            qp2 = jnp.where(lane >= cols - 2, pltpu.roll(h, cols - 2, 1), pltpu.roll(q, cols - 2, 1))
-            div_x = face_flux(ue, qm1, q, qp1, qp2) - face_flux(uw, qm2, qm1, q, qp1)
-            s2 = jnp.broadcast_to(yh[0:1], (rows, cols))
-            s1 = jnp.broadcast_to(yh[1:2], (rows, cols))
-            n1 = jnp.broadcast_to(yh[2:3], (rows, cols))
-            n2 = jnp.broadcast_to(yh[3:4], (rows, cols))
-            qs1 = jnp.where(row < 1, s1, pltpu.roll(q, 1, 0))
-            qs2 = jnp.where(row < 1, s2, jnp.where(row < 2, s1, pltpu.roll(q, 2, 0)))
-            qn1 = jnp.where(row >= rows - 1, n1, pltpu.roll(q, rows - 1, 0))
-            qn2 = jnp.where(row >= rows - 1, n2, jnp.where(row >= rows - 2, n1, pltpu.roll(q, rows - 2, 0)))
-            div_y = face_flux(vn, qs1, q, qn1, qn2) - face_flux(vs, qs2, qs1, q, qn1)
-            change = -(div_x + div_y)
-            change = change + (fv[f, k + 1] - fv[f, k])
-            after = (b + 2.0 * change) * m
-            afters.append(after)
+            below = jnp.where(sub8 == 6, jnp.broadcast_to(yh[0:1], (8, cols)),
+                              jnp.broadcast_to(yh[1:2], (8, cols)))
+            above = jnp.where(sub8 == 0, jnp.broadcast_to(yh[2:3], (8, cols)),
+                              jnp.broadcast_to(yh[3:4], (8, cols)))
+            qx = [below] + q + [above]
+            fv_lo, fv_hi = split(fv[f, k]), split(fv[f, k + 1])
+            pack = jnp.zeros((8, cols), jnp.float32)
+            for a in range(strips):
+                qa, ha = q[a], hs[a]
+                if f == 0:
+                    if a == 0:
+                        uws, vss = [], []
+                    uws.append(jnp.where(lane8 < 1, lane_roll(ha, cols - 4), lane_roll(ue[a], 1)))
+                    prev_v = south_v if a == 0 else vn[a - 1]
+                    vss.append(jnp.where(sub8 < 1, sub_roll(prev_v, 1), sub_roll(vn[a], 1)))
+                uw, vs = uws[a], vss[a]
+                qm1 = jnp.where(lane8 < 1, lane_roll(ha, cols - 3), lane_roll(qa, 1))
+                qm2 = jnp.where(lane8 < 2, lane_roll(ha, cols - 2), lane_roll(qa, 2))
+                qp1 = jnp.where(lane8 >= cols - 1, lane_roll(ha, cols - 1), lane_roll(qa, cols - 1))
+                qp2 = jnp.where(lane8 >= cols - 2, lane_roll(ha, cols - 2), lane_roll(qa, cols - 2))
+                div_x = face_flux(ue[a], qm1, qa, qp1, qp2) - face_flux(uw, qm2, qm1, qa, qp1)
+                lo, hi = qx[a], qx[a + 2]
+                qs1 = jnp.where(sub8 < 1, sub_roll(lo, 1), sub_roll(qa, 1))
+                qs2 = jnp.where(sub8 < 2, sub_roll(lo, 2), sub_roll(qa, 2))
+                qn1 = jnp.where(sub8 >= 7, sub_roll(hi, 7), sub_roll(qa, 7))
+                qn2 = jnp.where(sub8 >= 6, sub_roll(hi, 6), sub_roll(qa, 6))
+                div_y = face_flux(vn[a], qs1, qa, qn1, qn2) - face_flux(vs, qs2, qs1, qa, qn1)
+                change = -(div_x + div_y)
+                change = change + (fv_hi[a] - fv_lo[a])
+                after = (b[a] + 2.0 * change) * m[a]
+                afters[f][a] = after
+                rs = pl.ds(8 * a, 8)
+                if not final:
+                    outs[f][k, rs, :] = qa + asselin_gamma * (b[a] - 2.0 * qa + after)
+                    outs[2 + f][k, rs, :] = after
+                else:
+                    outs[f][k, rs, :] = after
             if not final:
-                outs[f][k] = q + asselin_gamma * (b - 2.0 * q + after)
-                outs[2 + f][k] = after
-                outs[4][f, k] = column_pack(after, ue)
-                write_rows(after, vn, outs[5], f, k)
+                whole = jnp.concatenate(afters[f], 0)
+                outs[4][f, k] = column_pack(whole, ue_ref[k])
+                write_rows(whole, vn_ref[k], outs[5], f, k)
         if final:
-            outs[0][k] = afters[0]
-            outs[1][k] = afters[1]
-            outs[2][k] = density_at(afters[0], afters[1], depth(k)) * m
+            for a in range(strips):
+                outs[2][k, pl.ds(8 * a, 8), :] = density_at(afters[0][a], afters[1][a], depth_k) * m[a]
         return carry
 
     lax.fori_loop(0, levels, level, 0)

time: 70.9 us -> 70.2 us (level)
  Pallas kernels: 28.4 us -> 27.6 us
    pallas_call x2, Pallas kernels: 24.4 us -> 23.7 us  [step_call(): pl.pallas_call(functools.partial(step_kernel, mask_inputs, final), out_sh...]
where the time goes in v6:
time: 70.2 us; the launch traced here: 69.9 us
  Pallas kernels  27.6 us (39%)
  starting transfers between devices  25.4 us (36%)
  waiting for transfers between devices  13.2 us (19%)
  local copies, waits for them, and re-layouts  1.99 us (3%)
  between operations  0.94 us (1%)
    pallas_call x2, Pallas kernels, step_call(): pl.pallas_call(functools.partial(step_kernel, mask_inputs, final), out_sh...  23.7 us
    ppermute x2, waiting for transfers between devices, exchange(): lax.ppermute(ypack, 'lat', [(i, i + 1) for i in range(lat_count - 1)])  13.2 us
    ppermute x2, starting transfers between devices, exchange(): lax.ppermute(xpack, 'lon', [(i, (i - 1) % lon_count) for i in range(lon_c...  10.7 us
    ppermute x2, starting transfers between devices, exchange(): lax.ppermute(ypack, 'lat', [(i, i - 1) for i in range(1, lat_count)])  7.28 us
    ppermute x2, starting transfers between devices, exchange(): lax.ppermute(ypack, 'lat', [(i, i + 1) for i in range(lat_count - 1)])  5.84 us
    pallas_call x1, Pallas kernels, edge_call(): pl.pallas_call(edge_kernel, out_shape=pack_shapes(levels, rows, cols), in...  3.94 us
    ppermute x2, starting transfers between devices, exchange(): partner = lax.ppermute(ypack[:, :, 2:4], ('lon', 'lat'), fold_pairs)  1.46 us
  transfers between devices with their start and end apart: 10, of which 2 were waited for; matrix products, arithmetic and copies ran while one was open for 1% of the time, Pallas kernels for 0%

profile of v6, /device:TPU:8, one launch (start us, length us, event | category | flops | bytes accessed | tf_op | source)
XLA Modules:
  0.0 69.9 jit_solution(12406606714323977920)
XLA Ops:
  0.6 0.0 copy-start.3
  0.6 3.9 %shard_map.94 = (f32[2,25,8,128]{3,2,1,0:T(8,128)}, f32[2,25,8,128]{3,2,1,0:T(8,128)}) custom-call(s32[64,128]{1,0:T(8,128)} %bl_ref.5, f32[25,64,128]{2,1,0:T(8,128)} %nt_ref.3, f32[25,64,128]{2,1,0:T(8,128)} %ns_ref.3, f32[25,64,128]{2,1,0:T(8,128)} %ue_ref.5, f32[25,64,128]{2,1,0:T(8,128)} %vn_ref.5), custom_call_target="tpu_custom_call" | custom-call | flops 6553600 | bytes 4096000 | tf_op jit(solution)/shard_map/pallas_call | solution.py:202
  4.6 0.0 copy-start.2
  4.6 1.0 %slice.37 = f32[2,25,2,128]{3,2,1,0:T(2,128)S(1)} slice(f32[2,25,8,128]{3,2,1,0:T(8,128)} %get-tuple-element.12), slice={[0:2], [0:25], [2:4], [0:128]} | slice | bytes 102400 | tf_op jit(solution)/shard_map/slice | solution.py:238
  5.6 0.7 collective-permute-start.3
  6.3 0.1 collective-permute-start.1
  6.4 5.3 %collective-permute-start = (f32[2,25,8,128]{3,2,1,0:T(8,128)}, f32[2,25,8,128]{3,2,1,0:T(8,128)S(1)}, u32[]{:S(2)}, u32[]{:S(2)}) collective-permute-start(f32[2,25,8,128]{3,2,1,0:T(8,128)} %get-tuple-element.11), channel_id=1, source_target_pairs={{0,120},{8,0},{16,8},{24,16},{32,24},{40,32},{48,40},{56,48},{64,5... | collective-permute-start | bytes 614408 | tf_op jit(solution)/shard_map/ppermute | solution.py:232
  11.7 5.4 %collective-permute-start.4 = (f32[2,25,8,128]{3,2,1,0:T(8,128)}, f32[2,25,8,128]{3,2,1,0:T(8,128)S(1)}, u32[]{:S(2)}, u32[]{:S(2)}) collective-permute-start(f32[2,25,8,128]{3,2,1,0:T(8,128)} %get-tuple-element.12), channel_id=1, source_target_pairs={{1,0},{2,1},{3,2},{4,3},{5,4},{6,5},{7,6},{9,8},{10,9},{11,10},{12... | collective-permute-start | bytes 614408 | tf_op jit(solution)/shard_map/ppermute | solution.py:234
  17.1 1.9 %collective-permute-start.2 = (f32[2,25,8,128]{3,2,1,0:T(8,128)}, f32[2,25,8,128]{3,2,1,0:T(8,128)S(1)}, u32[]{:S(2)}, u32[]{:S(2)}) collective-permute-start(f32[2,25,8,128]{3,2,1,0:T(8,128)} %get-tuple-element.12), channel_id=1, source_target_pairs={{0,1},{1,2},{2,3},{3,4},{4,5},{5,6},{6,7},{8,9},{9,10},{10,11},{11... | collective-permute-start | bytes 614408 | tf_op jit(solution)/shard_map/ppermute | solution.py:235
  19.0 0.1 pad.9.clone
  19.1 0.0 collective-permute-done.3
  19.1 0.2 fusion.2
  19.4 7.7 %collective-permute-done.2 = f32[2,25,8,128]{3,2,1,0:T(8,128)S(1)} collective-permute-done((f32[2,25,8,128]{3,2,1,0:T(8,128)}, f32[2,25,8,128]{3,2,1,0:T(8,128)S(1)}, u32[]{:S(2)}, u32[]{:S(2)}) %collective-permute-start.2) | collective-permute-done | bytes 204832 | tf_op jit(solution)/shard_map/ppermute | solution.py:235
  27.1 0.0 collective-permute-done.4
  27.1 0.1 slice_select_fusion.1
  27.2 0.0 copy-start.4
  27.2 0.1 maximum_maximum_fusion.yh_ref
  27.3 0.0 collective-permute-done.1.xw_ref
  27.3 0.0 collective-permute-done.xe_ref
  27.3 0.0 copy-done.3
  27.3 0.0 copy-done.2
  27.3 0.6 copy-done.4
  28.0 0.0 copy-start.1
  28.0 13.2 %shard_map.95 = (f32[25,64,128]{2,1,0:T(8,128)S(1)}, f32[25,64,128]{2,1,0:T(8,128)S(1)}, f32[25,64,128]{2,1,0:T(8,128)S(1)}, f32[25,64,128]{2,1,0:T(8,128)S(1)},...) custom-call(s32[64,128]{1,0:T(8,128)S(1)} %copy-done.4, f32[25,64,128]{2,1,0:T(8,128)S(1)} %copy-done.2, ...), custom_call_target="tpu_custom_call" | custom-call | flops 163840000 | bytes 12288000 | tf_op jit(solution)/shard_map/pallas_call | solution.py:217
  41.2 0.0 copy-start
  41.2 0.8 %collective-permute-start.8 = (f32[2,25,2,128]{3,2,1,0:T(2,128)S(1)}, f32[2,25,2,128]{3,2,1,0:T(2,128)S(1)}, u32[]{:S(2)}, u32[]{:S(2)}) collective-permute-start(f32[2,25,2,128]{3,2,1,0:T(2,128)S(1)} %slice.43), channel_id=1, source_target_pairs={{7,127},{15,119},{23,111},{31,103},{39,95},{47,87},{55,79},{63,71}... | collective-permute-start | bytes 153608 | tf_op jit(solution)/shard_map/ppermute | solution.py:238
  42.0 0.1 collective-permute-start.6
  42.1 5.3 %collective-permute-start.5 = (f32[2,25,8,128]{3,2,1,0:T(8,128)S(1)}, f32[2,25,8,128]{3,2,1,0:T(8,128)S(1)}, u32[]{:S(2)}, u32[]{:S(2)}) collective-permute-start(f32[2,25,8,128]{3,2,1,0:T(8,128)S(1)} %get-tuple-element.17), channel_id=1, source_target_pairs={{0,120},{8,0},{16,8},{24,16},{32,24},{40,32},{48,40},{56,48},{64,5... | collective-permute-start | bytes 614408 | tf_op jit(solution)/shard_map/ppermute | solution.py:232
  47.4 1.9 %collective-permute-start.9 = (f32[2,25,8,128]{3,2,1,0:T(8,128)S(1)}, f32[2,25,8,128]{3,2,1,0:T(8,128)S(1)}, u32[]{:S(2)}, u32[]{:S(2)}) collective-permute-start(f32[2,25,8,128]{3,2,1,0:T(8,128)S(1)} %get-tuple-element.18), channel_id=1, source_target_pairs={{1,0},{2,1},{3,2},{4,3},{5,4},{6,5},{7,6},{9,8},{10,9},{11,10},{12... | collective-permute-start | bytes 614408 | tf_op jit(solution)/shard_map/ppermute | solution.py:234
  49.3 3.9 %collective-permute-start.7 = (f32[2,25,8,128]{3,2,1,0:T(8,128)S(1)}, f32[2,25,8,128]{3,2,1,0:T(8,128)S(1)}, u32[]{:S(2)}, u32[]{:S(2)}) collective-permute-start(f32[2,25,8,128]{3,2,1,0:T(8,128)S(1)} %get-tuple-element.18), channel_id=1, source_target_pairs={{0,1},{1,2},{2,3},{3,4},{4,5},{5,6},{6,7},{8,9},{9,10},{10,11},{11... | collective-permute-start | bytes 614408 | tf_op jit(solution)/shard_map/ppermute | solution.py:235
  53.3 0.0 collective-permute-done.8
  53.3 0.2 fusion
  53.6 5.5 %collective-permute-done.7 = f32[2,25,8,128]{3,2,1,0:T(8,128)S(1)} collective-permute-done((f32[2,25,8,128]{3,2,1,0:T(8,128)S(1)}, f32[2,25,8,128]{3,2,1,0:T(8,128)S(1)}, u32[]{:S(2)}, u32[]{:S(2)}) %collective-permute-start.7) | collective-permute-done | bytes 204832 | tf_op jit(solution)/shard_map/ppermute | solution.py:235
  59.2 0.0 collective-permute-done.9
  59.2 0.1 slice_select_fusion
  59.2 0.1 maximum_maximum_fusion.1.yh_ref
  59.3 0.0 collective-permute-done.6.xw_ref
  59.3 0.0 collective-permute-done.5.xe_ref
  59.4 0.0 copy-done.1
  59.4 0.0 copy-done
  59.4 10.5 %shard_map.96 = (f32[25,64,128]{2,1,0:T(8,128)}, f32[25,64,128]{2,1,0:T(8,128)}, f32[25,64,128]{2,1,0:T(8,128)}) custom-call(s32[64,128]{1,0:T(8,128)S(1)} %copy-done.4, f32[25,64,128]{2,1,0:T(8,128)S(1)} %get-tuple-element.13.nt_ref, f32[25,64,128]{2,1,0:T(8,128)S(1)} %get-tuple-element.14.ns_ref, f32[25,64,128]{2,1,0:T(8,128)S(1)} %get-tuple-element.15.bt_ref, ...), custom_call_target="tpu_custom_call" | custom-call | flops 163840000 | bytes 9830400 | tf_op jit(solution)/shard_map/pallas_call | solution.py:217
  (12 shorter events, 0.2 us)
Async XLA Ops:
  0.6 26.7 %copy-start.3 = (f32[25,64,128]{2,1,0:T(8,128)S(1)}, f32[25,64,128]{2,1,0:T(8,128)}, u32[]{:S(2)}) copy-start(f32[25,64,128]{2,1,0:T(8,128)} %ns_ref.3) | copy-start | bytes 2457604
  4.6 22.8 %copy-start.2 = (f32[25,64,128]{2,1,0:T(8,128)S(1)}, f32[25,64,128]{2,1,0:T(8,128)}, u32[]{:S(2)}) copy-start(f32[25,64,128]{2,1,0:T(8,128)} %nt_ref.3) | copy-start | bytes 2457604
  5.6 13.5 %collective-permute-start.3 = (f32[2,25,2,128]{3,2,1,0:T(2,128)S(1)}, f32[2,25,2,128]{3,2,1,0:T(2,128)S(1)}, u32[]{:S(2)}, u32[]{:S(2)}) collective-permute-start(f32[2,25,2,128]{3,2,1,0:T(2,128)S(1)} %slice.37), channel_id=1, source_target_pairs={{7,127},{15,119},{23,111},{31,103},{39,95},{47,87},{55,79},{63,71}... | collective-permute-start | bytes 153608 | tf_op jit(solution)/shard_map/ppermute | solution.py:238
  6.3 21.0 %collective-permute-start.1 = (f32[2,25,8,128]{3,2,1,0:T(8,128)}, f32[2,25,8,128]{3,2,1,0:T(8,128)S(1)}, u32[]{:S(2)}, u32[]{:S(2)}) collective-permute-start(f32[2,25,8,128]{3,2,1,0:T(8,128)} %get-tuple-element.11), channel_id=1, source_target_pairs={{0,8},{8,16},{16,24},{24,32},{32,40},{40,48},{48,56},{56,64},{64,7... | collective-permute-start | bytes 614408 | tf_op jit(solution)/shard_map/ppermute | solution.py:233
  6.4 20.9 %collective-permute-start = (f32[2,25,8,128]{3,2,1,0:T(8,128)}, f32[2,25,8,128]{3,2,1,0:T(8,128)S(1)}, u32[]{:S(2)}, u32[]{:S(2)}) collective-permute-start(f32[2,25,8,128]{3,2,1,0:T(8,128)} %get-tuple-element.11), channel_id=1, source_target_pairs={{0,120},{8,0},{16,8},{24,16},{32,24},{40,32},{48,40},{56,48},{64,5... | collective-permute-start | bytes 614408 | tf_op jit(solution)/shard_map/ppermute | solution.py:232
  11.7 15.4 %collective-permute-start.4 = (f32[2,25,8,128]{3,2,1,0:T(8,128)}, f32[2,25,8,128]{3,2,1,0:T(8,128)S(1)}, u32[]{:S(2)}, u32[]{:S(2)}) collective-permute-start(f32[2,25,8,128]{3,2,1,0:T(8,128)} %get-tuple-element.12), channel_id=1, source_target_pairs={{1,0},{2,1},{3,2},{4,3},{5,4},{6,5},{7,6},{9,8},{10,9},{11,10},{12... | collective-permute-start | bytes 614408 | tf_op jit(solution)/shard_map/ppermute | solution.py:234
  17.1 10.0 %collective-permute-start.2 = (f32[2,25,8,128]{3,2,1,0:T(8,128)}, f32[2,25,8,128]{3,2,1,0:T(8,128)S(1)}, u32[]{:S(2)}, u32[]{:S(2)}) collective-permute-start(f32[2,25,8,128]{3,2,1,0:T(8,128)} %get-tuple-element.12), channel_id=1, source_target_pairs={{0,1},{1,2},{2,3},{3,4},{4,5},{5,6},{6,7},{8,9},{9,10},{10,11},{11... | collective-permute-start | bytes 614408 | tf_op jit(solution)/shard_map/ppermute | solution.py:235
  27.2 0.8 %copy-start.4 = (s32[64,128]{1,0:T(8,128)S(1)}, s32[64,128]{1,0:T(8,128)}, u32[]{:S(2)}) copy-start(s32[64,128]{1,0:T(8,128)} %bl_ref.5) | copy-start | bytes 98308
  28.0 31.4 %copy-start.1 = (f32[25,64,128]{2,1,0:T(8,128)S(1)}, f32[25,64,128]{2,1,0:T(8,128)}, u32[]{:S(2)}) copy-start(f32[25,64,128]{2,1,0:T(8,128)} %vn_ref.5) | copy-start | bytes 2457604
  41.2 18.2 %copy-start = (f32[25,64,128]{2,1,0:T(8,128)S(1)}, f32[25,64,128]{2,1,0:T(8,128)}, u32[]{:S(2)}) copy-start(f32[25,64,128]{2,1,0:T(8,128)} %ue_ref.5) | copy-start | bytes 2457604
  41.2 12.1 %collective-permute-start.8 = (f32[2,25,2,128]{3,2,1,0:T(2,128)S(1)}, f32[2,25,2,128]{3,2,1,0:T(2,128)S(1)}, u32[]{:S(2)}, u32[]{:S(2)}) collective-permute-start(f32[2,25,2,128]{3,2,1,0:T(2,128)S(1)} %slice.43), channel_id=1, source_target_pairs={{7,127},{15,119},{23,111},{31,103},{39,95},{47,87},{55,79},{63,71}... | collective-permute-start | bytes 153608 | tf_op jit(solution)/shard_map/ppermute | solution.py:238
  42.0 17.3 %collective-permute-start.6 = (f32[2,25,8,128]{3,2,1,0:T(8,128)S(1)}, f32[2,25,8,128]{3,2,1,0:T(8,128)S(1)}, u32[]{:S(2)}, u32[]{:S(2)}) collective-permute-start(f32[2,25,8,128]{3,2,1,0:T(8,128)S(1)} %get-tuple-element.17), channel_id=1, source_target_pairs={{0,8},{8,16},{16,24},{24,32},{32,40},{40,48},{48,56},{56,64},{64,7... | collective-permute-start | bytes 614408 | tf_op jit(solution)/shard_map/ppermute | solution.py:233
  42.1 17.3 %collective-permute-start.5 = (f32[2,25,8,128]{3,2,1,0:T(8,128)S(1)}, f32[2,25,8,128]{3,2,1,0:T(8,128)S(1)}, u32[]{:S(2)}, u32[]{:S(2)}) collective-permute-start(f32[2,25,8,128]{3,2,1,0:T(8,128)S(1)} %get-tuple-element.17), channel_id=1, source_target_pairs={{0,120},{8,0},{16,8},{24,16},{32,24},{40,32},{48,40},{56,48},{64,5... | collective-permute-start | bytes 614408 | tf_op jit(solution)/shard_map/ppermute | solution.py:232
  47.4 11.7 %collective-permute-start.9 = (f32[2,25,8,128]{3,2,1,0:T(8,128)S(1)}, f32[2,25,8,128]{3,2,1,0:T(8,128)S(1)}, u32[]{:S(2)}, u32[]{:S(2)}) collective-permute-start(f32[2,25,8,128]{3,2,1,0:T(8,128)S(1)} %get-tuple-element.18), channel_id=1, source_target_pairs={{1,0},{2,1},{3,2},{4,3},{5,4},{6,5},{7,6},{9,8},{10,9},{11,10},{12... | collective-permute-start | bytes 614408 | tf_op jit(solution)/shard_map/ppermute | solution.py:234
  49.3 9.8 %collective-permute-start.7 = (f32[2,25,8,128]{3,2,1,0:T(8,128)S(1)}, f32[2,25,8,128]{3,2,1,0:T(8,128)S(1)}, u32[]{:S(2)}, u32[]{:S(2)}) collective-permute-start(f32[2,25,8,128]{3,2,1,0:T(8,128)S(1)} %get-tuple-element.18), channel_id=1, source_target_pairs={{0,1},{1,2},{2,3},{3,4},{4,5},{5,6},{6,7},{8,9},{9,10},{10,11},{11... | collective-permute-start | bytes 614408 | tf_op jit(solution)/shard_map/ppermute | solution.py:235

commit v7 on v6

--- a/solution.py
+++ b/solution.py
@@ -26,8 +26,8 @@
 
 
 def face_flux(u, q1, q2, q3, q4):
-    flux = u * (7.0 * (q2 + q3) - (q1 + q4)) / 12.0
-    return flux + jnp.abs(u) * ((q4 - q1) - 3.0 * (q3 - q2)) / 12.0
+    flux = u * (7.0 * (q2 + q3) - (q1 + q4)) + jnp.abs(u) * ((q4 - q1) - 3.0 * (q3 - q2))
+    return flux * (1.0 / 12.0)
 
 
 def lane_roll(value, shift):
@@ -40,9 +40,10 @@
     lane = lax.broadcasted_iota(jnp.int32, (8, cols), 1)
     pack = jnp.zeros((8, cols), jnp.float32)
     for a in range(rows // 8):
-        part = value[8 * a:8 * a + 8]
-        pack = jnp.where((lane >= 4 * a) & (lane < 4 * a + 2), lane_roll(part, 4 * a), pack)
-        pack = jnp.where((lane >= 4 * a + 2) & (lane < 4 * a + 4), lane_roll(part, 4 * a + 4), pack)
+        part = lane_roll(value[8 * a:8 * a + 8], 4 * a)
+        lo_lane = (4 * a - 2) % cols
+        pack = jnp.where((lane >= 4 * a) & (lane < 4 * a + 2), part, pack)
+        pack = jnp.where((lane >= lo_lane) & (lane < lo_lane + 2), part, pack)
         pack = jnp.where(lane == 64 + 4 * a, lane_roll(east_v[8 * a:8 * a + 8], 4 * a + 65), pack)
     return pack
 
@@ -51,13 +52,7 @@
     cols = from_east.shape[-1]
     lane = lax.broadcasted_iota(jnp.int32, (8, cols), 1)
     both = jnp.where(lane % 4 < 2, from_east, from_west)
-    parts = []
-    for a in range(8):
-        part = lane_roll(both, -4 * a)
-        if with_velocity:
-            part = jnp.where(lane == 4, lane_roll(from_west, 68 - 4 * a), part)
-        parts.append(part)
-    return parts
+    return both, [lane_roll(both, -4 * a) for a in range(8)]
 
 
 def sub_roll(value, shift):
@@ -131,42 +126,43 @@
     def level(k, carry):
         m = split(mask(k))
         ue, vn = split(ue_ref[k]), split(vn_ref[k])
-        yh0 = yh_ref[0, k]
-        south_v = jnp.where(sub8 == 7, jnp.broadcast_to(yh0[4:5], (8, cols)), 0.0)
+        south_v = jnp.where(sub8 == 7, jnp.broadcast_to(yh_ref[0, k][4:5], (8, cols)), 0.0)
         depth_k = depth(k)
         afters = [[None] * strips for _ in range(2)]
         for f in range(2):
             q = split(load(now_refs[f], k, mask(k)))
             b = split(load(bef_refs[f], k, mask(k)))
-            hs = column_unpack(xe_ref[f, k], xw_ref[f, k], f == 0)
+            from_west = xw_ref[f, k]
+            both, hs = column_unpack(xe_ref[f, k], from_west, False)
+            own = jnp.zeros((8, cols), jnp.float32)
+            for a in range(strips):
+                own = jnp.where((lane8 >= 4 * a) & (lane8 < 4 * a + 2), lane_roll(q[a], 4 * a), own)
+            west_face = face_flux(lane_roll(from_west, -64), lane_roll(both, 2), lane_roll(both, 1),
+                                  own, lane_roll(own, -1))
             yh = yh_ref[f, k]
             below = jnp.where(sub8 == 6, jnp.broadcast_to(yh[0:1], (8, cols)),
                               jnp.broadcast_to(yh[1:2], (8, cols)))
             above = jnp.where(sub8 == 0, jnp.broadcast_to(yh[2:3], (8, cols)),
                               jnp.broadcast_to(yh[3:4], (8, cols)))
-            qx = [below] + q + [above]
+            qx = q + [above]
+            north_prev = face_flux(south_v, sub_roll(below, 1), below, sub_roll(q[0], 7), sub_roll(q[0], 6))
+            lo = below
             fv_lo, fv_hi = split(fv[f, k]), split(fv[f, k + 1])
-            pack = jnp.zeros((8, cols), jnp.float32)
             for a in range(strips):
-                qa, ha = q[a], hs[a]
-                if f == 0:
-                    if a == 0:
-                        uws, vss = [], []
-                    uws.append(jnp.where(lane8 < 1, lane_roll(ha, cols - 4), lane_roll(ue[a], 1)))
-                    prev_v = south_v if a == 0 else vn[a - 1]
-                    vss.append(jnp.where(sub8 < 1, sub_roll(prev_v, 1), sub_roll(vn[a], 1)))
-                uw, vs = uws[a], vss[a]
-                qm1 = jnp.where(lane8 < 1, lane_roll(ha, cols - 3), lane_roll(qa, 1))
-                qm2 = jnp.where(lane8 < 2, lane_roll(ha, cols - 2), lane_roll(qa, 2))
-                qp1 = jnp.where(lane8 >= cols - 1, lane_roll(ha, cols - 1), lane_roll(qa, cols - 1))
-                qp2 = jnp.where(lane8 >= cols - 2, lane_roll(ha, cols - 2), lane_roll(qa, cols - 2))
-                div_x = face_flux(ue[a], qm1, qa, qp1, qp2) - face_flux(uw, qm2, qm1, qa, qp1)
-                lo, hi = qx[a], qx[a + 2]
-                qs1 = jnp.where(sub8 < 1, sub_roll(lo, 1), sub_roll(qa, 1))
-                qs2 = jnp.where(sub8 < 2, sub_roll(lo, 2), sub_roll(qa, 2))
-                qn1 = jnp.where(sub8 >= 7, sub_roll(hi, 7), sub_roll(qa, 7))
-                qn2 = jnp.where(sub8 >= 6, sub_roll(hi, 6), sub_roll(qa, 6))
-                div_y = face_flux(vn[a], qs1, qa, qn1, qn2) - face_flux(vs, qs2, qs1, qa, qn1)
+                qa, ha, hi = q[a], hs[a], qx[a + 1]
+                qm1 = lane_roll(jnp.where(lane8 == cols - 1, ha, qa), 1)
+                qp1 = lane_roll(jnp.where(lane8 < 1, ha, qa), -1)
+                qp2 = lane_roll(jnp.where(lane8 < 2, ha, qa), -2)
+                east_f = face_flux(ue[a], qm1, qa, qp1, qp2)
+                west_f = jnp.where(lane8 < 1, lane_roll(west_face, -4 * a), lane_roll(east_f, 1))
+                qs1 = sub_roll(jnp.where(sub8 == 7, lo, qa), 1)
+                qn1 = sub_roll(jnp.where(sub8 < 1, hi, qa), 7)
+                qn2 = sub_roll(jnp.where(sub8 < 2, hi, qa), 6)
+                north_f = face_flux(vn[a], qs1, qa, qn1, qn2)
+                south_f = sub_roll(jnp.where(sub8 == 7, north_prev, north_f), 1)
+                north_prev, lo = north_f, qa
+                div_x = east_f - west_f
+                div_y = north_f - south_f
                 change = -(div_x + div_y)
                 change = change + (fv_hi[a] - fv_lo[a])
                 after = (b[a] + 2.0 * change) * m[a]

time: 70.2 us -> 69.3 us (0.987)
  Pallas kernels: 27.6 us -> 26.8 us
where the time goes in v7:
time: 69.3 us; the launch traced here: 69 us
  Pallas kernels  26.8 us (39%)
  starting transfers between devices  25.4 us (37%)
  waiting for transfers between devices  13.2 us (19%)
  local copies, waits for them, and re-layouts  1.99 us (3%)
  between operations  0.94 us (1%)
    pallas_call x2, Pallas kernels, step_call(): pl.pallas_call(functools.partial(step_kernel, mask_inputs, final), out_sh...  23.2 us
    ppermute x2, waiting for transfers between devices, exchange(): lax.ppermute(ypack, 'lat', [(i, i + 1) for i in range(lat_count - 1)])  13.2 us
    ppermute x2, starting transfers between devices, exchange(): lax.ppermute(xpack, 'lon', [(i, (i - 1) % lon_count) for i in range(lon_c...  10.7 us
    ppermute x2, starting transfers between devices, exchange(): lax.ppermute(ypack, 'lat', [(i, i - 1) for i in range(1, lat_count)])  7.28 us
    ppermute x2, starting transfers between devices, exchange(): lax.ppermute(ypack, 'lat', [(i, i + 1) for i in range(lat_count - 1)])  5.84 us
    pallas_call x1, Pallas kernels, edge_call(): pl.pallas_call(edge_kernel, out_shape=pack_shapes(levels, rows, cols), in...  3.52 us
    ppermute x2, starting transfers between devices, exchange(): partner = lax.ppermute(ypack[:, :, 2:4], ('lon', 'lat'), fold_pairs)  1.46 us
  transfers between devices with their start and end apart: 10, of which 2 were waited for; matrix products, arithmetic and copies ran while one was open for 1% of the time, Pallas kernels for 0%

profile of v7, /device:TPU:8, one launch (start us, length us, event | category | flops | bytes accessed | tf_op | source)
XLA Modules:
  0.0 69.0 jit_solution(6621350013012531222)
XLA Ops:
  0.6 0.0 copy-start.3
  0.6 3.5 %shard_map.94 = (f32[2,25,8,128]{3,2,1,0:T(8,128)}, f32[2,25,8,128]{3,2,1,0:T(8,128)}) custom-call(s32[64,128]{1,0:T(8,128)} %bl_ref.5, f32[25,64,128]{2,1,0:T(8,128)} %nt_ref.3, f32[25,64,128]{2,1,0:T(8,128)} %ns_ref.3, f32[25,64,128]{2,1,0:T(8,128)} %ue_ref.5, f32[25,64,128]{2,1,0:T(8,128)} %vn_ref.5), custom_call_target="tpu_custom_call" | custom-call | flops 6553600 | bytes 4096000 | tf_op jit(solution)/shard_map/pallas_call | solution.py:198
  4.2 0.0 copy-start.2
  4.2 1.0 %slice.37 = f32[2,25,2,128]{3,2,1,0:T(2,128)S(1)} slice(f32[2,25,8,128]{3,2,1,0:T(8,128)} %get-tuple-element.12), slice={[0:2], [0:25], [2:4], [0:128]} | slice | bytes 102400 | tf_op jit(solution)/shard_map/slice | solution.py:234
  5.2 0.7 collective-permute-start.3
  5.9 0.1 collective-permute-start.1
  5.9 5.3 %collective-permute-start = (f32[2,25,8,128]{3,2,1,0:T(8,128)}, f32[2,25,8,128]{3,2,1,0:T(8,128)S(1)}, u32[]{:S(2)}, u32[]{:S(2)}) collective-permute-start(f32[2,25,8,128]{3,2,1,0:T(8,128)} %get-tuple-element.11), channel_id=1, source_target_pairs={{0,120},{8,0},{16,8},{24,16},{32,24},{40,32},{48,40},{56,48},{64,5... | collective-permute-start | bytes 614408 | tf_op jit(solution)/shard_map/ppermute | solution.py:228
  11.3 5.4 %collective-permute-start.4 = (f32[2,25,8,128]{3,2,1,0:T(8,128)}, f32[2,25,8,128]{3,2,1,0:T(8,128)S(1)}, u32[]{:S(2)}, u32[]{:S(2)}) collective-permute-start(f32[2,25,8,128]{3,2,1,0:T(8,128)} %get-tuple-element.12), channel_id=1, source_target_pairs={{1,0},{2,1},{3,2},{4,3},{5,4},{6,5},{7,6},{9,8},{10,9},{11,10},{12... | collective-permute-start | bytes 614408 | tf_op jit(solution)/shard_map/ppermute | solution.py:230
  16.7 1.9 %collective-permute-start.2 = (f32[2,25,8,128]{3,2,1,0:T(8,128)}, f32[2,25,8,128]{3,2,1,0:T(8,128)S(1)}, u32[]{:S(2)}, u32[]{:S(2)}) collective-permute-start(f32[2,25,8,128]{3,2,1,0:T(8,128)} %get-tuple-element.12), channel_id=1, source_target_pairs={{0,1},{1,2},{2,3},{3,4},{4,5},{5,6},{6,7},{8,9},{9,10},{10,11},{11... | collective-permute-start | bytes 614408 | tf_op jit(solution)/shard_map/ppermute | solution.py:231
  18.6 0.1 pad.9.clone
  18.7 0.0 collective-permute-done.3
  18.7 0.2 fusion.2
  19.0 7.7 %collective-permute-done.2 = f32[2,25,8,128]{3,2,1,0:T(8,128)S(1)} collective-permute-done((f32[2,25,8,128]{3,2,1,0:T(8,128)}, f32[2,25,8,128]{3,2,1,0:T(8,128)S(1)}, u32[]{:S(2)}, u32[]{:S(2)}) %collective-permute-start.2) | collective-permute-done | bytes 204832 | tf_op jit(solution)/shard_map/ppermute | solution.py:231
  26.7 0.0 collective-permute-done.4
  26.7 0.1 slice_select_fusion.1
  26.8 0.0 copy-start.4
  26.8 0.1 maximum_maximum_fusion.yh_ref
  26.9 0.0 collective-permute-done.1.xw_ref
  26.9 0.0 collective-permute-done.xe_ref
  26.9 0.0 copy-done.3
  26.9 0.0 copy-done.2
  26.9 0.6 copy-done.4
  27.5 0.0 copy-start.1
  27.5 12.7 %shard_map.95 = (f32[25,64,128]{2,1,0:T(8,128)S(1)}, f32[25,64,128]{2,1,0:T(8,128)S(1)}, f32[25,64,128]{2,1,0:T(8,128)S(1)}, f32[25,64,128]{2,1,0:T(8,128)S(1)},...) custom-call(s32[64,128]{1,0:T(8,128)S(1)} %copy-done.4, f32[25,64,128]{2,1,0:T(8,128)S(1)} %copy-done.2, ...), custom_call_target="tpu_custom_call" | custom-call | flops 163840000 | bytes 12288000 | tf_op jit(solution)/shard_map/pallas_call | solution.py:213
  40.2 0.0 copy-start
  40.3 0.8 %collective-permute-start.8 = (f32[2,25,2,128]{3,2,1,0:T(2,128)S(1)}, f32[2,25,2,128]{3,2,1,0:T(2,128)S(1)}, u32[]{:S(2)}, u32[]{:S(2)}) collective-permute-start(f32[2,25,2,128]{3,2,1,0:T(2,128)S(1)} %slice.43), channel_id=1, source_target_pairs={{7,127},{15,119},{23,111},{31,103},{39,95},{47,87},{55,79},{63,71}... | collective-permute-start | bytes 153608 | tf_op jit(solution)/shard_map/ppermute | solution.py:234
  41.1 0.1 collective-permute-start.6
  41.1 5.3 %collective-permute-start.5 = (f32[2,25,8,128]{3,2,1,0:T(8,128)S(1)}, f32[2,25,8,128]{3,2,1,0:T(8,128)S(1)}, u32[]{:S(2)}, u32[]{:S(2)}) collective-permute-start(f32[2,25,8,128]{3,2,1,0:T(8,128)S(1)} %get-tuple-element.17), channel_id=1, source_target_pairs={{0,120},{8,0},{16,8},{24,16},{32,24},{40,32},{48,40},{56,48},{64,5... | collective-permute-start | bytes 614408 | tf_op jit(solution)/shard_map/ppermute | solution.py:228
  46.5 1.9 %collective-permute-start.9 = (f32[2,25,8,128]{3,2,1,0:T(8,128)S(1)}, f32[2,25,8,128]{3,2,1,0:T(8,128)S(1)}, u32[]{:S(2)}, u32[]{:S(2)}) collective-permute-start(f32[2,25,8,128]{3,2,1,0:T(8,128)S(1)} %get-tuple-element.18), channel_id=1, source_target_pairs={{1,0},{2,1},{3,2},{4,3},{5,4},{6,5},{7,6},{9,8},{10,9},{11,10},{12... | collective-permute-start | bytes 614408 | tf_op jit(solution)/shard_map/ppermute | solution.py:230
  48.4 3.9 %collective-permute-start.7 = (f32[2,25,8,128]{3,2,1,0:T(8,128)S(1)}, f32[2,25,8,128]{3,2,1,0:T(8,128)S(1)}, u32[]{:S(2)}, u32[]{:S(2)}) collective-permute-start(f32[2,25,8,128]{3,2,1,0:T(8,128)S(1)} %get-tuple-element.18), channel_id=1, source_target_pairs={{0,1},{1,2},{2,3},{3,4},{4,5},{5,6},{6,7},{8,9},{9,10},{10,11},{11... | collective-permute-start | bytes 614408 | tf_op jit(solution)/shard_map/ppermute | solution.py:231
  52.3 0.0 collective-permute-done.8
  52.3 0.2 fusion
  52.6 5.5 %collective-permute-done.7 = f32[2,25,8,128]{3,2,1,0:T(8,128)S(1)} collective-permute-done((f32[2,25,8,128]{3,2,1,0:T(8,128)S(1)}, f32[2,25,8,128]{3,2,1,0:T(8,128)S(1)}, u32[]{:S(2)}, u32[]{:S(2)}) %collective-permute-start.7) | collective-permute-done | bytes 204832 | tf_op jit(solution)/shard_map/ppermute | solution.py:231
  58.2 0.0 collective-permute-done.9
  58.2 0.1 slice_select_fusion
  58.3 0.1 maximum_maximum_fusion.1.yh_ref
  58.4 0.0 collective-permute-done.6.xw_ref
  58.4 0.0 collective-permute-done.5.xe_ref
  58.4 0.0 copy-done.1
  58.4 0.0 copy-done
  58.4 10.6 %shard_map.96 = (f32[25,64,128]{2,1,0:T(8,128)}, f32[25,64,128]{2,1,0:T(8,128)}, f32[25,64,128]{2,1,0:T(8,128)}) custom-call(s32[64,128]{1,0:T(8,128)S(1)} %copy-done.4, f32[25,64,128]{2,1,0:T(8,128)S(1)} %get-tuple-element.13.nt_ref, f32[25,64,128]{2,1,0:T(8,128)S(1)} %get-tuple-element.14.ns_ref, f32[25,64,128]{2,1,0:T(8,128)S(1)} %get-tuple-element.15.bt_ref, ...), custom_call_target="tpu_custom_call" | custom-call | flops 163840000 | bytes 9830400 | tf_op jit(solution)/shard_map/pallas_call | solution.py:213
  (12 shorter events, 0.2 us)
Async XLA Ops:
  0.6 26.3 %copy-start.3 = (f32[25,64,128]{2,1,0:T(8,128)S(1)}, f32[25,64,128]{2,1,0:T(8,128)}, u32[]{:S(2)}) copy-start(f32[25,64,128]{2,1,0:T(8,128)} %ns_ref.3) | copy-start | bytes 2457604
  4.2 22.8 %copy-start.2 = (f32[25,64,128]{2,1,0:T(8,128)S(1)}, f32[25,64,128]{2,1,0:T(8,128)}, u32[]{:S(2)}) copy-start(f32[25,64,128]{2,1,0:T(8,128)} %nt_ref.3) | copy-start | bytes 2457604
  5.2 13.5 %collective-permute-start.3 = (f32[2,25,2,128]{3,2,1,0:T(2,128)S(1)}, f32[2,25,2,128]{3,2,1,0:T(2,128)S(1)}, u32[]{:S(2)}, u32[]{:S(2)}) collective-permute-start(f32[2,25,2,128]{3,2,1,0:T(2,128)S(1)} %slice.37), channel_id=1, source_target_pairs={{7,127},{15,119},{23,111},{31,103},{39,95},{47,87},{55,79},{63,71}... | collective-permute-start | bytes 153608 | tf_op jit(solution)/shard_map/ppermute | solution.py:234
  5.9 21.0 %collective-permute-start.1 = (f32[2,25,8,128]{3,2,1,0:T(8,128)}, f32[2,25,8,128]{3,2,1,0:T(8,128)S(1)}, u32[]{:S(2)}, u32[]{:S(2)}) collective-permute-start(f32[2,25,8,128]{3,2,1,0:T(8,128)} %get-tuple-element.11), channel_id=1, source_target_pairs={{0,8},{8,16},{16,24},{24,32},{32,40},{40,48},{48,56},{56,64},{64,7... | collective-permute-start | bytes 614408 | tf_op jit(solution)/shard_map/ppermute | solution.py:229
  5.9 20.9 %collective-permute-start = (f32[2,25,8,128]{3,2,1,0:T(8,128)}, f32[2,25,8,128]{3,2,1,0:T(8,128)S(1)}, u32[]{:S(2)}, u32[]{:S(2)}) collective-permute-start(f32[2,25,8,128]{3,2,1,0:T(8,128)} %get-tuple-element.11), channel_id=1, source_target_pairs={{0,120},{8,0},{16,8},{24,16},{32,24},{40,32},{48,40},{56,48},{64,5... | collective-permute-start | bytes 614408 | tf_op jit(solution)/shard_map/ppermute | solution.py:228
  11.3 15.4 %collective-permute-start.4 = (f32[2,25,8,128]{3,2,1,0:T(8,128)}, f32[2,25,8,128]{3,2,1,0:T(8,128)S(1)}, u32[]{:S(2)}, u32[]{:S(2)}) collective-permute-start(f32[2,25,8,128]{3,2,1,0:T(8,128)} %get-tuple-element.12), channel_id=1, source_target_pairs={{1,0},{2,1},{3,2},{4,3},{5,4},{6,5},{7,6},{9,8},{10,9},{11,10},{12... | collective-permute-start | bytes 614408 | tf_op jit(solution)/shard_map/ppermute | solution.py:230
  16.7 10.0 %collective-permute-start.2 = (f32[2,25,8,128]{3,2,1,0:T(8,128)}, f32[2,25,8,128]{3,2,1,0:T(8,128)S(1)}, u32[]{:S(2)}, u32[]{:S(2)}) collective-permute-start(f32[2,25,8,128]{3,2,1,0:T(8,128)} %get-tuple-element.12), channel_id=1, source_target_pairs={{0,1},{1,2},{2,3},{3,4},{4,5},{5,6},{6,7},{8,9},{9,10},{10,11},{11... | collective-permute-start | bytes 614408 | tf_op jit(solution)/shard_map/ppermute | solution.py:231
  26.8 0.8 %copy-start.4 = (s32[64,128]{1,0:T(8,128)S(1)}, s32[64,128]{1,0:T(8,128)}, u32[]{:S(2)}) copy-start(s32[64,128]{1,0:T(8,128)} %bl_ref.5) | copy-start | bytes 98308
  27.5 30.9 %copy-start.1 = (f32[25,64,128]{2,1,0:T(8,128)S(1)}, f32[25,64,128]{2,1,0:T(8,128)}, u32[]{:S(2)}) copy-start(f32[25,64,128]{2,1,0:T(8,128)} %vn_ref.5) | copy-start | bytes 2457604
  40.2 18.2 %copy-start = (f32[25,64,128]{2,1,0:T(8,128)S(1)}, f32[25,64,128]{2,1,0:T(8,128)}, u32[]{:S(2)}) copy-start(f32[25,64,128]{2,1,0:T(8,128)} %ue_ref.5) | copy-start | bytes 2457604
  40.3 12.1 %collective-permute-start.8 = (f32[2,25,2,128]{3,2,1,0:T(2,128)S(1)}, f32[2,25,2,128]{3,2,1,0:T(2,128)S(1)}, u32[]{:S(2)}, u32[]{:S(2)}) collective-permute-start(f32[2,25,2,128]{3,2,1,0:T(2,128)S(1)} %slice.43), channel_id=1, source_target_pairs={{7,127},{15,119},{23,111},{31,103},{39,95},{47,87},{55,79},{63,71}... | collective-permute-start | bytes 153608 | tf_op jit(solution)/shard_map/ppermute | solution.py:234
  41.1 17.3 %collective-permute-start.6 = (f32[2,25,8,128]{3,2,1,0:T(8,128)S(1)}, f32[2,25,8,128]{3,2,1,0:T(8,128)S(1)}, u32[]{:S(2)}, u32[]{:S(2)}) collective-permute-start(f32[2,25,8,128]{3,2,1,0:T(8,128)S(1)} %get-tuple-element.17), channel_id=1, source_target_pairs={{0,8},{8,16},{16,24},{24,32},{32,40},{40,48},{48,56},{56,64},{64,7... | collective-permute-start | bytes 614408 | tf_op jit(solution)/shard_map/ppermute | solution.py:229
  41.1 17.3 %collective-permute-start.5 = (f32[2,25,8,128]{3,2,1,0:T(8,128)S(1)}, f32[2,25,8,128]{3,2,1,0:T(8,128)S(1)}, u32[]{:S(2)}, u32[]{:S(2)}) collective-permute-start(f32[2,25,8,128]{3,2,1,0:T(8,128)S(1)} %get-tuple-element.17), channel_id=1, source_target_pairs={{0,120},{8,0},{16,8},{24,16},{32,24},{40,32},{48,40},{56,48},{64,5... | collective-permute-start | bytes 614408 | tf_op jit(solution)/shard_map/ppermute | solution.py:228
  46.5 11.7 %collective-permute-start.9 = (f32[2,25,8,128]{3,2,1,0:T(8,128)S(1)}, f32[2,25,8,128]{3,2,1,0:T(8,128)S(1)}, u32[]{:S(2)}, u32[]{:S(2)}) collective-permute-start(f32[2,25,8,128]{3,2,1,0:T(8,128)S(1)} %get-tuple-element.18), channel_id=1, source_target_pairs={{1,0},{2,1},{3,2},{4,3},{5,4},{6,5},{7,6},{9,8},{10,9},{11,10},{12... | collective-permute-start | bytes 614408 | tf_op jit(solution)/shard_map/ppermute | solution.py:230
  48.4 9.8 %collective-permute-start.7 = (f32[2,25,8,128]{3,2,1,0:T(8,128)S(1)}, f32[2,25,8,128]{3,2,1,0:T(8,128)S(1)}, u32[]{:S(2)}, u32[]{:S(2)}) collective-permute-start(f32[2,25,8,128]{3,2,1,0:T(8,128)S(1)} %get-tuple-element.18), channel_id=1, source_target_pairs={{0,1},{1,2},{2,3},{3,4},{4,5},{5,6},{6,7},{8,9},{9,10},{10,11},{11... | collective-permute-start | bytes 614408 | tf_op jit(solution)/shard_map/ppermute | solution.py:231

commit v8 on v7

--- a/solution.py
+++ b/solution.py
@@ -82,13 +82,9 @@
     lax.fori_loop(0, levels, level, 0, unroll=True)
 
 
-def step_kernel(mask_inputs, final, bl_ref, nt_ref, ns_ref, bt_ref, bs_ref, xe_ref, xw_ref, yh_ref,
-                ue_ref, vn_ref, *rest):
-    outs, fv = rest[:-1], rest[-1]
+def mixing_kernel(mask_inputs, bl_ref, nt_ref, ns_ref, bt_ref, bs_ref, fv):
     levels, rows, cols = nt_ref.shape
-    lane = lax.broadcasted_iota(jnp.int32, (rows, cols), 1)
-    row = lax.broadcasted_iota(jnp.int32, (rows, cols), 0)
-    now_refs, bef_refs = (nt_ref, ns_ref), (bt_ref, bs_ref)
+    bef_refs = (bt_ref, bs_ref)
 
     def mask(k):
         return (k < bl_ref[...]).astype(jnp.float32)
@@ -115,6 +111,24 @@
         return carry
 
     lax.fori_loop(0, levels - 1, mixing, 0)
+
+
+def step_kernel(mask_inputs, final, bl_ref, nt_ref, ns_ref, bt_ref, bs_ref, xe_ref, xw_ref, yh_ref,
+                ue_ref, vn_ref, fv, *outs):
+    levels, rows, cols = nt_ref.shape
+    lane = lax.broadcasted_iota(jnp.int32, (rows, cols), 1)
+    row = lax.broadcasted_iota(jnp.int32, (rows, cols), 0)
+    now_refs, bef_refs = (nt_ref, ns_ref), (bt_ref, bs_ref)
+
+    def mask(k):
+        return (k < bl_ref[...]).astype(jnp.float32)
+
+    def depth(k):
+        return level_depth * (k.astype(jnp.float32) + 0.5)
+
+    def load(ref, k, m):
+        v = ref[k]
+        return v * m if mask_inputs else v
 
     strips = rows // 8
     lane8 = lax.broadcasted_iota(jnp.int32, (8, cols), 1)
@@ -206,21 +220,34 @@
     )(bl, nt, ns, ue, vn)
 
 
+def mixing_call(mask_inputs, bl, nt, ns, bt, bs):
+    levels, rows, cols = nt.shape
+    return pl.pallas_call(
+        functools.partial(mixing_kernel, mask_inputs),
+        out_shape=jax.ShapeDtypeStruct((2, levels + 1, rows, cols), jnp.float32),
+        in_specs=[VMEM_SPEC] * 5,
+        out_specs=VMEM_SPEC,
+        cost_estimate=pl.CostEstimate(
+            flops=60 * levels * rows * cols, transcendentals=levels * rows * cols,
+            bytes_accessed=4 * levels * rows * cols * 7),
+    )(bl, nt, ns, bt, bs)
+
+
 def step_call(mask_inputs, final, bl, nt, ns, bt, bs, xe, xw, yh, ue, vn):
     levels, rows, cols = nt.shape
+    fv = mixing_call(mask_inputs, bl, nt, ns, bt, bs)
     field = jax.ShapeDtypeStruct(nt.shape, jnp.float32)
     out_shape = (field,) * 3 if final else (field,) * 4 + pack_shapes(levels, rows, cols)
     return pl.pallas_call(
         functools.partial(step_kernel, mask_inputs, final),
         out_shape=out_shape,
-        in_specs=[VMEM_SPEC] * 10,
+        in_specs=[VMEM_SPEC] * 11,
         out_specs=tuple([VMEM_SPEC] * len(out_shape)),
-        scratch_shapes=[pltpu.VMEM((2, levels + 1, rows, cols), jnp.float32)],
         compiler_params=pltpu.CompilerParams(vmem_limit_bytes=48 * 1024 * 1024),
         cost_estimate=pl.CostEstimate(
-            flops=400 * 2 * levels * rows * cols, transcendentals=levels * rows * cols,
+            flops=300 * 2 * levels * rows * cols, transcendentals=0,
             bytes_accessed=4 * levels * rows * cols * (9 + len(out_shape))),
-    )(bl, nt, ns, bt, bs, xe, xw, yh, ue, vn)
+    )(bl, nt, ns, bt, bs, xe, xw, yh, ue, vn, fv)
 
 
 def exchange(xpack, ypack, at_fold):

time: 69.3 us -> 80.9 us (1.17)
  Pallas kernels: 26.8 us -> 36.1 us
  waiting for transfers between devices: 13.2 us -> 4.49 us
  local copies, waits for them, and re-layouts: 1.99 us -> 10.6 us
  other arithmetic: 0.29 us -> 1.22 us
    pallas_call x0 -> x2, Pallas kernels: none -> 9.47 us  [mixing_call(): pl.pallas_call(functools.partial(mixing_kernel, mask_inputs), out_shape=j...]
    ppermute x2, waiting for transfers between devices: 13.2 us -> 4.47 us  [exchange(): lax.ppermute(ypack, 'lat', [(i, i + 1) for i in range(lat_count - 1)])]
    unnamed x14 -> x32, local copies, waits for them, and re-layouts: 0.75 us -> 6 us
    slice x2, local copies, waits for them, and re-layouts: 1.05 us -> 2.52 us  [exchange(): partner = lax.ppermute(ypack[:, :, 2:4], ('lon', 'lat'), fold_pairs)]
    ppermute x2, starting transfers between devices: 7.28 us -> 8.54 us  [exchange(): lax.ppermute(ypack, 'lat', [(i, i - 1) for i in range(1, lat_count)])]
    ppermute x2, starting transfers between devices: 5.84 us -> 4.58 us  [exchange(): lax.ppermute(ypack, 'lat', [(i, i + 1) for i in range(lat_count - 1)])]
    slice x2, local copies, waits for them, and re-layouts: 0.05 us -> 0.98 us  [exchange(): from_south[:, :, 2:4]]
    slice x2, local copies, waits for them, and re-layouts: 0.05 us -> 0.98 us  [exchange(): from_south[:, :, 4:5]]
  transfers between devices with their start and end apart: 10 -> 10, of which waited for: 2 -> 2; matrix products, arithmetic and copies ran while one was open for 1% -> 6% of each run, Pallas kernels for 0% -> 12%
where the time goes in v8:
time: 80.9 us; the launch traced here: 80.4 us
  Pallas kernels  36.1 us (45%)
  starting transfers between devices  25.8 us (32%)
  local copies, waits for them, and re-layouts  10.6 us (13%)
  waiting for transfers between devices  4.49 us (6%)
  other arithmetic  1.22 us (2%)
  matrix products  1.16 us (1%)
  between operations  0.96 us (1%)
    pallas_call x2, Pallas kernels, step_call(): pl.pallas_call(functools.partial(step_kernel, mask_inputs, final), out_sh...  23.2 us
    ppermute x2, starting transfers between devices, exchange(): lax.ppermute(xpack, 'lon', [(i, (i - 1) % lon_count) for i in range(lon_c...  10.7 us
    pallas_call x2, Pallas kernels, mixing_call(): pl.pallas_call(functools.partial(mixing_kernel, mask_inputs), out_shape=j...  9.47 us
    ppermute x2, starting transfers between devices, exchange(): lax.ppermute(ypack, 'lat', [(i, i - 1) for i in range(1, lat_count)])  8.54 us
    unnamed x32, local copies, waits for them, and re-layouts  6 us
    ppermute x2, starting transfers between devices, exchange(): lax.ppermute(ypack, 'lat', [(i, i + 1) for i in range(lat_count - 1)])  4.58 us
    ppermute x2, waiting for transfers between devices, exchange(): lax.ppermute(ypack, 'lat', [(i, i + 1) for i in range(lat_count - 1)])  4.47 us
    pallas_call x1, Pallas kernels, edge_call(): pl.pallas_call(edge_kernel, out_shape=pack_shapes(levels, rows, cols), in...  3.45 us
  transfers between devices with their start and end apart: 10, of which 2 were waited for; matrix products, arithmetic and copies ran while one was open for 6% of the time, Pallas kernels for 12%

profile of v8, /device:TPU:8, one launch (start us, length us, event | category | flops | bytes accessed | tf_op | source)
XLA Modules:
  0.0 80.4 jit_solution(7769003188315002973)
XLA Ops:
  0.6 3.4 %shard_map.94 = (f32[2,25,8,128]{3,2,1,0:T(8,128)}, f32[2,25,8,128]{3,2,1,0:T(8,128)}) custom-call(s32[64,128]{1,0:T(8,128)} %bl_ref.9, f32[25,64,128]{2,1,0:T(8,128)} %nt_ref.5, f32[25,64,128]{2,1,0:T(8,128)} %ns_ref.5, f32[25,64,128]{2,1,0:T(8,128)} %ue_ref.5, f32[25,64,128]{2,1,0:T(8,128)} %vn_ref.5), custom_call_target="tpu_custom_call" | custom-call | flops 6553600 | bytes 4096000 | tf_op jit(solution)/shard_map/pallas_call | solution.py:212
  4.1 1.0 %slice.37 = f32[2,25,2,128]{3,2,1,0:T(2,128)S(1)} slice(f32[2,25,8,128]{3,2,1,0:T(8,128)} %get-tuple-element.12), slice={[0:2], [0:25], [2:4], [0:128]} | slice | bytes 102400 | tf_op jit(solution)/shard_map/slice | solution.py:261
  5.0 0.7 collective-permute-start.3
  5.7 0.1 collective-permute-start.1
  5.8 5.3 %collective-permute-start = (f32[2,25,8,128]{3,2,1,0:T(8,128)}, f32[2,25,8,128]{3,2,1,0:T(8,128)S(1)}, u32[]{:S(2)}, u32[]{:S(2)}) collective-permute-start(f32[2,25,8,128]{3,2,1,0:T(8,128)} %get-tuple-element.11), channel_id=1, source_target_pairs={{0,120},{8,0},{16,8},{24,16},{32,24},{40,32},{48,40},{56,48},{64,5... | collective-permute-start | bytes 614408 | tf_op jit(solution)/shard_map/ppermute | solution.py:255
  11.1 5.4 %collective-permute-start.4 = (f32[2,25,8,128]{3,2,1,0:T(8,128)}, f32[2,25,8,128]{3,2,1,0:T(8,128)S(1)}, u32[]{:S(2)}, u32[]{:S(2)}) collective-permute-start(f32[2,25,8,128]{3,2,1,0:T(8,128)} %get-tuple-element.12), channel_id=1, source_target_pairs={{1,0},{2,1},{3,2},{4,3},{5,4},{6,5},{7,6},{9,8},{10,9},{11,10},{12... | collective-permute-start | bytes 614408 | tf_op jit(solution)/shard_map/ppermute | solution.py:257
  16.5 1.9 %collective-permute-start.2 = (f32[2,25,8,128]{3,2,1,0:T(8,128)}, f32[2,25,8,128]{3,2,1,0:T(8,128)S(1)}, u32[]{:S(2)}, u32[]{:S(2)}) collective-permute-start(f32[2,25,8,128]{3,2,1,0:T(8,128)} %get-tuple-element.12), channel_id=1, source_target_pairs={{0,1},{1,2},{2,3},{3,4},{4,5},{5,6},{6,7},{8,9},{9,10},{10,11},{11... | collective-permute-start | bytes 614408 | tf_op jit(solution)/shard_map/ppermute | solution.py:258
  18.5 0.1 pad.9.clone
  18.5 4.8 %shard_map.95.fv = f32[2,26,64,128]{3,2,1,0:T(8,128)} custom-call(s32[64,128]{1,0:T(8,128)} %bl_ref.9, f32[25,64,128]{2,1,0:T(8,128)} %nt_ref.5, f32[25,64,128]{2,1,0:T(8,128)} %ns_ref.5, f32[25,64,128]{2,1,0:T(8,128)} %bt_ref.3, f32[25,64,128]{2,1,0:T(8,128)} %bs_ref.3), custom_call_target="tpu_custom_call" | custom-call | flops 12288000 | bytes 5734400 | tf_op jit(solution)/shard_map/pallas_call | solution.py:225
  23.3 0.0 collective-permute-done.3
  23.3 0.2 fusion.2
  23.6 2.9 %collective-permute-done.2 = f32[2,25,8,128]{3,2,1,0:T(8,128)S(1)} collective-permute-done((f32[2,25,8,128]{3,2,1,0:T(8,128)}, f32[2,25,8,128]{3,2,1,0:T(8,128)S(1)}, u32[]{:S(2)}, u32[]{:S(2)}) %collective-permute-start.2) | collective-permute-done | bytes 204832 | tf_op jit(solution)/shard_map/ppermute | solution.py:258
  26.5 0.0 collective-permute-done.4
  26.6 0.1 slice_select_fusion.1
  26.6 0.1 maximum_maximum_fusion.yh_ref
  26.7 0.0 collective-permute-done.1.xw_ref
  26.7 0.0 collective-permute-done.xe_ref
  26.7 0.0 copy-done
  26.8 12.4 %shard_map.96 = (f32[25,64,128]{2,1,0:T(8,128)S(1)}, f32[25,64,128]{2,1,0:T(8,128)S(1)}, f32[25,64,128]{2,1,0:T(8,128)S(1)}, f32[25,64,128]{2,1,0:T(8,128)S(1)},...) custom-call(s32[64,128]{1,0:T(8,128)S(1)} %copy-done.12, f32[25,64,128]{2,1,0:T(8,128)S(1)} %copy-done, ...), custom_call_target="tpu_custom_call" | custom-call | flops 122880000 | bytes 12288000 | tf_op jit(solution)/shard_map/pallas_call | solution.py:241
  39.2 0.9 %copy-done.4 = f32[25,64,128]{2,1,0:T(8,128)} copy-done((f32[25,64,128]{2,1,0:T(8,128)}, f32[25,64,128]{2,1,0:T(8,128)S(1)}, u32[]{:S(2)}) %copy-start.4) | copy-done | bytes 819224
  40.1 0.9 %copy-done.6 = f32[25,64,128]{2,1,0:T(8,128)} copy-done((f32[25,64,128]{2,1,0:T(8,128)}, f32[25,64,128]{2,1,0:T(8,128)S(1)}, u32[]{:S(2)}) %copy-start.6) | copy-done | bytes 819224
  41.0 0.9 %copy-done.8 = f32[25,64,128]{2,1,0:T(8,128)} copy-done((f32[25,64,128]{2,1,0:T(8,128)}, f32[25,64,128]{2,1,0:T(8,128)S(1)}, u32[]{:S(2)}) %copy-start.8) | copy-done | bytes 819224
  41.9 0.9 %copy-done.10 = f32[25,64,128]{2,1,0:T(8,128)} copy-done((f32[25,64,128]{2,1,0:T(8,128)}, f32[25,64,128]{2,1,0:T(8,128)S(1)}, u32[]{:S(2)}) %copy-start.10) | copy-done | bytes 819224
  42.8 1.6 %slice.43 = f32[2,25,2,128]{3,2,1,0:T(2,128)} slice(f32[2,25,8,128]{3,2,1,0:T(8,128)} %get-tuple-element.18), slice={[0:2], [0:25], [2:4], [0:128]} | slice | bytes 102400 | tf_op jit(solution)/shard_map/slice | solution.py:261
  44.3 1.3 %collective-permute-start.8 = (f32[2,25,2,128]{3,2,1,0:T(2,128)}, f32[2,25,2,128]{3,2,1,0:T(2,128)}, u32[]{:S(2)}, u32[]{:S(2)}) collective-permute-start(f32[2,25,2,128]{3,2,1,0:T(2,128)} %slice.43), channel_id=1, source_target_pairs={{7,127},{15,119},{23,111},{31,103},{39,95},{47,87},{55,79},{63,71}... | collective-permute-start | bytes 153608 | tf_op jit(solution)/shard_map/ppermute | solution.py:261
  45.6 0.0 collective-permute-start.6
  45.6 5.4 %collective-permute-start.5 = (f32[2,25,8,128]{3,2,1,0:T(8,128)}, f32[2,25,8,128]{3,2,1,0:T(8,128)}, u32[]{:S(2)}, u32[]{:S(2)}) collective-permute-start(f32[2,25,8,128]{3,2,1,0:T(8,128)} %get-tuple-element.17), channel_id=1, source_target_pairs={{0,120},{8,0},{16,8},{24,16},{32,24},{40,32},{48,40},{56,48},{64,5... | collective-permute-start | bytes 614408 | tf_op jit(solution)/shard_map/ppermute | solution.py:255
  51.0 3.2 %collective-permute-start.9 = (f32[2,25,8,128]{3,2,1,0:T(8,128)}, f32[2,25,8,128]{3,2,1,0:T(8,128)}, u32[]{:S(2)}, u32[]{:S(2)}) collective-permute-start(f32[2,25,8,128]{3,2,1,0:T(8,128)} %get-tuple-element.18), channel_id=1, source_target_pairs={{1,0},{2,1},{3,2},{4,3},{5,4},{6,5},{7,6},{9,8},{10,9},{11,10},{12... | collective-permute-start | bytes 614408 | tf_op jit(solution)/shard_map/ppermute | solution.py:257
  54.1 2.7 %collective-permute-start.7 = (f32[2,25,8,128]{3,2,1,0:T(8,128)}, f32[2,25,8,128]{3,2,1,0:T(8,128)}, u32[]{:S(2)}, u32[]{:S(2)}) collective-permute-start(f32[2,25,8,128]{3,2,1,0:T(8,128)} %get-tuple-element.18), channel_id=1, source_target_pairs={{0,1},{1,2},{2,3},{3,4},{4,5},{5,6},{6,7},{8,9},{9,10},{10,11},{11... | collective-permute-start | bytes 614408 | tf_op jit(solution)/shard_map/ppermute | solution.py:258
  56.8 0.0 copy-start.2
  56.8 0.0 copy-start.3
  56.8 0.0 copy-start.5
  56.9 0.0 copy-start.13
  56.9 4.7 %shard_map.97.fv = f32[2,26,64,128]{3,2,1,0:T(8,128)} custom-call(s32[64,128]{1,0:T(8,128)} %bl_ref.9, f32[25,64,128]{2,1,0:T(8,128)} %copy-done.8, f32[25,64,128]{2,1,0:T(8,128)} %copy-done.10, f32[25,64,128]{2,1,0:T(8,128)} %copy-done.4, f32[25,64,128]{2,1,0:T(8,128)} %copy-done.6), custom_call_target="tpu_custom_call" | custom-call | flops 12288000 | bytes 5734400 | tf_op jit(solution)/shard_map/pallas_call | solution.py:225
  61.5 0.0 collective-permute-done.8
  61.5 1.0 %fusion = f32[2,25,2,128]{3,1,2,0:T(8,128)S(1)} fusion(f32[2,25,2,128]{3,2,1,0:T(2,128)} %collective-permute-done.8), kind=kOutput, calls=%fused_computation.2 | convolution fusion | flops 19693568 | bytes 102400 | tf_op jit(solution)/shard_map/fkrc,cd->fkrd/dot_general | solution.py:264
  62.6 1.6 %collective-permute-done.7 = f32[2,25,8,128]{3,2,1,0:T(8,128)} collective-permute-done((f32[2,25,8,128]{3,2,1,0:T(8,128)}, f32[2,25,8,128]{3,2,1,0:T(8,128)}, u32[]{:S(2)}, u32[]{:S(2)}) %collective-permute-start.7) | collective-permute-done | bytes 204832 | tf_op jit(solution)/shard_map/ppermute | solution.py:258
  64.2 1.0 %slice.57 = f32[2,25,1,128]{3,2,1,0:T(1,128)S(1)} slice(f32[2,25,8,128]{3,2,1,0:T(8,128)} %collective-permute-done.7), slice={[0:2], [0:25], [4:5], [0:128]} | slice | bytes 51200 | tf_op jit(solution)/shard_map/slice | solution.py:270
  65.2 1.0 %slice.53 = f32[2,25,2,128]{3,2,1,0:T(2,128)S(1)} slice(f32[2,25,8,128]{3,2,1,0:T(8,128)} %collective-permute-done.7), slice={[0:2], [0:25], [2:4], [0:128]} | slice | bytes 102400 | tf_op jit(solution)/shard_map/slice | solution.py:269
  66.1 0.0 collective-permute-done.9
  66.1 1.0 %slice_select_fusion = f32[2,25,2,128]{3,2,1,0:T(2,128)S(1)} fusion(f32[2,25,8,128]{3,2,1,0:T(8,128)} %collective-permute-done.9, f32[2,25,1,128]{3,2,1,0:T(1,128)S(1)} %copy.20, f32[2,25,1,128]{3,2,1,0:T(1,128)S(1)} %copy.19, pred[]{:T(512)S(6)} %eq.9), kind=kLoop, calls=%fused_computation.8 | loop fusion | flops 25600 | bytes 153601 | tf_op jit(solution)/shard_map/jit(_where)/select_n | solution.py:266
  67.1 0.1 maximum_maximum_fusion.1.yh_ref
  67.2 0.0 collective-permute-done.6.xw_ref
  67.2 0.0 collective-permute-done.5.xe_ref
  67.3 0.0 copy-start.9
  67.3 1.1 %copy-done.9 = f32[25,64,128]{2,1,0:T(8,128)S(1)} copy-done((f32[25,64,128]{2,1,0:T(8,128)S(1)}, f32[25,64,128]{2,1,0:T(8,128)}, u32[]{:S(2)}) %copy-start.9) | copy-done | bytes 819224
  68.4 1.1 %copy-done.11 = f32[25,64,128]{2,1,0:T(8,128)S(1)} copy-done((f32[25,64,128]{2,1,0:T(8,128)S(1)}, f32[25,64,128]{2,1,0:T(8,128)}, u32[]{:S(2)}) %copy-start.11) | copy-done | bytes 819224
  69.6 10.8 %shard_map.98 = (f32[25,64,128]{2,1,0:T(8,128)}, f32[25,64,128]{2,1,0:T(8,128)}, f32[25,64,128]{2,1,0:T(8,128)}) custom-call(s32[64,128]{1,0:T(8,128)S(1)} %copy-done.13, f32[25,64,128]{2,1,0:T(8,128)S(1)} %copy-done.9, f32[25,64,128]{2,1,0:T(8,128)S(1)} %copy-done.11, f32[25,64,128]{2,1,0:T(8,128)S(1)} %copy-done.5, f32[25,64,128]{2,1,0:T(8,128)S(1)} %copy-done.7, ...), custom_call_target="tpu_custom_call" | custom-call | flops 122880000 | bytes 9830400 | tf_op jit(solution)/shard_map/pallas_call | solution.py:241
  (25 shorter events, 0.2 us)
Async XLA Ops:
  5.0 18.3 %collective-permute-start.3 = (f32[2,25,2,128]{3,2,1,0:T(2,128)S(1)}, f32[2,25,2,128]{3,2,1,0:T(2,128)S(1)}, u32[]{:S(2)}, u32[]{:S(2)}) collective-permute-start(f32[2,25,2,128]{3,2,1,0:T(2,128)S(1)} %slice.37), channel_id=1, source_target_pairs={{7,127},{15,119},{23,111},{31,103},{39,95},{47,87},{55,79},{63,71}... | collective-permute-start | bytes 153608 | tf_op jit(solution)/shard_map/ppermute | solution.py:261
  5.7 21.0 %collective-permute-start.1 = (f32[2,25,8,128]{3,2,1,0:T(8,128)}, f32[2,25,8,128]{3,2,1,0:T(8,128)S(1)}, u32[]{:S(2)}, u32[]{:S(2)}) collective-permute-start(f32[2,25,8,128]{3,2,1,0:T(8,128)} %get-tuple-element.11), channel_id=1, source_target_pairs={{0,8},{8,16},{16,24},{24,32},{32,40},{40,48},{48,56},{56,64},{64,7... | collective-permute-start | bytes 614408 | tf_op jit(solution)/shard_map/ppermute | solution.py:256
  5.8 20.9 %collective-permute-start = (f32[2,25,8,128]{3,2,1,0:T(8,128)}, f32[2,25,8,128]{3,2,1,0:T(8,128)S(1)}, u32[]{:S(2)}, u32[]{:S(2)}) collective-permute-start(f32[2,25,8,128]{3,2,1,0:T(8,128)} %get-tuple-element.11), channel_id=1, source_target_pairs={{0,120},{8,0},{16,8},{24,16},{32,24},{40,32},{48,40},{56,48},{64,5... | collective-permute-start | bytes 614408 | tf_op jit(solution)/shard_map/ppermute | solution.py:255
  11.1 15.4 %collective-permute-start.4 = (f32[2,25,8,128]{3,2,1,0:T(8,128)}, f32[2,25,8,128]{3,2,1,0:T(8,128)S(1)}, u32[]{:S(2)}, u32[]{:S(2)}) collective-permute-start(f32[2,25,8,128]{3,2,1,0:T(8,128)} %get-tuple-element.12), channel_id=1, source_target_pairs={{1,0},{2,1},{3,2},{4,3},{5,4},{6,5},{7,6},{9,8},{10,9},{11,10},{12... | collective-permute-start | bytes 614408 | tf_op jit(solution)/shard_map/ppermute | solution.py:257
  16.5 10.0 %collective-permute-start.2 = (f32[2,25,8,128]{3,2,1,0:T(8,128)}, f32[2,25,8,128]{3,2,1,0:T(8,128)S(1)}, u32[]{:S(2)}, u32[]{:S(2)}) collective-permute-start(f32[2,25,8,128]{3,2,1,0:T(8,128)} %get-tuple-element.12), channel_id=1, source_target_pairs={{0,1},{1,2},{2,3},{3,4},{4,5},{5,6},{6,7},{8,9},{9,10},{10,11},{11... | collective-permute-start | bytes 614408 | tf_op jit(solution)/shard_map/ppermute | solution.py:258
  18.5 8.2 %copy-start = (f32[25,64,128]{2,1,0:T(8,128)S(1)}, f32[25,64,128]{2,1,0:T(8,128)}, u32[]{:S(2)}) copy-start(f32[25,64,128]{2,1,0:T(8,128)} %nt_ref.5) | copy-start | bytes 2457604
  18.5 8.2 %copy-start.1 = (f32[25,64,128]{2,1,0:T(8,128)S(1)}, f32[25,64,128]{2,1,0:T(8,128)}, u32[]{:S(2)}) copy-start(f32[25,64,128]{2,1,0:T(8,128)} %ns_ref.5) | copy-start | bytes 2457604
  18.5 8.2 %copy-start.12 = (s32[64,128]{1,0:T(8,128)S(1)}, s32[64,128]{1,0:T(8,128)}, u32[]{:S(2)}) copy-start(s32[64,128]{1,0:T(8,128)} %bl_ref.9) | copy-start | bytes 98308
  39.2 0.9 %copy-start.4 = (f32[25,64,128]{2,1,0:T(8,128)}, f32[25,64,128]{2,1,0:T(8,128)S(1)}, u32[]{:S(2)}) copy-start(f32[25,64,128]{2,1,0:T(8,128)S(1)} %get-tuple-element.15.bt_ref) | copy-start | bytes 2457604
  40.1 0.9 %copy-start.6 = (f32[25,64,128]{2,1,0:T(8,128)}, f32[25,64,128]{2,1,0:T(8,128)S(1)}, u32[]{:S(2)}) copy-start(f32[25,64,128]{2,1,0:T(8,128)S(1)} %get-tuple-element.16.bs_ref) | copy-start | bytes 2457604
  41.0 0.9 %copy-start.8 = (f32[25,64,128]{2,1,0:T(8,128)}, f32[25,64,128]{2,1,0:T(8,128)S(1)}, u32[]{:S(2)}) copy-start(f32[25,64,128]{2,1,0:T(8,128)S(1)} %get-tuple-element.13.nt_ref) | copy-start | bytes 2457604
  41.9 0.9 %copy-start.10 = (f32[25,64,128]{2,1,0:T(8,128)}, f32[25,64,128]{2,1,0:T(8,128)S(1)}, u32[]{:S(2)}) copy-start(f32[25,64,128]{2,1,0:T(8,128)S(1)} %get-tuple-element.14.ns_ref) | copy-start | bytes 2457604
  44.3 17.2 %collective-permute-start.8 = (f32[2,25,2,128]{3,2,1,0:T(2,128)}, f32[2,25,2,128]{3,2,1,0:T(2,128)}, u32[]{:S(2)}, u32[]{:S(2)}) collective-permute-start(f32[2,25,2,128]{3,2,1,0:T(2,128)} %slice.43), channel_id=1, source_target_pairs={{7,127},{15,119},{23,111},{31,103},{39,95},{47,87},{55,79},{63,71}... | collective-permute-start | bytes 153608 | tf_op jit(solution)/shard_map/ppermute | solution.py:261
  45.6 21.6 %collective-permute-start.6 = (f32[2,25,8,128]{3,2,1,0:T(8,128)}, f32[2,25,8,128]{3,2,1,0:T(8,128)S(1)}, u32[]{:S(2)}, u32[]{:S(2)}) collective-permute-start(f32[2,25,8,128]{3,2,1,0:T(8,128)} %get-tuple-element.17), channel_id=1, source_target_pairs={{0,8},{8,16},{16,24},{24,32},{32,40},{40,48},{48,56},{56,64},{64,7... | collective-permute-start | bytes 614408 | tf_op jit(solution)/shard_map/ppermute | solution.py:256
  45.6 21.6 %collective-permute-start.5 = (f32[2,25,8,128]{3,2,1,0:T(8,128)}, f32[2,25,8,128]{3,2,1,0:T(8,128)}, u32[]{:S(2)}, u32[]{:S(2)}) collective-permute-start(f32[2,25,8,128]{3,2,1,0:T(8,128)} %get-tuple-element.17), channel_id=1, source_target_pairs={{0,120},{8,0},{16,8},{24,16},{32,24},{40,32},{48,40},{56,48},{64,5... | collective-permute-start | bytes 614408 | tf_op jit(solution)/shard_map/ppermute | solution.py:255
  51.0 15.2 %collective-permute-start.9 = (f32[2,25,8,128]{3,2,1,0:T(8,128)}, f32[2,25,8,128]{3,2,1,0:T(8,128)}, u32[]{:S(2)}, u32[]{:S(2)}) collective-permute-start(f32[2,25,8,128]{3,2,1,0:T(8,128)} %get-tuple-element.18), channel_id=1, source_target_pairs={{1,0},{2,1},{3,2},{4,3},{5,4},{6,5},{7,6},{9,8},{10,9},{11,10},{12... | collective-permute-start | bytes 614408 | tf_op jit(solution)/shard_map/ppermute | solution.py:257
  54.1 10.1 %collective-permute-start.7 = (f32[2,25,8,128]{3,2,1,0:T(8,128)}, f32[2,25,8,128]{3,2,1,0:T(8,128)}, u32[]{:S(2)}, u32[]{:S(2)}) collective-permute-start(f32[2,25,8,128]{3,2,1,0:T(8,128)} %get-tuple-element.18), channel_id=1, source_target_pairs={{0,1},{1,2},{2,3},{3,4},{4,5},{5,6},{6,7},{8,9},{9,10},{10,11},{11... | collective-permute-start | bytes 614408 | tf_op jit(solution)/shard_map/ppermute | solution.py:258
  56.8 10.4 %copy-start.2 = (f32[25,64,128]{2,1,0:T(8,128)S(1)}, f32[25,64,128]{2,1,0:T(8,128)}, u32[]{:S(2)}) copy-start(f32[25,64,128]{2,1,0:T(8,128)} %ue_ref.5) | copy-start | bytes 2457604
  56.8 10.4 %copy-start.3 = (f32[25,64,128]{2,1,0:T(8,128)S(1)}, f32[25,64,128]{2,1,0:T(8,128)}, u32[]{:S(2)}) copy-start(f32[25,64,128]{2,1,0:T(8,128)} %vn_ref.5) | copy-start | bytes 2457604
  56.8 10.4 %copy-start.5 = (f32[25,64,128]{2,1,0:T(8,128)S(1)}, f32[25,64,128]{2,1,0:T(8,128)}, u32[]{:S(2)}) copy-start(f32[25,64,128]{2,1,0:T(8,128)} %copy-done.4) | copy-start | bytes 2457604
  56.8 10.4 %copy-start.7 = (f32[25,64,128]{2,1,0:T(8,128)S(1)}, f32[25,64,128]{2,1,0:T(8,128)}, u32[]{:S(2)}) copy-start(f32[25,64,128]{2,1,0:T(8,128)} %copy-done.6) | copy-start | bytes 2457604
  56.9 10.4 %copy-start.13 = (s32[64,128]{1,0:T(8,128)S(1)}, s32[64,128]{1,0:T(8,128)}, u32[]{:S(2)}) copy-start(s32[64,128]{1,0:T(8,128)} %bl_ref.9) | copy-start | bytes 98308
  67.3 1.1 %copy-start.9 = (f32[25,64,128]{2,1,0:T(8,128)S(1)}, f32[25,64,128]{2,1,0:T(8,128)}, u32[]{:S(2)}) copy-start(f32[25,64,128]{2,1,0:T(8,128)} %copy-done.8) | copy-start | bytes 2457604
  68.4 1.1 %copy-start.11 = (f32[25,64,128]{2,1,0:T(8,128)S(1)}, f32[25,64,128]{2,1,0:T(8,128)}, u32[]{:S(2)}) copy-start(f32[25,64,128]{2,1,0:T(8,128)} %copy-done.10) | copy-start | bytes 2457604

commit v9 on v7

--- a/solution.py
+++ b/solution.py
@@ -35,15 +35,18 @@
     return value if shift == 0 else pltpu.roll(value, shift, 1)
 
 
-def column_pack(value, east_v):
-    rows, cols = value.shape
+def column_pack(values, east_v):
+    rows, cols = values[0].shape
     lane = lax.broadcasted_iota(jnp.int32, (8, cols), 1)
     pack = jnp.zeros((8, cols), jnp.float32)
+    for f, value in enumerate(values):
+        for a in range(rows // 8):
+            part = lane_roll(value[8 * a:8 * a + 8], 4 * a + 32 * f)
+            hi_lane = 4 * a + 32 * f
+            lo_lane = (hi_lane - 2) % cols
+            pack = jnp.where((lane >= hi_lane) & (lane < hi_lane + 2), part, pack)
+            pack = jnp.where((lane >= lo_lane) & (lane < lo_lane + 2), part, pack)
     for a in range(rows // 8):
-        part = lane_roll(value[8 * a:8 * a + 8], 4 * a)
-        lo_lane = (4 * a - 2) % cols
-        pack = jnp.where((lane >= 4 * a) & (lane < 4 * a + 2), part, pack)
-        pack = jnp.where((lane >= lo_lane) & (lane < lo_lane + 2), part, pack)
         pack = jnp.where(lane == 64 + 4 * a, lane_roll(east_v[8 * a:8 * a + 8], 4 * a + 65), pack)
     return pack
 
@@ -60,23 +63,24 @@
     return value if shift == 0 else pltpu.roll(value, shift, 0)
 
 
-def write_rows(value, north_v, ypack_ref, f, k):
-    rows, cols = value.shape
-    ypack_ref[f, k, 0:2, :] = value[0:2]
-    ypack_ref[f, k, 2:4, :] = value[rows - 2:rows]
-    ypack_ref[f, k, 4:5, :] = north_v[rows - 1:rows]
-    ypack_ref[f, k, 5:8, :] = jnp.zeros((3, cols), jnp.float32)
-
-
-def edge_kernel(bl_ref, nt_ref, ns_ref, ue_ref, vn_ref, xpack_ref, ypack_ref):
+def write_rows(values, north_v, north_ref, south_ref, k):
+    rows, cols = values[0].shape
+    for f, value in enumerate(values):
+        north_ref[k, 2 * f:2 * f + 2, :] = value[rows - 2:rows]
+        south_ref[k, 2 * f:2 * f + 2, :] = value[0:2]
+    north_ref[k, 4:5, :] = north_v[rows - 1:rows]
+    north_ref[k, 5:8, :] = jnp.zeros((3, cols), jnp.float32)
+    south_ref[k, 4:8, :] = jnp.zeros((4, cols), jnp.float32)
+
+
+def edge_kernel(bl_ref, nt_ref, ns_ref, ue_ref, vn_ref, xpack_ref, north_ref, south_ref):
     levels, rows, cols = nt_ref.shape
 
     def level(k, carry):
         m = (k < bl_ref[...]).astype(jnp.float32)
-        for f, ref in enumerate((nt_ref, ns_ref)):
-            value = ref[k] * m
-            xpack_ref[f, k] = column_pack(value, ue_ref[k])
-            write_rows(value, vn_ref[k], ypack_ref, f, k)
+        values = (nt_ref[k] * m, ns_ref[k] * m)
+        xpack_ref[k] = column_pack(values, ue_ref[k])
+        write_rows(values, vn_ref[k], north_ref, south_ref, k)
         return carry
 
     lax.fori_loop(0, levels, level, 0, unroll=True)
@@ -127,17 +131,18 @@
         m = split(mask(k))
         ue, vn = split(ue_ref[k]), split(vn_ref[k])
         south_v = jnp.where(sub8 == 7, jnp.broadcast_to(yh_ref[0, k][4:5], (8, cols)), 0.0)
+        east_all, west_all = xe_ref[k], xw_ref[k]
+        west_v = lane_roll(west_all, -64)
         depth_k = depth(k)
         afters = [[None] * strips for _ in range(2)]
         for f in range(2):
             q = split(load(now_refs[f], k, mask(k)))
             b = split(load(bef_refs[f], k, mask(k)))
-            from_west = xw_ref[f, k]
-            both, hs = column_unpack(xe_ref[f, k], from_west, False)
+            both, hs = column_unpack(lane_roll(east_all, -32 * f), lane_roll(west_all, -32 * f), False)
             own = jnp.zeros((8, cols), jnp.float32)
             for a in range(strips):
                 own = jnp.where((lane8 >= 4 * a) & (lane8 < 4 * a + 2), lane_roll(q[a], 4 * a), own)
-            west_face = face_flux(lane_roll(from_west, -64), lane_roll(both, 2), lane_roll(both, 1),
+            west_face = face_flux(west_v, lane_roll(both, 2), lane_roll(both, 1),
                                   own, lane_roll(own, -1))
             yh = yh_ref[f, k]
             below = jnp.where(sub8 == 6, jnp.broadcast_to(yh[0:1], (8, cols)),
@@ -173,10 +178,10 @@
                     outs[2 + f][k, rs, :] = after
                 else:
                     outs[f][k, rs, :] = after
-            if not final:
-                whole = jnp.concatenate(afters[f], 0)
-                outs[4][f, k] = column_pack(whole, ue_ref[k])
-                write_rows(whole, vn_ref[k], outs[5], f, k)
+        if not final:
+            wholes = [jnp.concatenate(afters[f], 0) for f in range(2)]
+            outs[4][k] = column_pack(wholes, ue_ref[k])
+            write_rows(wholes, vn_ref[k], outs[5], outs[6], k)
         if final:
             for a in range(strips):
                 outs[2][k, pl.ds(8 * a, 8), :] = density_at(afters[0][a], afters[1][a], depth_k) * m[a]
@@ -189,8 +194,7 @@
 
 
 def pack_shapes(levels, rows, cols):
-    return (jax.ShapeDtypeStruct((2, levels, 8, cols), jnp.float32),
-            jax.ShapeDtypeStruct((2, levels, 8, cols), jnp.float32))
+    return (jax.ShapeDtypeStruct((levels, 8, cols), jnp.float32),) * 3
 
 
 def edge_call(bl, nt, ns, ue, vn):
@@ -199,7 +203,7 @@
         edge_kernel,
         out_shape=pack_shapes(levels, rows, cols),
         in_specs=[VMEM_SPEC] * 5,
-        out_specs=(VMEM_SPEC, VMEM_SPEC),
+        out_specs=(VMEM_SPEC,) * 3,
         cost_estimate=pl.CostEstimate(
             flops=2 * 2 * levels * 8 * rows * cols, transcendentals=0,
             bytes_accessed=4 * levels * rows * cols * 5),
@@ -223,37 +227,39 @@
     )(bl, nt, ns, bt, bs, xe, xw, yh, ue, vn)
 
 
-def exchange(xpack, ypack, at_fold):
+def exchange(xpack, north_pack, south_pack, at_fold):
     lon_count, lat_count = (lax.axis_size("lon"), lax.axis_size("lat"))
     from_east = lax.ppermute(xpack, "lon", [(i, (i - 1) % lon_count) for i in range(lon_count)])
     from_west = lax.ppermute(xpack, "lon", [(i, (i + 1) % lon_count) for i in range(lon_count)])
-    from_north = lax.ppermute(ypack, "lat", [(i, i - 1) for i in range(1, lat_count)])
-    from_south = lax.ppermute(ypack, "lat", [(i, i + 1) for i in range(lat_count - 1)])
+    from_north = lax.ppermute(south_pack, "lat", [(i, i - 1) for i in range(1, lat_count)])
+    from_south = lax.ppermute(north_pack, "lat", [(i, i + 1) for i in range(lat_count - 1)])
     top = lat_count - 1
     fold_pairs = [(d * lat_count + top, (lon_count - 1 - d) * lat_count + top) for d in range(lon_count)]
-    partner = lax.ppermute(ypack[:, :, 2:4], ("lon", "lat"), fold_pairs)
-    cols = ypack.shape[-1]
+    partner = lax.ppermute(north_pack[:, 0:4], ("lon", "lat"), fold_pairs)
+    cols = xpack.shape[-1]
     flip = (jnp.arange(cols)[:, None] + jnp.arange(cols)[None, :] == cols - 1).astype(jnp.float32)
-    flipped = jnp.einsum("fkrc,cd->fkrd", partner, flip, precision=lax.Precision.HIGHEST)
-    mirror = jnp.concatenate([flipped[:, :, 1:2], flipped[:, :, 0:1]], 2)
-    north = jnp.where(at_fold, mirror, from_north[:, :, 0:2])
-    two, levels = xpack.shape[:2]
-    halo_y = jnp.concatenate(
-        [from_south[:, :, 2:4], north,
-         from_south[:, :, 4:5], jnp.zeros((two, levels, 3, cols), jnp.float32)], 2)
-    return from_east, from_west, halo_y
+    flipped = jnp.einsum("krc,cd->krd", partner, flip, precision=lax.Precision.HIGHEST)
+    levels = xpack.shape[0]
+    halo_y = []
+    for f in range(2):
+        mirror = jnp.concatenate([flipped[:, 2 * f + 1:2 * f + 2], flipped[:, 2 * f:2 * f + 1]], 1)
+        north = jnp.where(at_fold, mirror, from_north[:, 2 * f:2 * f + 2])
+        halo_y.append(jnp.concatenate(
+            [from_south[:, 2 * f:2 * f + 2], north, from_south[:, 4:5],
+             jnp.zeros((levels, 3, cols), jnp.float32)], 1))
+    return from_east, from_west, jnp.stack(halo_y)
 
 
 def on_device(
     temp_before, temp_now, salt_before, salt_now, east_velocity, north_velocity, bottom_level
 ):
     at_fold = lax.axis_index("lat") == lax.axis_size("lat") - 1
-    xpack, ypack = edge_call(bottom_level, temp_now, salt_now, east_velocity, north_velocity)
-    from_east, from_west, halo_y = exchange(xpack, ypack, at_fold)
-    ft, fs, at, as_, xpack, ypack = step_call(
+    packs = edge_call(bottom_level, temp_now, salt_now, east_velocity, north_velocity)
+    from_east, from_west, halo_y = exchange(*packs, at_fold)
+    ft, fs, at, as_, *packs = step_call(
         True, False, bottom_level, temp_now, salt_now, temp_before, salt_before,
         from_east, from_west, halo_y, east_velocity, north_velocity)
-    from_east, from_west, halo_y = exchange(xpack, ypack, at_fold)
+    from_east, from_west, halo_y = exchange(*packs, at_fold)
     return step_call(False, True, bottom_level, at, as_, ft, fs, from_east, from_west, halo_y,
                      east_velocity, north_velocity)
 

time: 69.3 us -> 69.7 us (level)
  waiting for transfers between devices: 13.2 us -> 6.4 us
  starting transfers between devices: 25.4 us -> 30.8 us
  Pallas kernels: 26.8 us -> 28 us
    ppermute x6, waiting for transfers between devices: 13.2 us -> 6.38 us  [the longest x2 5.86 us: exchange(): lax.ppermute(south_pack, 'lat', [(i, i - 1) for i in range(1, lat_count)])]
    ppermute x6, starting transfers between devices: 14.6 us -> 20 us  [the longest x2 12.1 us: exchange(): lax.ppermute(north_pack, 'lat', [(i, i + 1) for i in range(lat_count - 1)])]
    pallas_call x2, Pallas kernels: 23.2 us -> 24.7 us  [step_call(): pl.pallas_call(functools.partial(step_kernel, mask_inputs, final), out_sh...]
  transfers between devices with their start and end apart: 10 -> 10, of which waited for: 2 -> 3; matrix products, arithmetic and copies ran while one was open for 1% -> 1% of each run, Pallas kernels for 0% -> 0%
where the time goes in v9:
time: 69.7 us; the launch traced here: 68.9 us
  starting transfers between devices  30.8 us (44%)
  Pallas kernels  28 us (40%)
  waiting for transfers between devices  6.4 us (9%)
  local copies, waits for them, and re-layouts  1.96 us (3%)
  between operations  0.96 us (1%)
    pallas_call x2, Pallas kernels, step_call(): pl.pallas_call(functools.partial(step_kernel, mask_inputs, final), out_sh...  24.7 us
    ppermute x2, starting transfers between devices, exchange(): lax.ppermute(north_pack, 'lat', [(i, i + 1) for i in range(lat_count - 1)])  12.1 us
    ppermute x2, starting transfers between devices, exchange(): lax.ppermute(xpack, 'lon', [(i, (i - 1) % lon_count) for i in range(lon_c...  10.7 us
    ppermute x2, starting transfers between devices, exchange(): lax.ppermute(south_pack, 'lat', [(i, i - 1) for i in range(1, lat_count)])  6.47 us
    ppermute x2, waiting for transfers between devices, exchange(): lax.ppermute(south_pack, 'lat', [(i, i - 1) for i in range(1, lat_count)])  5.86 us
    pallas_call x1, Pallas kernels, edge_call(): pl.pallas_call(edge_kernel, out_shape=pack_shapes(levels, rows, cols), in...  3.3 us
    ppermute x2, starting transfers between devices, exchange(): partner = lax.ppermute(north_pack[:, 0:4], ('lon', 'lat'), fold_pairs)  1.45 us
  transfers between devices with their start and end apart: 10, of which 3 were waited for; matrix products, arithmetic and copies ran while one was open for 1% of the time, Pallas kernels for 0%

profile of v9, /device:TPU:8, one launch (start us, length us, event | category | flops | bytes accessed | tf_op | source)
XLA Modules:
  0.0 68.9 jit_solution(2119103658876428014)
XLA Ops:
  0.6 0.0 copy-start.3
  0.6 3.3 %shard_map.94 = (f32[25,8,128]{2,1,0:T(8,128)}, f32[25,8,128]{2,1,0:T(8,128)}, f32[25,8,128]{2,1,0:T(8,128)}) custom-call(s32[64,128]{1,0:T(8,128)} %bl_ref.5, f32[25,64,128]{2,1,0:T(8,128)} %nt_ref.3, f32[25,64,128]{2,1,0:T(8,128)} %ns_ref.3, f32[25,64,128]{2,1,0:T(8,128)} %ue_ref.5, f32[25,64,128]{2,1,0:T(8,128)} %vn_ref.5), custom_call_target="tpu_custom_call" | custom-call | flops 6553600 | bytes 4096000 | tf_op jit(solution)/shard_map/pallas_call | solution.py:202
  3.9 0.0 copy-start.2
  3.9 1.0 %slice.63 = f32[25,4,128]{2,1,0:T(4,128)S(1)} slice(f32[25,8,128]{2,1,0:T(8,128)} %get-tuple-element.14), slice={[0:25], [0:4], [0:128]} | slice | bytes 102400 | tf_op jit(solution)/shard_map/slice | solution.py:238
  4.9 0.7 collective-permute-start.3
  5.6 0.1 collective-permute-start.1
  5.7 5.3 %collective-permute-start = (f32[25,8,128]{2,1,0:T(8,128)}, f32[25,8,128]{2,1,0:T(8,128)S(1)}, u32[]{:S(2)}, u32[]{:S(2)}) collective-permute-start(f32[25,8,128]{2,1,0:T(8,128)} %get-tuple-element.13), channel_id=1, source_target_pairs={{0,120},{8,0},{16,8},{24,16},{32,24},{40,32},{48,40},{56,48},{64,5... | collective-permute-start | bytes 307208 | tf_op jit(solution)/shard_map/ppermute | solution.py:232
  11.0 3.4 %collective-permute-start.2 = (f32[25,8,128]{2,1,0:T(8,128)}, f32[25,8,128]{2,1,0:T(8,128)S(1)}, u32[]{:S(2)}, u32[]{:S(2)}) collective-permute-start(f32[25,8,128]{2,1,0:T(8,128)} %get-tuple-element.14), channel_id=1, source_target_pairs={{0,1},{1,2},{2,3},{3,4},{4,5},{5,6},{6,7},{8,9},{9,10},{10,11},{11... | collective-permute-start | bytes 307208 | tf_op jit(solution)/shard_map/ppermute | solution.py:235
  14.4 4.6 %collective-permute-start.4 = (f32[25,8,128]{2,1,0:T(8,128)}, f32[25,8,128]{2,1,0:T(8,128)S(1)}, u32[]{:S(2)}, u32[]{:S(2)}) collective-permute-start(f32[25,8,128]{2,1,0:T(8,128)} %get-tuple-element.15), channel_id=1, source_target_pairs={{1,0},{2,1},{3,2},{4,3},{5,4},{6,5},{7,6},{9,8},{10,9},{11,10},{12... | collective-permute-start | bytes 307208 | tf_op jit(solution)/shard_map/ppermute | solution.py:234
  19.0 0.1 pad.25.clone
  19.1 0.0 collective-permute-done.3
  19.1 0.2 fusion.10
  19.4 0.5 collective-permute-done.2
  19.9 1.6 %collective-permute-done.4 = f32[25,8,128]{2,1,0:T(8,128)S(1)} collective-permute-done((f32[25,8,128]{2,1,0:T(8,128)}, f32[25,8,128]{2,1,0:T(8,128)S(1)}, u32[]{:S(2)}, u32[]{:S(2)}) %collective-permute-start.4) | collective-permute-done | bytes 102432 | tf_op jit(solution)/shard_map/ppermute | solution.py:234
  21.5 0.1 slice_select_fusion.3
  21.6 0.1 fusion.5
  21.7 0.0 copy-start.4
  21.7 0.0 collective-permute-done.1.xw_ref
  21.7 0.0 collective-permute-done.xe_ref
  21.7 0.0 copy-done.3
  21.7 0.0 copy-done.2
  21.7 0.7 copy-done.4
  22.4 0.0 copy-start.1
  22.4 13.2 %shard_map.95 = (f32[25,64,128]{2,1,0:T(8,128)S(1)}, f32[25,64,128]{2,1,0:T(8,128)S(1)}, f32[25,64,128]{2,1,0:T(8,128)S(1)}, f32[25,64,128]{2,1,0:T(8,128)S(1)},...) custom-call(s32[64,128]{1,0:T(8,128)S(1)} %copy-done.4, ...), custom_call_target="tpu_custom_call" | custom-call | flops 163840000 | bytes 13107200 | tf_op jit(solution)/shard_map/pallas_call | solution.py:217
  35.6 0.0 copy-start
  35.7 0.8 %collective-permute-start.8 = (f32[25,4,128]{2,1,0:T(4,128)S(1)}, f32[25,4,128]{2,1,0:T(4,128)S(1)}, u32[]{:S(2)}, u32[]{:S(2)}) collective-permute-start(f32[25,4,128]{2,1,0:T(4,128)S(1)} %slice.73), channel_id=1, source_target_pairs={{7,127},{15,119},{23,111},{31,103},{39,95},{47,87},{55,79},{63,71}... | collective-permute-start | bytes 153608 | tf_op jit(solution)/shard_map/ppermute | solution.py:238
  36.5 0.1 collective-permute-start.6
  36.6 5.3 %collective-permute-start.5 = (f32[25,8,128]{2,1,0:T(8,128)S(1)}, f32[25,8,128]{2,1,0:T(8,128)S(1)}, u32[]{:S(2)}, u32[]{:S(2)}) collective-permute-start(f32[25,8,128]{2,1,0:T(8,128)S(1)} %get-tuple-element.20), channel_id=1, source_target_pairs={{0,120},{8,0},{16,8},{24,16},{32,24},{40,32},{48,40},{56,48},{64,5... | collective-permute-start | bytes 307208 | tf_op jit(solution)/shard_map/ppermute | solution.py:232
  41.9 8.7 %collective-permute-start.7 = (f32[25,8,128]{2,1,0:T(8,128)S(1)}, f32[25,8,128]{2,1,0:T(8,128)S(1)}, u32[]{:S(2)}, u32[]{:S(2)}) collective-permute-start(f32[25,8,128]{2,1,0:T(8,128)S(1)} %get-tuple-element.21), channel_id=1, source_target_pairs={{0,1},{1,2},{2,3},{3,4},{4,5},{5,6},{6,7},{8,9},{9,10},{10,11},{11... | collective-permute-start | bytes 307208 | tf_op jit(solution)/shard_map/ppermute | solution.py:235
  50.6 1.9 %collective-permute-start.9 = (f32[25,8,128]{2,1,0:T(8,128)S(1)}, f32[25,8,128]{2,1,0:T(8,128)S(1)}, u32[]{:S(2)}, u32[]{:S(2)}) collective-permute-start(f32[25,8,128]{2,1,0:T(8,128)S(1)} %get-tuple-element.22), channel_id=1, source_target_pairs={{1,0},{2,1},{3,2},{4,3},{5,4},{6,5},{7,6},{9,8},{10,9},{11,10},{12... | collective-permute-start | bytes 307208 | tf_op jit(solution)/shard_map/ppermute | solution.py:234
  52.5 0.0 collective-permute-done.8
  52.5 0.2 fusion.8
  52.8 0.0 collective-permute-done.7
  52.9 4.3 %collective-permute-done.9 = f32[25,8,128]{2,1,0:T(8,128)S(1)} collective-permute-done((f32[25,8,128]{2,1,0:T(8,128)S(1)}, f32[25,8,128]{2,1,0:T(8,128)S(1)}, u32[]{:S(2)}, u32[]{:S(2)}) %collective-permute-start.9) | collective-permute-done | bytes 102432 | tf_op jit(solution)/shard_map/ppermute | solution.py:234
  57.1 0.1 slice_select_fusion.1
  57.2 0.1 fusion.1
  57.3 0.0 collective-permute-done.6.xw_ref
  57.3 0.0 collective-permute-done.5.xe_ref
  57.3 0.0 copy-done.1
  57.4 0.0 copy-done
  57.4 11.5 %shard_map.96 = (f32[25,64,128]{2,1,0:T(8,128)}, f32[25,64,128]{2,1,0:T(8,128)}, f32[25,64,128]{2,1,0:T(8,128)}) custom-call(s32[64,128]{1,0:T(8,128)S(1)} %copy-done.4, f32[25,64,128]{2,1,0:T(8,128)S(1)} %get-tuple-element.16.nt_ref, f32[25,64,128]{2,1,0:T(8,128)S(1)} %get-tuple-element.17.ns_ref, f32[25,64,128]{2,1,0:T(8,128)S(1)} %get-tuple-element.18.bt_ref, ...), custom_call_target="tpu_custom_call" | custom-call | flops 163840000 | bytes 9830400 | tf_op jit(solution)/shard_map/pallas_call | solution.py:217
  (18 shorter events, 0.3 us)
Async XLA Ops:
  0.6 21.1 %copy-start.3 = (f32[25,64,128]{2,1,0:T(8,128)S(1)}, f32[25,64,128]{2,1,0:T(8,128)}, u32[]{:S(2)}) copy-start(f32[25,64,128]{2,1,0:T(8,128)} %ns_ref.3) | copy-start | bytes 2457604
  3.9 17.8 %copy-start.2 = (f32[25,64,128]{2,1,0:T(8,128)S(1)}, f32[25,64,128]{2,1,0:T(8,128)}, u32[]{:S(2)}) copy-start(f32[25,64,128]{2,1,0:T(8,128)} %nt_ref.3) | copy-start | bytes 2457604
  4.9 14.1 %collective-permute-start.3 = (f32[25,4,128]{2,1,0:T(4,128)S(1)}, f32[25,4,128]{2,1,0:T(4,128)S(1)}, u32[]{:S(2)}, u32[]{:S(2)}) collective-permute-start(f32[25,4,128]{2,1,0:T(4,128)S(1)} %slice.63), channel_id=1, source_target_pairs={{7,127},{15,119},{23,111},{31,103},{39,95},{47,87},{55,79},{63,71}... | collective-permute-start | bytes 153608 | tf_op jit(solution)/shard_map/ppermute | solution.py:238
  5.6 16.1 %collective-permute-start.1 = (f32[25,8,128]{2,1,0:T(8,128)}, f32[25,8,128]{2,1,0:T(8,128)S(1)}, u32[]{:S(2)}, u32[]{:S(2)}) collective-permute-start(f32[25,8,128]{2,1,0:T(8,128)} %get-tuple-element.13), channel_id=1, source_target_pairs={{0,8},{8,16},{16,24},{24,32},{32,40},{40,48},{48,56},{56,64},{64,7... | collective-permute-start | bytes 307208 | tf_op jit(solution)/shard_map/ppermute | solution.py:233
  5.7 16.0 %collective-permute-start = (f32[25,8,128]{2,1,0:T(8,128)}, f32[25,8,128]{2,1,0:T(8,128)S(1)}, u32[]{:S(2)}, u32[]{:S(2)}) collective-permute-start(f32[25,8,128]{2,1,0:T(8,128)} %get-tuple-element.13), channel_id=1, source_target_pairs={{0,120},{8,0},{16,8},{24,16},{32,24},{40,32},{48,40},{56,48},{64,5... | collective-permute-start | bytes 307208 | tf_op jit(solution)/shard_map/ppermute | solution.py:232
  11.0 8.9 %collective-permute-start.2 = (f32[25,8,128]{2,1,0:T(8,128)}, f32[25,8,128]{2,1,0:T(8,128)S(1)}, u32[]{:S(2)}, u32[]{:S(2)}) collective-permute-start(f32[25,8,128]{2,1,0:T(8,128)} %get-tuple-element.14), channel_id=1, source_target_pairs={{0,1},{1,2},{2,3},{3,4},{4,5},{5,6},{6,7},{8,9},{9,10},{10,11},{11... | collective-permute-start | bytes 307208 | tf_op jit(solution)/shard_map/ppermute | solution.py:235
  14.4 7.1 %collective-permute-start.4 = (f32[25,8,128]{2,1,0:T(8,128)}, f32[25,8,128]{2,1,0:T(8,128)S(1)}, u32[]{:S(2)}, u32[]{:S(2)}) collective-permute-start(f32[25,8,128]{2,1,0:T(8,128)} %get-tuple-element.15), channel_id=1, source_target_pairs={{1,0},{2,1},{3,2},{4,3},{5,4},{6,5},{7,6},{9,8},{10,9},{11,10},{12... | collective-permute-start | bytes 307208 | tf_op jit(solution)/shard_map/ppermute | solution.py:234
  21.7 0.8 %copy-start.4 = (s32[64,128]{1,0:T(8,128)S(1)}, s32[64,128]{1,0:T(8,128)}, u32[]{:S(2)}) copy-start(s32[64,128]{1,0:T(8,128)} %bl_ref.5) | copy-start | bytes 98308
  22.4 34.9 %copy-start.1 = (f32[25,64,128]{2,1,0:T(8,128)S(1)}, f32[25,64,128]{2,1,0:T(8,128)}, u32[]{:S(2)}) copy-start(f32[25,64,128]{2,1,0:T(8,128)} %vn_ref.5) | copy-start | bytes 2457604
  35.6 21.7 %copy-start = (f32[25,64,128]{2,1,0:T(8,128)S(1)}, f32[25,64,128]{2,1,0:T(8,128)}, u32[]{:S(2)}) copy-start(f32[25,64,128]{2,1,0:T(8,128)} %ue_ref.5) | copy-start | bytes 2457604
  35.7 16.9 %collective-permute-start.8 = (f32[25,4,128]{2,1,0:T(4,128)S(1)}, f32[25,4,128]{2,1,0:T(4,128)S(1)}, u32[]{:S(2)}, u32[]{:S(2)}) collective-permute-start(f32[25,4,128]{2,1,0:T(4,128)S(1)} %slice.73), channel_id=1, source_target_pairs={{7,127},{15,119},{23,111},{31,103},{39,95},{47,87},{55,79},{63,71}... | collective-permute-start | bytes 153608 | tf_op jit(solution)/shard_map/ppermute | solution.py:238
  36.5 20.9 %collective-permute-start.6 = (f32[25,8,128]{2,1,0:T(8,128)S(1)}, f32[25,8,128]{2,1,0:T(8,128)S(1)}, u32[]{:S(2)}, u32[]{:S(2)}) collective-permute-start(f32[25,8,128]{2,1,0:T(8,128)S(1)} %get-tuple-element.20), channel_id=1, source_target_pairs={{0,8},{8,16},{16,24},{24,32},{32,40},{40,48},{48,56},{56,64},{64,7... | collective-permute-start | bytes 307208 | tf_op jit(solution)/shard_map/ppermute | solution.py:233
  36.6 20.8 %collective-permute-start.5 = (f32[25,8,128]{2,1,0:T(8,128)S(1)}, f32[25,8,128]{2,1,0:T(8,128)S(1)}, u32[]{:S(2)}, u32[]{:S(2)}) collective-permute-start(f32[25,8,128]{2,1,0:T(8,128)S(1)} %get-tuple-element.20), channel_id=1, source_target_pairs={{0,120},{8,0},{16,8},{24,16},{32,24},{40,32},{48,40},{56,48},{64,5... | collective-permute-start | bytes 307208 | tf_op jit(solution)/shard_map/ppermute | solution.py:232
  41.9 10.9 %collective-permute-start.7 = (f32[25,8,128]{2,1,0:T(8,128)S(1)}, f32[25,8,128]{2,1,0:T(8,128)S(1)}, u32[]{:S(2)}, u32[]{:S(2)}) collective-permute-start(f32[25,8,128]{2,1,0:T(8,128)S(1)} %get-tuple-element.21), channel_id=1, source_target_pairs={{0,1},{1,2},{2,3},{3,4},{4,5},{5,6},{6,7},{8,9},{9,10},{10,11},{11... | collective-permute-start | bytes 307208 | tf_op jit(solution)/shard_map/ppermute | solution.py:235
  50.6 6.6 %collective-permute-start.9 = (f32[25,8,128]{2,1,0:T(8,128)S(1)}, f32[25,8,128]{2,1,0:T(8,128)S(1)}, u32[]{:S(2)}, u32[]{:S(2)}) collective-permute-start(f32[25,8,128]{2,1,0:T(8,128)S(1)} %get-tuple-element.22), channel_id=1, source_target_pairs={{1,0},{2,1},{3,2},{4,3},{5,4},{6,5},{7,6},{9,8},{10,9},{11,10},{12... | collective-permute-start | bytes 307208 | tf_op jit(solution)/shard_map/ppermute | solution.py:234

commit v10 on v7

--- a/solution.py
+++ b/solution.py
@@ -182,7 +182,7 @@
                 outs[2][k, pl.ds(8 * a, 8), :] = density_at(afters[0][a], afters[1][a], depth_k) * m[a]
         return carry
 
-    lax.fori_loop(0, levels, level, 0)
+    lax.fori_loop(0, levels, level, 0, unroll=2)
 
 
 VMEM_SPEC = pl.BlockSpec(memory_space=pltpu.VMEM)

time: 69.3 us -> 67 us (0.967)
  Pallas kernels: 26.8 us -> 24.4 us
    pallas_call x2, Pallas kernels: 23.2 us -> 20.9 us  [step_call(): pl.pallas_call(functools.partial(step_kernel, mask_inputs, final), out_sh...]
where the time goes in v10:
time: 67 us; the launch traced here: 66.7 us
  starting transfers between devices  25.4 us (38%)
  Pallas kernels  24.4 us (36%)
  waiting for transfers between devices  13.2 us (20%)
  local copies, waits for them, and re-layouts  1.99 us (3%)
  between operations  0.94 us (1%)
    pallas_call x2, Pallas kernels, step_call(): pl.pallas_call(functools.partial(step_kernel, mask_inputs, final), out_sh...  20.9 us
    ppermute x2, waiting for transfers between devices, exchange(): lax.ppermute(ypack, 'lat', [(i, i + 1) for i in range(lat_count - 1)])  13.2 us
    ppermute x2, starting transfers between devices, exchange(): lax.ppermute(xpack, 'lon', [(i, (i - 1) % lon_count) for i in range(lon_c...  10.7 us
    ppermute x2, starting transfers between devices, exchange(): lax.ppermute(ypack, 'lat', [(i, i - 1) for i in range(1, lat_count)])  7.28 us
    ppermute x2, starting transfers between devices, exchange(): lax.ppermute(ypack, 'lat', [(i, i + 1) for i in range(lat_count - 1)])  5.84 us
    pallas_call x1, Pallas kernels, edge_call(): pl.pallas_call(edge_kernel, out_shape=pack_shapes(levels, rows, cols), in...  3.52 us
    ppermute x2, starting transfers between devices, exchange(): partner = lax.ppermute(ypack[:, :, 2:4], ('lon', 'lat'), fold_pairs)  1.46 us
  transfers between devices with their start and end apart: 10, of which 2 were waited for; matrix products, arithmetic and copies ran while one was open for 1% of the time, Pallas kernels for 0%

profile of v10, /device:TPU:8, one launch (start us, length us, event | category | flops | bytes accessed | tf_op | source)
XLA Modules:
  0.0 66.7 jit_solution(7341789176556644891)
XLA Ops:
  0.6 0.0 copy-start.3
  0.6 3.5 %shard_map.94 = (f32[2,25,8,128]{3,2,1,0:T(8,128)}, f32[2,25,8,128]{3,2,1,0:T(8,128)}) custom-call(s32[64,128]{1,0:T(8,128)} %bl_ref.5, f32[25,64,128]{2,1,0:T(8,128)} %nt_ref.3, f32[25,64,128]{2,1,0:T(8,128)} %ns_ref.3, f32[25,64,128]{2,1,0:T(8,128)} %ue_ref.5, f32[25,64,128]{2,1,0:T(8,128)} %vn_ref.5), custom_call_target="tpu_custom_call" | custom-call | flops 6553600 | bytes 4096000 | tf_op jit(solution)/shard_map/pallas_call | solution.py:198
  4.2 0.0 copy-start.2
  4.2 1.0 %slice.37 = f32[2,25,2,128]{3,2,1,0:T(2,128)S(1)} slice(f32[2,25,8,128]{3,2,1,0:T(8,128)} %get-tuple-element.12), slice={[0:2], [0:25], [2:4], [0:128]} | slice | bytes 102400 | tf_op jit(solution)/shard_map/slice | solution.py:234
  5.2 0.7 collective-permute-start.3
  5.9 0.1 collective-permute-start.1
  5.9 5.3 %collective-permute-start = (f32[2,25,8,128]{3,2,1,0:T(8,128)}, f32[2,25,8,128]{3,2,1,0:T(8,128)S(1)}, u32[]{:S(2)}, u32[]{:S(2)}) collective-permute-start(f32[2,25,8,128]{3,2,1,0:T(8,128)} %get-tuple-element.11), channel_id=1, source_target_pairs={{0,120},{8,0},{16,8},{24,16},{32,24},{40,32},{48,40},{56,48},{64,5... | collective-permute-start | bytes 614408 | tf_op jit(solution)/shard_map/ppermute | solution.py:228
  11.3 5.4 %collective-permute-start.4 = (f32[2,25,8,128]{3,2,1,0:T(8,128)}, f32[2,25,8,128]{3,2,1,0:T(8,128)S(1)}, u32[]{:S(2)}, u32[]{:S(2)}) collective-permute-start(f32[2,25,8,128]{3,2,1,0:T(8,128)} %get-tuple-element.12), channel_id=1, source_target_pairs={{1,0},{2,1},{3,2},{4,3},{5,4},{6,5},{7,6},{9,8},{10,9},{11,10},{12... | collective-permute-start | bytes 614408 | tf_op jit(solution)/shard_map/ppermute | solution.py:230
  16.7 1.9 %collective-permute-start.2 = (f32[2,25,8,128]{3,2,1,0:T(8,128)}, f32[2,25,8,128]{3,2,1,0:T(8,128)S(1)}, u32[]{:S(2)}, u32[]{:S(2)}) collective-permute-start(f32[2,25,8,128]{3,2,1,0:T(8,128)} %get-tuple-element.12), channel_id=1, source_target_pairs={{0,1},{1,2},{2,3},{3,4},{4,5},{5,6},{6,7},{8,9},{9,10},{10,11},{11... | collective-permute-start | bytes 614408 | tf_op jit(solution)/shard_map/ppermute | solution.py:231
  18.6 0.1 pad.9.clone
  18.7 0.0 collective-permute-done.3
  18.7 0.2 fusion.2
  19.0 7.7 %collective-permute-done.2 = f32[2,25,8,128]{3,2,1,0:T(8,128)S(1)} collective-permute-done((f32[2,25,8,128]{3,2,1,0:T(8,128)}, f32[2,25,8,128]{3,2,1,0:T(8,128)S(1)}, u32[]{:S(2)}, u32[]{:S(2)}) %collective-permute-start.2) | collective-permute-done | bytes 204832 | tf_op jit(solution)/shard_map/ppermute | solution.py:231
  26.7 0.0 collective-permute-done.4
  26.7 0.1 slice_select_fusion.1
  26.8 0.0 copy-start.4
  26.8 0.1 maximum_maximum_fusion.yh_ref
  26.9 0.0 collective-permute-done.1.xw_ref
  26.9 0.0 collective-permute-done.xe_ref
  26.9 0.0 copy-done.3
  26.9 0.0 copy-done.2
  26.9 0.6 copy-done.4
  27.5 0.0 copy-start.1
  27.5 12.0 %shard_map.95 = (f32[25,64,128]{2,1,0:T(8,128)S(1)}, f32[25,64,128]{2,1,0:T(8,128)S(1)}, f32[25,64,128]{2,1,0:T(8,128)S(1)}, f32[25,64,128]{2,1,0:T(8,128)S(1)},...) custom-call(s32[64,128]{1,0:T(8,128)S(1)} %copy-done.4, f32[25,64,128]{2,1,0:T(8,128)S(1)} %copy-done.2, ...), custom_call_target="tpu_custom_call" | custom-call | flops 163840000 | bytes 12288000 | tf_op jit(solution)/shard_map/pallas_call | solution.py:213
  39.6 0.0 copy-start
  39.6 0.8 %collective-permute-start.8 = (f32[2,25,2,128]{3,2,1,0:T(2,128)S(1)}, f32[2,25,2,128]{3,2,1,0:T(2,128)S(1)}, u32[]{:S(2)}, u32[]{:S(2)}) collective-permute-start(f32[2,25,2,128]{3,2,1,0:T(2,128)S(1)} %slice.43), channel_id=1, source_target_pairs={{7,127},{15,119},{23,111},{31,103},{39,95},{47,87},{55,79},{63,71}... | collective-permute-start | bytes 153608 | tf_op jit(solution)/shard_map/ppermute | solution.py:234
  40.4 0.1 collective-permute-start.6
  40.5 5.3 %collective-permute-start.5 = (f32[2,25,8,128]{3,2,1,0:T(8,128)S(1)}, f32[2,25,8,128]{3,2,1,0:T(8,128)S(1)}, u32[]{:S(2)}, u32[]{:S(2)}) collective-permute-start(f32[2,25,8,128]{3,2,1,0:T(8,128)S(1)} %get-tuple-element.17), channel_id=1, source_target_pairs={{0,120},{8,0},{16,8},{24,16},{32,24},{40,32},{48,40},{56,48},{64,5... | collective-permute-start | bytes 614408 | tf_op jit(solution)/shard_map/ppermute | solution.py:228
  45.9 1.9 %collective-permute-start.9 = (f32[2,25,8,128]{3,2,1,0:T(8,128)S(1)}, f32[2,25,8,128]{3,2,1,0:T(8,128)S(1)}, u32[]{:S(2)}, u32[]{:S(2)}) collective-permute-start(f32[2,25,8,128]{3,2,1,0:T(8,128)S(1)} %get-tuple-element.18), channel_id=1, source_target_pairs={{1,0},{2,1},{3,2},{4,3},{5,4},{6,5},{7,6},{9,8},{10,9},{11,10},{12... | collective-permute-start | bytes 614408 | tf_op jit(solution)/shard_map/ppermute | solution.py:230
  47.8 3.9 %collective-permute-start.7 = (f32[2,25,8,128]{3,2,1,0:T(8,128)S(1)}, f32[2,25,8,128]{3,2,1,0:T(8,128)S(1)}, u32[]{:S(2)}, u32[]{:S(2)}) collective-permute-start(f32[2,25,8,128]{3,2,1,0:T(8,128)S(1)} %get-tuple-element.18), channel_id=1, source_target_pairs={{0,1},{1,2},{2,3},{3,4},{4,5},{5,6},{6,7},{8,9},{9,10},{10,11},{11... | collective-permute-start | bytes 614408 | tf_op jit(solution)/shard_map/ppermute | solution.py:231
  51.7 0.0 collective-permute-done.8
  51.7 0.2 fusion
  52.0 5.5 %collective-permute-done.7 = f32[2,25,8,128]{3,2,1,0:T(8,128)S(1)} collective-permute-done((f32[2,25,8,128]{3,2,1,0:T(8,128)S(1)}, f32[2,25,8,128]{3,2,1,0:T(8,128)S(1)}, u32[]{:S(2)}, u32[]{:S(2)}) %collective-permute-start.7) | collective-permute-done | bytes 204832 | tf_op jit(solution)/shard_map/ppermute | solution.py:231
  57.6 0.0 collective-permute-done.9
  57.6 0.1 slice_select_fusion
  57.7 0.1 maximum_maximum_fusion.1.yh_ref
  57.8 0.0 collective-permute-done.6.xw_ref
  57.8 0.0 collective-permute-done.5.xe_ref
  57.8 0.0 copy-done.1
  57.8 0.0 copy-done
  57.8 8.9 %shard_map.96 = (f32[25,64,128]{2,1,0:T(8,128)}, f32[25,64,128]{2,1,0:T(8,128)}, f32[25,64,128]{2,1,0:T(8,128)}) custom-call(s32[64,128]{1,0:T(8,128)S(1)} %copy-done.4, f32[25,64,128]{2,1,0:T(8,128)S(1)} %get-tuple-element.13.nt_ref, f32[25,64,128]{2,1,0:T(8,128)S(1)} %get-tuple-element.14.ns_ref, f32[25,64,128]{2,1,0:T(8,128)S(1)} %get-tuple-element.15.bt_ref, ...), custom_call_target="tpu_custom_call" | custom-call | flops 163840000 | bytes 9830400 | tf_op jit(solution)/shard_map/pallas_call | solution.py:213
  (12 shorter events, 0.2 us)
Async XLA Ops:
  0.6 26.3 %copy-start.3 = (f32[25,64,128]{2,1,0:T(8,128)S(1)}, f32[25,64,128]{2,1,0:T(8,128)}, u32[]{:S(2)}) copy-start(f32[25,64,128]{2,1,0:T(8,128)} %ns_ref.3) | copy-start | bytes 2457604
  4.2 22.8 %copy-start.2 = (f32[25,64,128]{2,1,0:T(8,128)S(1)}, f32[25,64,128]{2,1,0:T(8,128)}, u32[]{:S(2)}) copy-start(f32[25,64,128]{2,1,0:T(8,128)} %nt_ref.3) | copy-start | bytes 2457604
  5.2 13.5 %collective-permute-start.3 = (f32[2,25,2,128]{3,2,1,0:T(2,128)S(1)}, f32[2,25,2,128]{3,2,1,0:T(2,128)S(1)}, u32[]{:S(2)}, u32[]{:S(2)}) collective-permute-start(f32[2,25,2,128]{3,2,1,0:T(2,128)S(1)} %slice.37), channel_id=1, source_target_pairs={{7,127},{15,119},{23,111},{31,103},{39,95},{47,87},{55,79},{63,71}... | collective-permute-start | bytes 153608 | tf_op jit(solution)/shard_map/ppermute | solution.py:234
  5.9 21.0 %collective-permute-start.1 = (f32[2,25,8,128]{3,2,1,0:T(8,128)}, f32[2,25,8,128]{3,2,1,0:T(8,128)S(1)}, u32[]{:S(2)}, u32[]{:S(2)}) collective-permute-start(f32[2,25,8,128]{3,2,1,0:T(8,128)} %get-tuple-element.11), channel_id=1, source_target_pairs={{0,8},{8,16},{16,24},{24,32},{32,40},{40,48},{48,56},{56,64},{64,7... | collective-permute-start | bytes 614408 | tf_op jit(solution)/shard_map/ppermute | solution.py:229
  5.9 20.9 %collective-permute-start = (f32[2,25,8,128]{3,2,1,0:T(8,128)}, f32[2,25,8,128]{3,2,1,0:T(8,128)S(1)}, u32[]{:S(2)}, u32[]{:S(2)}) collective-permute-start(f32[2,25,8,128]{3,2,1,0:T(8,128)} %get-tuple-element.11), channel_id=1, source_target_pairs={{0,120},{8,0},{16,8},{24,16},{32,24},{40,32},{48,40},{56,48},{64,5... | collective-permute-start | bytes 614408 | tf_op jit(solution)/shard_map/ppermute | solution.py:228
  11.3 15.4 %collective-permute-start.4 = (f32[2,25,8,128]{3,2,1,0:T(8,128)}, f32[2,25,8,128]{3,2,1,0:T(8,128)S(1)}, u32[]{:S(2)}, u32[]{:S(2)}) collective-permute-start(f32[2,25,8,128]{3,2,1,0:T(8,128)} %get-tuple-element.12), channel_id=1, source_target_pairs={{1,0},{2,1},{3,2},{4,3},{5,4},{6,5},{7,6},{9,8},{10,9},{11,10},{12... | collective-permute-start | bytes 614408 | tf_op jit(solution)/shard_map/ppermute | solution.py:230
  16.7 10.0 %collective-permute-start.2 = (f32[2,25,8,128]{3,2,1,0:T(8,128)}, f32[2,25,8,128]{3,2,1,0:T(8,128)S(1)}, u32[]{:S(2)}, u32[]{:S(2)}) collective-permute-start(f32[2,25,8,128]{3,2,1,0:T(8,128)} %get-tuple-element.12), channel_id=1, source_target_pairs={{0,1},{1,2},{2,3},{3,4},{4,5},{5,6},{6,7},{8,9},{9,10},{10,11},{11... | collective-permute-start | bytes 614408 | tf_op jit(solution)/shard_map/ppermute | solution.py:231
  26.8 0.8 %copy-start.4 = (s32[64,128]{1,0:T(8,128)S(1)}, s32[64,128]{1,0:T(8,128)}, u32[]{:S(2)}) copy-start(s32[64,128]{1,0:T(8,128)} %bl_ref.5) | copy-start | bytes 98308
  27.5 30.2 %copy-start.1 = (f32[25,64,128]{2,1,0:T(8,128)S(1)}, f32[25,64,128]{2,1,0:T(8,128)}, u32[]{:S(2)}) copy-start(f32[25,64,128]{2,1,0:T(8,128)} %vn_ref.5) | copy-start | bytes 2457604
  39.6 18.2 %copy-start = (f32[25,64,128]{2,1,0:T(8,128)S(1)}, f32[25,64,128]{2,1,0:T(8,128)}, u32[]{:S(2)}) copy-start(f32[25,64,128]{2,1,0:T(8,128)} %ue_ref.5) | copy-start | bytes 2457604
  39.6 12.1 %collective-permute-start.8 = (f32[2,25,2,128]{3,2,1,0:T(2,128)S(1)}, f32[2,25,2,128]{3,2,1,0:T(2,128)S(1)}, u32[]{:S(2)}, u32[]{:S(2)}) collective-permute-start(f32[2,25,2,128]{3,2,1,0:T(2,128)S(1)} %slice.43), channel_id=1, source_target_pairs={{7,127},{15,119},{23,111},{31,103},{39,95},{47,87},{55,79},{63,71}... | collective-permute-start | bytes 153608 | tf_op jit(solution)/shard_map/ppermute | solution.py:234
  40.4 17.3 %collective-permute-start.6 = (f32[2,25,8,128]{3,2,1,0:T(8,128)S(1)}, f32[2,25,8,128]{3,2,1,0:T(8,128)S(1)}, u32[]{:S(2)}, u32[]{:S(2)}) collective-permute-start(f32[2,25,8,128]{3,2,1,0:T(8,128)S(1)} %get-tuple-element.17), channel_id=1, source_target_pairs={{0,8},{8,16},{16,24},{24,32},{32,40},{40,48},{48,56},{56,64},{64,7... | collective-permute-start | bytes 614408 | tf_op jit(solution)/shard_map/ppermute | solution.py:229
  40.5 17.3 %collective-permute-start.5 = (f32[2,25,8,128]{3,2,1,0:T(8,128)S(1)}, f32[2,25,8,128]{3,2,1,0:T(8,128)S(1)}, u32[]{:S(2)}, u32[]{:S(2)}) collective-permute-start(f32[2,25,8,128]{3,2,1,0:T(8,128)S(1)} %get-tuple-element.17), channel_id=1, source_target_pairs={{0,120},{8,0},{16,8},{24,16},{32,24},{40,32},{48,40},{56,48},{64,5... | collective-permute-start | bytes 614408 | tf_op jit(solution)/shard_map/ppermute | solution.py:228
  45.9 11.7 %collective-permute-start.9 = (f32[2,25,8,128]{3,2,1,0:T(8,128)S(1)}, f32[2,25,8,128]{3,2,1,0:T(8,128)S(1)}, u32[]{:S(2)}, u32[]{:S(2)}) collective-permute-start(f32[2,25,8,128]{3,2,1,0:T(8,128)S(1)} %get-tuple-element.18), channel_id=1, source_target_pairs={{1,0},{2,1},{3,2},{4,3},{5,4},{6,5},{7,6},{9,8},{10,9},{11,10},{12... | collective-permute-start | bytes 614408 | tf_op jit(solution)/shard_map/ppermute | solution.py:230
  47.8 9.8 %collective-permute-start.7 = (f32[2,25,8,128]{3,2,1,0:T(8,128)S(1)}, f32[2,25,8,128]{3,2,1,0:T(8,128)S(1)}, u32[]{:S(2)}, u32[]{:S(2)}) collective-permute-start(f32[2,25,8,128]{3,2,1,0:T(8,128)S(1)} %get-tuple-element.18), channel_id=1, source_target_pairs={{0,1},{1,2},{2,3},{3,4},{4,5},{5,6},{6,7},{8,9},{9,10},{10,11},{11... | collective-permute-start | bytes 614408 | tf_op jit(solution)/shard_map/ppermute | solution.py:231

commit v11 on v10

--- a/solution.py
+++ b/solution.py
@@ -123,13 +123,13 @@
     def split(value):
         return [value[8 * a:8 * a + 8] for a in range(strips)]
 
-    def level(k, carry):
+    def level(k, carry, fields=(0, 1)):
         m = split(mask(k))
         ue, vn = split(ue_ref[k]), split(vn_ref[k])
         south_v = jnp.where(sub8 == 7, jnp.broadcast_to(yh_ref[0, k][4:5], (8, cols)), 0.0)
         depth_k = depth(k)
         afters = [[None] * strips for _ in range(2)]
-        for f in range(2):
+        for f in fields:
             q = split(load(now_refs[f], k, mask(k)))
             b = split(load(bef_refs[f], k, mask(k)))
             from_west = xw_ref[f, k]
@@ -182,7 +182,11 @@
                 outs[2][k, pl.ds(8 * a, 8), :] = density_at(afters[0][a], afters[1][a], depth_k) * m[a]
         return carry
 
-    lax.fori_loop(0, levels, level, 0, unroll=2)
+    if final:
+        lax.fori_loop(0, levels, level, 0, unroll=2)
+    else:
+        for f in range(2):
+            lax.fori_loop(0, levels, functools.partial(level, fields=(f,)), 0, unroll=3)
 
 
 VMEM_SPEC = pl.BlockSpec(memory_space=pltpu.VMEM)

time: 67 us -> 65.8 us (0.982)
  Pallas kernels: 24.4 us -> 23.2 us
    pallas_call x2, Pallas kernels: 20.9 us -> 19.7 us  [step_call(): pl.pallas_call(functools.partial(step_kernel, mask_inputs, final), out_sh...]
where the time goes in v11:
time: 65.8 us; the launch traced here: 65.4 us
  starting transfers between devices  25.4 us (39%)
  Pallas kernels  23.2 us (35%)
  waiting for transfers between devices  13.2 us (20%)
  local copies, waits for them, and re-layouts  1.99 us (3%)
  between operations  0.94 us (1%)
    pallas_call x2, Pallas kernels, step_call(): pl.pallas_call(functools.partial(step_kernel, mask_inputs, final), out_sh...  19.7 us
    ppermute x2, waiting for transfers between devices, exchange(): lax.ppermute(ypack, 'lat', [(i, i + 1) for i in range(lat_count - 1)])  13.2 us
    ppermute x2, starting transfers between devices, exchange(): lax.ppermute(xpack, 'lon', [(i, (i - 1) % lon_count) for i in range(lon_c...  10.7 us
    ppermute x2, starting transfers between devices, exchange(): lax.ppermute(ypack, 'lat', [(i, i - 1) for i in range(1, lat_count)])  7.28 us
    ppermute x2, starting transfers between devices, exchange(): lax.ppermute(ypack, 'lat', [(i, i + 1) for i in range(lat_count - 1)])  5.84 us
    pallas_call x1, Pallas kernels, edge_call(): pl.pallas_call(edge_kernel, out_shape=pack_shapes(levels, rows, cols), in...  3.52 us
    ppermute x2, starting transfers between devices, exchange(): partner = lax.ppermute(ypack[:, :, 2:4], ('lon', 'lat'), fold_pairs)  1.46 us
  transfers between devices with their start and end apart: 10, of which 2 were waited for; matrix products, arithmetic and copies ran while one was open for 1% of the time, Pallas kernels for 0%

profile of v11, /device:TPU:8, one launch (start us, length us, event | category | flops | bytes accessed | tf_op | source)
XLA Modules:
  0.0 65.4 jit_solution(15502601853494541411)
XLA Ops:
  0.6 0.0 copy-start.3
  0.6 3.5 %shard_map.94 = (f32[2,25,8,128]{3,2,1,0:T(8,128)}, f32[2,25,8,128]{3,2,1,0:T(8,128)}) custom-call(s32[64,128]{1,0:T(8,128)} %bl_ref.5, f32[25,64,128]{2,1,0:T(8,128)} %nt_ref.3, f32[25,64,128]{2,1,0:T(8,128)} %ns_ref.3, f32[25,64,128]{2,1,0:T(8,128)} %ue_ref.5, f32[25,64,128]{2,1,0:T(8,128)} %vn_ref.5), custom_call_target="tpu_custom_call" | custom-call | flops 6553600 | bytes 4096000 | tf_op jit(solution)/shard_map/pallas_call | solution.py:202
  4.2 0.0 copy-start.2
  4.2 1.0 %slice.37 = f32[2,25,2,128]{3,2,1,0:T(2,128)S(1)} slice(f32[2,25,8,128]{3,2,1,0:T(8,128)} %get-tuple-element.12), slice={[0:2], [0:25], [2:4], [0:128]} | slice | bytes 102400 | tf_op jit(solution)/shard_map/slice | solution.py:238
  5.2 0.7 %collective-permute-start.3 = (f32[2,25,2,128]{3,2,1,0:T(2,128)S(1)}, f32[2,25,2,128]{3,2,1,0:T(2,128)S(1)}, u32[]{:S(2)}, u32[]{:S(2)}) collective-permute-start(f32[2,25,2,128]{3,2,1,0:T(2,128)S(1)} %slice.37), channel_id=1, source_target_pairs={{7,127},{15,119},{23,111},{31,103},{39,95},{47,87},{55,79},{63,71}... | collective-permute-start | bytes 153608 | tf_op jit(solution)/shard_map/ppermute | solution.py:238
  5.9 0.1 collective-permute-start.1
  5.9 5.3 %collective-permute-start = (f32[2,25,8,128]{3,2,1,0:T(8,128)}, f32[2,25,8,128]{3,2,1,0:T(8,128)S(1)}, u32[]{:S(2)}, u32[]{:S(2)}) collective-permute-start(f32[2,25,8,128]{3,2,1,0:T(8,128)} %get-tuple-element.11), channel_id=1, source_target_pairs={{0,120},{8,0},{16,8},{24,16},{32,24},{40,32},{48,40},{56,48},{64,5... | collective-permute-start | bytes 614408 | tf_op jit(solution)/shard_map/ppermute | solution.py:232
  11.3 5.4 %collective-permute-start.4 = (f32[2,25,8,128]{3,2,1,0:T(8,128)}, f32[2,25,8,128]{3,2,1,0:T(8,128)S(1)}, u32[]{:S(2)}, u32[]{:S(2)}) collective-permute-start(f32[2,25,8,128]{3,2,1,0:T(8,128)} %get-tuple-element.12), channel_id=1, source_target_pairs={{1,0},{2,1},{3,2},{4,3},{5,4},{6,5},{7,6},{9,8},{10,9},{11,10},{12... | collective-permute-start | bytes 614408 | tf_op jit(solution)/shard_map/ppermute | solution.py:234
  16.7 1.9 %collective-permute-start.2 = (f32[2,25,8,128]{3,2,1,0:T(8,128)}, f32[2,25,8,128]{3,2,1,0:T(8,128)S(1)}, u32[]{:S(2)}, u32[]{:S(2)}) collective-permute-start(f32[2,25,8,128]{3,2,1,0:T(8,128)} %get-tuple-element.12), channel_id=1, source_target_pairs={{0,1},{1,2},{2,3},{3,4},{4,5},{5,6},{6,7},{8,9},{9,10},{10,11},{11... | collective-permute-start | bytes 614408 | tf_op jit(solution)/shard_map/ppermute | solution.py:235
  18.6 0.1 pad.9.clone
  18.7 0.0 collective-permute-done.3
  18.7 0.2 fusion.2
  19.0 7.7 %collective-permute-done.2 = f32[2,25,8,128]{3,2,1,0:T(8,128)S(1)} collective-permute-done((f32[2,25,8,128]{3,2,1,0:T(8,128)}, f32[2,25,8,128]{3,2,1,0:T(8,128)S(1)}, u32[]{:S(2)}, u32[]{:S(2)}) %collective-permute-start.2) | collective-permute-done | bytes 204832 | tf_op jit(solution)/shard_map/ppermute | solution.py:235
  26.7 0.0 collective-permute-done.4
  26.7 0.1 slice_select_fusion.1
  26.8 0.0 copy-start.4
  26.8 0.1 maximum_maximum_fusion.yh_ref
  26.9 0.0 collective-permute-done.1.xw_ref
  26.9 0.0 collective-permute-done.xe_ref
  26.9 0.0 copy-done.3
  26.9 0.0 copy-done.2
  26.9 0.6 copy-done.4
  27.5 0.0 copy-start.1
  27.5 10.8 %shard_map.95 = (f32[25,64,128]{2,1,0:T(8,128)S(1)}, f32[25,64,128]{2,1,0:T(8,128)S(1)}, f32[25,64,128]{2,1,0:T(8,128)S(1)}, f32[25,64,128]{2,1,0:T(8,128)S(1)},...) custom-call(s32[64,128]{1,0:T(8,128)S(1)} %copy-done.4, f32[25,64,128]{2,1,0:T(8,128)S(1)} %copy-done.2, ...), custom_call_target="tpu_custom_call" | custom-call | flops 163840000 | bytes 12288000 | tf_op jit(solution)/shard_map/pallas_call | solution.py:217
  38.3 0.0 copy-start
  38.4 0.8 %collective-permute-start.8 = (f32[2,25,2,128]{3,2,1,0:T(2,128)S(1)}, f32[2,25,2,128]{3,2,1,0:T(2,128)S(1)}, u32[]{:S(2)}, u32[]{:S(2)}) collective-permute-start(f32[2,25,2,128]{3,2,1,0:T(2,128)S(1)} %slice.43), channel_id=1, source_target_pairs={{7,127},{15,119},{23,111},{31,103},{39,95},{47,87},{55,79},{63,71}... | collective-permute-start | bytes 153608 | tf_op jit(solution)/shard_map/ppermute | solution.py:238
  39.2 0.1 collective-permute-start.6
  39.3 5.3 %collective-permute-start.5 = (f32[2,25,8,128]{3,2,1,0:T(8,128)S(1)}, f32[2,25,8,128]{3,2,1,0:T(8,128)S(1)}, u32[]{:S(2)}, u32[]{:S(2)}) collective-permute-start(f32[2,25,8,128]{3,2,1,0:T(8,128)S(1)} %get-tuple-element.17), channel_id=1, source_target_pairs={{0,120},{8,0},{16,8},{24,16},{32,24},{40,32},{48,40},{56,48},{64,5... | collective-permute-start | bytes 614408 | tf_op jit(solution)/shard_map/ppermute | solution.py:232
  44.6 1.9 %collective-permute-start.9 = (f32[2,25,8,128]{3,2,1,0:T(8,128)S(1)}, f32[2,25,8,128]{3,2,1,0:T(8,128)S(1)}, u32[]{:S(2)}, u32[]{:S(2)}) collective-permute-start(f32[2,25,8,128]{3,2,1,0:T(8,128)S(1)} %get-tuple-element.18), channel_id=1, source_target_pairs={{1,0},{2,1},{3,2},{4,3},{5,4},{6,5},{7,6},{9,8},{10,9},{11,10},{12... | collective-permute-start | bytes 614408 | tf_op jit(solution)/shard_map/ppermute | solution.py:234
  46.5 3.9 %collective-permute-start.7 = (f32[2,25,8,128]{3,2,1,0:T(8,128)S(1)}, f32[2,25,8,128]{3,2,1,0:T(8,128)S(1)}, u32[]{:S(2)}, u32[]{:S(2)}) collective-permute-start(f32[2,25,8,128]{3,2,1,0:T(8,128)S(1)} %get-tuple-element.18), channel_id=1, source_target_pairs={{0,1},{1,2},{2,3},{3,4},{4,5},{5,6},{6,7},{8,9},{9,10},{10,11},{11... | collective-permute-start | bytes 614408 | tf_op jit(solution)/shard_map/ppermute | solution.py:235
  50.5 0.0 collective-permute-done.8
  50.5 0.2 fusion
  50.7 5.5 %collective-permute-done.7 = f32[2,25,8,128]{3,2,1,0:T(8,128)S(1)} collective-permute-done((f32[2,25,8,128]{3,2,1,0:T(8,128)S(1)}, f32[2,25,8,128]{3,2,1,0:T(8,128)S(1)}, u32[]{:S(2)}, u32[]{:S(2)}) %collective-permute-start.7) | collective-permute-done | bytes 204832 | tf_op jit(solution)/shard_map/ppermute | solution.py:235
  56.4 0.0 collective-permute-done.9
  56.4 0.1 slice_select_fusion
  56.4 0.1 maximum_maximum_fusion.1.yh_ref
  56.5 0.0 collective-permute-done.6.xw_ref
  56.5 0.0 collective-permute-done.5.xe_ref
  56.5 0.0 copy-done.1
  56.5 0.0 copy-done
  56.6 8.9 %shard_map.96 = (f32[25,64,128]{2,1,0:T(8,128)}, f32[25,64,128]{2,1,0:T(8,128)}, f32[25,64,128]{2,1,0:T(8,128)}) custom-call(s32[64,128]{1,0:T(8,128)S(1)} %copy-done.4, f32[25,64,128]{2,1,0:T(8,128)S(1)} %get-tuple-element.13.nt_ref, f32[25,64,128]{2,1,0:T(8,128)S(1)} %get-tuple-element.14.ns_ref, f32[25,64,128]{2,1,0:T(8,128)S(1)} %get-tuple-element.15.bt_ref, ...), custom_call_target="tpu_custom_call" | custom-call | flops 163840000 | bytes 9830400 | tf_op jit(solution)/shard_map/pallas_call | solution.py:217
  (12 shorter events, 0.2 us)
Async XLA Ops:
  0.6 26.3 %copy-start.3 = (f32[25,64,128]{2,1,0:T(8,128)S(1)}, f32[25,64,128]{2,1,0:T(8,128)}, u32[]{:S(2)}) copy-start(f32[25,64,128]{2,1,0:T(8,128)} %ns_ref.3) | copy-start | bytes 2457604
  4.2 22.8 %copy-start.2 = (f32[25,64,128]{2,1,0:T(8,128)S(1)}, f32[25,64,128]{2,1,0:T(8,128)}, u32[]{:S(2)}) copy-start(f32[25,64,128]{2,1,0:T(8,128)} %nt_ref.3) | copy-start | bytes 2457604
  5.2 13.5 %collective-permute-start.3 = (f32[2,25,2,128]{3,2,1,0:T(2,128)S(1)}, f32[2,25,2,128]{3,2,1,0:T(2,128)S(1)}, u32[]{:S(2)}, u32[]{:S(2)}) collective-permute-start(f32[2,25,2,128]{3,2,1,0:T(2,128)S(1)} %slice.37), channel_id=1, source_target_pairs={{7,127},{15,119},{23,111},{31,103},{39,95},{47,87},{55,79},{63,71}... | collective-permute-start | bytes 153608 | tf_op jit(solution)/shard_map/ppermute | solution.py:238
  5.9 21.0 %collective-permute-start.1 = (f32[2,25,8,128]{3,2,1,0:T(8,128)}, f32[2,25,8,128]{3,2,1,0:T(8,128)S(1)}, u32[]{:S(2)}, u32[]{:S(2)}) collective-permute-start(f32[2,25,8,128]{3,2,1,0:T(8,128)} %get-tuple-element.11), channel_id=1, source_target_pairs={{0,8},{8,16},{16,24},{24,32},{32,40},{40,48},{48,56},{56,64},{64,7... | collective-permute-start | bytes 614408 | tf_op jit(solution)/shard_map/ppermute | solution.py:233
  5.9 20.9 %collective-permute-start = (f32[2,25,8,128]{3,2,1,0:T(8,128)}, f32[2,25,8,128]{3,2,1,0:T(8,128)S(1)}, u32[]{:S(2)}, u32[]{:S(2)}) collective-permute-start(f32[2,25,8,128]{3,2,1,0:T(8,128)} %get-tuple-element.11), channel_id=1, source_target_pairs={{0,120},{8,0},{16,8},{24,16},{32,24},{40,32},{48,40},{56,48},{64,5... | collective-permute-start | bytes 614408 | tf_op jit(solution)/shard_map/ppermute | solution.py:232
  11.3 15.4 %collective-permute-start.4 = (f32[2,25,8,128]{3,2,1,0:T(8,128)}, f32[2,25,8,128]{3,2,1,0:T(8,128)S(1)}, u32[]{:S(2)}, u32[]{:S(2)}) collective-permute-start(f32[2,25,8,128]{3,2,1,0:T(8,128)} %get-tuple-element.12), channel_id=1, source_target_pairs={{1,0},{2,1},{3,2},{4,3},{5,4},{6,5},{7,6},{9,8},{10,9},{11,10},{12... | collective-permute-start | bytes 614408 | tf_op jit(solution)/shard_map/ppermute | solution.py:234
  16.7 10.0 %collective-permute-start.2 = (f32[2,25,8,128]{3,2,1,0:T(8,128)}, f32[2,25,8,128]{3,2,1,0:T(8,128)S(1)}, u32[]{:S(2)}, u32[]{:S(2)}) collective-permute-start(f32[2,25,8,128]{3,2,1,0:T(8,128)} %get-tuple-element.12), channel_id=1, source_target_pairs={{0,1},{1,2},{2,3},{3,4},{4,5},{5,6},{6,7},{8,9},{9,10},{10,11},{11... | collective-permute-start | bytes 614408 | tf_op jit(solution)/shard_map/ppermute | solution.py:235
  26.8 0.8 %copy-start.4 = (s32[64,128]{1,0:T(8,128)S(1)}, s32[64,128]{1,0:T(8,128)}, u32[]{:S(2)}) copy-start(s32[64,128]{1,0:T(8,128)} %bl_ref.5) | copy-start | bytes 98308
  27.5 29.0 %copy-start.1 = (f32[25,64,128]{2,1,0:T(8,128)S(1)}, f32[25,64,128]{2,1,0:T(8,128)}, u32[]{:S(2)}) copy-start(f32[25,64,128]{2,1,0:T(8,128)} %vn_ref.5) | copy-start | bytes 2457604
  38.3 18.2 %copy-start = (f32[25,64,128]{2,1,0:T(8,128)S(1)}, f32[25,64,128]{2,1,0:T(8,128)}, u32[]{:S(2)}) copy-start(f32[25,64,128]{2,1,0:T(8,128)} %ue_ref.5) | copy-start | bytes 2457604
  38.4 12.1 %collective-permute-start.8 = (f32[2,25,2,128]{3,2,1,0:T(2,128)S(1)}, f32[2,25,2,128]{3,2,1,0:T(2,128)S(1)}, u32[]{:S(2)}, u32[]{:S(2)}) collective-permute-start(f32[2,25,2,128]{3,2,1,0:T(2,128)S(1)} %slice.43), channel_id=1, source_target_pairs={{7,127},{15,119},{23,111},{31,103},{39,95},{47,87},{55,79},{63,71}... | collective-permute-start | bytes 153608 | tf_op jit(solution)/shard_map/ppermute | solution.py:238
  39.2 17.3 %collective-permute-start.6 = (f32[2,25,8,128]{3,2,1,0:T(8,128)S(1)}, f32[2,25,8,128]{3,2,1,0:T(8,128)S(1)}, u32[]{:S(2)}, u32[]{:S(2)}) collective-permute-start(f32[2,25,8,128]{3,2,1,0:T(8,128)S(1)} %get-tuple-element.17), channel_id=1, source_target_pairs={{0,8},{8,16},{16,24},{24,32},{32,40},{40,48},{48,56},{56,64},{64,7... | collective-permute-start | bytes 614408 | tf_op jit(solution)/shard_map/ppermute | solution.py:233
  39.3 17.3 %collective-permute-start.5 = (f32[2,25,8,128]{3,2,1,0:T(8,128)S(1)}, f32[2,25,8,128]{3,2,1,0:T(8,128)S(1)}, u32[]{:S(2)}, u32[]{:S(2)}) collective-permute-start(f32[2,25,8,128]{3,2,1,0:T(8,128)S(1)} %get-tuple-element.17), channel_id=1, source_target_pairs={{0,120},{8,0},{16,8},{24,16},{32,24},{40,32},{48,40},{56,48},{64,5... | collective-permute-start | bytes 614408 | tf_op jit(solution)/shard_map/ppermute | solution.py:232
  44.6 11.7 %collective-permute-start.9 = (f32[2,25,8,128]{3,2,1,0:T(8,128)S(1)}, f32[2,25,8,128]{3,2,1,0:T(8,128)S(1)}, u32[]{:S(2)}, u32[]{:S(2)}) collective-permute-start(f32[2,25,8,128]{3,2,1,0:T(8,128)S(1)} %get-tuple-element.18), channel_id=1, source_target_pairs={{1,0},{2,1},{3,2},{4,3},{5,4},{6,5},{7,6},{9,8},{10,9},{11,10},{12... | collective-permute-start | bytes 614408 | tf_op jit(solution)/shard_map/ppermute | solution.py:234
  46.5 9.8 %collective-permute-start.7 = (f32[2,25,8,128]{3,2,1,0:T(8,128)S(1)}, f32[2,25,8,128]{3,2,1,0:T(8,128)S(1)}, u32[]{:S(2)}, u32[]{:S(2)}) collective-permute-start(f32[2,25,8,128]{3,2,1,0:T(8,128)S(1)} %get-tuple-element.18), channel_id=1, source_target_pairs={{0,1},{1,2},{2,3},{3,4},{4,5},{5,6},{6,7},{8,9},{9,10},{10,11},{11... | collective-permute-start | bytes 614408 | tf_op jit(solution)/shard_map/ppermute | solution.py:235

commit v12 on v11

--- a/solution.py
+++ b/solution.py
@@ -235,7 +235,7 @@
     from_south = lax.ppermute(ypack, "lat", [(i, i + 1) for i in range(lat_count - 1)])
     top = lat_count - 1
     fold_pairs = [(d * lat_count + top, (lon_count - 1 - d) * lat_count + top) for d in range(lon_count)]
-    partner = lax.ppermute(ypack[:, :, 2:4], ("lon", "lat"), fold_pairs)
+    partner = lax.ppermute(ypack, ("lon", "lat"), fold_pairs)[:, :, 2:4]
     cols = ypack.shape[-1]
     flip = (jnp.arange(cols)[:, None] + jnp.arange(cols)[None, :] == cols - 1).astype(jnp.float32)
     flipped = jnp.einsum("fkrc,cd->fkrd", partner, flip, precision=lax.Precision.HIGHEST)

time: 65.8 us -> 65 us (0.988)
  local copies, waits for them, and re-layouts: 1.99 us -> 0.99 us
    slice x2, local copies, waits for them, and re-layouts: 1.05 us -> 0.05 us  [exchange(): partner = lax.ppermute(ypack, ('lon', 'lat'), fold_pairs)[:, :, 2:4]]
  transfers between devices with their start and end apart: 10 -> 10, of which waited for: 2 -> 2; matrix products, arithmetic and copies ran while one was open for 1% -> 2% of each run, Pallas kernels for 0% -> 0%
where the time goes in v12:
time: 65 us; the launch traced here: 64.5 us
  starting transfers between devices  25.6 us (39%)
  Pallas kernels  23.2 us (36%)
  waiting for transfers between devices  13.2 us (20%)
  local copies, waits for them, and re-layouts  0.99 us (2%)
  between operations  0.94 us (1%)
    pallas_call x2, Pallas kernels, step_call(): pl.pallas_call(functools.partial(step_kernel, mask_inputs, final), out_sh...  19.7 us
    ppermute x2, waiting for transfers between devices, exchange(): lax.ppermute(ypack, 'lat', [(i, i + 1) for i in range(lat_count - 1)])  13.2 us
    ppermute x2, starting transfers between devices, exchange(): lax.ppermute(xpack, 'lon', [(i, (i - 1) % lon_count) for i in range(lon_c...  10.7 us
    ppermute x2, starting transfers between devices, exchange(): lax.ppermute(ypack, 'lat', [(i, i - 1) for i in range(1, lat_count)])  7.28 us
    ppermute x2, starting transfers between devices, exchange(): lax.ppermute(ypack, 'lat', [(i, i + 1) for i in range(lat_count - 1)])  5.84 us
    pallas_call x1, Pallas kernels, edge_call(): pl.pallas_call(edge_kernel, out_shape=pack_shapes(levels, rows, cols), in...  3.52 us
    ppermute x2, starting transfers between devices, exchange(): partner = lax.ppermute(ypack, ('lon', 'lat'), fold_pairs)[:, :, 2:4]  1.6 us
  transfers between devices with their start and end apart: 10, of which 2 were waited for; matrix products, arithmetic and copies ran while one was open for 2% of the time, Pallas kernels for 0%

profile of v12, /device:TPU:8, one launch (start us, length us, event | category | flops | bytes accessed | tf_op | source)
XLA Modules:
  0.0 64.5 jit_solution(9019515718852618897)
XLA Ops:
  0.6 0.0 copy-start.3
  0.6 3.5 %shard_map.94 = (f32[2,25,8,128]{3,2,1,0:T(8,128)}, f32[2,25,8,128]{3,2,1,0:T(8,128)}) custom-call(s32[64,128]{1,0:T(8,128)} %bl_ref.5, f32[25,64,128]{2,1,0:T(8,128)} %nt_ref.3, f32[25,64,128]{2,1,0:T(8,128)} %ns_ref.3, f32[25,64,128]{2,1,0:T(8,128)} %ue_ref.5, f32[25,64,128]{2,1,0:T(8,128)} %vn_ref.5), custom_call_target="tpu_custom_call" | custom-call | flops 6553600 | bytes 4096000 | tf_op jit(solution)/shard_map/pallas_call | solution.py:202
  4.2 0.0 copy-start.2
  4.2 0.8 %collective-permute-start.3 = (f32[2,25,8,128]{3,2,1,0:T(8,128)}, f32[2,25,8,128]{3,2,1,0:T(8,128)S(1)}, u32[]{:S(2)}, u32[]{:S(2)}) collective-permute-start(f32[2,25,8,128]{3,2,1,0:T(8,128)} %get-tuple-element.12), channel_id=1, source_target_pairs={{7,127},{15,119},{23,111},{31,103},{39,95},{47,87},{55,79},{63,71}... | collective-permute-start | bytes 614408 | tf_op jit(solution)/shard_map/ppermute | solution.py:238
  5.0 0.1 collective-permute-start.1
  5.0 5.3 %collective-permute-start = (f32[2,25,8,128]{3,2,1,0:T(8,128)}, f32[2,25,8,128]{3,2,1,0:T(8,128)S(1)}, u32[]{:S(2)}, u32[]{:S(2)}) collective-permute-start(f32[2,25,8,128]{3,2,1,0:T(8,128)} %get-tuple-element.11), channel_id=1, source_target_pairs={{0,120},{8,0},{16,8},{24,16},{32,24},{40,32},{48,40},{56,48},{64,5... | collective-permute-start | bytes 614408 | tf_op jit(solution)/shard_map/ppermute | solution.py:232
  10.4 5.4 %collective-permute-start.4 = (f32[2,25,8,128]{3,2,1,0:T(8,128)}, f32[2,25,8,128]{3,2,1,0:T(8,128)S(1)}, u32[]{:S(2)}, u32[]{:S(2)}) collective-permute-start(f32[2,25,8,128]{3,2,1,0:T(8,128)} %get-tuple-element.12), channel_id=1, source_target_pairs={{1,0},{2,1},{3,2},{4,3},{5,4},{6,5},{7,6},{9,8},{10,9},{11,10},{12... | collective-permute-start | bytes 614408 | tf_op jit(solution)/shard_map/ppermute | solution.py:234
  15.8 1.9 %collective-permute-start.2 = (f32[2,25,8,128]{3,2,1,0:T(8,128)}, f32[2,25,8,128]{3,2,1,0:T(8,128)S(1)}, u32[]{:S(2)}, u32[]{:S(2)}) collective-permute-start(f32[2,25,8,128]{3,2,1,0:T(8,128)} %get-tuple-element.12), channel_id=1, source_target_pairs={{0,1},{1,2},{2,3},{3,4},{4,5},{5,6},{6,7},{8,9},{9,10},{10,11},{11... | collective-permute-start | bytes 614408 | tf_op jit(solution)/shard_map/ppermute | solution.py:235
  17.7 0.1 pad.9.clone
  17.8 0.0 collective-permute-done.3
  17.8 0.2 fusion.2
  18.1 7.6 %collective-permute-done.2 = f32[2,25,8,128]{3,2,1,0:T(8,128)S(1)} collective-permute-done((f32[2,25,8,128]{3,2,1,0:T(8,128)}, f32[2,25,8,128]{3,2,1,0:T(8,128)S(1)}, u32[]{:S(2)}, u32[]{:S(2)}) %collective-permute-start.2) | collective-permute-done | bytes 204832 | tf_op jit(solution)/shard_map/ppermute | solution.py:235
  25.8 0.0 collective-permute-done.4
  25.8 0.1 slice_select_fusion.1
  25.9 0.0 copy-start.4
  25.9 0.1 maximum_maximum_fusion.yh_ref
  26.0 0.0 collective-permute-done.1.xw_ref
  26.0 0.0 collective-permute-done.xe_ref
  26.0 0.0 copy-done.3
  26.0 0.0 copy-done.2
  26.0 0.6 copy-done.4
  26.6 0.0 copy-start.1
  26.6 10.8 %shard_map.95 = (f32[25,64,128]{2,1,0:T(8,128)S(1)}, f32[25,64,128]{2,1,0:T(8,128)S(1)}, f32[25,64,128]{2,1,0:T(8,128)S(1)}, f32[25,64,128]{2,1,0:T(8,128)S(1)},...) custom-call(s32[64,128]{1,0:T(8,128)S(1)} %copy-done.4, f32[25,64,128]{2,1,0:T(8,128)S(1)} %copy-done.2, ...), custom_call_target="tpu_custom_call" | custom-call | flops 163840000 | bytes 12288000 | tf_op jit(solution)/shard_map/pallas_call | solution.py:217
  37.4 0.0 copy-start
  37.4 0.8 %collective-permute-start.8 = (f32[2,25,8,128]{3,2,1,0:T(8,128)S(1)}, f32[2,25,8,128]{3,2,1,0:T(8,128)S(1)}, u32[]{:S(2)}, u32[]{:S(2)}) collective-permute-start(f32[2,25,8,128]{3,2,1,0:T(8,128)S(1)} %get-tuple-element.18), channel_id=1, source_target_pairs={{7,127},{15,119},{23,111},{31,103},{39,95},{47,87},{55,79},{63,71}... | collective-permute-start | bytes 614408 | tf_op jit(solution)/shard_map/ppermute | solution.py:238
  38.3 0.1 collective-permute-start.6
  38.3 5.3 %collective-permute-start.5 = (f32[2,25,8,128]{3,2,1,0:T(8,128)S(1)}, f32[2,25,8,128]{3,2,1,0:T(8,128)S(1)}, u32[]{:S(2)}, u32[]{:S(2)}) collective-permute-start(f32[2,25,8,128]{3,2,1,0:T(8,128)S(1)} %get-tuple-element.17), channel_id=1, source_target_pairs={{0,120},{8,0},{16,8},{24,16},{32,24},{40,32},{48,40},{56,48},{64,5... | collective-permute-start | bytes 614408 | tf_op jit(solution)/shard_map/ppermute | solution.py:232
  43.7 1.9 %collective-permute-start.9 = (f32[2,25,8,128]{3,2,1,0:T(8,128)S(1)}, f32[2,25,8,128]{3,2,1,0:T(8,128)S(1)}, u32[]{:S(2)}, u32[]{:S(2)}) collective-permute-start(f32[2,25,8,128]{3,2,1,0:T(8,128)S(1)} %get-tuple-element.18), channel_id=1, source_target_pairs={{1,0},{2,1},{3,2},{4,3},{5,4},{6,5},{7,6},{9,8},{10,9},{11,10},{12... | collective-permute-start | bytes 614408 | tf_op jit(solution)/shard_map/ppermute | solution.py:234
  45.6 3.9 %collective-permute-start.7 = (f32[2,25,8,128]{3,2,1,0:T(8,128)S(1)}, f32[2,25,8,128]{3,2,1,0:T(8,128)S(1)}, u32[]{:S(2)}, u32[]{:S(2)}) collective-permute-start(f32[2,25,8,128]{3,2,1,0:T(8,128)S(1)} %get-tuple-element.18), channel_id=1, source_target_pairs={{0,1},{1,2},{2,3},{3,4},{4,5},{5,6},{6,7},{8,9},{9,10},{10,11},{11... | collective-permute-start | bytes 614408 | tf_op jit(solution)/shard_map/ppermute | solution.py:235
  49.5 0.0 collective-permute-done.8
  49.6 0.2 fusion
  49.9 5.5 %collective-permute-done.7 = f32[2,25,8,128]{3,2,1,0:T(8,128)S(1)} collective-permute-done((f32[2,25,8,128]{3,2,1,0:T(8,128)S(1)}, f32[2,25,8,128]{3,2,1,0:T(8,128)S(1)}, u32[]{:S(2)}, u32[]{:S(2)}) %collective-permute-start.7) | collective-permute-done | bytes 204832 | tf_op jit(solution)/shard_map/ppermute | solution.py:235
  55.4 0.0 collective-permute-done.9
  55.4 0.1 slice_select_fusion
  55.5 0.1 maximum_maximum_fusion.1.yh_ref
  55.6 0.0 collective-permute-done.6.xw_ref
  55.6 0.0 collective-permute-done.5.xe_ref
  55.6 0.0 copy-done.1
  55.6 0.0 copy-done
  55.6 8.9 %shard_map.96 = (f32[25,64,128]{2,1,0:T(8,128)}, f32[25,64,128]{2,1,0:T(8,128)}, f32[25,64,128]{2,1,0:T(8,128)}) custom-call(s32[64,128]{1,0:T(8,128)S(1)} %copy-done.4, f32[25,64,128]{2,1,0:T(8,128)S(1)} %get-tuple-element.13.nt_ref, f32[25,64,128]{2,1,0:T(8,128)S(1)} %get-tuple-element.14.ns_ref, f32[25,64,128]{2,1,0:T(8,128)S(1)} %get-tuple-element.15.bt_ref, ...), custom_call_target="tpu_custom_call" | custom-call | flops 163840000 | bytes 9830400 | tf_op jit(solution)/shard_map/pallas_call | solution.py:217
  (13 shorter events, 0.3 us)
Async XLA Ops:
  0.6 25.4 %copy-start.3 = (f32[25,64,128]{2,1,0:T(8,128)S(1)}, f32[25,64,128]{2,1,0:T(8,128)}, u32[]{:S(2)}) copy-start(f32[25,64,128]{2,1,0:T(8,128)} %ns_ref.3) | copy-start | bytes 2457604
  4.2 21.9 %copy-start.2 = (f32[25,64,128]{2,1,0:T(8,128)S(1)}, f32[25,64,128]{2,1,0:T(8,128)}, u32[]{:S(2)}) copy-start(f32[25,64,128]{2,1,0:T(8,128)} %nt_ref.3) | copy-start | bytes 2457604
  4.2 13.6 %collective-permute-start.3 = (f32[2,25,8,128]{3,2,1,0:T(8,128)}, f32[2,25,8,128]{3,2,1,0:T(8,128)S(1)}, u32[]{:S(2)}, u32[]{:S(2)}) collective-permute-start(f32[2,25,8,128]{3,2,1,0:T(8,128)} %get-tuple-element.12), channel_id=1, source_target_pairs={{7,127},{15,119},{23,111},{31,103},{39,95},{47,87},{55,79},{63,71}... | collective-permute-start | bytes 614408 | tf_op jit(solution)/shard_map/ppermute | solution.py:238
  5.0 21.0 %collective-permute-start.1 = (f32[2,25,8,128]{3,2,1,0:T(8,128)}, f32[2,25,8,128]{3,2,1,0:T(8,128)S(1)}, u32[]{:S(2)}, u32[]{:S(2)}) collective-permute-start(f32[2,25,8,128]{3,2,1,0:T(8,128)} %get-tuple-element.11), channel_id=1, source_target_pairs={{0,8},{8,16},{16,24},{24,32},{32,40},{40,48},{48,56},{56,64},{64,7... | collective-permute-start | bytes 614408 | tf_op jit(solution)/shard_map/ppermute | solution.py:233
  5.0 20.9 %collective-permute-start = (f32[2,25,8,128]{3,2,1,0:T(8,128)}, f32[2,25,8,128]{3,2,1,0:T(8,128)S(1)}, u32[]{:S(2)}, u32[]{:S(2)}) collective-permute-start(f32[2,25,8,128]{3,2,1,0:T(8,128)} %get-tuple-element.11), channel_id=1, source_target_pairs={{0,120},{8,0},{16,8},{24,16},{32,24},{40,32},{48,40},{56,48},{64,5... | collective-permute-start | bytes 614408 | tf_op jit(solution)/shard_map/ppermute | solution.py:232
  10.4 15.4 %collective-permute-start.4 = (f32[2,25,8,128]{3,2,1,0:T(8,128)}, f32[2,25,8,128]{3,2,1,0:T(8,128)S(1)}, u32[]{:S(2)}, u32[]{:S(2)}) collective-permute-start(f32[2,25,8,128]{3,2,1,0:T(8,128)} %get-tuple-element.12), channel_id=1, source_target_pairs={{1,0},{2,1},{3,2},{4,3},{5,4},{6,5},{7,6},{9,8},{10,9},{11,10},{12... | collective-permute-start | bytes 614408 | tf_op jit(solution)/shard_map/ppermute | solution.py:234
  15.8 10.0 %collective-permute-start.2 = (f32[2,25,8,128]{3,2,1,0:T(8,128)}, f32[2,25,8,128]{3,2,1,0:T(8,128)S(1)}, u32[]{:S(2)}, u32[]{:S(2)}) collective-permute-start(f32[2,25,8,128]{3,2,1,0:T(8,128)} %get-tuple-element.12), channel_id=1, source_target_pairs={{0,1},{1,2},{2,3},{3,4},{4,5},{5,6},{6,7},{8,9},{9,10},{10,11},{11... | collective-permute-start | bytes 614408 | tf_op jit(solution)/shard_map/ppermute | solution.py:235
  25.9 0.8 %copy-start.4 = (s32[64,128]{1,0:T(8,128)S(1)}, s32[64,128]{1,0:T(8,128)}, u32[]{:S(2)}) copy-start(s32[64,128]{1,0:T(8,128)} %bl_ref.5) | copy-start | bytes 98308
  26.6 29.0 %copy-start.1 = (f32[25,64,128]{2,1,0:T(8,128)S(1)}, f32[25,64,128]{2,1,0:T(8,128)}, u32[]{:S(2)}) copy-start(f32[25,64,128]{2,1,0:T(8,128)} %vn_ref.5) | copy-start | bytes 2457604
  37.4 18.2 %copy-start = (f32[25,64,128]{2,1,0:T(8,128)S(1)}, f32[25,64,128]{2,1,0:T(8,128)}, u32[]{:S(2)}) copy-start(f32[25,64,128]{2,1,0:T(8,128)} %ue_ref.5) | copy-start | bytes 2457604
  37.4 12.1 %collective-permute-start.8 = (f32[2,25,8,128]{3,2,1,0:T(8,128)S(1)}, f32[2,25,8,128]{3,2,1,0:T(8,128)S(1)}, u32[]{:S(2)}, u32[]{:S(2)}) collective-permute-start(f32[2,25,8,128]{3,2,1,0:T(8,128)S(1)} %get-tuple-element.18), channel_id=1, source_target_pairs={{7,127},{15,119},{23,111},{31,103},{39,95},{47,87},{55,79},{63,71}... | collective-permute-start | bytes 614408 | tf_op jit(solution)/shard_map/ppermute | solution.py:238
  38.3 17.3 %collective-permute-start.6 = (f32[2,25,8,128]{3,2,1,0:T(8,128)S(1)}, f32[2,25,8,128]{3,2,1,0:T(8,128)S(1)}, u32[]{:S(2)}, u32[]{:S(2)}) collective-permute-start(f32[2,25,8,128]{3,2,1,0:T(8,128)S(1)} %get-tuple-element.17), channel_id=1, source_target_pairs={{0,8},{8,16},{16,24},{24,32},{32,40},{40,48},{48,56},{56,64},{64,7... | collective-permute-start | bytes 614408 | tf_op jit(solution)/shard_map/ppermute | solution.py:233
  38.3 17.3 %collective-permute-start.5 = (f32[2,25,8,128]{3,2,1,0:T(8,128)S(1)}, f32[2,25,8,128]{3,2,1,0:T(8,128)S(1)}, u32[]{:S(2)}, u32[]{:S(2)}) collective-permute-start(f32[2,25,8,128]{3,2,1,0:T(8,128)S(1)} %get-tuple-element.17), channel_id=1, source_target_pairs={{0,120},{8,0},{16,8},{24,16},{32,24},{40,32},{48,40},{56,48},{64,5... | collective-permute-start | bytes 614408 | tf_op jit(solution)/shard_map/ppermute | solution.py:232
  43.7 11.7 %collective-permute-start.9 = (f32[2,25,8,128]{3,2,1,0:T(8,128)S(1)}, f32[2,25,8,128]{3,2,1,0:T(8,128)S(1)}, u32[]{:S(2)}, u32[]{:S(2)}) collective-permute-start(f32[2,25,8,128]{3,2,1,0:T(8,128)S(1)} %get-tuple-element.18), channel_id=1, source_target_pairs={{1,0},{2,1},{3,2},{4,3},{5,4},{6,5},{7,6},{9,8},{10,9},{11,10},{12... | collective-permute-start | bytes 614408 | tf_op jit(solution)/shard_map/ppermute | solution.py:234
  45.6 9.8 %collective-permute-start.7 = (f32[2,25,8,128]{3,2,1,0:T(8,128)S(1)}, f32[2,25,8,128]{3,2,1,0:T(8,128)S(1)}, u32[]{:S(2)}, u32[]{:S(2)}) collective-permute-start(f32[2,25,8,128]{3,2,1,0:T(8,128)S(1)} %get-tuple-element.18), channel_id=1, source_target_pairs={{0,1},{1,2},{2,3},{3,4},{4,5},{5,6},{6,7},{8,9},{9,10},{10,11},{11... | collective-permute-start | bytes 614408 | tf_op jit(solution)/shard_map/ppermute | solution.py:235

commit v13 on v12

--- a/solution.py
+++ b/solution.py
@@ -44,7 +44,8 @@
         lo_lane = (4 * a - 2) % cols
         pack = jnp.where((lane >= 4 * a) & (lane < 4 * a + 2), part, pack)
         pack = jnp.where((lane >= lo_lane) & (lane < lo_lane + 2), part, pack)
-        pack = jnp.where(lane == 64 + 4 * a, lane_roll(east_v[8 * a:8 * a + 8], 4 * a + 65), pack)
+        if east_v is not None:
+            pack = jnp.where(lane == 64 + 4 * a, lane_roll(east_v[8 * a:8 * a + 8], 4 * a + 65), pack)
     return pack
 
 
@@ -75,7 +76,7 @@
         m = (k < bl_ref[...]).astype(jnp.float32)
         for f, ref in enumerate((nt_ref, ns_ref)):
             value = ref[k] * m
-            xpack_ref[f, k] = column_pack(value, ue_ref[k])
+            xpack_ref[f, k] = column_pack(value, ue_ref[k] if f == 0 else None)
             write_rows(value, vn_ref[k], ypack_ref, f, k)
         return carry
 
@@ -137,7 +138,7 @@
             own = jnp.zeros((8, cols), jnp.float32)
             for a in range(strips):
                 own = jnp.where((lane8 >= 4 * a) & (lane8 < 4 * a + 2), lane_roll(q[a], 4 * a), own)
-            west_face = face_flux(lane_roll(from_west, -64), lane_roll(both, 2), lane_roll(both, 1),
+            west_face = face_flux(lane_roll(xw_ref[0, k], -64), lane_roll(both, 2), lane_roll(both, 1),
                                   own, lane_roll(own, -1))
             yh = yh_ref[f, k]
             below = jnp.where(sub8 == 6, jnp.broadcast_to(yh[0:1], (8, cols)),
@@ -175,7 +176,7 @@
                     outs[f][k, rs, :] = after
             if not final:
                 whole = jnp.concatenate(afters[f], 0)
-                outs[4][f, k] = column_pack(whole, ue_ref[k])
+                outs[4][f, k] = column_pack(whole, ue_ref[k] if f == 0 else None)
                 write_rows(whole, vn_ref[k], outs[5], f, k)
         if final:
             for a in range(strips):

time: 65 us -> 64.8 us (level)
  no operation moved by 1% of the time
where the time goes in v13:
time: 64.8 us; the launch traced here: 64.3 us
  starting transfers between devices  25.6 us (40%)
  Pallas kernels  22.9 us (35%)
  waiting for transfers between devices  13.2 us (20%)
  local copies, waits for them, and re-layouts  0.99 us (2%)
  between operations  0.94 us (1%)
    pallas_call x2, Pallas kernels, step_call(): pl.pallas_call(functools.partial(step_kernel, mask_inputs, final), out_sh...  19.6 us
    ppermute x2, waiting for transfers between devices, exchange(): lax.ppermute(ypack, 'lat', [(i, i + 1) for i in range(lat_count - 1)])  13.2 us
    ppermute x2, starting transfers between devices, exchange(): lax.ppermute(xpack, 'lon', [(i, (i - 1) % lon_count) for i in range(lon_c...  10.7 us
    ppermute x2, starting transfers between devices, exchange(): lax.ppermute(ypack, 'lat', [(i, i - 1) for i in range(1, lat_count)])  7.28 us
    ppermute x2, starting transfers between devices, exchange(): lax.ppermute(ypack, 'lat', [(i, i + 1) for i in range(lat_count - 1)])  5.84 us
    pallas_call x1, Pallas kernels, edge_call(): pl.pallas_call(edge_kernel, out_shape=pack_shapes(levels, rows, cols), in...  3.31 us
    ppermute x2, starting transfers between devices, exchange(): partner = lax.ppermute(ypack, ('lon', 'lat'), fold_pairs)[:, :, 2:4]  1.6 us
  transfers between devices with their start and end apart: 10, of which 2 were waited for; matrix products, arithmetic and copies ran while one was open for 2% of the time, Pallas kernels for 0%

profile of v13, /device:TPU:8, one launch (start us, length us, event | category | flops | bytes accessed | tf_op | source)
XLA Modules:
  0.0 64.3 jit_solution(13355123050197592723)
XLA Ops:
  0.6 0.0 copy-start.3
  0.6 3.3 %shard_map.94 = (f32[2,25,8,128]{3,2,1,0:T(8,128)}, f32[2,25,8,128]{3,2,1,0:T(8,128)}) custom-call(s32[64,128]{1,0:T(8,128)} %bl_ref.5, f32[25,64,128]{2,1,0:T(8,128)} %nt_ref.3, f32[25,64,128]{2,1,0:T(8,128)} %ns_ref.3, f32[25,64,128]{2,1,0:T(8,128)} %ue_ref.5, f32[25,64,128]{2,1,0:T(8,128)} %vn_ref.5), custom_call_target="tpu_custom_call" | custom-call | flops 6553600 | bytes 4096000 | tf_op jit(solution)/shard_map/pallas_call | solution.py:203
  4.0 0.0 copy-start.2
  4.0 0.8 %collective-permute-start.3 = (f32[2,25,8,128]{3,2,1,0:T(8,128)}, f32[2,25,8,128]{3,2,1,0:T(8,128)S(1)}, u32[]{:S(2)}, u32[]{:S(2)}) collective-permute-start(f32[2,25,8,128]{3,2,1,0:T(8,128)} %get-tuple-element.12), channel_id=1, source_target_pairs={{7,127},{15,119},{23,111},{31,103},{39,95},{47,87},{55,79},{63,71}... | collective-permute-start | bytes 614408 | tf_op jit(solution)/shard_map/ppermute | solution.py:239
  4.8 0.1 collective-permute-start.1
  4.8 5.3 %collective-permute-start = (f32[2,25,8,128]{3,2,1,0:T(8,128)}, f32[2,25,8,128]{3,2,1,0:T(8,128)S(1)}, u32[]{:S(2)}, u32[]{:S(2)}) collective-permute-start(f32[2,25,8,128]{3,2,1,0:T(8,128)} %get-tuple-element.11), channel_id=1, source_target_pairs={{0,120},{8,0},{16,8},{24,16},{32,24},{40,32},{48,40},{56,48},{64,5... | collective-permute-start | bytes 614408 | tf_op jit(solution)/shard_map/ppermute | solution.py:233
  10.2 5.4 %collective-permute-start.4 = (f32[2,25,8,128]{3,2,1,0:T(8,128)}, f32[2,25,8,128]{3,2,1,0:T(8,128)S(1)}, u32[]{:S(2)}, u32[]{:S(2)}) collective-permute-start(f32[2,25,8,128]{3,2,1,0:T(8,128)} %get-tuple-element.12), channel_id=1, source_target_pairs={{1,0},{2,1},{3,2},{4,3},{5,4},{6,5},{7,6},{9,8},{10,9},{11,10},{12... | collective-permute-start | bytes 614408 | tf_op jit(solution)/shard_map/ppermute | solution.py:235
  15.6 1.9 %collective-permute-start.2 = (f32[2,25,8,128]{3,2,1,0:T(8,128)}, f32[2,25,8,128]{3,2,1,0:T(8,128)S(1)}, u32[]{:S(2)}, u32[]{:S(2)}) collective-permute-start(f32[2,25,8,128]{3,2,1,0:T(8,128)} %get-tuple-element.12), channel_id=1, source_target_pairs={{0,1},{1,2},{2,3},{3,4},{4,5},{5,6},{6,7},{8,9},{9,10},{10,11},{11... | collective-permute-start | bytes 614408 | tf_op jit(solution)/shard_map/ppermute | solution.py:236
  17.5 0.1 pad.9.clone
  17.6 0.0 collective-permute-done.3
  17.6 0.2 fusion.2
  17.9 7.6 %collective-permute-done.2 = f32[2,25,8,128]{3,2,1,0:T(8,128)S(1)} collective-permute-done((f32[2,25,8,128]{3,2,1,0:T(8,128)}, f32[2,25,8,128]{3,2,1,0:T(8,128)S(1)}, u32[]{:S(2)}, u32[]{:S(2)}) %collective-permute-start.2) | collective-permute-done | bytes 204832 | tf_op jit(solution)/shard_map/ppermute | solution.py:236
  25.6 0.0 collective-permute-done.4
  25.6 0.1 slice_select_fusion.1
  25.7 0.0 copy-start.4
  25.7 0.1 maximum_maximum_fusion.yh_ref
  25.8 0.0 collective-permute-done.1.xw_ref
  25.8 0.0 collective-permute-done.xe_ref
  25.8 0.0 copy-done.3
  25.8 0.0 copy-done.2
  25.8 0.6 copy-done.4
  26.4 0.0 copy-start.1
  26.4 10.7 %shard_map.95 = (f32[25,64,128]{2,1,0:T(8,128)S(1)}, f32[25,64,128]{2,1,0:T(8,128)S(1)}, f32[25,64,128]{2,1,0:T(8,128)S(1)}, f32[25,64,128]{2,1,0:T(8,128)S(1)},...) custom-call(s32[64,128]{1,0:T(8,128)S(1)} %copy-done.4, f32[25,64,128]{2,1,0:T(8,128)S(1)} %copy-done.2, ...), custom_call_target="tpu_custom_call" | custom-call | flops 163840000 | bytes 12288000 | tf_op jit(solution)/shard_map/pallas_call | solution.py:218
  37.2 0.0 copy-start
  37.2 0.8 %collective-permute-start.8 = (f32[2,25,8,128]{3,2,1,0:T(8,128)S(1)}, f32[2,25,8,128]{3,2,1,0:T(8,128)S(1)}, u32[]{:S(2)}, u32[]{:S(2)}) collective-permute-start(f32[2,25,8,128]{3,2,1,0:T(8,128)S(1)} %get-tuple-element.18), channel_id=1, source_target_pairs={{7,127},{15,119},{23,111},{31,103},{39,95},{47,87},{55,79},{63,71}... | collective-permute-start | bytes 614408 | tf_op jit(solution)/shard_map/ppermute | solution.py:239
  38.0 0.1 collective-permute-start.6
  38.1 5.3 %collective-permute-start.5 = (f32[2,25,8,128]{3,2,1,0:T(8,128)S(1)}, f32[2,25,8,128]{3,2,1,0:T(8,128)S(1)}, u32[]{:S(2)}, u32[]{:S(2)}) collective-permute-start(f32[2,25,8,128]{3,2,1,0:T(8,128)S(1)} %get-tuple-element.17), channel_id=1, source_target_pairs={{0,120},{8,0},{16,8},{24,16},{32,24},{40,32},{48,40},{56,48},{64,5... | collective-permute-start | bytes 614408 | tf_op jit(solution)/shard_map/ppermute | solution.py:233
  43.4 1.9 %collective-permute-start.9 = (f32[2,25,8,128]{3,2,1,0:T(8,128)S(1)}, f32[2,25,8,128]{3,2,1,0:T(8,128)S(1)}, u32[]{:S(2)}, u32[]{:S(2)}) collective-permute-start(f32[2,25,8,128]{3,2,1,0:T(8,128)S(1)} %get-tuple-element.18), channel_id=1, source_target_pairs={{1,0},{2,1},{3,2},{4,3},{5,4},{6,5},{7,6},{9,8},{10,9},{11,10},{12... | collective-permute-start | bytes 614408 | tf_op jit(solution)/shard_map/ppermute | solution.py:235
  45.4 3.9 %collective-permute-start.7 = (f32[2,25,8,128]{3,2,1,0:T(8,128)S(1)}, f32[2,25,8,128]{3,2,1,0:T(8,128)S(1)}, u32[]{:S(2)}, u32[]{:S(2)}) collective-permute-start(f32[2,25,8,128]{3,2,1,0:T(8,128)S(1)} %get-tuple-element.18), channel_id=1, source_target_pairs={{0,1},{1,2},{2,3},{3,4},{4,5},{5,6},{6,7},{8,9},{9,10},{10,11},{11... | collective-permute-start | bytes 614408 | tf_op jit(solution)/shard_map/ppermute | solution.py:236
  49.3 0.0 collective-permute-done.8
  49.3 0.2 fusion
  49.6 5.5 %collective-permute-done.7 = f32[2,25,8,128]{3,2,1,0:T(8,128)S(1)} collective-permute-done((f32[2,25,8,128]{3,2,1,0:T(8,128)S(1)}, f32[2,25,8,128]{3,2,1,0:T(8,128)S(1)}, u32[]{:S(2)}, u32[]{:S(2)}) %collective-permute-start.7) | collective-permute-done | bytes 204832 | tf_op jit(solution)/shard_map/ppermute | solution.py:236
  55.2 0.0 collective-permute-done.9
  55.2 0.1 slice_select_fusion
  55.3 0.1 maximum_maximum_fusion.1.yh_ref
  55.3 0.0 collective-permute-done.6.xw_ref
  55.4 0.0 collective-permute-done.5.xe_ref
  55.4 0.0 copy-done.1
  55.4 0.0 copy-done
  55.4 8.9 %shard_map.96 = (f32[25,64,128]{2,1,0:T(8,128)}, f32[25,64,128]{2,1,0:T(8,128)}, f32[25,64,128]{2,1,0:T(8,128)}) custom-call(s32[64,128]{1,0:T(8,128)S(1)} %copy-done.4, f32[25,64,128]{2,1,0:T(8,128)S(1)} %get-tuple-element.13.nt_ref, f32[25,64,128]{2,1,0:T(8,128)S(1)} %get-tuple-element.14.ns_ref, f32[25,64,128]{2,1,0:T(8,128)S(1)} %get-tuple-element.15.bt_ref, ...), custom_call_target="tpu_custom_call" | custom-call | flops 163840000 | bytes 9830400 | tf_op jit(solution)/shard_map/pallas_call | solution.py:218
  (13 shorter events, 0.3 us)
Async XLA Ops:
  0.6 25.2 %copy-start.3 = (f32[25,64,128]{2,1,0:T(8,128)S(1)}, f32[25,64,128]{2,1,0:T(8,128)}, u32[]{:S(2)}) copy-start(f32[25,64,128]{2,1,0:T(8,128)} %ns_ref.3) | copy-start | bytes 2457604
  4.0 21.9 %copy-start.2 = (f32[25,64,128]{2,1,0:T(8,128)S(1)}, f32[25,64,128]{2,1,0:T(8,128)}, u32[]{:S(2)}) copy-start(f32[25,64,128]{2,1,0:T(8,128)} %nt_ref.3) | copy-start | bytes 2457604
  4.0 13.6 %collective-permute-start.3 = (f32[2,25,8,128]{3,2,1,0:T(8,128)}, f32[2,25,8,128]{3,2,1,0:T(8,128)S(1)}, u32[]{:S(2)}, u32[]{:S(2)}) collective-permute-start(f32[2,25,8,128]{3,2,1,0:T(8,128)} %get-tuple-element.12), channel_id=1, source_target_pairs={{7,127},{15,119},{23,111},{31,103},{39,95},{47,87},{55,79},{63,71}... | collective-permute-start | bytes 614408 | tf_op jit(solution)/shard_map/ppermute | solution.py:239
  4.8 21.0 %collective-permute-start.1 = (f32[2,25,8,128]{3,2,1,0:T(8,128)}, f32[2,25,8,128]{3,2,1,0:T(8,128)S(1)}, u32[]{:S(2)}, u32[]{:S(2)}) collective-permute-start(f32[2,25,8,128]{3,2,1,0:T(8,128)} %get-tuple-element.11), channel_id=1, source_target_pairs={{0,8},{8,16},{16,24},{24,32},{32,40},{40,48},{48,56},{56,64},{64,7... | collective-permute-start | bytes 614408 | tf_op jit(solution)/shard_map/ppermute | solution.py:234
  4.8 20.9 %collective-permute-start = (f32[2,25,8,128]{3,2,1,0:T(8,128)}, f32[2,25,8,128]{3,2,1,0:T(8,128)S(1)}, u32[]{:S(2)}, u32[]{:S(2)}) collective-permute-start(f32[2,25,8,128]{3,2,1,0:T(8,128)} %get-tuple-element.11), channel_id=1, source_target_pairs={{0,120},{8,0},{16,8},{24,16},{32,24},{40,32},{48,40},{56,48},{64,5... | collective-permute-start | bytes 614408 | tf_op jit(solution)/shard_map/ppermute | solution.py:233
  10.2 15.4 %collective-permute-start.4 = (f32[2,25,8,128]{3,2,1,0:T(8,128)}, f32[2,25,8,128]{3,2,1,0:T(8,128)S(1)}, u32[]{:S(2)}, u32[]{:S(2)}) collective-permute-start(f32[2,25,8,128]{3,2,1,0:T(8,128)} %get-tuple-element.12), channel_id=1, source_target_pairs={{1,0},{2,1},{3,2},{4,3},{5,4},{6,5},{7,6},{9,8},{10,9},{11,10},{12... | collective-permute-start | bytes 614408 | tf_op jit(solution)/shard_map/ppermute | solution.py:235
  15.6 10.0 %collective-permute-start.2 = (f32[2,25,8,128]{3,2,1,0:T(8,128)}, f32[2,25,8,128]{3,2,1,0:T(8,128)S(1)}, u32[]{:S(2)}, u32[]{:S(2)}) collective-permute-start(f32[2,25,8,128]{3,2,1,0:T(8,128)} %get-tuple-element.12), channel_id=1, source_target_pairs={{0,1},{1,2},{2,3},{3,4},{4,5},{5,6},{6,7},{8,9},{9,10},{10,11},{11... | collective-permute-start | bytes 614408 | tf_op jit(solution)/shard_map/ppermute | solution.py:236
  25.7 0.8 %copy-start.4 = (s32[64,128]{1,0:T(8,128)S(1)}, s32[64,128]{1,0:T(8,128)}, u32[]{:S(2)}) copy-start(s32[64,128]{1,0:T(8,128)} %bl_ref.5) | copy-start | bytes 98308
  26.4 28.9 %copy-start.1 = (f32[25,64,128]{2,1,0:T(8,128)S(1)}, f32[25,64,128]{2,1,0:T(8,128)}, u32[]{:S(2)}) copy-start(f32[25,64,128]{2,1,0:T(8,128)} %vn_ref.5) | copy-start | bytes 2457604
  37.2 18.2 %copy-start = (f32[25,64,128]{2,1,0:T(8,128)S(1)}, f32[25,64,128]{2,1,0:T(8,128)}, u32[]{:S(2)}) copy-start(f32[25,64,128]{2,1,0:T(8,128)} %ue_ref.5) | copy-start | bytes 2457604
  37.2 12.1 %collective-permute-start.8 = (f32[2,25,8,128]{3,2,1,0:T(8,128)S(1)}, f32[2,25,8,128]{3,2,1,0:T(8,128)S(1)}, u32[]{:S(2)}, u32[]{:S(2)}) collective-permute-start(f32[2,25,8,128]{3,2,1,0:T(8,128)S(1)} %get-tuple-element.18), channel_id=1, source_target_pairs={{7,127},{15,119},{23,111},{31,103},{39,95},{47,87},{55,79},{63,71}... | collective-permute-start | bytes 614408 | tf_op jit(solution)/shard_map/ppermute | solution.py:239
  38.0 17.3 %collective-permute-start.6 = (f32[2,25,8,128]{3,2,1,0:T(8,128)S(1)}, f32[2,25,8,128]{3,2,1,0:T(8,128)S(1)}, u32[]{:S(2)}, u32[]{:S(2)}) collective-permute-start(f32[2,25,8,128]{3,2,1,0:T(8,128)S(1)} %get-tuple-element.17), channel_id=1, source_target_pairs={{0,8},{8,16},{16,24},{24,32},{32,40},{40,48},{48,56},{56,64},{64,7... | collective-permute-start | bytes 614408 | tf_op jit(solution)/shard_map/ppermute | solution.py:234
  38.1 17.3 %collective-permute-start.5 = (f32[2,25,8,128]{3,2,1,0:T(8,128)S(1)}, f32[2,25,8,128]{3,2,1,0:T(8,128)S(1)}, u32[]{:S(2)}, u32[]{:S(2)}) collective-permute-start(f32[2,25,8,128]{3,2,1,0:T(8,128)S(1)} %get-tuple-element.17), channel_id=1, source_target_pairs={{0,120},{8,0},{16,8},{24,16},{32,24},{40,32},{48,40},{56,48},{64,5... | collective-permute-start | bytes 614408 | tf_op jit(solution)/shard_map/ppermute | solution.py:233
  43.4 11.7 %collective-permute-start.9 = (f32[2,25,8,128]{3,2,1,0:T(8,128)S(1)}, f32[2,25,8,128]{3,2,1,0:T(8,128)S(1)}, u32[]{:S(2)}, u32[]{:S(2)}) collective-permute-start(f32[2,25,8,128]{3,2,1,0:T(8,128)S(1)} %get-tuple-element.18), channel_id=1, source_target_pairs={{1,0},{2,1},{3,2},{4,3},{5,4},{6,5},{7,6},{9,8},{10,9},{11,10},{12... | collective-permute-start | bytes 614408 | tf_op jit(solution)/shard_map/ppermute | solution.py:235
  45.4 9.8 %collective-permute-start.7 = (f32[2,25,8,128]{3,2,1,0:T(8,128)S(1)}, f32[2,25,8,128]{3,2,1,0:T(8,128)S(1)}, u32[]{:S(2)}, u32[]{:S(2)}) collective-permute-start(f32[2,25,8,128]{3,2,1,0:T(8,128)S(1)} %get-tuple-element.18), channel_id=1, source_target_pairs={{0,1},{1,2},{2,3},{3,4},{4,5},{5,6},{6,7},{8,9},{9,10},{10,11},{11... | collective-permute-start | bytes 614408 | tf_op jit(solution)/shard_map/ppermute | solution.py:236

commit v14 on v13

--- a/solution.py
+++ b/solution.py
@@ -115,7 +115,7 @@
             fv[f, k + 1] = rates * (load(bef_refs[f], k + 1, m1) - load(bef_refs[f], k, m0))
         return carry
 
-    lax.fori_loop(0, levels - 1, mixing, 0)
+    lax.fori_loop(0, levels - 1, mixing, 0, unroll=2)
 
     strips = rows // 8
     lane8 = lax.broadcasted_iota(jnp.int32, (8, cols), 1)

time: 64.8 us -> 64.1 us (0.989)
    pallas_call x2, Pallas kernels: 19.6 us -> 18.9 us  [step_call(): pl.pallas_call(functools.partial(step_kernel, mask_inputs, final), out_sh...]
where the time goes in v14:
time: 64.1 us; the launch traced here: 63.6 us
  starting transfers between devices  25.6 us (40%)
  Pallas kernels  22.3 us (35%)
  waiting for transfers between devices  13.2 us (21%)
  local copies, waits for them, and re-layouts  0.99 us (2%)
  between operations  0.94 us (1%)
    pallas_call x2, Pallas kernels, step_call(): pl.pallas_call(functools.partial(step_kernel, mask_inputs, final), out_sh...  18.9 us
    ppermute x2, waiting for transfers between devices, exchange(): lax.ppermute(ypack, 'lat', [(i, i + 1) for i in range(lat_count - 1)])  13.2 us
    ppermute x2, starting transfers between devices, exchange(): lax.ppermute(xpack, 'lon', [(i, (i - 1) % lon_count) for i in range(lon_c...  10.7 us
    ppermute x2, starting transfers between devices, exchange(): lax.ppermute(ypack, 'lat', [(i, i - 1) for i in range(1, lat_count)])  7.28 us
    ppermute x2, starting transfers between devices, exchange(): lax.ppermute(ypack, 'lat', [(i, i + 1) for i in range(lat_count - 1)])  5.84 us
    pallas_call x1, Pallas kernels, edge_call(): pl.pallas_call(edge_kernel, out_shape=pack_shapes(levels, rows, cols), in...  3.31 us
    ppermute x2, starting transfers between devices, exchange(): partner = lax.ppermute(ypack, ('lon', 'lat'), fold_pairs)[:, :, 2:4]  1.6 us
  transfers between devices with their start and end apart: 10, of which 2 were waited for; matrix products, arithmetic and copies ran while one was open for 2% of the time, Pallas kernels for 0%

profile of v14, /device:TPU:8, one launch (start us, length us, event | category | flops | bytes accessed | tf_op | source)
XLA Modules:
  0.0 63.6 jit_solution(12827672223416809750)
XLA Ops:
  0.6 0.0 copy-start.3
  0.6 3.3 %shard_map.94 = (f32[2,25,8,128]{3,2,1,0:T(8,128)}, f32[2,25,8,128]{3,2,1,0:T(8,128)}) custom-call(s32[64,128]{1,0:T(8,128)} %bl_ref.5, f32[25,64,128]{2,1,0:T(8,128)} %nt_ref.3, f32[25,64,128]{2,1,0:T(8,128)} %ns_ref.3, f32[25,64,128]{2,1,0:T(8,128)} %ue_ref.5, f32[25,64,128]{2,1,0:T(8,128)} %vn_ref.5), custom_call_target="tpu_custom_call" | custom-call | flops 6553600 | bytes 4096000 | tf_op jit(solution)/shard_map/pallas_call | solution.py:203
  4.0 0.0 copy-start.2
  4.0 0.8 %collective-permute-start.3 = (f32[2,25,8,128]{3,2,1,0:T(8,128)}, f32[2,25,8,128]{3,2,1,0:T(8,128)S(1)}, u32[]{:S(2)}, u32[]{:S(2)}) collective-permute-start(f32[2,25,8,128]{3,2,1,0:T(8,128)} %get-tuple-element.12), channel_id=1, source_target_pairs={{7,127},{15,119},{23,111},{31,103},{39,95},{47,87},{55,79},{63,71}... | collective-permute-start | bytes 614408 | tf_op jit(solution)/shard_map/ppermute | solution.py:239
  4.8 0.1 collective-permute-start.1
  4.8 5.3 %collective-permute-start = (f32[2,25,8,128]{3,2,1,0:T(8,128)}, f32[2,25,8,128]{3,2,1,0:T(8,128)S(1)}, u32[]{:S(2)}, u32[]{:S(2)}) collective-permute-start(f32[2,25,8,128]{3,2,1,0:T(8,128)} %get-tuple-element.11), channel_id=1, source_target_pairs={{0,120},{8,0},{16,8},{24,16},{32,24},{40,32},{48,40},{56,48},{64,5... | collective-permute-start | bytes 614408 | tf_op jit(solution)/shard_map/ppermute | solution.py:233
  10.2 5.4 %collective-permute-start.4 = (f32[2,25,8,128]{3,2,1,0:T(8,128)}, f32[2,25,8,128]{3,2,1,0:T(8,128)S(1)}, u32[]{:S(2)}, u32[]{:S(2)}) collective-permute-start(f32[2,25,8,128]{3,2,1,0:T(8,128)} %get-tuple-element.12), channel_id=1, source_target_pairs={{1,0},{2,1},{3,2},{4,3},{5,4},{6,5},{7,6},{9,8},{10,9},{11,10},{12... | collective-permute-start | bytes 614408 | tf_op jit(solution)/shard_map/ppermute | solution.py:235
  15.6 1.9 %collective-permute-start.2 = (f32[2,25,8,128]{3,2,1,0:T(8,128)}, f32[2,25,8,128]{3,2,1,0:T(8,128)S(1)}, u32[]{:S(2)}, u32[]{:S(2)}) collective-permute-start(f32[2,25,8,128]{3,2,1,0:T(8,128)} %get-tuple-element.12), channel_id=1, source_target_pairs={{0,1},{1,2},{2,3},{3,4},{4,5},{5,6},{6,7},{8,9},{9,10},{10,11},{11... | collective-permute-start | bytes 614408 | tf_op jit(solution)/shard_map/ppermute | solution.py:236
  17.5 0.1 pad.9.clone
  17.6 0.0 collective-permute-done.3
  17.6 0.2 fusion.2
  17.9 7.6 %collective-permute-done.2 = f32[2,25,8,128]{3,2,1,0:T(8,128)S(1)} collective-permute-done((f32[2,25,8,128]{3,2,1,0:T(8,128)}, f32[2,25,8,128]{3,2,1,0:T(8,128)S(1)}, u32[]{:S(2)}, u32[]{:S(2)}) %collective-permute-start.2) | collective-permute-done | bytes 204832 | tf_op jit(solution)/shard_map/ppermute | solution.py:236
  25.6 0.0 collective-permute-done.4
  25.6 0.1 slice_select_fusion.1
  25.7 0.0 copy-start.4
  25.7 0.1 maximum_maximum_fusion.yh_ref
  25.8 0.0 collective-permute-done.1.xw_ref
  25.8 0.0 collective-permute-done.xe_ref
  25.8 0.0 copy-done.3
  25.8 0.0 copy-done.2
  25.8 0.6 copy-done.4
  26.4 0.0 copy-start.1
  26.4 10.4 %shard_map.95 = (f32[25,64,128]{2,1,0:T(8,128)S(1)}, f32[25,64,128]{2,1,0:T(8,128)S(1)}, f32[25,64,128]{2,1,0:T(8,128)S(1)}, f32[25,64,128]{2,1,0:T(8,128)S(1)},...) custom-call(s32[64,128]{1,0:T(8,128)S(1)} %copy-done.4, f32[25,64,128]{2,1,0:T(8,128)S(1)} %copy-done.2, ...), custom_call_target="tpu_custom_call" | custom-call | flops 163840000 | bytes 12288000 | tf_op jit(solution)/shard_map/pallas_call | solution.py:218
  36.9 0.0 copy-start
  36.9 0.8 %collective-permute-start.8 = (f32[2,25,8,128]{3,2,1,0:T(8,128)S(1)}, f32[2,25,8,128]{3,2,1,0:T(8,128)S(1)}, u32[]{:S(2)}, u32[]{:S(2)}) collective-permute-start(f32[2,25,8,128]{3,2,1,0:T(8,128)S(1)} %get-tuple-element.18), channel_id=1, source_target_pairs={{7,127},{15,119},{23,111},{31,103},{39,95},{47,87},{55,79},{63,71}... | collective-permute-start | bytes 614408 | tf_op jit(solution)/shard_map/ppermute | solution.py:239
  37.7 0.1 collective-permute-start.6
  37.8 5.3 %collective-permute-start.5 = (f32[2,25,8,128]{3,2,1,0:T(8,128)S(1)}, f32[2,25,8,128]{3,2,1,0:T(8,128)S(1)}, u32[]{:S(2)}, u32[]{:S(2)}) collective-permute-start(f32[2,25,8,128]{3,2,1,0:T(8,128)S(1)} %get-tuple-element.17), channel_id=1, source_target_pairs={{0,120},{8,0},{16,8},{24,16},{32,24},{40,32},{48,40},{56,48},{64,5... | collective-permute-start | bytes 614408 | tf_op jit(solution)/shard_map/ppermute | solution.py:233
  43.1 1.9 %collective-permute-start.9 = (f32[2,25,8,128]{3,2,1,0:T(8,128)S(1)}, f32[2,25,8,128]{3,2,1,0:T(8,128)S(1)}, u32[]{:S(2)}, u32[]{:S(2)}) collective-permute-start(f32[2,25,8,128]{3,2,1,0:T(8,128)S(1)} %get-tuple-element.18), channel_id=1, source_target_pairs={{1,0},{2,1},{3,2},{4,3},{5,4},{6,5},{7,6},{9,8},{10,9},{11,10},{12... | collective-permute-start | bytes 614408 | tf_op jit(solution)/shard_map/ppermute | solution.py:235
  45.0 3.9 %collective-permute-start.7 = (f32[2,25,8,128]{3,2,1,0:T(8,128)S(1)}, f32[2,25,8,128]{3,2,1,0:T(8,128)S(1)}, u32[]{:S(2)}, u32[]{:S(2)}) collective-permute-start(f32[2,25,8,128]{3,2,1,0:T(8,128)S(1)} %get-tuple-element.18), channel_id=1, source_target_pairs={{0,1},{1,2},{2,3},{3,4},{4,5},{5,6},{6,7},{8,9},{9,10},{10,11},{11... | collective-permute-start | bytes 614408 | tf_op jit(solution)/shard_map/ppermute | solution.py:236
  49.0 0.0 collective-permute-done.8
  49.0 0.2 fusion
  49.3 5.5 %collective-permute-done.7 = f32[2,25,8,128]{3,2,1,0:T(8,128)S(1)} collective-permute-done((f32[2,25,8,128]{3,2,1,0:T(8,128)S(1)}, f32[2,25,8,128]{3,2,1,0:T(8,128)S(1)}, u32[]{:S(2)}, u32[]{:S(2)}) %collective-permute-start.7) | collective-permute-done | bytes 204832 | tf_op jit(solution)/shard_map/ppermute | solution.py:236
  54.9 0.0 collective-permute-done.9
  54.9 0.1 slice_select_fusion
  54.9 0.1 maximum_maximum_fusion.1.yh_ref
  55.0 0.0 collective-permute-done.6.xw_ref
  55.0 0.0 collective-permute-done.5.xe_ref
  55.1 0.0 copy-done.1
  55.1 0.0 copy-done
  55.1 8.5 %shard_map.96 = (f32[25,64,128]{2,1,0:T(8,128)}, f32[25,64,128]{2,1,0:T(8,128)}, f32[25,64,128]{2,1,0:T(8,128)}) custom-call(s32[64,128]{1,0:T(8,128)S(1)} %copy-done.4, f32[25,64,128]{2,1,0:T(8,128)S(1)} %get-tuple-element.13.nt_ref, f32[25,64,128]{2,1,0:T(8,128)S(1)} %get-tuple-element.14.ns_ref, f32[25,64,128]{2,1,0:T(8,128)S(1)} %get-tuple-element.15.bt_ref, ...), custom_call_target="tpu_custom_call" | custom-call | flops 163840000 | bytes 9830400 | tf_op jit(solution)/shard_map/pallas_call | solution.py:218
  (13 shorter events, 0.3 us)
Async XLA Ops:
  0.6 25.2 %copy-start.3 = (f32[25,64,128]{2,1,0:T(8,128)S(1)}, f32[25,64,128]{2,1,0:T(8,128)}, u32[]{:S(2)}) copy-start(f32[25,64,128]{2,1,0:T(8,128)} %ns_ref.3) | copy-start | bytes 2457604
  4.0 21.9 %copy-start.2 = (f32[25,64,128]{2,1,0:T(8,128)S(1)}, f32[25,64,128]{2,1,0:T(8,128)}, u32[]{:S(2)}) copy-start(f32[25,64,128]{2,1,0:T(8,128)} %nt_ref.3) | copy-start | bytes 2457604
  4.0 13.6 %collective-permute-start.3 = (f32[2,25,8,128]{3,2,1,0:T(8,128)}, f32[2,25,8,128]{3,2,1,0:T(8,128)S(1)}, u32[]{:S(2)}, u32[]{:S(2)}) collective-permute-start(f32[2,25,8,128]{3,2,1,0:T(8,128)} %get-tuple-element.12), channel_id=1, source_target_pairs={{7,127},{15,119},{23,111},{31,103},{39,95},{47,87},{55,79},{63,71}... | collective-permute-start | bytes 614408 | tf_op jit(solution)/shard_map/ppermute | solution.py:239
  4.8 21.0 %collective-permute-start.1 = (f32[2,25,8,128]{3,2,1,0:T(8,128)}, f32[2,25,8,128]{3,2,1,0:T(8,128)S(1)}, u32[]{:S(2)}, u32[]{:S(2)}) collective-permute-start(f32[2,25,8,128]{3,2,1,0:T(8,128)} %get-tuple-element.11), channel_id=1, source_target_pairs={{0,8},{8,16},{16,24},{24,32},{32,40},{40,48},{48,56},{56,64},{64,7... | collective-permute-start | bytes 614408 | tf_op jit(solution)/shard_map/ppermute | solution.py:234
  4.8 20.9 %collective-permute-start = (f32[2,25,8,128]{3,2,1,0:T(8,128)}, f32[2,25,8,128]{3,2,1,0:T(8,128)S(1)}, u32[]{:S(2)}, u32[]{:S(2)}) collective-permute-start(f32[2,25,8,128]{3,2,1,0:T(8,128)} %get-tuple-element.11), channel_id=1, source_target_pairs={{0,120},{8,0},{16,8},{24,16},{32,24},{40,32},{48,40},{56,48},{64,5... | collective-permute-start | bytes 614408 | tf_op jit(solution)/shard_map/ppermute | solution.py:233
  10.2 15.4 %collective-permute-start.4 = (f32[2,25,8,128]{3,2,1,0:T(8,128)}, f32[2,25,8,128]{3,2,1,0:T(8,128)S(1)}, u32[]{:S(2)}, u32[]{:S(2)}) collective-permute-start(f32[2,25,8,128]{3,2,1,0:T(8,128)} %get-tuple-element.12), channel_id=1, source_target_pairs={{1,0},{2,1},{3,2},{4,3},{5,4},{6,5},{7,6},{9,8},{10,9},{11,10},{12... | collective-permute-start | bytes 614408 | tf_op jit(solution)/shard_map/ppermute | solution.py:235
  15.6 10.0 %collective-permute-start.2 = (f32[2,25,8,128]{3,2,1,0:T(8,128)}, f32[2,25,8,128]{3,2,1,0:T(8,128)S(1)}, u32[]{:S(2)}, u32[]{:S(2)}) collective-permute-start(f32[2,25,8,128]{3,2,1,0:T(8,128)} %get-tuple-element.12), channel_id=1, source_target_pairs={{0,1},{1,2},{2,3},{3,4},{4,5},{5,6},{6,7},{8,9},{9,10},{10,11},{11... | collective-permute-start | bytes 614408 | tf_op jit(solution)/shard_map/ppermute | solution.py:236
  25.7 0.8 %copy-start.4 = (s32[64,128]{1,0:T(8,128)S(1)}, s32[64,128]{1,0:T(8,128)}, u32[]{:S(2)}) copy-start(s32[64,128]{1,0:T(8,128)} %bl_ref.5) | copy-start | bytes 98308
  26.4 28.6 %copy-start.1 = (f32[25,64,128]{2,1,0:T(8,128)S(1)}, f32[25,64,128]{2,1,0:T(8,128)}, u32[]{:S(2)}) copy-start(f32[25,64,128]{2,1,0:T(8,128)} %vn_ref.5) | copy-start | bytes 2457604
  36.9 18.2 %copy-start = (f32[25,64,128]{2,1,0:T(8,128)S(1)}, f32[25,64,128]{2,1,0:T(8,128)}, u32[]{:S(2)}) copy-start(f32[25,64,128]{2,1,0:T(8,128)} %ue_ref.5) | copy-start | bytes 2457604
  36.9 12.1 %collective-permute-start.8 = (f32[2,25,8,128]{3,2,1,0:T(8,128)S(1)}, f32[2,25,8,128]{3,2,1,0:T(8,128)S(1)}, u32[]{:S(2)}, u32[]{:S(2)}) collective-permute-start(f32[2,25,8,128]{3,2,1,0:T(8,128)S(1)} %get-tuple-element.18), channel_id=1, source_target_pairs={{7,127},{15,119},{23,111},{31,103},{39,95},{47,87},{55,79},{63,71}... | collective-permute-start | bytes 614408 | tf_op jit(solution)/shard_map/ppermute | solution.py:239
  37.7 17.3 %collective-permute-start.6 = (f32[2,25,8,128]{3,2,1,0:T(8,128)S(1)}, f32[2,25,8,128]{3,2,1,0:T(8,128)S(1)}, u32[]{:S(2)}, u32[]{:S(2)}) collective-permute-start(f32[2,25,8,128]{3,2,1,0:T(8,128)S(1)} %get-tuple-element.17), channel_id=1, source_target_pairs={{0,8},{8,16},{16,24},{24,32},{32,40},{40,48},{48,56},{56,64},{64,7... | collective-permute-start | bytes 614408 | tf_op jit(solution)/shard_map/ppermute | solution.py:234
  37.8 17.3 %collective-permute-start.5 = (f32[2,25,8,128]{3,2,1,0:T(8,128)S(1)}, f32[2,25,8,128]{3,2,1,0:T(8,128)S(1)}, u32[]{:S(2)}, u32[]{:S(2)}) collective-permute-start(f32[2,25,8,128]{3,2,1,0:T(8,128)S(1)} %get-tuple-element.17), channel_id=1, source_target_pairs={{0,120},{8,0},{16,8},{24,16},{32,24},{40,32},{48,40},{56,48},{64,5... | collective-permute-start | bytes 614408 | tf_op jit(solution)/shard_map/ppermute | solution.py:233
  43.1 11.7 %collective-permute-start.9 = (f32[2,25,8,128]{3,2,1,0:T(8,128)S(1)}, f32[2,25,8,128]{3,2,1,0:T(8,128)S(1)}, u32[]{:S(2)}, u32[]{:S(2)}) collective-permute-start(f32[2,25,8,128]{3,2,1,0:T(8,128)S(1)} %get-tuple-element.18), channel_id=1, source_target_pairs={{1,0},{2,1},{3,2},{4,3},{5,4},{6,5},{7,6},{9,8},{10,9},{11,10},{12... | collective-permute-start | bytes 614408 | tf_op jit(solution)/shard_map/ppermute | solution.py:235
  45.0 9.8 %collective-permute-start.7 = (f32[2,25,8,128]{3,2,1,0:T(8,128)S(1)}, f32[2,25,8,128]{3,2,1,0:T(8,128)S(1)}, u32[]{:S(2)}, u32[]{:S(2)}) collective-permute-start(f32[2,25,8,128]{3,2,1,0:T(8,128)S(1)} %get-tuple-element.18), channel_id=1, source_target_pairs={{0,1},{1,2},{2,3},{3,4},{4,5},{5,6},{6,7},{8,9},{9,10},{10,11},{11... | collective-permute-start | bytes 614408 | tf_op jit(solution)/shard_map/ppermute | solution.py:236

commit v15 on v14

--- a/solution.py
+++ b/solution.py
@@ -65,8 +65,11 @@
     rows, cols = value.shape
     ypack_ref[f, k, 0:2, :] = value[0:2]
     ypack_ref[f, k, 2:4, :] = value[rows - 2:rows]
-    ypack_ref[f, k, 4:5, :] = north_v[rows - 1:rows]
-    ypack_ref[f, k, 5:8, :] = jnp.zeros((3, cols), jnp.float32)
+    if f == 0:
+        ypack_ref[f, k, 4:5, :] = north_v[rows - 1:rows]
+        ypack_ref[f, k, 5:8, :] = jnp.zeros((3, cols), jnp.float32)
+    else:
+        ypack_ref[f, k, 4:8, :] = jnp.zeros((4, cols), jnp.float32)
 
 
 def edge_kernel(bl_ref, nt_ref, ns_ref, ue_ref, vn_ref, xpack_ref, ypack_ref):

time: 64.1 us -> 64.1 us (level)
  no operation moved by 1% of the time
where the time goes in v15:
time: 64.1 us; the launch traced here: 63.6 us
  starting transfers between devices  25.6 us (40%)
  Pallas kernels  22.3 us (35%)
  waiting for transfers between devices  13.2 us (21%)
  local copies, waits for them, and re-layouts  0.99 us (2%)
  between operations  0.94 us (1%)
    pallas_call x2, Pallas kernels, step_call(): pl.pallas_call(functools.partial(step_kernel, mask_inputs, final), out_sh...  18.9 us
    ppermute x2, waiting for transfers between devices, exchange(): lax.ppermute(ypack, 'lat', [(i, i + 1) for i in range(lat_count - 1)])  13.2 us
    ppermute x2, starting transfers between devices, exchange(): lax.ppermute(xpack, 'lon', [(i, (i - 1) % lon_count) for i in range(lon_c...  10.7 us
    ppermute x2, starting transfers between devices, exchange(): lax.ppermute(ypack, 'lat', [(i, i - 1) for i in range(1, lat_count)])  7.28 us
    ppermute x2, starting transfers between devices, exchange(): lax.ppermute(ypack, 'lat', [(i, i + 1) for i in range(lat_count - 1)])  5.84 us
    pallas_call x1, Pallas kernels, edge_call(): pl.pallas_call(edge_kernel, out_shape=pack_shapes(levels, rows, cols), in...  3.31 us
    ppermute x2, starting transfers between devices, exchange(): partner = lax.ppermute(ypack, ('lon', 'lat'), fold_pairs)[:, :, 2:4]  1.6 us
  transfers between devices with their start and end apart: 10, of which 2 were waited for; matrix products, arithmetic and copies ran while one was open for 2% of the time, Pallas kernels for 0%

profile of v15, /device:TPU:8, one launch (start us, length us, event | category | flops | bytes accessed | tf_op | source)
XLA Modules:
  0.0 63.6 jit_solution(6900656773769345178)
XLA Ops:
  0.6 0.0 copy-start.3
  0.6 3.3 %shard_map.94 = (f32[2,25,8,128]{3,2,1,0:T(8,128)}, f32[2,25,8,128]{3,2,1,0:T(8,128)}) custom-call(s32[64,128]{1,0:T(8,128)} %bl_ref.5, f32[25,64,128]{2,1,0:T(8,128)} %nt_ref.3, f32[25,64,128]{2,1,0:T(8,128)} %ns_ref.3, f32[25,64,128]{2,1,0:T(8,128)} %ue_ref.5, f32[25,64,128]{2,1,0:T(8,128)} %vn_ref.5), custom_call_target="tpu_custom_call" | custom-call | flops 6553600 | bytes 4096000 | tf_op jit(solution)/shard_map/pallas_call | solution.py:206
  3.9 0.0 copy-start.2
  4.0 0.8 %collective-permute-start.3 = (f32[2,25,8,128]{3,2,1,0:T(8,128)}, f32[2,25,8,128]{3,2,1,0:T(8,128)S(1)}, u32[]{:S(2)}, u32[]{:S(2)}) collective-permute-start(f32[2,25,8,128]{3,2,1,0:T(8,128)} %get-tuple-element.12), channel_id=1, source_target_pairs={{7,127},{15,119},{23,111},{31,103},{39,95},{47,87},{55,79},{63,71}... | collective-permute-start | bytes 614408 | tf_op jit(solution)/shard_map/ppermute | solution.py:242
  4.8 0.1 collective-permute-start.1
  4.8 5.3 %collective-permute-start = (f32[2,25,8,128]{3,2,1,0:T(8,128)}, f32[2,25,8,128]{3,2,1,0:T(8,128)S(1)}, u32[]{:S(2)}, u32[]{:S(2)}) collective-permute-start(f32[2,25,8,128]{3,2,1,0:T(8,128)} %get-tuple-element.11), channel_id=1, source_target_pairs={{0,120},{8,0},{16,8},{24,16},{32,24},{40,32},{48,40},{56,48},{64,5... | collective-permute-start | bytes 614408 | tf_op jit(solution)/shard_map/ppermute | solution.py:236
  10.2 5.4 %collective-permute-start.4 = (f32[2,25,8,128]{3,2,1,0:T(8,128)}, f32[2,25,8,128]{3,2,1,0:T(8,128)S(1)}, u32[]{:S(2)}, u32[]{:S(2)}) collective-permute-start(f32[2,25,8,128]{3,2,1,0:T(8,128)} %get-tuple-element.12), channel_id=1, source_target_pairs={{1,0},{2,1},{3,2},{4,3},{5,4},{6,5},{7,6},{9,8},{10,9},{11,10},{12... | collective-permute-start | bytes 614408 | tf_op jit(solution)/shard_map/ppermute | solution.py:238
  15.6 1.9 %collective-permute-start.2 = (f32[2,25,8,128]{3,2,1,0:T(8,128)}, f32[2,25,8,128]{3,2,1,0:T(8,128)S(1)}, u32[]{:S(2)}, u32[]{:S(2)}) collective-permute-start(f32[2,25,8,128]{3,2,1,0:T(8,128)} %get-tuple-element.12), channel_id=1, source_target_pairs={{0,1},{1,2},{2,3},{3,4},{4,5},{5,6},{6,7},{8,9},{9,10},{10,11},{11... | collective-permute-start | bytes 614408 | tf_op jit(solution)/shard_map/ppermute | solution.py:239
  17.5 0.1 pad.9.clone
  17.6 0.0 collective-permute-done.3
  17.6 0.2 fusion.2
  17.9 7.6 %collective-permute-done.2 = f32[2,25,8,128]{3,2,1,0:T(8,128)S(1)} collective-permute-done((f32[2,25,8,128]{3,2,1,0:T(8,128)}, f32[2,25,8,128]{3,2,1,0:T(8,128)S(1)}, u32[]{:S(2)}, u32[]{:S(2)}) %collective-permute-start.2) | collective-permute-done | bytes 204832 | tf_op jit(solution)/shard_map/ppermute | solution.py:239
  25.6 0.0 collective-permute-done.4
  25.6 0.1 slice_select_fusion.1
  25.7 0.0 copy-start.4
  25.7 0.1 maximum_maximum_fusion.yh_ref
  25.8 0.0 collective-permute-done.1.xw_ref
  25.8 0.0 collective-permute-done.xe_ref
  25.8 0.0 copy-done.3
  25.8 0.0 copy-done.2
  25.8 0.6 copy-done.4
  26.4 0.0 copy-start.1
  26.4 10.4 %shard_map.95 = (f32[25,64,128]{2,1,0:T(8,128)S(1)}, f32[25,64,128]{2,1,0:T(8,128)S(1)}, f32[25,64,128]{2,1,0:T(8,128)S(1)}, f32[25,64,128]{2,1,0:T(8,128)S(1)},...) custom-call(s32[64,128]{1,0:T(8,128)S(1)} %copy-done.4, f32[25,64,128]{2,1,0:T(8,128)S(1)} %copy-done.2, ...), custom_call_target="tpu_custom_call" | custom-call | flops 163840000 | bytes 12288000 | tf_op jit(solution)/shard_map/pallas_call | solution.py:221
  36.9 0.0 copy-start
  36.9 0.8 %collective-permute-start.8 = (f32[2,25,8,128]{3,2,1,0:T(8,128)S(1)}, f32[2,25,8,128]{3,2,1,0:T(8,128)S(1)}, u32[]{:S(2)}, u32[]{:S(2)}) collective-permute-start(f32[2,25,8,128]{3,2,1,0:T(8,128)S(1)} %get-tuple-element.18), channel_id=1, source_target_pairs={{7,127},{15,119},{23,111},{31,103},{39,95},{47,87},{55,79},{63,71}... | collective-permute-start | bytes 614408 | tf_op jit(solution)/shard_map/ppermute | solution.py:242
  37.7 0.1 collective-permute-start.6
  37.8 5.3 %collective-permute-start.5 = (f32[2,25,8,128]{3,2,1,0:T(8,128)S(1)}, f32[2,25,8,128]{3,2,1,0:T(8,128)S(1)}, u32[]{:S(2)}, u32[]{:S(2)}) collective-permute-start(f32[2,25,8,128]{3,2,1,0:T(8,128)S(1)} %get-tuple-element.17), channel_id=1, source_target_pairs={{0,120},{8,0},{16,8},{24,16},{32,24},{40,32},{48,40},{56,48},{64,5... | collective-permute-start | bytes 614408 | tf_op jit(solution)/shard_map/ppermute | solution.py:236
  43.1 1.9 %collective-permute-start.9 = (f32[2,25,8,128]{3,2,1,0:T(8,128)S(1)}, f32[2,25,8,128]{3,2,1,0:T(8,128)S(1)}, u32[]{:S(2)}, u32[]{:S(2)}) collective-permute-start(f32[2,25,8,128]{3,2,1,0:T(8,128)S(1)} %get-tuple-element.18), channel_id=1, source_target_pairs={{1,0},{2,1},{3,2},{4,3},{5,4},{6,5},{7,6},{9,8},{10,9},{11,10},{12... | collective-permute-start | bytes 614408 | tf_op jit(solution)/shard_map/ppermute | solution.py:238
  45.0 3.9 %collective-permute-start.7 = (f32[2,25,8,128]{3,2,1,0:T(8,128)S(1)}, f32[2,25,8,128]{3,2,1,0:T(8,128)S(1)}, u32[]{:S(2)}, u32[]{:S(2)}) collective-permute-start(f32[2,25,8,128]{3,2,1,0:T(8,128)S(1)} %get-tuple-element.18), channel_id=1, source_target_pairs={{0,1},{1,2},{2,3},{3,4},{4,5},{5,6},{6,7},{8,9},{9,10},{10,11},{11... | collective-permute-start | bytes 614408 | tf_op jit(solution)/shard_map/ppermute | solution.py:239
  49.0 0.0 collective-permute-done.8
  49.0 0.2 fusion
  49.3 5.5 %collective-permute-done.7 = f32[2,25,8,128]{3,2,1,0:T(8,128)S(1)} collective-permute-done((f32[2,25,8,128]{3,2,1,0:T(8,128)S(1)}, f32[2,25,8,128]{3,2,1,0:T(8,128)S(1)}, u32[]{:S(2)}, u32[]{:S(2)}) %collective-permute-start.7) | collective-permute-done | bytes 204832 | tf_op jit(solution)/shard_map/ppermute | solution.py:239
  54.9 0.0 collective-permute-done.9
  54.9 0.1 slice_select_fusion
  54.9 0.1 maximum_maximum_fusion.1.yh_ref
  55.0 0.0 collective-permute-done.6.xw_ref
  55.0 0.0 collective-permute-done.5.xe_ref
  55.1 0.0 copy-done.1
  55.1 0.0 copy-done
  55.1 8.5 %shard_map.96 = (f32[25,64,128]{2,1,0:T(8,128)}, f32[25,64,128]{2,1,0:T(8,128)}, f32[25,64,128]{2,1,0:T(8,128)}) custom-call(s32[64,128]{1,0:T(8,128)S(1)} %copy-done.4, f32[25,64,128]{2,1,0:T(8,128)S(1)} %get-tuple-element.13.nt_ref, f32[25,64,128]{2,1,0:T(8,128)S(1)} %get-tuple-element.14.ns_ref, f32[25,64,128]{2,1,0:T(8,128)S(1)} %get-tuple-element.15.bt_ref, ...), custom_call_target="tpu_custom_call" | custom-call | flops 163840000 | bytes 9830400 | tf_op jit(solution)/shard_map/pallas_call | solution.py:221
  (13 shorter events, 0.3 us)
Async XLA Ops:
  0.6 25.2 %copy-start.3 = (f32[25,64,128]{2,1,0:T(8,128)S(1)}, f32[25,64,128]{2,1,0:T(8,128)}, u32[]{:S(2)}) copy-start(f32[25,64,128]{2,1,0:T(8,128)} %ns_ref.3) | copy-start | bytes 2457604
  3.9 21.9 %copy-start.2 = (f32[25,64,128]{2,1,0:T(8,128)S(1)}, f32[25,64,128]{2,1,0:T(8,128)}, u32[]{:S(2)}) copy-start(f32[25,64,128]{2,1,0:T(8,128)} %nt_ref.3) | copy-start | bytes 2457604
  4.0 13.6 %collective-permute-start.3 = (f32[2,25,8,128]{3,2,1,0:T(8,128)}, f32[2,25,8,128]{3,2,1,0:T(8,128)S(1)}, u32[]{:S(2)}, u32[]{:S(2)}) collective-permute-start(f32[2,25,8,128]{3,2,1,0:T(8,128)} %get-tuple-element.12), channel_id=1, source_target_pairs={{7,127},{15,119},{23,111},{31,103},{39,95},{47,87},{55,79},{63,71}... | collective-permute-start | bytes 614408 | tf_op jit(solution)/shard_map/ppermute | solution.py:242
  4.8 21.0 %collective-permute-start.1 = (f32[2,25,8,128]{3,2,1,0:T(8,128)}, f32[2,25,8,128]{3,2,1,0:T(8,128)S(1)}, u32[]{:S(2)}, u32[]{:S(2)}) collective-permute-start(f32[2,25,8,128]{3,2,1,0:T(8,128)} %get-tuple-element.11), channel_id=1, source_target_pairs={{0,8},{8,16},{16,24},{24,32},{32,40},{40,48},{48,56},{56,64},{64,7... | collective-permute-start | bytes 614408 | tf_op jit(solution)/shard_map/ppermute | solution.py:237
  4.8 20.9 %collective-permute-start = (f32[2,25,8,128]{3,2,1,0:T(8,128)}, f32[2,25,8,128]{3,2,1,0:T(8,128)S(1)}, u32[]{:S(2)}, u32[]{:S(2)}) collective-permute-start(f32[2,25,8,128]{3,2,1,0:T(8,128)} %get-tuple-element.11), channel_id=1, source_target_pairs={{0,120},{8,0},{16,8},{24,16},{32,24},{40,32},{48,40},{56,48},{64,5... | collective-permute-start | bytes 614408 | tf_op jit(solution)/shard_map/ppermute | solution.py:236
  10.2 15.4 %collective-permute-start.4 = (f32[2,25,8,128]{3,2,1,0:T(8,128)}, f32[2,25,8,128]{3,2,1,0:T(8,128)S(1)}, u32[]{:S(2)}, u32[]{:S(2)}) collective-permute-start(f32[2,25,8,128]{3,2,1,0:T(8,128)} %get-tuple-element.12), channel_id=1, source_target_pairs={{1,0},{2,1},{3,2},{4,3},{5,4},{6,5},{7,6},{9,8},{10,9},{11,10},{12... | collective-permute-start | bytes 614408 | tf_op jit(solution)/shard_map/ppermute | solution.py:238
  15.6 10.0 %collective-permute-start.2 = (f32[2,25,8,128]{3,2,1,0:T(8,128)}, f32[2,25,8,128]{3,2,1,0:T(8,128)S(1)}, u32[]{:S(2)}, u32[]{:S(2)}) collective-permute-start(f32[2,25,8,128]{3,2,1,0:T(8,128)} %get-tuple-element.12), channel_id=1, source_target_pairs={{0,1},{1,2},{2,3},{3,4},{4,5},{5,6},{6,7},{8,9},{9,10},{10,11},{11... | collective-permute-start | bytes 614408 | tf_op jit(solution)/shard_map/ppermute | solution.py:239
  25.7 0.8 %copy-start.4 = (s32[64,128]{1,0:T(8,128)S(1)}, s32[64,128]{1,0:T(8,128)}, u32[]{:S(2)}) copy-start(s32[64,128]{1,0:T(8,128)} %bl_ref.5) | copy-start | bytes 98308
  26.4 28.6 %copy-start.1 = (f32[25,64,128]{2,1,0:T(8,128)S(1)}, f32[25,64,128]{2,1,0:T(8,128)}, u32[]{:S(2)}) copy-start(f32[25,64,128]{2,1,0:T(8,128)} %vn_ref.5) | copy-start | bytes 2457604
  36.9 18.2 %copy-start = (f32[25,64,128]{2,1,0:T(8,128)S(1)}, f32[25,64,128]{2,1,0:T(8,128)}, u32[]{:S(2)}) copy-start(f32[25,64,128]{2,1,0:T(8,128)} %ue_ref.5) | copy-start | bytes 2457604
  36.9 12.1 %collective-permute-start.8 = (f32[2,25,8,128]{3,2,1,0:T(8,128)S(1)}, f32[2,25,8,128]{3,2,1,0:T(8,128)S(1)}, u32[]{:S(2)}, u32[]{:S(2)}) collective-permute-start(f32[2,25,8,128]{3,2,1,0:T(8,128)S(1)} %get-tuple-element.18), channel_id=1, source_target_pairs={{7,127},{15,119},{23,111},{31,103},{39,95},{47,87},{55,79},{63,71}... | collective-permute-start | bytes 614408 | tf_op jit(solution)/shard_map/ppermute | solution.py:242
  37.7 17.3 %collective-permute-start.6 = (f32[2,25,8,128]{3,2,1,0:T(8,128)S(1)}, f32[2,25,8,128]{3,2,1,0:T(8,128)S(1)}, u32[]{:S(2)}, u32[]{:S(2)}) collective-permute-start(f32[2,25,8,128]{3,2,1,0:T(8,128)S(1)} %get-tuple-element.17), channel_id=1, source_target_pairs={{0,8},{8,16},{16,24},{24,32},{32,40},{40,48},{48,56},{56,64},{64,7... | collective-permute-start | bytes 614408 | tf_op jit(solution)/shard_map/ppermute | solution.py:237
  37.8 17.3 %collective-permute-start.5 = (f32[2,25,8,128]{3,2,1,0:T(8,128)S(1)}, f32[2,25,8,128]{3,2,1,0:T(8,128)S(1)}, u32[]{:S(2)}, u32[]{:S(2)}) collective-permute-start(f32[2,25,8,128]{3,2,1,0:T(8,128)S(1)} %get-tuple-element.17), channel_id=1, source_target_pairs={{0,120},{8,0},{16,8},{24,16},{32,24},{40,32},{48,40},{56,48},{64,5... | collective-permute-start | bytes 614408 | tf_op jit(solution)/shard_map/ppermute | solution.py:236
  43.1 11.7 %collective-permute-start.9 = (f32[2,25,8,128]{3,2,1,0:T(8,128)S(1)}, f32[2,25,8,128]{3,2,1,0:T(8,128)S(1)}, u32[]{:S(2)}, u32[]{:S(2)}) collective-permute-start(f32[2,25,8,128]{3,2,1,0:T(8,128)S(1)} %get-tuple-element.18), channel_id=1, source_target_pairs={{1,0},{2,1},{3,2},{4,3},{5,4},{6,5},{7,6},{9,8},{10,9},{11,10},{12... | collective-permute-start | bytes 614408 | tf_op jit(solution)/shard_map/ppermute | solution.py:238
  45.0 9.8 %collective-permute-start.7 = (f32[2,25,8,128]{3,2,1,0:T(8,128)S(1)}, f32[2,25,8,128]{3,2,1,0:T(8,128)S(1)}, u32[]{:S(2)}, u32[]{:S(2)}) collective-permute-start(f32[2,25,8,128]{3,2,1,0:T(8,128)S(1)} %get-tuple-element.18), channel_id=1, source_target_pairs={{0,1},{1,2},{2,3},{3,4},{4,5},{5,6},{6,7},{8,9},{9,10},{10,11},{11... | collective-permute-start | bytes 614408 | tf_op jit(solution)/shard_map/ppermute | solution.py:239

commit v16 on v15

--- a/solution.py
+++ b/solution.py
@@ -67,9 +67,6 @@
     ypack_ref[f, k, 2:4, :] = value[rows - 2:rows]
     if f == 0:
         ypack_ref[f, k, 4:5, :] = north_v[rows - 1:rows]
-        ypack_ref[f, k, 5:8, :] = jnp.zeros((3, cols), jnp.float32)
-    else:
-        ypack_ref[f, k, 4:8, :] = jnp.zeros((4, cols), jnp.float32)
 
 
 def edge_kernel(bl_ref, nt_ref, ns_ref, ue_ref, vn_ref, xpack_ref, ypack_ref):

time: 64.1 us -> 64.1 us (level)
  no operation moved by 1% of the time
where the time goes in v16:
time: 64.1 us; the launch traced here: 63.6 us
  starting transfers between devices  25.6 us (40%)
  Pallas kernels  22.3 us (35%)
  waiting for transfers between devices  13.2 us (21%)
  local copies, waits for them, and re-layouts  0.99 us (2%)
  between operations  0.94 us (1%)
    pallas_call x2, Pallas kernels, step_call(): pl.pallas_call(functools.partial(step_kernel, mask_inputs, final), out_sh...  19 us
    ppermute x2, waiting for transfers between devices, exchange(): lax.ppermute(ypack, 'lat', [(i, i + 1) for i in range(lat_count - 1)])  13.2 us
    ppermute x2, starting transfers between devices, exchange(): lax.ppermute(xpack, 'lon', [(i, (i - 1) % lon_count) for i in range(lon_c...  10.7 us
    ppermute x2, starting transfers between devices, exchange(): lax.ppermute(ypack, 'lat', [(i, i - 1) for i in range(1, lat_count)])  7.28 us
    ppermute x2, starting transfers between devices, exchange(): lax.ppermute(ypack, 'lat', [(i, i + 1) for i in range(lat_count - 1)])  5.84 us
    pallas_call x1, Pallas kernels, edge_call(): pl.pallas_call(edge_kernel, out_shape=pack_shapes(levels, rows, cols), in...  3.31 us
    ppermute x2, starting transfers between devices, exchange(): partner = lax.ppermute(ypack, ('lon', 'lat'), fold_pairs)[:, :, 2:4]  1.6 us
  transfers between devices with their start and end apart: 10, of which 2 were waited for; matrix products, arithmetic and copies ran while one was open for 2% of the time, Pallas kernels for 0%

profile of v16, /device:TPU:8, one launch (start us, length us, event | category | flops | bytes accessed | tf_op | source)
XLA Modules:
  0.0 63.6 jit_solution(7674417868004031295)
XLA Ops:
  0.6 0.0 copy-start.3
  0.6 3.3 %shard_map.94 = (f32[2,25,8,128]{3,2,1,0:T(8,128)}, f32[2,25,8,128]{3,2,1,0:T(8,128)}) custom-call(s32[64,128]{1,0:T(8,128)} %bl_ref.5, f32[25,64,128]{2,1,0:T(8,128)} %nt_ref.3, f32[25,64,128]{2,1,0:T(8,128)} %ns_ref.3, f32[25,64,128]{2,1,0:T(8,128)} %ue_ref.5, f32[25,64,128]{2,1,0:T(8,128)} %vn_ref.5), custom_call_target="tpu_custom_call" | custom-call | flops 6553600 | bytes 4096000 | tf_op jit(solution)/shard_map/pallas_call | solution.py:203
  3.9 0.0 copy-start.2
  3.9 0.8 %collective-permute-start.3 = (f32[2,25,8,128]{3,2,1,0:T(8,128)}, f32[2,25,8,128]{3,2,1,0:T(8,128)S(1)}, u32[]{:S(2)}, u32[]{:S(2)}) collective-permute-start(f32[2,25,8,128]{3,2,1,0:T(8,128)} %get-tuple-element.12), channel_id=1, source_target_pairs={{7,127},{15,119},{23,111},{31,103},{39,95},{47,87},{55,79},{63,71}... | collective-permute-start | bytes 614408 | tf_op jit(solution)/shard_map/ppermute | solution.py:239
  4.8 0.1 collective-permute-start.1
  4.8 5.3 %collective-permute-start = (f32[2,25,8,128]{3,2,1,0:T(8,128)}, f32[2,25,8,128]{3,2,1,0:T(8,128)S(1)}, u32[]{:S(2)}, u32[]{:S(2)}) collective-permute-start(f32[2,25,8,128]{3,2,1,0:T(8,128)} %get-tuple-element.11), channel_id=1, source_target_pairs={{0,120},{8,0},{16,8},{24,16},{32,24},{40,32},{48,40},{56,48},{64,5... | collective-permute-start | bytes 614408 | tf_op jit(solution)/shard_map/ppermute | solution.py:233
  10.2 5.4 %collective-permute-start.4 = (f32[2,25,8,128]{3,2,1,0:T(8,128)}, f32[2,25,8,128]{3,2,1,0:T(8,128)S(1)}, u32[]{:S(2)}, u32[]{:S(2)}) collective-permute-start(f32[2,25,8,128]{3,2,1,0:T(8,128)} %get-tuple-element.12), channel_id=1, source_target_pairs={{1,0},{2,1},{3,2},{4,3},{5,4},{6,5},{7,6},{9,8},{10,9},{11,10},{12... | collective-permute-start | bytes 614408 | tf_op jit(solution)/shard_map/ppermute | solution.py:235
  15.6 1.9 %collective-permute-start.2 = (f32[2,25,8,128]{3,2,1,0:T(8,128)}, f32[2,25,8,128]{3,2,1,0:T(8,128)S(1)}, u32[]{:S(2)}, u32[]{:S(2)}) collective-permute-start(f32[2,25,8,128]{3,2,1,0:T(8,128)} %get-tuple-element.12), channel_id=1, source_target_pairs={{0,1},{1,2},{2,3},{3,4},{4,5},{5,6},{6,7},{8,9},{9,10},{10,11},{11... | collective-permute-start | bytes 614408 | tf_op jit(solution)/shard_map/ppermute | solution.py:236
  17.5 0.1 pad.9.clone
  17.6 0.0 collective-permute-done.3
  17.6 0.2 fusion.2
  17.9 7.6 %collective-permute-done.2 = f32[2,25,8,128]{3,2,1,0:T(8,128)S(1)} collective-permute-done((f32[2,25,8,128]{3,2,1,0:T(8,128)}, f32[2,25,8,128]{3,2,1,0:T(8,128)S(1)}, u32[]{:S(2)}, u32[]{:S(2)}) %collective-permute-start.2) | collective-permute-done | bytes 204832 | tf_op jit(solution)/shard_map/ppermute | solution.py:236
  25.6 0.0 collective-permute-done.4
  25.6 0.1 slice_select_fusion.1
  25.7 0.0 copy-start.4
  25.7 0.1 maximum_maximum_fusion.yh_ref
  25.8 0.0 collective-permute-done.1.xw_ref
  25.8 0.0 collective-permute-done.xe_ref
  25.8 0.0 copy-done.3
  25.8 0.0 copy-done.2
  25.8 0.6 copy-done.4
  26.4 0.0 copy-start.1
  26.4 10.4 %shard_map.95 = (f32[25,64,128]{2,1,0:T(8,128)S(1)}, f32[25,64,128]{2,1,0:T(8,128)S(1)}, f32[25,64,128]{2,1,0:T(8,128)S(1)}, f32[25,64,128]{2,1,0:T(8,128)S(1)},...) custom-call(s32[64,128]{1,0:T(8,128)S(1)} %copy-done.4, f32[25,64,128]{2,1,0:T(8,128)S(1)} %copy-done.2, ...), custom_call_target="tpu_custom_call" | custom-call | flops 163840000 | bytes 12288000 | tf_op jit(solution)/shard_map/pallas_call | solution.py:218
  36.9 0.0 copy-start
  36.9 0.8 %collective-permute-start.8 = (f32[2,25,8,128]{3,2,1,0:T(8,128)S(1)}, f32[2,25,8,128]{3,2,1,0:T(8,128)S(1)}, u32[]{:S(2)}, u32[]{:S(2)}) collective-permute-start(f32[2,25,8,128]{3,2,1,0:T(8,128)S(1)} %get-tuple-element.18), channel_id=1, source_target_pairs={{7,127},{15,119},{23,111},{31,103},{39,95},{47,87},{55,79},{63,71}... | collective-permute-start | bytes 614408 | tf_op jit(solution)/shard_map/ppermute | solution.py:239
  37.7 0.1 collective-permute-start.6
  37.8 5.3 %collective-permute-start.5 = (f32[2,25,8,128]{3,2,1,0:T(8,128)S(1)}, f32[2,25,8,128]{3,2,1,0:T(8,128)S(1)}, u32[]{:S(2)}, u32[]{:S(2)}) collective-permute-start(f32[2,25,8,128]{3,2,1,0:T(8,128)S(1)} %get-tuple-element.17), channel_id=1, source_target_pairs={{0,120},{8,0},{16,8},{24,16},{32,24},{40,32},{48,40},{56,48},{64,5... | collective-permute-start | bytes 614408 | tf_op jit(solution)/shard_map/ppermute | solution.py:233
  43.1 1.9 %collective-permute-start.9 = (f32[2,25,8,128]{3,2,1,0:T(8,128)S(1)}, f32[2,25,8,128]{3,2,1,0:T(8,128)S(1)}, u32[]{:S(2)}, u32[]{:S(2)}) collective-permute-start(f32[2,25,8,128]{3,2,1,0:T(8,128)S(1)} %get-tuple-element.18), channel_id=1, source_target_pairs={{1,0},{2,1},{3,2},{4,3},{5,4},{6,5},{7,6},{9,8},{10,9},{11,10},{12... | collective-permute-start | bytes 614408 | tf_op jit(solution)/shard_map/ppermute | solution.py:235
  45.0 3.9 %collective-permute-start.7 = (f32[2,25,8,128]{3,2,1,0:T(8,128)S(1)}, f32[2,25,8,128]{3,2,1,0:T(8,128)S(1)}, u32[]{:S(2)}, u32[]{:S(2)}) collective-permute-start(f32[2,25,8,128]{3,2,1,0:T(8,128)S(1)} %get-tuple-element.18), channel_id=1, source_target_pairs={{0,1},{1,2},{2,3},{3,4},{4,5},{5,6},{6,7},{8,9},{9,10},{10,11},{11... | collective-permute-start | bytes 614408 | tf_op jit(solution)/shard_map/ppermute | solution.py:236
  49.0 0.0 collective-permute-done.8
  49.0 0.2 fusion
  49.3 5.5 %collective-permute-done.7 = f32[2,25,8,128]{3,2,1,0:T(8,128)S(1)} collective-permute-done((f32[2,25,8,128]{3,2,1,0:T(8,128)S(1)}, f32[2,25,8,128]{3,2,1,0:T(8,128)S(1)}, u32[]{:S(2)}, u32[]{:S(2)}) %collective-permute-start.7) | collective-permute-done | bytes 204832 | tf_op jit(solution)/shard_map/ppermute | solution.py:236
  54.9 0.0 collective-permute-done.9
  54.9 0.1 slice_select_fusion
  54.9 0.1 maximum_maximum_fusion.1.yh_ref
  55.0 0.0 collective-permute-done.6.xw_ref
  55.0 0.0 collective-permute-done.5.xe_ref
  55.1 0.0 copy-done.1
  55.1 0.0 copy-done
  55.1 8.5 %shard_map.96 = (f32[25,64,128]{2,1,0:T(8,128)}, f32[25,64,128]{2,1,0:T(8,128)}, f32[25,64,128]{2,1,0:T(8,128)}) custom-call(s32[64,128]{1,0:T(8,128)S(1)} %copy-done.4, f32[25,64,128]{2,1,0:T(8,128)S(1)} %get-tuple-element.13.nt_ref, f32[25,64,128]{2,1,0:T(8,128)S(1)} %get-tuple-element.14.ns_ref, f32[25,64,128]{2,1,0:T(8,128)S(1)} %get-tuple-element.15.bt_ref, ...), custom_call_target="tpu_custom_call" | custom-call | flops 163840000 | bytes 9830400 | tf_op jit(solution)/shard_map/pallas_call | solution.py:218
  (13 shorter events, 0.3 us)
Async XLA Ops:
  0.6 25.2 %copy-start.3 = (f32[25,64,128]{2,1,0:T(8,128)S(1)}, f32[25,64,128]{2,1,0:T(8,128)}, u32[]{:S(2)}) copy-start(f32[25,64,128]{2,1,0:T(8,128)} %ns_ref.3) | copy-start | bytes 2457604
  3.9 21.9 %copy-start.2 = (f32[25,64,128]{2,1,0:T(8,128)S(1)}, f32[25,64,128]{2,1,0:T(8,128)}, u32[]{:S(2)}) copy-start(f32[25,64,128]{2,1,0:T(8,128)} %nt_ref.3) | copy-start | bytes 2457604
  3.9 13.6 %collective-permute-start.3 = (f32[2,25,8,128]{3,2,1,0:T(8,128)}, f32[2,25,8,128]{3,2,1,0:T(8,128)S(1)}, u32[]{:S(2)}, u32[]{:S(2)}) collective-permute-start(f32[2,25,8,128]{3,2,1,0:T(8,128)} %get-tuple-element.12), channel_id=1, source_target_pairs={{7,127},{15,119},{23,111},{31,103},{39,95},{47,87},{55,79},{63,71}... | collective-permute-start | bytes 614408 | tf_op jit(solution)/shard_map/ppermute | solution.py:239
  4.8 21.0 %collective-permute-start.1 = (f32[2,25,8,128]{3,2,1,0:T(8,128)}, f32[2,25,8,128]{3,2,1,0:T(8,128)S(1)}, u32[]{:S(2)}, u32[]{:S(2)}) collective-permute-start(f32[2,25,8,128]{3,2,1,0:T(8,128)} %get-tuple-element.11), channel_id=1, source_target_pairs={{0,8},{8,16},{16,24},{24,32},{32,40},{40,48},{48,56},{56,64},{64,7... | collective-permute-start | bytes 614408 | tf_op jit(solution)/shard_map/ppermute | solution.py:234
  4.8 20.9 %collective-permute-start = (f32[2,25,8,128]{3,2,1,0:T(8,128)}, f32[2,25,8,128]{3,2,1,0:T(8,128)S(1)}, u32[]{:S(2)}, u32[]{:S(2)}) collective-permute-start(f32[2,25,8,128]{3,2,1,0:T(8,128)} %get-tuple-element.11), channel_id=1, source_target_pairs={{0,120},{8,0},{16,8},{24,16},{32,24},{40,32},{48,40},{56,48},{64,5... | collective-permute-start | bytes 614408 | tf_op jit(solution)/shard_map/ppermute | solution.py:233
  10.2 15.4 %collective-permute-start.4 = (f32[2,25,8,128]{3,2,1,0:T(8,128)}, f32[2,25,8,128]{3,2,1,0:T(8,128)S(1)}, u32[]{:S(2)}, u32[]{:S(2)}) collective-permute-start(f32[2,25,8,128]{3,2,1,0:T(8,128)} %get-tuple-element.12), channel_id=1, source_target_pairs={{1,0},{2,1},{3,2},{4,3},{5,4},{6,5},{7,6},{9,8},{10,9},{11,10},{12... | collective-permute-start | bytes 614408 | tf_op jit(solution)/shard_map/ppermute | solution.py:235
  15.6 10.0 %collective-permute-start.2 = (f32[2,25,8,128]{3,2,1,0:T(8,128)}, f32[2,25,8,128]{3,2,1,0:T(8,128)S(1)}, u32[]{:S(2)}, u32[]{:S(2)}) collective-permute-start(f32[2,25,8,128]{3,2,1,0:T(8,128)} %get-tuple-element.12), channel_id=1, source_target_pairs={{0,1},{1,2},{2,3},{3,4},{4,5},{5,6},{6,7},{8,9},{9,10},{10,11},{11... | collective-permute-start | bytes 614408 | tf_op jit(solution)/shard_map/ppermute | solution.py:236
  25.7 0.8 %copy-start.4 = (s32[64,128]{1,0:T(8,128)S(1)}, s32[64,128]{1,0:T(8,128)}, u32[]{:S(2)}) copy-start(s32[64,128]{1,0:T(8,128)} %bl_ref.5) | copy-start | bytes 98308
  26.4 28.6 %copy-start.1 = (f32[25,64,128]{2,1,0:T(8,128)S(1)}, f32[25,64,128]{2,1,0:T(8,128)}, u32[]{:S(2)}) copy-start(f32[25,64,128]{2,1,0:T(8,128)} %vn_ref.5) | copy-start | bytes 2457604
  36.9 18.2 %copy-start = (f32[25,64,128]{2,1,0:T(8,128)S(1)}, f32[25,64,128]{2,1,0:T(8,128)}, u32[]{:S(2)}) copy-start(f32[25,64,128]{2,1,0:T(8,128)} %ue_ref.5) | copy-start | bytes 2457604
  36.9 12.1 %collective-permute-start.8 = (f32[2,25,8,128]{3,2,1,0:T(8,128)S(1)}, f32[2,25,8,128]{3,2,1,0:T(8,128)S(1)}, u32[]{:S(2)}, u32[]{:S(2)}) collective-permute-start(f32[2,25,8,128]{3,2,1,0:T(8,128)S(1)} %get-tuple-element.18), channel_id=1, source_target_pairs={{7,127},{15,119},{23,111},{31,103},{39,95},{47,87},{55,79},{63,71}... | collective-permute-start | bytes 614408 | tf_op jit(solution)/shard_map/ppermute | solution.py:239
  37.7 17.3 %collective-permute-start.6 = (f32[2,25,8,128]{3,2,1,0:T(8,128)S(1)}, f32[2,25,8,128]{3,2,1,0:T(8,128)S(1)}, u32[]{:S(2)}, u32[]{:S(2)}) collective-permute-start(f32[2,25,8,128]{3,2,1,0:T(8,128)S(1)} %get-tuple-element.17), channel_id=1, source_target_pairs={{0,8},{8,16},{16,24},{24,32},{32,40},{40,48},{48,56},{56,64},{64,7... | collective-permute-start | bytes 614408 | tf_op jit(solution)/shard_map/ppermute | solution.py:234
  37.8 17.3 %collective-permute-start.5 = (f32[2,25,8,128]{3,2,1,0:T(8,128)S(1)}, f32[2,25,8,128]{3,2,1,0:T(8,128)S(1)}, u32[]{:S(2)}, u32[]{:S(2)}) collective-permute-start(f32[2,25,8,128]{3,2,1,0:T(8,128)S(1)} %get-tuple-element.17), channel_id=1, source_target_pairs={{0,120},{8,0},{16,8},{24,16},{32,24},{40,32},{48,40},{56,48},{64,5... | collective-permute-start | bytes 614408 | tf_op jit(solution)/shard_map/ppermute | solution.py:233
  43.1 11.7 %collective-permute-start.9 = (f32[2,25,8,128]{3,2,1,0:T(8,128)S(1)}, f32[2,25,8,128]{3,2,1,0:T(8,128)S(1)}, u32[]{:S(2)}, u32[]{:S(2)}) collective-permute-start(f32[2,25,8,128]{3,2,1,0:T(8,128)S(1)} %get-tuple-element.18), channel_id=1, source_target_pairs={{1,0},{2,1},{3,2},{4,3},{5,4},{6,5},{7,6},{9,8},{10,9},{11,10},{12... | collective-permute-start | bytes 614408 | tf_op jit(solution)/shard_map/ppermute | solution.py:235
  45.0 9.8 %collective-permute-start.7 = (f32[2,25,8,128]{3,2,1,0:T(8,128)S(1)}, f32[2,25,8,128]{3,2,1,0:T(8,128)S(1)}, u32[]{:S(2)}, u32[]{:S(2)}) collective-permute-start(f32[2,25,8,128]{3,2,1,0:T(8,128)S(1)} %get-tuple-element.18), channel_id=1, source_target_pairs={{0,1},{1,2},{2,3},{3,4},{4,5},{5,6},{6,7},{8,9},{9,10},{10,11},{11... | collective-permute-start | bytes 614408 | tf_op jit(solution)/shard_map/ppermute | solution.py:236
